TPU v7x, 128 devices: a whole 4x4x4 slice. The times are simulated.
128 devices in a mesh: grp: 4 (over y_hi, core), blk: 32 (over x, z, y_lo).
Axes of the slice: x: 4, y: 4 (y_hi: 2, y_lo: 2; y = y_hi * 2 + y_lo), z: 4, core: 2. Of those that a mesh axis runs over, the one named last changes fastest.
Arguments:
- tokens: bfloat16 [16384, 2048], P(('grp', 'blk')), may hold values from -6 to 6
- expert_ids: int32 [16384, 6], P(('grp', 'blk')), may hold values from 0 to 7, all different within a row; in each aligned block of 128 rows (0 to 127, 128 to 255, ...) at most 128 rows name the same one
- gate_weights: float32 [16384, 6], P(('grp', 'blk')), may hold values from 0.1 to 1
- w_gate: bfloat16 [8, 1408, 2048], P('grp', 'blk'), may hold values from -0.125 to 0.125
- w_up: bfloat16 [8, 1408, 2048], P('grp', 'blk'), may hold values from -0.125 to 0.125
- w_down: bfloat16 [8, 1408, 2048], P('grp', 'blk'), may hold values from -0.15625 to 0.15625
Outputs:
- mixed: bfloat16 [16384, 2048], P(('grp', 'blk'))
Inputs may be any that keep to these rules, and one draw needn't show every extreme that they name: `expert_ids`: each token names 6 different experts. Among the tokens of one device (aligned blocks of 128 tokens) no expert is named more than 128 times, a bound that some block reaches.
All inputs are finite; a program needn't handle non-finite values.
Results may differ from a plain program's by a relative error of at most 0.008.
Values may be sent and summed in bfloat16 or wider, within the bound.
No kernel may reach another device: no remote copies, remote signals or barrier semaphores. Data moves between devices by JAX's collectives and lax.ppermute only.
A program may use at most 128 MiB of HBM per device.

v0:
```python
import jax
import jax.numpy as jnp
from jax import lax
from jax.sharding import Mesh
from jax.sharding import PartitionSpec as P

CHIPS = ("yhi", "ylo")
SWAP = [(0, 1), (1, 0)]


def ring_of_four(value, axis):
    ahead = [(i, (i + 1) % 4) for i in range(4)]
    behind = [(i, (i - 1) % 4) for i in range(4)]
    from_minus = lax.ppermute(value, axis, perm=ahead)
    from_plus = lax.ppermute(value, axis, perm=behind)
    half = value.shape[-1] // 2
    far = jnp.concatenate(
        [
            lax.ppermute(from_minus[..., :half], axis, perm=ahead),
            lax.ppermute(from_plus[..., half:], axis, perm=behind),
        ],
        axis=-1,
    )
    return jnp.stack([value, from_plus, far, from_minus])


def expert_weights(w_gate, w_up, w_down, ylo):
    stacked = jnp.stack([w_gate, w_up, w_down], axis=1)
    rows = stacked.shape[2]
    padded = -(-rows // 16) * 16
    stacked = jnp.pad(stacked, ((0, 0), (0, 0), (0, padded - rows), (0, 0)))
    keep = lax.dynamic_index_in_dim(stacked, ylo, axis=0, keepdims=False)
    send = lax.dynamic_index_in_dim(stacked, 1 - ylo, axis=0, keepdims=False)
    got = lax.ppermute(send, "ylo", perm=SWAP)
    set_a = ring_of_four(ring_of_four(keep, "z"), "x")
    set_b = ring_of_four(ring_of_four(got, "x"), "z")
    width = stacked.shape[-1]
    return [
        jnp.moveaxis(part, 2, 0).reshape(3, -1, width) for part in (set_a, set_b)
    ]


def spread(value, chips):
    sent = jnp.broadcast_to(value[None], (chips,) + value.shape)
    mine = lax.all_to_all(sent, CHIPS, split_axis=0, concat_axis=0, tiled=True)
    other = lax.ppermute(mine, "core", perm=SWAP)
    return mine, other


def per_device(tokens, expert_ids, gate_weights, w_gate, w_up, w_down):
    ylo = lax.axis_index("ylo")
    chips = lax.axis_size("yhi") * lax.axis_size("ylo")
    expert = (lax.axis_index("yhi") * lax.axis_size("core") + lax.axis_index("core")) * 2 + ylo
    token_count, model_width = tokens.shape

    sets = expert_weights(w_gate, w_up, w_down, ylo)

    experts = jnp.arange(lax.axis_size("core") * chips, dtype=jnp.int32)
    weight = jnp.sum(
        jnp.where(expert_ids[:, :, None] == experts, gate_weights[:, :, None], 0.0), axis=1
    )
    rows_mine, rows_other = spread(tokens, chips)
    weight_mine, weight_other = spread(weight, chips)
    rows = jnp.concatenate([rows_mine, rows_other]).reshape(-1, model_width)
    table = jnp.concatenate([weight_mine, weight_other]).reshape(-1, experts.shape[0])
    scale = lax.dynamic_index_in_dim(table, expert, axis=1, keepdims=True)

    out = None
    for weights in sets:
        gate_part = jnp.dot(rows, weights[0].T, preferred_element_type=jnp.float32)
        up_part = jnp.dot(rows, weights[1].T, preferred_element_type=jnp.float32)
        hidden = (jax.nn.silu(gate_part) * up_part).astype(jnp.bfloat16)
        part = jnp.dot(hidden, weights[2], preferred_element_type=jnp.float32)
        out = part if out is None else out + part
    out = out.astype(jnp.bfloat16)
    scaled = (out.astype(jnp.float32) * scale).reshape(2, chips, token_count, model_width)

    partner = lax.ppermute(scaled[1], "core", perm=SWAP)
    partial = (scaled[0] + partner).astype(jnp.bfloat16)
    back = lax.all_to_all(partial, CHIPS, split_axis=0, concat_axis=0, tiled=True)
    mixed = jnp.sum(back.astype(jnp.float32), axis=0)
    return mixed.astype(jnp.bfloat16)


def solution(mesh):
    grp, blk = mesh.devices.shape
    ylo = 2
    fine = Mesh(
        mesh.devices.reshape(2, grp // 2, 4, blk // (4 * ylo), ylo),
        ("yhi", "core", "x", "z", "ylo"),
    )
    rows = P(("yhi", "core", "x", "z", "ylo"), None)
    weights = P(("yhi", "core"), ("x", "z", "ylo"), None)
    return jax.shard_map(
        per_device,
        mesh=fine,
        in_specs=(rows, rows, rows, weights, weights, weights),
        out_specs=rows,
        check_vma=False,
    )
```

profile of v0, /device:TPU:0, one launch (start us, length us, event | category | flops | bytes accessed | tf_op | source)
XLA Modules:
  0.0 282.0 jit_solution(3332313682208472711)
XLA Ops:
  2.7 4.2 %collective-permute-start.1 = (bf16[3,48,2048]{2,1,0:T(8,128)(2,1)S(1)}, bf16[3,48,2048]{2,1,0:T(8,128)(2,1)S(1)}, u32[]{:S(2)}, u32[]{:S(2)}) collective-permute-start(bf16[3,48,2048]{2,1,0:T(8,128)(2,1)S(1)} %bitcast.69), channel_id=1, source_target_pairs={{0,6},{2,0},{4,2},{6,4},{1,7},{3,1},{5,3},{7,5},{8,14},{10,8},{12,... | collective-permute-start | bytes 1769480 | tf_op jit(solution)/shard_map/ppermute | solution.py:15
  8.4 11.0 %collective-permute-done.1 = bf16[3,48,2048]{2,1,0:T(8,128)(2,1)S(1)} collective-permute-done((bf16[3,48,2048]{2,1,0:T(8,128)(2,1)S(1)}, bf16[3,48,2048]{2,1,0:T(8,128)(2,1)S(1)}, u32[]{:S(2)}, u32[]{:S(2)}) %collective-permute-start.1) | collective-permute-done | bytes 589856 | tf_op jit(solution)/shard_map/ppermute | solution.py:15
  20.2 3.7 %collective-permute-start.4 = (bf16[3,48,1024]{2,1,0:T(8,128)(2,1)}, bf16[3,48,1024]{2,1,0:T(8,128)(2,1)}, u32[]{:S(2)}, u32[]{:S(2)}) collective-permute-start(bf16[3,48,1024]{2,1,0:T(8,128)(2,1)} %slice.73), channel_id=1, source_target_pairs={{0,6},{2,0},{4,2},{6,4},{1,7},{3,1},{5,3},{7,5},{8,14},{10,8},{12,... | collective-permute-start | bytes 884744 | tf_op jit(solution)/shard_map/ppermute | solution.py:20
  26.4 4.5 %all-to-all-start = ((bf16[4,128,2048]{2,1,0:T(8,128)(2,1)}), bf16[4,128,2048]{2,1,0:T(8,128)(2,1)}, u32[]{:S(2)}, u32[]{:S(2)}) async-start(bf16[4,128,2048]{2,1,0:T(8,128)(2,1)} %broadcast_in_dim.16), calls=%async_computation | async-start | bytes 4194304 | tf_op jit(solution)/shard_map/all_to_all | solution.py:45
  40.4 8.4 %collective-permute-done.10 = bf16[3,48,2048]{2,1,0:T(8,128)(2,1)S(1)} collective-permute-done((bf16[3,48,2048]{2,1,0:T(8,128)(2,1)}, bf16[3,48,2048]{2,1,0:T(8,128)(2,1)S(1)}, u32[]{:S(2)}, u32[]{:S(2)}) %collective-permute-start.10) | collective-permute-done | bytes 589856 | tf_op jit(solution)/shard_map/ppermute | solution.py:15
  48.9 3.0 %collective-permute-start.13 = (bf16[3,48,1024]{2,1,0:T(8,128)(2,1)S(1)}, bf16[3,48,1024]{2,1,0:T(8,128)(2,1)S(1)}, u32[]{:S(2)}, u32[]{:S(2)}) collective-permute-start(bf16[3,48,1024]{2,1,0:T(8,128)(2,1)S(1)} %slice.80), channel_id=1, source_target_pairs={{0,24},{8,0},{16,8},{24,16},{1,25},{9,1},{17,9},{25,17},{2,26},{10... | collective-permute-start | bytes 884744 | tf_op jit(solution)/shard_map/ppermute | solution.py:20
  52.0 51.1 %collective-permute-done.13 = bf16[3,48,1024]{2,1,0:T(8,128)(2,1)S(1)} collective-permute-done((bf16[3,48,1024]{2,1,0:T(8,128)(2,1)S(1)}, bf16[3,48,1024]{2,1,0:T(8,128)(2,1)S(1)}, u32[]{:S(2)}, u32[]{:S(2)}) %collective-permute-start.13) | collective-permute-done | bytes 294944 | tf_op jit(solution)/shard_map/ppermute | solution.py:20
  103.3 3.5 %fusion.10 = (bf16[1,4,3,48,2048]{4,3,2,1,0:T(8,128)(2,1)}, bf16[4,3,48,2048]{3,2,1,0:T(8,128)(2,1)}) fusion(bf16[1,3,48,2048]{3,2,1,0:T(8,128)(2,1)S(1)} %bitcast.72, bf16[1,3,48,2048]{3,2,1,0:T(8,128)(2,1)S(1)} %maximum_bitcast_fusion.5, bf16[1,3,48,2048]{3,2,1,0:T(8,128)(2,1)} %bitcast.73, bf16[1,3,48,2048]{3,2,1,0:T(8,128)(2,1)} %bitcast.17), kind=kLoop, calls=%fused_computation.34 | loop fusion | flops 3538944 | bytes 7077888 | tf_op jit(solution)/shard_map/stack | solution.py:24
  109.7 9.6 %all_to_all.15 = f32[4,128,8]{1,2,0:T(8,128)S(1)} all-to-all(f32[4,128,8]{1,2,0:T(8,128)S(1)} %broadcast_in_dim.30), channel_id=1, replica_groups=mesh['yhi'=2,'core'=2,'x'=4,'z'=4,'ylo'=2] {'yhi','ylo'}, dimensions={0} | all-to-all | bytes 32768 | tf_op jit(solution)/shard_map/all_to_all | solution.py:45
  120.8 3.0 %collective-permute-start.8 = (bf16[4,3,48,1024]{3,2,1,0:T(8,128)(2,1)S(1)}, bf16[4,3,48,1024]{3,2,1,0:T(8,128)(2,1)}, u32[]{:S(2)}, u32[]{:S(2)}) collective-permute-start(bf16[4,3,48,1024]{3,2,1,0:T(8,128)(2,1)S(1)} %slice.75), channel_id=1, source_target_pairs={{0,24},{8,0},{16,8},{24,16},{1,25},{9,1},{17,9},{25,17},{2,26},{10... | collective-permute-start | bytes 3538952 | tf_op jit(solution)/shard_map/ppermute | solution.py:20
  130.2 31.0 %collective-permute-done.14 = bf16[4,3,48,2048]{3,2,1,0:T(8,128)(2,1)} collective-permute-done((bf16[4,3,48,2048]{3,2,1,0:T(8,128)(2,1)}, bf16[4,3,48,2048]{3,2,1,0:T(8,128)(2,1)}, u32[]{:S(2)}, u32[]{:S(2)}) %collective-permute-start.14) | collective-permute-done | bytes 2359328 | tf_op jit(solution)/shard_map/ppermute | solution.py:15
  162.5 3.8 %collective-permute-start.17 = (bf16[4,3,48,1024]{3,2,1,0:T(8,128)(2,1)S(1)}, bf16[4,3,48,1024]{3,2,1,0:T(8,128)(2,1)S(1)}, u32[]{:S(2)}, u32[]{:S(2)}) collective-permute-start(bf16[4,3,48,1024]{3,2,1,0:T(8,128)(2,1)S(1)} %slice.82), channel_id=1, source_target_pairs={{0,6},{2,0},{4,2},{6,4},{1,7},{3,1},{5,3},{7,5},{8,14},{10,8},{12,... | collective-permute-start | bytes 3538952 | tf_op jit(solution)/shard_map/ppermute | solution.py:20
  169.8 3.5 %maximum_bitcast_fusion = bf16[3,4,4,48,2048]{4,3,0,2,1:T(8,128)(2,1)S(1)} fusion(bf16[1,4,3,48,2048]{4,3,2,1,0:T(8,128)(2,1)} %bitcast.11, bf16[1,4,3,48,2048]{4,3,2,1,0:T(8,128)(2,1)S(1)} %maximum_bitcast_fusion.2, bf16[1,4,3,48,2048]{4,3,2,1,0:T(8,128)(2,1)} %bitcast.9, bf16[1,4,3,48,2048]{4,3,2,1,0:T(8,128)(2,1)S(1)} %get-tuple-element.13), kind=kLoop, calls=%fused_computation | loop fusion | flops 14155776 | bytes 18874368 | tf_op jit(solution)/shard_map/transpose | solution.py:39
  175.7 5.2 %fusion.19 = f32[1024,768]{1,0:T(8,128)} fusion(bf16[1024,2048]{1,0:T(8,128)(2,1)S(1)} %bitcast.58, bf16[768,2048]{1,0:T(8,128)(2,1)S(1)} %bitcast.67), kind=kOutput, calls=%fused_computation.41 | convolution fusion | flops 3221225472 | bytes 10485760 | tf_op jit(solution)/shard_map/dot_general | solution.py:70
  180.9 10.5 %collective-permute-done.17 = bf16[4,3,48,1024]{3,2,1,0:T(8,128)(2,1)S(1)} collective-permute-done((bf16[4,3,48,1024]{3,2,1,0:T(8,128)(2,1)S(1)}, bf16[4,3,48,1024]{3,2,1,0:T(8,128)(2,1)S(1)}, u32[]{:S(2)}, u32[]{:S(2)}) %collective-permute-start.17) | collective-permute-done | bytes 1179680 | tf_op jit(solution)/shard_map/ppermute | solution.py:20
  191.4 5.0 %collective-permute-done.16 = bf16[4,3,48,1024]{3,2,1,0:T(8,128)(2,1)S(1)} collective-permute-done((bf16[4,3,48,1024]{3,2,1,0:T(8,128)(2,1)S(1)}, bf16[4,3,48,1024]{3,2,1,0:T(8,128)(2,1)S(1)}, u32[]{:S(2)}, u32[]{:S(2)}) %collective-permute-start.16) | collective-permute-done | bytes 1179680 | tf_op jit(solution)/shard_map/ppermute | solution.py:19
  196.7 3.5 %maximum_bitcast_fusion.1 = bf16[3,4,4,48,2048]{4,3,0,2,1:T(8,128)(2,1)S(1)} fusion(bf16[1,4,3,48,2048]{4,3,2,1,0:T(8,128)(2,1)} %bitcast.24, bf16[1,4,3,48,2048]{4,3,2,1,0:T(8,128)(2,1)S(1)} %maximum_bitcast_fusion.3, bf16[1,4,3,48,2048]{4,3,2,1,0:T(8,128)(2,1)} %bitcast.22, bf16[1,4,3,48,2048]{4,3,2,1,0:T(8,128)(2,1)S(1)} %copy-done), kind=kLoop, calls=%fused_computation.1 | loop fusion | flops 14155776 | bytes 18874368 | tf_op jit(solution)/shard_map/transpose | solution.py:39
  200.2 3.4 %fusion.13 = (bf16[1,4,4,48,2048]{4,3,0,2,1:T(8,128)(2,1)S(1)}, bf16[1,4,4,48,2048]{4,3,0,2,1:T(8,128)(2,1)}, bf16[1,4,4,48,2048]{4,3,0,2,1:T(8,128)(2,1)}) fusion(bf16[3,4,4,48,2048]{4,3,0,2,1:T(8,128)(2,1)S(1)} %maximum_bitcast_fusion.1), kind=kLoop, calls=%fused_computation.37 | loop fusion | bytes 18874368 | tf_op jit(solution)/shard_map/slice | solution.py:70
  203.6 5.2 %fusion.20 = f32[1024,768]{1,0:T(8,128)} fusion(bf16[1024,2048]{1,0:T(8,128)(2,1)S(1)} %bitcast.59, bf16[768,2048]{1,0:T(8,128)(2,1)S(1)} %bitcast.68), kind=kOutput, calls=%fused_computation.42 | convolution fusion | flops 3221225472 | bytes 10485760 | tf_op jit(solution)/shard_map/dot_general | solution.py:70
  208.8 14.0 %fusion.3 = f32[1024,2048]{1,0:T(8,128)} fusion(bf16[768,2048]{1,0:T(8,128)(2,1)} %bitcast.65, f32[1024,768]{1,0:T(8,128)} %fusion.20, bf16[1024,2048]{1,0:T(8,128)(2,1)} %bitcast.60, bf16[768,2048]{1,0:T(8,128)(2,1)} %bitcast.66), kind=kOutput, calls=%fused_computation.16 | convolution fusion | flops 6447169536 | bytes 22020096 | tf_op jit(solution)/shard_map/dot_general | solution.py:73
  222.8 14.7 %convert_multiply_fusion = f32[1024,2048]{1,0:T(8,128)} fusion(f32[1024,2048]{1,0:T(8,128)} %fusion.3, f32[1024]{0:T(1024)S(1)} %bitcast.76, bf16[768,2048]{1,0:T(8,128)(2,1)S(1)} %bitcast.63, f32[1024,768]{1,0:T(8,128)} %fusion.19, bf16[1024,2048]{1,0:T(8,128)(2,1)} %bitcast.61, bf16[768,2048]{1,0:T(8,128)(2,1)} %bitcast.64), kind=kOutput, calls=%fused_computation.2 | convolution fusion | flops 6455558144 | bytes 30412800 | tf_op jit(solution)/shard_map/dot_general | solution.py:73
  237.5 4.0 %fusion.14 = (f32[512,2048]{1,0:T(8,128)S(1)}, f32[512,2048]{1,0:T(8,128)S(1)}) fusion(f32[1024,2048]{1,0:T(8,128)} %convert_multiply_fusion), kind=kLoop, calls=%fused_computation.38 | loop fusion | bytes 16777216 | tf_op jit(solution)/shard_map/slice | solution.py:78
  241.7 7.1 %collective-permute-done.19 = f32[4,128,2048]{2,1,0:T(8,128)S(1)} collective-permute-done((f32[4,128,2048]{2,1,0:T(8,128)S(1)}, f32[4,128,2048]{2,1,0:T(8,128)S(1)}, u32[]{:S(2)}, u32[]{:S(2)}) %collective-permute-start.19) | collective-permute-done | bytes 4194336 | tf_op jit(solution)/shard_map/ppermute | solution.py:78
  249.8 30.9 %all_to_all.16 = bf16[4,128,2048]{2,1,0:T(8,128)(2,1)S(1)} all-to-all(bf16[4,128,2048]{2,1,0:T(8,128)(2,1)S(1)} %add_convert_fusion.1), channel_id=1, replica_groups=mesh['yhi'=2,'core'=2,'x'=4,'z'=4,'ylo'=2] {'yhi','ylo'}, dimensions={0} | all-to-all | bytes 4194304 | tf_op jit(solution)/shard_map/all_to_all | solution.py:80
  (73 shorter events, 37.7 us)
Async XLA Ops:
  2.4 22.3 %copy-start.5 = (bf16[128,2048]{1,0:T(8,128)(2,1)S(1)}, bf16[128,2048]{1,0:T(8,128)(2,1)}, u32[]{:S(2)}) copy-start(bf16[128,2048]{1,0:T(8,128)(2,1)} %param.6) | copy-start | bytes 1572868
  2.7 16.8 %collective-permute-start.1 = (bf16[3,48,2048]{2,1,0:T(8,128)(2,1)S(1)}, bf16[3,48,2048]{2,1,0:T(8,128)(2,1)S(1)}, u32[]{:S(2)}, u32[]{:S(2)}) collective-permute-start(bf16[3,48,2048]{2,1,0:T(8,128)(2,1)S(1)} %bitcast.69), channel_id=1, source_target_pairs={{0,6},{2,0},{4,2},{6,4},{1,7},{3,1},{5,3},{7,5},{8,14},{10,8},{12,... | collective-permute-start | bytes 1769480 | tf_op jit(solution)/shard_map/ppermute | solution.py:15
  6.9 17.1 %collective-permute-start.2 = (bf16[3,48,2048]{2,1,0:T(8,128)(2,1)S(1)}, bf16[3,48,2048]{2,1,0:T(8,128)(2,1)S(1)}, u32[]{:S(2)}, u32[]{:S(2)}) collective-permute-start(bf16[3,48,2048]{2,1,0:T(8,128)(2,1)S(1)} %bitcast.70), channel_id=1, source_target_pairs={{0,2},{2,4},{4,6},{6,0},{1,3},{3,5},{5,7},{7,1},{8,10},{10,12},{12... | collective-permute-start | bytes 1769480 | tf_op jit(solution)/shard_map/ppermute | solution.py:14
  6.9 24.0 %collective-permute-start.9 = (bf16[3,48,2048]{2,1,0:T(8,128)(2,1)S(1)}, bf16[3,48,2048]{2,1,0:T(8,128)(2,1)}, u32[]{:S(2)}, u32[]{:S(2)}) collective-permute-start(bf16[3,48,2048]{2,1,0:T(8,128)(2,1)S(1)} %get-tuple-element.18), channel_id=1, source_target_pairs={{0,1},{1,0},{2,3},{3,2},{4,5},{5,4},{6,7},{7,6},{8,9},{9,8},{10,11... | collective-permute-start | bytes 1769480 | tf_op jit(solution)/shard_map/ppermute | solution.py:34
  20.2 13.9 %collective-permute-start.4 = (bf16[3,48,1024]{2,1,0:T(8,128)(2,1)}, bf16[3,48,1024]{2,1,0:T(8,128)(2,1)}, u32[]{:S(2)}, u32[]{:S(2)}) collective-permute-start(bf16[3,48,1024]{2,1,0:T(8,128)(2,1)} %slice.73), channel_id=1, source_target_pairs={{0,6},{2,0},{4,2},{6,4},{1,7},{3,1},{5,3},{7,5},{8,14},{10,8},{12,... | collective-permute-start | bytes 884744 | tf_op jit(solution)/shard_map/ppermute | solution.py:20
  24.7 9.4 %collective-permute-start.3 = (bf16[3,48,1024]{2,1,0:T(8,128)(2,1)}, bf16[3,48,1024]{2,1,0:T(8,128)(2,1)}, u32[]{:S(2)}, u32[]{:S(2)}) collective-permute-start(bf16[3,48,1024]{2,1,0:T(8,128)(2,1)} %slice.72), channel_id=1, source_target_pairs={{0,2},{2,4},{4,6},{6,0},{1,3},{3,5},{5,7},{7,1},{8,10},{10,12},{12... | collective-permute-start | bytes 884744 | tf_op jit(solution)/shard_map/ppermute | solution.py:19
  26.4 76.8 %all-to-all-start = ((bf16[4,128,2048]{2,1,0:T(8,128)(2,1)}), bf16[4,128,2048]{2,1,0:T(8,128)(2,1)}, u32[]{:S(2)}, u32[]{:S(2)}) async-start(bf16[4,128,2048]{2,1,0:T(8,128)(2,1)} %broadcast_in_dim.16), calls=%async_computation | async-start | bytes 4194304 | tf_op jit(solution)/shard_map/all_to_all | solution.py:45
  30.8 21.1 %collective-permute-start.11 = (bf16[3,48,2048]{2,1,0:T(8,128)(2,1)}, bf16[3,48,2048]{2,1,0:T(8,128)(2,1)S(1)}, u32[]{:S(2)}, u32[]{:S(2)}) collective-permute-start(bf16[3,48,2048]{2,1,0:T(8,128)(2,1)} %collective-permute-done.9), channel_id=1, source_target_pairs={{0,8},{8,16},{16,24},{24,0},{1,9},{9,17},{17,25},{25,1},{2,10},{10... | collective-permute-start | bytes 1769480 | tf_op jit(solution)/shard_map/ppermute | solution.py:14
  32.4 16.5 %collective-permute-start.10 = (bf16[3,48,2048]{2,1,0:T(8,128)(2,1)}, bf16[3,48,2048]{2,1,0:T(8,128)(2,1)S(1)}, u32[]{:S(2)}, u32[]{:S(2)}) collective-permute-start(bf16[3,48,2048]{2,1,0:T(8,128)(2,1)} %collective-permute-done.9), channel_id=1, source_target_pairs={{0,24},{8,0},{16,8},{24,16},{1,25},{9,1},{17,9},{25,17},{2,26},{10... | collective-permute-start | bytes 1769480 | tf_op jit(solution)/shard_map/ppermute | solution.py:15
  37.9 81.4 %collective-permute-start.5 = (bf16[4,3,48,2048]{3,2,1,0:T(8,128)(2,1)}, bf16[4,3,48,2048]{3,2,1,0:T(8,128)(2,1)}, u32[]{:S(2)}, u32[]{:S(2)}) collective-permute-start(bf16[4,3,48,2048]{3,2,1,0:T(8,128)(2,1)} %get-tuple-element.14), channel_id=1, source_target_pairs={{0,24},{8,0},{16,8},{24,16},{1,25},{9,1},{17,9},{25,17},{2,26},{10... | collective-permute-start | bytes 7077896 | tf_op jit(solution)/shard_map/ppermute | solution.py:15
  40.4 80.4 %collective-permute-start.6 = (bf16[4,3,48,2048]{3,2,1,0:T(8,128)(2,1)}, bf16[4,3,48,2048]{3,2,1,0:T(8,128)(2,1)}, u32[]{:S(2)}, u32[]{:S(2)}) collective-permute-start(bf16[4,3,48,2048]{3,2,1,0:T(8,128)(2,1)} %get-tuple-element.14), channel_id=1, source_target_pairs={{0,8},{8,16},{16,24},{24,0},{1,9},{9,17},{17,25},{25,1},{2,10},{10... | collective-permute-start | bytes 7077896 | tf_op jit(solution)/shard_map/ppermute | solution.py:14
  48.8 54.3 %copy-start.2 = (bf16[3,48,2048]{2,1,0:T(8,128)(2,1)}, bf16[3,48,2048]{2,1,0:T(8,128)(2,1)S(1)}, u32[]{:S(2)}) copy-start(bf16[3,48,2048]{2,1,0:T(8,128)(2,1)S(1)} %collective-permute-done.10) | copy-start | bytes 1769476
  48.9 54.2 %collective-permute-start.13 = (bf16[3,48,1024]{2,1,0:T(8,128)(2,1)S(1)}, bf16[3,48,1024]{2,1,0:T(8,128)(2,1)S(1)}, u32[]{:S(2)}, u32[]{:S(2)}) collective-permute-start(bf16[3,48,1024]{2,1,0:T(8,128)(2,1)S(1)} %slice.80), channel_id=1, source_target_pairs={{0,24},{8,0},{16,8},{24,16},{1,25},{9,1},{17,9},{25,17},{2,26},{10... | collective-permute-start | bytes 884744 | tf_op jit(solution)/shard_map/ppermute | solution.py:20
  51.9 51.2 %collective-permute-start.12 = (bf16[3,48,1024]{2,1,0:T(8,128)(2,1)S(1)}, bf16[3,48,1024]{2,1,0:T(8,128)(2,1)S(1)}, u32[]{:S(2)}, u32[]{:S(2)}) collective-permute-start(bf16[3,48,1024]{2,1,0:T(8,128)(2,1)S(1)} %slice.79), channel_id=1, source_target_pairs={{0,8},{8,16},{16,24},{24,0},{1,9},{9,17},{17,25},{25,1},{2,10},{10... | collective-permute-start | bytes 884744 | tf_op jit(solution)/shard_map/ppermute | solution.py:19
  103.2 24.4 %collective-permute-start = (bf16[4,128,2048]{2,1,0:T(8,128)(2,1)}, bf16[4,128,2048]{2,1,0:T(8,128)(2,1)}, u32[]{:S(2)}, u32[]{:S(2)}) collective-permute-start(bf16[4,128,2048]{2,1,0:T(8,128)(2,1)} %all-to-all-done), channel_id=1, source_target_pairs={{0,32},{32,0},{1,33},{33,1},{2,34},{34,2},{3,35},{35,3},{4,36},{36... | collective-permute-start | bytes 6291464 | tf_op jit(solution)/shard_map/ppermute | solution.py:46
  106.7 54.4 %collective-permute-start.14 = (bf16[4,3,48,2048]{3,2,1,0:T(8,128)(2,1)}, bf16[4,3,48,2048]{3,2,1,0:T(8,128)(2,1)}, u32[]{:S(2)}, u32[]{:S(2)}) collective-permute-start(bf16[4,3,48,2048]{3,2,1,0:T(8,128)(2,1)} %get-tuple-element.16), channel_id=1, source_target_pairs={{0,6},{2,0},{4,2},{6,4},{1,7},{3,1},{5,3},{7,5},{8,14},{10,8},{12,... | collective-permute-start | bytes 7077896 | tf_op jit(solution)/shard_map/ppermute | solution.py:15
  109.7 56.6 %collective-permute-start.15 = (bf16[4,3,48,2048]{3,2,1,0:T(8,128)(2,1)}, bf16[4,3,48,2048]{3,2,1,0:T(8,128)(2,1)}, u32[]{:S(2)}, u32[]{:S(2)}) collective-permute-start(bf16[4,3,48,2048]{3,2,1,0:T(8,128)(2,1)} %get-tuple-element.16), channel_id=1, source_target_pairs={{0,2},{2,4},{4,6},{6,0},{1,3},{3,5},{5,7},{7,1},{8,10},{10,12},{12... | collective-permute-start | bytes 7077896 | tf_op jit(solution)/shard_map/ppermute | solution.py:14
  119.4 6.9 %collective-permute-start.18 = (f32[4,128,8]{1,2,0:T(8,128)S(1)}, f32[4,128,8]{1,2,0:T(8,128)S(1)}, u32[]{:S(2)}, u32[]{:S(2)}) collective-permute-start(f32[4,128,8]{1,2,0:T(8,128)S(1)} %all_to_all.15), channel_id=1, source_target_pairs={{0,32},{32,0},{1,33},{33,1},{2,34},{34,2},{3,35},{35,3},{4,36},{36... | collective-permute-start | bytes 49160 | tf_op jit(solution)/shard_map/ppermute | solution.py:46
  120.8 47.2 %collective-permute-start.8 = (bf16[4,3,48,1024]{3,2,1,0:T(8,128)(2,1)S(1)}, bf16[4,3,48,1024]{3,2,1,0:T(8,128)(2,1)}, u32[]{:S(2)}, u32[]{:S(2)}) collective-permute-start(bf16[4,3,48,1024]{3,2,1,0:T(8,128)(2,1)S(1)} %slice.75), channel_id=1, source_target_pairs={{0,24},{8,0},{16,8},{24,16},{1,25},{9,1},{17,9},{25,17},{2,26},{10... | collective-permute-start | bytes 3538952 | tf_op jit(solution)/shard_map/ppermute | solution.py:20
  126.8 41.1 %collective-permute-start.7 = (bf16[4,3,48,1024]{3,2,1,0:T(8,128)(2,1)}, bf16[4,3,48,1024]{3,2,1,0:T(8,128)(2,1)}, u32[]{:S(2)}, u32[]{:S(2)}) collective-permute-start(bf16[4,3,48,1024]{3,2,1,0:T(8,128)(2,1)} %slice.74), channel_id=1, source_target_pairs={{0,8},{8,16},{16,24},{24,0},{1,9},{9,17},{17,25},{25,1},{2,10},{10... | collective-permute-start | bytes 3538952 | tf_op jit(solution)/shard_map/ppermute | solution.py:19
  130.2 73.5 %copy-start.1 = (bf16[8,128,2048]{2,1,0:T(8,128)(2,1)}, bf16[8,128,2048]{2,1,0:T(8,128)(2,1)S(1)}, u32[]{:S(2)}) copy-start(bf16[8,128,2048]{2,1,0:T(8,128)(2,1)S(1)} %pad_maximum_fusion) | copy-start | bytes 12582916
  162.5 28.9 %collective-permute-start.17 = (bf16[4,3,48,1024]{3,2,1,0:T(8,128)(2,1)S(1)}, bf16[4,3,48,1024]{3,2,1,0:T(8,128)(2,1)S(1)}, u32[]{:S(2)}, u32[]{:S(2)}) collective-permute-start(bf16[4,3,48,1024]{3,2,1,0:T(8,128)(2,1)S(1)} %slice.82), channel_id=1, source_target_pairs={{0,6},{2,0},{4,2},{6,4},{1,7},{3,1},{5,3},{7,5},{8,14},{10,8},{12,... | collective-permute-start | bytes 3538952 | tf_op jit(solution)/shard_map/ppermute | solution.py:20
  167.7 28.8 %collective-permute-start.16 = (bf16[4,3,48,1024]{3,2,1,0:T(8,128)(2,1)S(1)}, bf16[4,3,48,1024]{3,2,1,0:T(8,128)(2,1)S(1)}, u32[]{:S(2)}, u32[]{:S(2)}) collective-permute-start(bf16[4,3,48,1024]{3,2,1,0:T(8,128)(2,1)S(1)} %slice.81), channel_id=1, source_target_pairs={{0,2},{2,4},{4,6},{6,0},{1,3},{3,5},{5,7},{7,1},{8,10},{10,12},{12... | collective-permute-start | bytes 3538952 | tf_op jit(solution)/shard_map/ppermute | solution.py:19
  241.6 7.2 %collective-permute-start.19 = (f32[4,128,2048]{2,1,0:T(8,128)S(1)}, f32[4,128,2048]{2,1,0:T(8,128)S(1)}, u32[]{:S(2)}, u32[]{:S(2)}) collective-permute-start(f32[4,128,2048]{2,1,0:T(8,128)S(1)} %bitcast.62), channel_id=1, source_target_pairs={{0,32},{32,0},{1,33},{33,1},{2,34},{34,2},{3,35},{35,3},{4,36},{36... | collective-permute-start | bytes 12582920 | tf_op jit(solution)/shard_map/ppermute | solution.py:78
  (6 other events, 38.6 us)
where the time goes:
time: 283 us; the launch traced here: 282 us
  waiting for transfers between devices  124 us (44%)
  blocking collectives  40.5 us (14%)
  matrix products  39.1 us (14%)
  starting transfers between devices  33 us (12%)
  local copies, waits for them, and re-layouts  22.7 us (8%)
  other arithmetic  22.2 us (8%)
    ppermute x4, waiting for transfers between devices, ring_of_four(): lax.ppermute(from_plus[..., half:], axis, perm=behind)  61.6 us
    ppermute x4, waiting for transfers between devices, ring_of_four(): from_plus = lax.ppermute(value, axis, perm=behind)  50.4 us
    all_to_all x1, blocking collectives, per_device(): lax.all_to_all(partial, CHIPS, split_axis=0, concat_axis=0, tiled=True)  30.9 us
    dot_general x2, matrix products, per_device(): part = jnp.dot(hidden, weights[2], preferred_element_type=jnp.float32)  28.7 us
    ppermute x4, starting transfers between devices, ring_of_four(): lax.ppermute(from_plus[..., half:], axis, perm=behind)  13.5 us
    ppermute x4, starting transfers between devices, ring_of_four(): from_plus = lax.ppermute(value, axis, perm=behind)  11.4 us
    dot_general x2, matrix products, per_device(): gate_part = jnp.dot(rows, weights[0].T, preferred_element_type=jnp.float32)  10.4 us
    all_to_all x1, blocking collectives, spread(): mine = lax.all_to_all(sent, CHIPS, split_axis=0, concat_axis=0, tiled=True)  9.64 us
  transfers between devices with their start and end apart: 21, of which 7 were waited for; matrix products, arithmetic and copies ran while one was open for 12% of the time, Pallas kernels for 0%

commit v1 on v0

--- a/solution.py
+++ b/solution.py
@@ -32,12 +32,22 @@
     keep = lax.dynamic_index_in_dim(stacked, ylo, axis=0, keepdims=False)
     send = lax.dynamic_index_in_dim(stacked, 1 - ylo, axis=0, keepdims=False)
     got = lax.ppermute(send, "ylo", perm=SWAP)
-    set_a = ring_of_four(ring_of_four(keep, "z"), "x")
-    set_b = ring_of_four(ring_of_four(got, "x"), "z")
+    first_a = ring_of_four(keep, "z")
+    first_b = ring_of_four(got, "x")
+    first_a, first_b = lax.optimization_barrier((first_a, first_b))
+    gate_up_a = ring_of_four(first_a[:, :2], "x")
+    gate_up_b = ring_of_four(first_b[:, :2], "z")
+    gate_up_a, gate_up_b, down_a, down_b = lax.optimization_barrier(
+        (gate_up_a, gate_up_b, first_a[:, 2], first_b[:, 2])
+    )
+    down_a = ring_of_four(down_a, "x")
+    down_b = ring_of_four(down_b, "z")
     width = stacked.shape[-1]
-    return [
-        jnp.moveaxis(part, 2, 0).reshape(3, -1, width) for part in (set_a, set_b)
-    ]
+    sets = []
+    for gate_up, down in ((gate_up_a, down_a), (gate_up_b, down_b)):
+        gate_up = jnp.moveaxis(gate_up, 2, 0).reshape(2, -1, width)
+        sets.append((gate_up[0], gate_up[1], down.reshape(-1, width)))
+    return sets
 
 
 def spread(value, chips):

time: 283 us -> 247 us (0.87)
  waiting for transfers between devices: 124 us -> 71.2 us
  starting transfers between devices: 33 us -> 47.8 us
  local copies, waits for them, and re-layouts: 22.7 us -> 26.9 us
    ppermute x4 -> x6, waiting for transfers between devices: 61.6 us -> 10.2 us  [ring_of_four(): lax.ppermute(from_plus[..., half:], axis, perm=behind)]
    ppermute x4 -> x6, waiting for transfers between devices: 50.4 us -> 28.2 us  [ring_of_four(): from_plus = lax.ppermute(value, axis, perm=behind)]
    ppermute x1, waiting for transfers between devices: 0.01 us -> 9.29 us  [expert_weights(): got = lax.ppermute(send, 'ylo', perm=SWAP)]
    ppermute x4 -> x6, waiting for transfers between devices: 5.05 us -> 13.2 us  [ring_of_four(): lax.ppermute(from_minus[..., :half], axis, perm=ahead)]
    ppermute x4 -> x6, starting transfers between devices: 13.5 us -> 21.6 us  [ring_of_four(): lax.ppermute(from_plus[..., half:], axis, perm=behind)]
    ppermute x4 -> x6, starting transfers between devices: 11.4 us -> 18.6 us  [ring_of_four(): from_plus = lax.ppermute(value, axis, perm=behind)]
    transpose x2 -> x0, other arithmetic: 7.09 us -> none  [expert_weights(): jnp.moveaxis(part, 2, 0).reshape(3, -1, width)]
    another operation x6 -> x12, other arithmetic: 9.35 us -> 14.3 us  [ring_of_four(): return jnp.stack([value, from_plus, far, from_minus])]
  transfers between devices with their start and end apart: 21 -> 29, of which waited for: 7 -> 14; matrix products, arithmetic and copies ran while one was open for 12% -> 23% of each run, Pallas kernels for 0% -> 0%
where the time goes in v1:
time: 247 us; the launch traced here: 246 us
  waiting for transfers between devices  71.2 us (29%)
  starting transfers between devices  47.8 us (19%)
  matrix products  40.5 us (16%)
  blocking collectives  39 us (16%)
  local copies, waits for them, and re-layouts  26.9 us (11%)
  other arithmetic  20 us (8%)
    dot_general x2, matrix products, per_device(): part = jnp.dot(hidden, weights[2], preferred_element_type=jnp.float32)  30.3 us
    all_to_all x1, blocking collectives, per_device(): lax.all_to_all(partial, CHIPS, split_axis=0, concat_axis=0, tiled=True)  29.4 us
    ppermute x6, waiting for transfers between devices, ring_of_four(): from_plus = lax.ppermute(value, axis, perm=behind)  28.2 us
    ppermute x6, starting transfers between devices, ring_of_four(): lax.ppermute(from_plus[..., half:], axis, perm=behind)  21.6 us
    ppermute x6, starting transfers between devices, ring_of_four(): from_plus = lax.ppermute(value, axis, perm=behind)  18.6 us
    another operation x12, other arithmetic, ring_of_four(): return jnp.stack([value, from_plus, far, from_minus])  14.3 us
    ppermute x6, waiting for transfers between devices, ring_of_four(): lax.ppermute(from_minus[..., :half], axis, perm=ahead)  13.2 us
    dot_general x2, matrix products, per_device(): gate_part = jnp.dot(rows, weights[0].T, preferred_element_type=jnp.float32)  10.3 us
  transfers between devices with their start and end apart: 29, of which 14 were waited for; matrix products, arithmetic and copies ran while one was open for 23% of the time, Pallas kernels for 0%

profile of v1, /device:TPU:0, one launch (start us, length us, event | category | flops | bytes accessed | tf_op | source)
XLA Modules:
  0.0 245.9 jit_solution(13478423493514648734)
XLA Ops:
  4.4 4.0 %collective-permute-start.1 = (bf16[3,48,2048]{2,1,0:T(8,128)(2,1)S(1)}, bf16[3,48,2048]{2,1,0:T(8,128)(2,1)S(1)}, u32[]{:S(2)}, u32[]{:S(2)}) collective-permute-start(bf16[3,48,2048]{2,1,0:T(8,128)(2,1)S(1)} %bitcast.85), channel_id=1, source_target_pairs={{0,6},{2,0},{4,2},{6,4},{1,7},{3,1},{5,3},{7,5},{8,14},{10,8},{12,... | collective-permute-start | bytes 1769480 | tf_op jit(solution)/shard_map/ppermute | solution.py:15
  8.5 9.3 %collective-permute-done.5 = bf16[3,48,2048]{2,1,0:T(8,128)(2,1)S(1)} collective-permute-done((bf16[3,48,2048]{2,1,0:T(8,128)(2,1)S(1)}, bf16[3,48,2048]{2,1,0:T(8,128)(2,1)S(1)}, u32[]{:S(2)}, u32[]{:S(2)}) %collective-permute-start.5) | collective-permute-done | bytes 589856 | tf_op jit(solution)/shard_map/ppermute | solution.py:34
  21.5 4.0 %collective-permute-start.4 = (bf16[3,48,1024]{2,1,0:T(8,128)(2,1)}, bf16[3,48,1024]{2,1,0:T(8,128)(2,1)}, u32[]{:S(2)}, u32[]{:S(2)}) collective-permute-start(bf16[3,48,1024]{2,1,0:T(8,128)(2,1)} %slice.95), channel_id=1, source_target_pairs={{0,6},{2,0},{4,2},{6,4},{1,7},{3,1},{5,3},{7,5},{8,14},{10,8},{12,... | collective-permute-start | bytes 884744 | tf_op jit(solution)/shard_map/ppermute | solution.py:20
  26.3 9.6 %all_to_all.15 = f32[4,128,8]{1,2,0:T(8,128)S(1)} all-to-all(f32[4,128,8]{1,2,0:T(8,128)S(1)} %broadcast_in_dim.30), channel_id=1, replica_groups=mesh['yhi'=2,'core'=2,'x'=4,'z'=4,'ylo'=2] {'yhi','ylo'}, dimensions={0} | all-to-all | bytes 32768 | tf_op jit(solution)/shard_map/all_to_all | solution.py:55
  38.5 4.4 %all-to-all-start = ((bf16[4,128,2048]{2,1,0:T(8,128)(2,1)}), bf16[4,128,2048]{2,1,0:T(8,128)(2,1)}, u32[]{:S(2)}, u32[]{:S(2)}) async-start(bf16[4,128,2048]{2,1,0:T(8,128)(2,1)} %broadcast_in_dim.16), calls=%async_computation | async-start | bytes 4194304 | tf_op jit(solution)/shard_map/all_to_all | solution.py:55
  43.1 3.3 %collective-permute-start.9 = (bf16[3,48,1024]{2,1,0:T(8,128)(2,1)S(1)}, bf16[3,48,1024]{2,1,0:T(8,128)(2,1)S(1)}, u32[]{:S(2)}, u32[]{:S(2)}) collective-permute-start(bf16[3,48,1024]{2,1,0:T(8,128)(2,1)S(1)} %slice.97), channel_id=1, source_target_pairs={{0,24},{8,0},{16,8},{24,16},{1,25},{9,1},{17,9},{25,17},{2,26},{10... | collective-permute-start | bytes 884744 | tf_op jit(solution)/shard_map/ppermute | solution.py:20
  48.1 5.2 %collective-permute-done.9 = bf16[3,48,1024]{2,1,0:T(8,128)(2,1)S(1)} collective-permute-done((bf16[3,48,1024]{2,1,0:T(8,128)(2,1)S(1)}, bf16[3,48,1024]{2,1,0:T(8,128)(2,1)S(1)}, u32[]{:S(2)}, u32[]{:S(2)}) %collective-permute-start.9) | collective-permute-done | bytes 294944 | tf_op jit(solution)/shard_map/ppermute | solution.py:20
  53.3 3.5 %collective-permute-done.8 = bf16[3,48,1024]{2,1,0:T(8,128)(2,1)S(1)} collective-permute-done((bf16[3,48,1024]{2,1,0:T(8,128)(2,1)S(1)}, bf16[3,48,1024]{2,1,0:T(8,128)(2,1)S(1)}, u32[]{:S(2)}, u32[]{:S(2)}) %collective-permute-start.8) | collective-permute-done | bytes 294944 | tf_op jit(solution)/shard_map/ppermute | solution.py:19
  60.5 3.2 %collective-permute-start.10 = (bf16[4,2,48,2048]{3,2,1,0:T(8,128)(2,1)}, bf16[4,2,48,2048]{3,2,1,0:T(8,128)(2,1)}, u32[]{:S(2)}, u32[]{:S(2)}) collective-permute-start(bf16[4,2,48,2048]{3,2,1,0:T(8,128)(2,1)} %get-tuple-element.26), channel_id=1, source_target_pairs={{0,24},{8,0},{16,8},{24,16},{1,25},{9,1},{17,9},{25,17},{2,26},{10... | collective-permute-start | bytes 4718600 | tf_op jit(solution)/shard_map/ppermute | solution.py:15
  63.8 3.1 %all-to-all-done = bf16[4,128,2048]{2,1,0:T(8,128)(2,1)} async-done(((bf16[4,128,2048]{2,1,0:T(8,128)(2,1)}), bf16[4,128,2048]{2,1,0:T(8,128)(2,1)}, u32[]{:S(2)}, u32[]{:S(2)}) %all-to-all-start) | async-done | bytes 2097184 | tf_op jit(solution)/shard_map/all_to_all | solution.py:55
  73.8 23.3 %collective-permute-done.10 = bf16[4,2,48,2048]{3,2,1,0:T(8,128)(2,1)} collective-permute-done((bf16[4,2,48,2048]{3,2,1,0:T(8,128)(2,1)}, bf16[4,2,48,2048]{3,2,1,0:T(8,128)(2,1)}, u32[]{:S(2)}, u32[]{:S(2)}) %collective-permute-start.10) | collective-permute-done | bytes 1572896 | tf_op jit(solution)/shard_map/ppermute | solution.py:15
  98.3 3.8 %collective-permute-start.13 = (bf16[4,2,48,1024]{3,2,1,0:T(8,128)(2,1)S(1)}, bf16[4,2,48,1024]{3,2,1,0:T(8,128)(2,1)S(1)}, u32[]{:S(2)}, u32[]{:S(2)}) collective-permute-start(bf16[4,2,48,1024]{3,2,1,0:T(8,128)(2,1)S(1)} %slice.99), channel_id=1, source_target_pairs={{0,24},{8,0},{16,8},{24,16},{1,25},{9,1},{17,9},{25,17},{2,26},{10... | collective-permute-start | bytes 2359304 | tf_op jit(solution)/shard_map/ppermute | solution.py:20
  107.7 3.8 %collective-permute-start.17 = (bf16[4,2,48,1024]{3,2,1,0:T(8,128)(2,1)S(1)}, bf16[4,2,48,1024]{3,2,1,0:T(8,128)(2,1)S(1)}, u32[]{:S(2)}, u32[]{:S(2)}) collective-permute-start(bf16[4,2,48,1024]{3,2,1,0:T(8,128)(2,1)S(1)} %slice.101), channel_id=1, source_target_pairs={{0,6},{2,0},{4,2},{6,4},{1,7},{3,1},{5,3},{7,5},{8,14},{10,8},{12,... | collective-permute-start | bytes 2359304 | tf_op jit(solution)/shard_map/ppermute | solution.py:20
  117.3 4.7 %collective-permute-done.12 = bf16[4,2,48,1024]{3,2,1,0:T(8,128)(2,1)S(1)} collective-permute-done((bf16[4,2,48,1024]{3,2,1,0:T(8,128)(2,1)S(1)}, bf16[4,2,48,1024]{3,2,1,0:T(8,128)(2,1)S(1)}, u32[]{:S(2)}, u32[]{:S(2)}) %collective-permute-start.12) | collective-permute-done | bytes 786464 | tf_op jit(solution)/shard_map/ppermute | solution.py:19
  128.1 4.7 %collective-permute-done.16 = bf16[4,2,48,1024]{3,2,1,0:T(8,128)(2,1)S(1)} collective-permute-done((bf16[4,2,48,1024]{3,2,1,0:T(8,128)(2,1)S(1)}, bf16[4,2,48,1024]{3,2,1,0:T(8,128)(2,1)S(1)}, u32[]{:S(2)}, u32[]{:S(2)}) %collective-permute-start.16) | collective-permute-done | bytes 786464 | tf_op jit(solution)/shard_map/ppermute | solution.py:19
  136.0 3.2 %collective-permute-start.22 = (bf16[4,48,2048]{2,1,0:T(8,128)(2,1)S(1)}, bf16[4,48,2048]{2,1,0:T(8,128)(2,1)S(1)}, u32[]{:S(2)}, u32[]{:S(2)}) collective-permute-start(bf16[4,48,2048]{2,1,0:T(8,128)(2,1)S(1)} %slice_bitcast_fusion), channel_id=1, source_target_pairs={{0,6},{2,0},{4,2},{6,4},{1,7},{3,1},{5,3},{7,5},{8,14},{10,8},{12,... | collective-permute-start | bytes 2359304 | tf_op jit(solution)/shard_map/ppermute | solution.py:15
  147.5 5.2 %fusion.18 = f32[1024,768]{1,0:T(8,128)} fusion(bf16[1024,2048]{1,0:T(8,128)(2,1)S(1)} %bitcast.72, bf16[768,2048]{1,0:T(8,128)(2,1)S(1)} %bitcast.84), kind=kOutput, calls=%fused_computation.48 | convolution fusion | flops 3221225472 | bytes 10485760 | tf_op jit(solution)/shard_map/dot_general | solution.py:80
  154.5 3.8 %collective-permute-start.25 = (bf16[4,48,1024]{2,1,0:T(8,128)(2,1)S(1)}, bf16[4,48,1024]{2,1,0:T(8,128)(2,1)S(1)}, u32[]{:S(2)}, u32[]{:S(2)}) collective-permute-start(bf16[4,48,1024]{2,1,0:T(8,128)(2,1)S(1)} %slice.109), channel_id=1, source_target_pairs={{0,6},{2,0},{4,2},{6,4},{1,7},{3,1},{5,3},{7,5},{8,14},{10,8},{12,... | collective-permute-start | bytes 1179656 | tf_op jit(solution)/shard_map/ppermute | solution.py:20
  158.4 5.1 %fusion.17 = f32[1024,768]{1,0:T(8,128)} fusion(bf16[1024,2048]{1,0:T(8,128)(2,1)S(1)} %bitcast.73, bf16[768,2048]{1,0:T(8,128)(2,1)S(1)} %bitcast.83), kind=kOutput, calls=%fused_computation.47 | convolution fusion | flops 3221225472 | bytes 10485760 | tf_op jit(solution)/shard_map/dot_general | solution.py:80
  169.6 14.0 %fusion.3 = f32[1024,2048]{1,0:T(8,128)} fusion(bf16[768,2048]{1,0:T(8,128)(2,1)} %bitcast.80, f32[1024,768]{1,0:T(8,128)} %fusion.18, bf16[1024,2048]{1,0:T(8,128)(2,1)} %bitcast.74, bf16[768,2048]{1,0:T(8,128)(2,1)} %bitcast.82), kind=kOutput, calls=%fused_computation.16 | convolution fusion | flops 6447169536 | bytes 22020096 | tf_op jit(solution)/shard_map/dot_general | solution.py:83
  186.7 16.2 %convert_multiply_fusion = f32[1024,2048]{1,0:T(8,128)} fusion(f32[1024,2048]{1,0:T(8,128)} %fusion.3, f32[1024]{0:T(1024)S(1)} %bitcast.97, bf16[768,2048]{1,0:T(8,128)(2,1)} %bitcast.79, f32[1024,768]{1,0:T(8,128)} %fusion.17, bf16[1024,2048]{1,0:T(8,128)(2,1)} %bitcast.75, bf16[768,2048]{1,0:T(8,128)(2,1)} %bitcast.81), kind=kOutput, calls=%fused_computation | convolution fusion | flops 6455558144 | bytes 30412800 | tf_op jit(solution)/shard_map/dot_general | solution.py:83
  203.0 4.0 %fusion.10 = (f32[512,2048]{1,0:T(8,128)S(1)}, f32[512,2048]{1,0:T(8,128)S(1)}) fusion(f32[1024,2048]{1,0:T(8,128)} %convert_multiply_fusion), kind=kLoop, calls=%fused_computation.42 | loop fusion | bytes 16777216 | tf_op jit(solution)/shard_map/slice | solution.py:88
  207.1 7.1 %collective-permute-done.27 = f32[4,128,2048]{2,1,0:T(8,128)S(1)} collective-permute-done((f32[4,128,2048]{2,1,0:T(8,128)S(1)}, f32[4,128,2048]{2,1,0:T(8,128)S(1)}, u32[]{:S(2)}, u32[]{:S(2)}) %collective-permute-start.27) | collective-permute-done | bytes 4194336 | tf_op jit(solution)/shard_map/ppermute | solution.py:88
  215.2 29.4 %all_to_all.16 = bf16[4,128,2048]{2,1,0:T(8,128)(2,1)S(1)} all-to-all(bf16[4,128,2048]{2,1,0:T(8,128)(2,1)S(1)} %add_convert_fusion.1), channel_id=1, replica_groups=mesh['yhi'=2,'core'=2,'x'=4,'z'=4,'ylo'=2] {'yhi','ylo'}, dimensions={0} | all-to-all | bytes 4194304 | tf_op jit(solution)/shard_map/all_to_all | solution.py:90
  (103 shorter events, 67.4 us)
Async XLA Ops:
  2.7 15.1 %collective-permute-start.5 = (bf16[3,48,2048]{2,1,0:T(8,128)(2,1)S(1)}, bf16[3,48,2048]{2,1,0:T(8,128)(2,1)S(1)}, u32[]{:S(2)}, u32[]{:S(2)}) collective-permute-start(bf16[3,48,2048]{2,1,0:T(8,128)(2,1)S(1)} %get-tuple-element.27), channel_id=1, source_target_pairs={{0,1},{1,0},{2,3},{3,2},{4,5},{5,4},{6,7},{7,6},{8,9},{9,8},{10,11... | collective-permute-start | bytes 1769480 | tf_op jit(solution)/shard_map/ppermute | solution.py:34
  4.4 16.3 %collective-permute-start.1 = (bf16[3,48,2048]{2,1,0:T(8,128)(2,1)S(1)}, bf16[3,48,2048]{2,1,0:T(8,128)(2,1)S(1)}, u32[]{:S(2)}, u32[]{:S(2)}) collective-permute-start(bf16[3,48,2048]{2,1,0:T(8,128)(2,1)S(1)} %bitcast.85), channel_id=1, source_target_pairs={{0,6},{2,0},{4,2},{6,4},{1,7},{3,1},{5,3},{7,5},{8,14},{10,8},{12,... | collective-permute-start | bytes 1769480 | tf_op jit(solution)/shard_map/ppermute | solution.py:15
  8.5 17.0 %collective-permute-start.2 = (bf16[3,48,2048]{2,1,0:T(8,128)(2,1)S(1)}, bf16[3,48,2048]{2,1,0:T(8,128)(2,1)S(1)}, u32[]{:S(2)}, u32[]{:S(2)}) collective-permute-start(bf16[3,48,2048]{2,1,0:T(8,128)(2,1)S(1)} %bitcast.86), channel_id=1, source_target_pairs={{0,2},{2,4},{4,6},{6,0},{1,3},{3,5},{5,7},{7,1},{8,10},{10,12},{12... | collective-permute-start | bytes 1769480 | tf_op jit(solution)/shard_map/ppermute | solution.py:14
  17.7 25.3 %collective-permute-start.6 = (bf16[3,48,2048]{2,1,0:T(8,128)(2,1)S(1)}, bf16[3,48,2048]{2,1,0:T(8,128)(2,1)S(1)}, u32[]{:S(2)}, u32[]{:S(2)}) collective-permute-start(bf16[3,48,2048]{2,1,0:T(8,128)(2,1)S(1)} %collective-permute-done.5), channel_id=1, source_target_pairs={{0,24},{8,0},{16,8},{24,16},{1,25},{9,1},{17,9},{25,17},{2,26},{10... | collective-permute-start | bytes 1769480 | tf_op jit(solution)/shard_map/ppermute | solution.py:15
  20.7 25.8 %collective-permute-start.7 = (bf16[3,48,2048]{2,1,0:T(8,128)(2,1)S(1)}, bf16[3,48,2048]{2,1,0:T(8,128)(2,1)S(1)}, u32[]{:S(2)}, u32[]{:S(2)}) collective-permute-start(bf16[3,48,2048]{2,1,0:T(8,128)(2,1)S(1)} %collective-permute-done.5), channel_id=1, source_target_pairs={{0,8},{8,16},{16,24},{24,0},{1,9},{9,17},{17,25},{25,1},{2,10},{10... | collective-permute-start | bytes 1769480 | tf_op jit(solution)/shard_map/ppermute | solution.py:14
  21.5 25.1 %collective-permute-start.4 = (bf16[3,48,1024]{2,1,0:T(8,128)(2,1)}, bf16[3,48,1024]{2,1,0:T(8,128)(2,1)}, u32[]{:S(2)}, u32[]{:S(2)}) collective-permute-start(bf16[3,48,1024]{2,1,0:T(8,128)(2,1)} %slice.95), channel_id=1, source_target_pairs={{0,6},{2,0},{4,2},{6,4},{1,7},{3,1},{5,3},{7,5},{8,14},{10,8},{12,... | collective-permute-start | bytes 884744 | tf_op jit(solution)/shard_map/ppermute | solution.py:20
  26.2 20.3 %collective-permute-start.3 = (bf16[3,48,1024]{2,1,0:T(8,128)(2,1)}, bf16[3,48,1024]{2,1,0:T(8,128)(2,1)}, u32[]{:S(2)}, u32[]{:S(2)}) collective-permute-start(bf16[3,48,1024]{2,1,0:T(8,128)(2,1)} %slice.94), channel_id=1, source_target_pairs={{0,2},{2,4},{4,6},{6,0},{1,3},{3,5},{5,7},{7,1},{8,10},{10,12},{12... | collective-permute-start | bytes 884744 | tf_op jit(solution)/shard_map/ppermute | solution.py:19
  38.5 28.3 %all-to-all-start = ((bf16[4,128,2048]{2,1,0:T(8,128)(2,1)}), bf16[4,128,2048]{2,1,0:T(8,128)(2,1)}, u32[]{:S(2)}, u32[]{:S(2)}) async-start(bf16[4,128,2048]{2,1,0:T(8,128)(2,1)} %broadcast_in_dim.16), calls=%async_computation | async-start | bytes 4194304 | tf_op jit(solution)/shard_map/all_to_all | solution.py:55
  43.0 28.9 %collective-permute-start.26 = (f32[4,128,8]{1,2,0:T(8,128)S(1)}, f32[4,128,8]{1,2,0:T(8,128)}, u32[]{:S(2)}, u32[]{:S(2)}) collective-permute-start(f32[4,128,8]{1,2,0:T(8,128)S(1)} %all_to_all.15), channel_id=1, source_target_pairs={{0,32},{32,0},{1,33},{33,1},{2,34},{34,2},{3,35},{35,3},{4,36},{36... | collective-permute-start | bytes 49160 | tf_op jit(solution)/shard_map/ppermute | solution.py:56
  60.5 41.5 %collective-permute-start.11 = (bf16[4,2,48,2048]{3,2,1,0:T(8,128)(2,1)}, bf16[4,2,48,2048]{3,2,1,0:T(8,128)(2,1)}, u32[]{:S(2)}, u32[]{:S(2)}) collective-permute-start(bf16[4,2,48,2048]{3,2,1,0:T(8,128)(2,1)} %get-tuple-element.26), channel_id=1, source_target_pairs={{0,8},{8,16},{16,24},{24,0},{1,9},{9,17},{17,25},{25,1},{2,10},{10... | collective-permute-start | bytes 4718600 | tf_op jit(solution)/shard_map/ppermute | solution.py:14
  60.5 36.6 %collective-permute-start.10 = (bf16[4,2,48,2048]{3,2,1,0:T(8,128)(2,1)}, bf16[4,2,48,2048]{3,2,1,0:T(8,128)(2,1)}, u32[]{:S(2)}, u32[]{:S(2)}) collective-permute-start(bf16[4,2,48,2048]{3,2,1,0:T(8,128)(2,1)} %get-tuple-element.26), channel_id=1, source_target_pairs={{0,24},{8,0},{16,8},{24,16},{1,25},{9,1},{17,9},{25,17},{2,26},{10... | collective-permute-start | bytes 4718600 | tf_op jit(solution)/shard_map/ppermute | solution.py:15
  66.9 45.9 %collective-permute-start = (bf16[4,128,2048]{2,1,0:T(8,128)(2,1)}, bf16[4,128,2048]{2,1,0:T(8,128)(2,1)}, u32[]{:S(2)}, u32[]{:S(2)}) collective-permute-start(bf16[4,128,2048]{2,1,0:T(8,128)(2,1)} %all-to-all-done), channel_id=1, source_target_pairs={{0,32},{32,0},{1,33},{33,1},{2,34},{34,2},{3,35},{35,3},{4,36},{36... | collective-permute-start | bytes 6291464 | tf_op jit(solution)/shard_map/ppermute | solution.py:56
  69.0 37.5 %collective-permute-start.14 = (bf16[4,2,48,2048]{3,2,1,0:T(8,128)(2,1)}, bf16[4,2,48,2048]{3,2,1,0:T(8,128)(2,1)}, u32[]{:S(2)}, u32[]{:S(2)}) collective-permute-start(bf16[4,2,48,2048]{3,2,1,0:T(8,128)(2,1)} %get-tuple-element.24), channel_id=1, source_target_pairs={{0,6},{2,0},{4,2},{6,4},{1,7},{3,1},{5,3},{7,5},{8,14},{10,8},{12,... | collective-permute-start | bytes 4718600 | tf_op jit(solution)/shard_map/ppermute | solution.py:15
  71.8 39.6 %collective-permute-start.15 = (bf16[4,2,48,2048]{3,2,1,0:T(8,128)(2,1)}, bf16[4,2,48,2048]{3,2,1,0:T(8,128)(2,1)}, u32[]{:S(2)}, u32[]{:S(2)}) collective-permute-start(bf16[4,2,48,2048]{3,2,1,0:T(8,128)(2,1)} %get-tuple-element.24), channel_id=1, source_target_pairs={{0,2},{2,4},{4,6},{6,0},{1,3},{3,5},{5,7},{7,1},{8,10},{10,12},{12... | collective-permute-start | bytes 4718600 | tf_op jit(solution)/shard_map/ppermute | solution.py:14
  98.3 19.0 %collective-permute-start.13 = (bf16[4,2,48,1024]{3,2,1,0:T(8,128)(2,1)S(1)}, bf16[4,2,48,1024]{3,2,1,0:T(8,128)(2,1)S(1)}, u32[]{:S(2)}, u32[]{:S(2)}) collective-permute-start(bf16[4,2,48,1024]{3,2,1,0:T(8,128)(2,1)S(1)} %slice.99), channel_id=1, source_target_pairs={{0,24},{8,0},{16,8},{24,16},{1,25},{9,1},{17,9},{25,17},{2,26},{10... | collective-permute-start | bytes 2359304 | tf_op jit(solution)/shard_map/ppermute | solution.py:20
  103.3 18.7 %collective-permute-start.12 = (bf16[4,2,48,1024]{3,2,1,0:T(8,128)(2,1)S(1)}, bf16[4,2,48,1024]{3,2,1,0:T(8,128)(2,1)S(1)}, u32[]{:S(2)}, u32[]{:S(2)}) collective-permute-start(bf16[4,2,48,1024]{3,2,1,0:T(8,128)(2,1)S(1)} %slice.98), channel_id=1, source_target_pairs={{0,8},{8,16},{16,24},{24,0},{1,9},{9,17},{17,25},{25,1},{2,10},{10... | collective-permute-start | bytes 2359304 | tf_op jit(solution)/shard_map/ppermute | solution.py:19
  107.7 20.5 %collective-permute-start.17 = (bf16[4,2,48,1024]{3,2,1,0:T(8,128)(2,1)S(1)}, bf16[4,2,48,1024]{3,2,1,0:T(8,128)(2,1)S(1)}, u32[]{:S(2)}, u32[]{:S(2)}) collective-permute-start(bf16[4,2,48,1024]{3,2,1,0:T(8,128)(2,1)S(1)} %slice.101), channel_id=1, source_target_pairs={{0,6},{2,0},{4,2},{6,4},{1,7},{3,1},{5,3},{7,5},{8,14},{10,8},{12,... | collective-permute-start | bytes 2359304 | tf_op jit(solution)/shard_map/ppermute | solution.py:20
  112.6 20.2 %collective-permute-start.16 = (bf16[4,2,48,1024]{3,2,1,0:T(8,128)(2,1)S(1)}, bf16[4,2,48,1024]{3,2,1,0:T(8,128)(2,1)S(1)}, u32[]{:S(2)}, u32[]{:S(2)}) collective-permute-start(bf16[4,2,48,1024]{3,2,1,0:T(8,128)(2,1)S(1)} %slice.100), channel_id=1, source_target_pairs={{0,2},{2,4},{4,6},{6,0},{1,3},{3,5},{5,7},{7,1},{8,10},{10,12},{12... | collective-permute-start | bytes 2359304 | tf_op jit(solution)/shard_map/ppermute | solution.py:19
  136.0 22.3 %collective-permute-start.23 = (bf16[4,48,2048]{2,1,0:T(8,128)(2,1)S(1)}, bf16[4,48,2048]{2,1,0:T(8,128)(2,1)S(1)}, u32[]{:S(2)}, u32[]{:S(2)}) collective-permute-start(bf16[4,48,2048]{2,1,0:T(8,128)(2,1)S(1)} %slice_bitcast_fusion), channel_id=1, source_target_pairs={{0,2},{2,4},{4,6},{6,0},{1,3},{3,5},{5,7},{7,1},{8,10},{10,12},{12... | collective-permute-start | bytes 2359304 | tf_op jit(solution)/shard_map/ppermute | solution.py:14
  136.0 18.4 %collective-permute-start.22 = (bf16[4,48,2048]{2,1,0:T(8,128)(2,1)S(1)}, bf16[4,48,2048]{2,1,0:T(8,128)(2,1)S(1)}, u32[]{:S(2)}, u32[]{:S(2)}) collective-permute-start(bf16[4,48,2048]{2,1,0:T(8,128)(2,1)S(1)} %slice_bitcast_fusion), channel_id=1, source_target_pairs={{0,6},{2,0},{4,2},{6,4},{1,7},{3,1},{5,3},{7,5},{8,14},{10,8},{12,... | collective-permute-start | bytes 2359304 | tf_op jit(solution)/shard_map/ppermute | solution.py:15
  139.3 27.3 %collective-permute-start.19 = (bf16[4,48,2048]{2,1,0:T(8,128)(2,1)S(1)}, bf16[4,48,2048]{2,1,0:T(8,128)(2,1)S(1)}, u32[]{:S(2)}, u32[]{:S(2)}) collective-permute-start(bf16[4,48,2048]{2,1,0:T(8,128)(2,1)S(1)} %slice_bitcast_fusion.1), channel_id=1, source_target_pairs={{0,8},{8,16},{16,24},{24,0},{1,9},{9,17},{17,25},{25,1},{2,10},{10... | collective-permute-start | bytes 2359304 | tf_op jit(solution)/shard_map/ppermute | solution.py:14
  140.2 23.3 %collective-permute-start.18 = (bf16[4,48,2048]{2,1,0:T(8,128)(2,1)S(1)}, bf16[4,48,2048]{2,1,0:T(8,128)(2,1)S(1)}, u32[]{:S(2)}, u32[]{:S(2)}) collective-permute-start(bf16[4,48,2048]{2,1,0:T(8,128)(2,1)S(1)} %slice_bitcast_fusion.1), channel_id=1, source_target_pairs={{0,24},{8,0},{16,8},{24,16},{1,25},{9,1},{17,9},{25,17},{2,26},{10... | collective-permute-start | bytes 2359304 | tf_op jit(solution)/shard_map/ppermute | solution.py:15
  163.5 20.1 %collective-permute-start.21 = (bf16[4,48,1024]{2,1,0:T(8,128)(2,1)S(1)}, bf16[4,48,1024]{2,1,0:T(8,128)(2,1)}, u32[]{:S(2)}, u32[]{:S(2)}) collective-permute-start(bf16[4,48,1024]{2,1,0:T(8,128)(2,1)S(1)} %slice.105), channel_id=1, source_target_pairs={{0,24},{8,0},{16,8},{24,16},{1,25},{9,1},{17,9},{25,17},{2,26},{10... | collective-permute-start | bytes 1179656 | tf_op jit(solution)/shard_map/ppermute | solution.py:20
  167.3 16.3 %collective-permute-start.20 = (bf16[4,48,1024]{2,1,0:T(8,128)(2,1)}, bf16[4,48,1024]{2,1,0:T(8,128)(2,1)}, u32[]{:S(2)}, u32[]{:S(2)}) collective-permute-start(bf16[4,48,1024]{2,1,0:T(8,128)(2,1)} %slice.104), channel_id=1, source_target_pairs={{0,8},{8,16},{16,24},{24,0},{1,9},{9,17},{17,25},{25,1},{2,10},{10... | collective-permute-start | bytes 1179656 | tf_op jit(solution)/shard_map/ppermute | solution.py:19
  (15 other events, 204.3 us)

commit v2 on v1

--- a/solution.py
+++ b/solution.py
@@ -50,9 +50,8 @@
     return sets
 
 
-def spread(value, chips):
-    sent = jnp.broadcast_to(value[None], (chips,) + value.shape)
-    mine = lax.all_to_all(sent, CHIPS, split_axis=0, concat_axis=0, tiled=True)
+def spread(value):
+    mine = lax.all_gather(value, CHIPS, axis=0, tiled=False)
     other = lax.ppermute(mine, "core", perm=SWAP)
     return mine, other
 
@@ -69,8 +68,8 @@
     weight = jnp.sum(
         jnp.where(expert_ids[:, :, None] == experts, gate_weights[:, :, None], 0.0), axis=1
     )
-    rows_mine, rows_other = spread(tokens, chips)
-    weight_mine, weight_other = spread(weight, chips)
+    rows_mine, rows_other = spread(tokens)
+    weight_mine, weight_other = spread(weight)
     rows = jnp.concatenate([rows_mine, rows_other]).reshape(-1, model_width)
     table = jnp.concatenate([weight_mine, weight_other]).reshape(-1, experts.shape[0])
     scale = lax.dynamic_index_in_dim(table, expert, axis=1, keepdims=True)

time: 247 us -> 256 us (1.036)
  between operations: 0.44 us -> 13.8 us
  waiting for transfers between devices: 71.2 us -> 65.9 us
  blocking collectives: 39 us -> 43.3 us
    all_gather x0 -> x1, blocking collectives: none -> 12.5 us  [spread(): mine = lax.all_gather(value, CHIPS, axis=0, tiled=False)]
    all_to_all x1 -> x0, blocking collectives: 9.63 us -> none  [spread(): mine = lax.all_to_all(sent, CHIPS, split_axis=0, concat_axis=0, tiled=True)]
    ppermute x6, waiting for transfers between devices: 28.2 us -> 20.3 us  [ring_of_four(): from_plus = lax.ppermute(value, axis, perm=behind)]
    ppermute x6, waiting for transfers between devices: 13.2 us -> 18.2 us  [ring_of_four(): lax.ppermute(from_minus[..., :half], axis, perm=ahead)]
    all_to_all x1 -> x0, starting transfers between devices: 4.44 us -> none  [spread(): mine = lax.all_to_all(sent, CHIPS, split_axis=0, concat_axis=0, tiled=True)]
    all_to_all x1 -> x0, waiting for transfers between devices: 3.08 us -> none  [spread(): mine = lax.all_to_all(sent, CHIPS, split_axis=0, concat_axis=0, tiled=True)]
    slice x2, local copies, waits for them, and re-layouts: 5.03 us -> 7.99 us  [expert_weights(): sets.append((gate_up[0], gate_up[1], down.reshape(-1, width)))]
    broadcast_in_dim x2 -> x0, local copies, waits for them, and re-layouts: 2.66 us -> none  [spread(): sent = jnp.broadcast_to(value[None], (chips,) + value.shape)]
  transfers between devices with their start and end apart: 29 -> 29, of which waited for: 14 -> 16; matrix products, arithmetic and copies ran while one was open for 23% -> 14% of each run, Pallas kernels for 0% -> 0%
where the time goes in v2:
time: 256 us; the launch traced here: 255 us
  waiting for transfers between devices  65.9 us (26%)
  starting transfers between devices  46.3 us (18%)
  blocking collectives  43.3 us (17%)
  matrix products  39.2 us (15%)
  local copies, waits for them, and re-layouts  27.4 us (11%)
  other arithmetic  19.3 us (8%)
  between operations  13.8 us (5%)
    all_to_all x1, blocking collectives, per_device(): lax.all_to_all(partial, CHIPS, split_axis=0, concat_axis=0, tiled=True)  30.9 us
    dot_general x2, matrix products, per_device(): part = jnp.dot(hidden, weights[2], preferred_element_type=jnp.float32)  29 us
    ppermute x6, starting transfers between devices, ring_of_four(): lax.ppermute(from_plus[..., half:], axis, perm=behind)  23.1 us
    ppermute x6, starting transfers between devices, ring_of_four(): from_plus = lax.ppermute(value, axis, perm=behind)  20.7 us
    ppermute x6, waiting for transfers between devices, ring_of_four(): from_plus = lax.ppermute(value, axis, perm=behind)  20.3 us
    ppermute x6, waiting for transfers between devices, ring_of_four(): lax.ppermute(from_minus[..., :half], axis, perm=ahead)  18.2 us
    another operation x12, other arithmetic, ring_of_four(): return jnp.stack([value, from_plus, far, from_minus])  16.5 us
    all_gather x1, blocking collectives, spread(): mine = lax.all_gather(value, CHIPS, axis=0, tiled=False)  12.5 us
  transfers between devices with their start and end apart: 29, of which 16 were waited for; matrix products, arithmetic and copies ran while one was open for 14% of the time, Pallas kernels for 0%

profile of v2, /device:TPU:0, one launch (start us, length us, event | category | flops | bytes accessed | tf_op | source)
XLA Modules:
  0.0 255.3 jit_solution(15624583038567841618)
XLA Ops:
  10.9 4.0 %collective-permute-start.1 = (bf16[3,48,2048]{2,1,0:T(8,128)(2,1)S(1)}, bf16[3,48,2048]{2,1,0:T(8,128)(2,1)S(1)}, u32[]{:S(2)}, u32[]{:S(2)}) collective-permute-start(bf16[3,48,2048]{2,1,0:T(8,128)(2,1)S(1)} %bitcast.89), channel_id=1, source_target_pairs={{0,6},{2,0},{4,2},{6,4},{1,7},{3,1},{5,3},{7,5},{8,14},{10,8},{12,... | collective-permute-start | bytes 1769480 | tf_op jit(solution)/shard_map/ppermute | solution.py:15
  15.0 9.3 %collective-permute-done.5 = bf16[3,48,2048]{2,1,0:T(8,128)(2,1)S(1)} collective-permute-done((bf16[3,48,2048]{2,1,0:T(8,128)(2,1)S(1)}, bf16[3,48,2048]{2,1,0:T(8,128)(2,1)S(1)}, u32[]{:S(2)}, u32[]{:S(2)}) %collective-permute-start.5) | collective-permute-done | bytes 589856 | tf_op jit(solution)/shard_map/ppermute | solution.py:34
  27.3 4.0 %collective-permute-start.4 = (bf16[3,48,1024]{2,1,0:T(8,128)(2,1)S(1)}, bf16[3,48,1024]{2,1,0:T(8,128)(2,1)S(1)}, u32[]{:S(2)}, u32[]{:S(2)}) collective-permute-start(bf16[3,48,1024]{2,1,0:T(8,128)(2,1)S(1)} %slice.95), channel_id=1, source_target_pairs={{0,6},{2,0},{4,2},{6,4},{1,7},{3,1},{5,3},{7,5},{8,14},{10,8},{12,... | collective-permute-start | bytes 884744 | tf_op jit(solution)/shard_map/ppermute | solution.py:20
  31.4 7.5 %collective-permute-done.6 = bf16[3,48,2048]{2,1,0:T(8,128)(2,1)S(1)} collective-permute-done((bf16[3,48,2048]{2,1,0:T(8,128)(2,1)S(1)}, bf16[3,48,2048]{2,1,0:T(8,128)(2,1)S(1)}, u32[]{:S(2)}, u32[]{:S(2)}) %collective-permute-start.6) | collective-permute-done | bytes 589856 | tf_op jit(solution)/shard_map/ppermute | solution.py:15
  38.9 3.8 %collective-permute-start.9 = (bf16[3,48,1024]{2,1,0:T(8,128)(2,1)S(1)}, bf16[3,48,1024]{2,1,0:T(8,128)(2,1)S(1)}, u32[]{:S(2)}, u32[]{:S(2)}) collective-permute-start(bf16[3,48,1024]{2,1,0:T(8,128)(2,1)S(1)} %slice.97), channel_id=1, source_target_pairs={{0,24},{8,0},{16,8},{24,16},{1,25},{9,1},{17,9},{25,17},{2,26},{10... | collective-permute-start | bytes 884744 | tf_op jit(solution)/shard_map/ppermute | solution.py:20
  43.2 4.0 %collective-permute-done.9 = bf16[3,48,1024]{2,1,0:T(8,128)(2,1)S(1)} collective-permute-done((bf16[3,48,1024]{2,1,0:T(8,128)(2,1)S(1)}, bf16[3,48,1024]{2,1,0:T(8,128)(2,1)S(1)}, u32[]{:S(2)}, u32[]{:S(2)}) %collective-permute-start.9) | collective-permute-done | bytes 294944 | tf_op jit(solution)/shard_map/ppermute | solution.py:20
  58.7 4.0 %collective-permute-start.14 = (bf16[4,2,48,2048]{3,2,1,0:T(8,128)(2,1)}, bf16[4,2,48,2048]{3,2,1,0:T(8,128)(2,1)}, u32[]{:S(2)}, u32[]{:S(2)}) collective-permute-start(bf16[4,2,48,2048]{3,2,1,0:T(8,128)(2,1)} %get-tuple-element.24), channel_id=1, source_target_pairs={{0,6},{2,0},{4,2},{6,4},{1,7},{3,1},{5,3},{7,5},{8,14},{10,8},{12,... | collective-permute-start | bytes 4718600 | tf_op jit(solution)/shard_map/ppermute | solution.py:15
  62.8 12.5 %all-gather.1 = f32[512,8]{0,1:T(8,128)S(1)} all-gather(f32[128,8]{0,1:T(8,128)S(1)} %select_reduce_fusion), channel_id=3, replica_groups=mesh['yhi'=2,'core'=2,'x'=4,'z'=4,'ylo'=2] {'yhi','ylo'}, dimensions={0}, use_global_device_ids=true | all-gather | bytes 20480 | tf_op jit(solution)/shard_map/all_gather | solution.py:54
  76.5 10.6 %collective-permute-done.10 = bf16[4,2,48,2048]{3,2,1,0:T(8,128)(2,1)} collective-permute-done((bf16[4,2,48,2048]{3,2,1,0:T(8,128)(2,1)}, bf16[4,2,48,2048]{3,2,1,0:T(8,128)(2,1)}, u32[]{:S(2)}, u32[]{:S(2)}) %collective-permute-start.10) | collective-permute-done | bytes 1572896 | tf_op jit(solution)/shard_map/ppermute | solution.py:15
  88.3 3.8 %collective-permute-start.13 = (bf16[4,2,48,1024]{3,2,1,0:T(8,128)(2,1)S(1)}, bf16[4,2,48,1024]{3,2,1,0:T(8,128)(2,1)S(1)}, u32[]{:S(2)}, u32[]{:S(2)}) collective-permute-start(bf16[4,2,48,1024]{3,2,1,0:T(8,128)(2,1)S(1)} %slice.99), channel_id=1, source_target_pairs={{0,24},{8,0},{16,8},{24,16},{1,25},{9,1},{17,9},{25,17},{2,26},{10... | collective-permute-start | bytes 2359304 | tf_op jit(solution)/shard_map/ppermute | solution.py:20
  94.5 4.1 %collective-permute-start.17 = (bf16[4,2,48,1024]{3,2,1,0:T(8,128)(2,1)S(1)}, bf16[4,2,48,1024]{3,2,1,0:T(8,128)(2,1)S(1)}, u32[]{:S(2)}, u32[]{:S(2)}) collective-permute-start(bf16[4,2,48,1024]{3,2,1,0:T(8,128)(2,1)S(1)} %slice.101), channel_id=1, source_target_pairs={{0,6},{2,0},{4,2},{6,4},{1,7},{3,1},{5,3},{7,5},{8,14},{10,8},{12,... | collective-permute-start | bytes 2359304 | tf_op jit(solution)/shard_map/ppermute | solution.py:20
  104.4 4.7 %collective-permute-done.12 = bf16[4,2,48,1024]{3,2,1,0:T(8,128)(2,1)S(1)} collective-permute-done((bf16[4,2,48,1024]{3,2,1,0:T(8,128)(2,1)S(1)}, bf16[4,2,48,1024]{3,2,1,0:T(8,128)(2,1)S(1)}, u32[]{:S(2)}, u32[]{:S(2)}) %collective-permute-start.12) | collective-permute-done | bytes 786464 | tf_op jit(solution)/shard_map/ppermute | solution.py:19
  110.8 4.7 %collective-permute-done.16 = bf16[4,2,48,1024]{3,2,1,0:T(8,128)(2,1)S(1)} collective-permute-done((bf16[4,2,48,1024]{3,2,1,0:T(8,128)(2,1)S(1)}, bf16[4,2,48,1024]{3,2,1,0:T(8,128)(2,1)S(1)}, u32[]{:S(2)}, u32[]{:S(2)}) %collective-permute-start.16) | collective-permute-done | bytes 786464 | tf_op jit(solution)/shard_map/ppermute | solution.py:19
  115.6 5.2 %pad_maximum_fusion = bf16[4,4,2,48,2048]{4,3,2,1,0:T(8,128)(2,1)} fusion(bf16[1,4,2,48,2048]{4,3,2,1,0:T(8,128)(2,1)} %bitcast.17, bf16[1,4,2,48,2048]{4,3,2,1,0:T(8,128)(2,1)S(1)} %maximum_bitcast_fusion, bf16[1,4,2,48,2048]{4,3,2,1,0:T(8,128)(2,1)} %bitcast.15, bf16[1,4,2,48,2048]{4,3,2,1,0:T(8,128)(2,1)S(1)} %copy-done.1), kind=kLoop, calls=%fused_computation.2 | loop fusion | flops 9437184 | bytes 12582912 | tf_op jit(solution)/shard_map/stack | solution.py:24
  120.8 5.1 %pad_maximum_fusion.1 = bf16[4,4,2,48,2048]{4,3,2,1,0:T(8,128)(2,1)} fusion(bf16[1,4,2,48,2048]{4,3,2,1,0:T(8,128)(2,1)} %bitcast.21, bf16[1,4,2,48,2048]{4,3,2,1,0:T(8,128)(2,1)S(1)} %maximum_bitcast_fusion.1, bf16[1,4,2,48,2048]{4,3,2,1,0:T(8,128)(2,1)} %bitcast.19, bf16[1,4,2,48,2048]{4,3,2,1,0:T(8,128)(2,1)S(1)} %copy-done.2), kind=kLoop, calls=%fused_computation.3 | loop fusion | flops 9437184 | bytes 12582912 | tf_op jit(solution)/shard_map/stack | solution.py:24
  132.7 5.5 %fusion.12 = (bf16[1,4,4,48,2048]{4,3,0,2,1:T(8,128)(2,1)S(1)}, bf16[1,4,4,48,2048]{4,3,0,2,1:T(8,128)(2,1)}) fusion(bf16[2,4,4,48,2048]{4,3,0,2,1:T(8,128)(2,1)} %bitcast.74), kind=kLoop, calls=%fused_computation.44 | loop fusion | bytes 12582912 | tf_op jit(solution)/shard_map/slice | solution.py:49
  154.4 4.8 %collective-permute-done.20 = bf16[4,48,1024]{2,1,0:T(8,128)(2,1)S(1)} collective-permute-done((bf16[4,48,1024]{2,1,0:T(8,128)(2,1)S(1)}, bf16[4,48,1024]{2,1,0:T(8,128)(2,1)S(1)}, u32[]{:S(2)}, u32[]{:S(2)}) %collective-permute-start.20) | collective-permute-done | bytes 393248 | tf_op jit(solution)/shard_map/ppermute | solution.py:19
  164.7 5.1 %fusion.18 = f32[1024,768]{1,0:T(8,128)} fusion(bf16[1024,2048]{1,0:T(8,128)(2,1)S(1)} %bitcast.76, bf16[768,2048]{1,0:T(8,128)(2,1)S(1)} %bitcast.86), kind=kOutput, calls=%fused_computation.48 | convolution fusion | flops 3221225472 | bytes 10485760 | tf_op jit(solution)/shard_map/dot_general | solution.py:79
  169.9 5.1 %fusion.17 = f32[1024,768]{1,0:T(8,128)} fusion(bf16[1024,2048]{1,0:T(8,128)(2,1)S(1)} %bitcast.77, bf16[768,2048]{1,0:T(8,128)(2,1)S(1)} %bitcast.88), kind=kOutput, calls=%fused_computation.47 | convolution fusion | flops 3221225472 | bytes 10485760 | tf_op jit(solution)/shard_map/dot_general | solution.py:79
  174.9 14.1 %fusion.3 = f32[1024,2048]{1,0:T(8,128)} fusion(bf16[768,2048]{1,0:T(8,128)(2,1)} %bitcast.84, f32[1024,768]{1,0:T(8,128)} %fusion.18, bf16[1024,2048]{1,0:T(8,128)(2,1)} %bitcast.78, bf16[768,2048]{1,0:T(8,128)(2,1)} %bitcast.85), kind=kOutput, calls=%fused_computation.16 | convolution fusion | flops 6447169536 | bytes 22020096 | tf_op jit(solution)/shard_map/dot_general | solution.py:82
  189.0 15.0 %convert_multiply_fusion = f32[1024,2048]{1,0:T(8,128)} fusion(f32[1024,2048]{1,0:T(8,128)} %fusion.3, f32[1024]{0:T(1024)S(1)} %bitcast.103, bf16[768,2048]{1,0:T(8,128)(2,1)S(1)} %bitcast.83, f32[1024,768]{1,0:T(8,128)} %fusion.17, bf16[1024,2048]{1,0:T(8,128)(2,1)} %bitcast.79, bf16[768,2048]{1,0:T(8,128)(2,1)} %bitcast.87), kind=kOutput, calls=%fused_computation | convolution fusion | flops 6455558144 | bytes 30412800 | tf_op jit(solution)/shard_map/dot_general | solution.py:82
  204.0 4.0 %fusion.10 = (f32[512,2048]{1,0:T(8,128)S(1)}, f32[512,2048]{1,0:T(8,128)S(1)}) fusion(f32[1024,2048]{1,0:T(8,128)} %convert_multiply_fusion), kind=kLoop, calls=%fused_computation.42 | loop fusion | bytes 16777216 | tf_op jit(solution)/shard_map/slice | solution.py:87
  208.1 7.1 %collective-permute-done.27 = f32[4,128,2048]{2,1,0:T(8,128)S(1)} collective-permute-done((f32[4,128,2048]{2,1,0:T(8,128)S(1)}, f32[4,128,2048]{2,1,0:T(8,128)S(1)}, u32[]{:S(2)}, u32[]{:S(2)}) %collective-permute-start.27) | collective-permute-done | bytes 4194336 | tf_op jit(solution)/shard_map/ppermute | solution.py:87
  216.2 30.9 %all_to_all.5 = bf16[4,128,2048]{2,1,0:T(8,128)(2,1)S(1)} all-to-all(bf16[4,128,2048]{2,1,0:T(8,128)(2,1)S(1)} %add_convert_fusion.1), channel_id=1, replica_groups=mesh['yhi'=2,'core'=2,'x'=4,'z'=4,'ylo'=2] {'yhi','ylo'}, dimensions={0} | all-to-all | bytes 4194304 | tf_op jit(solution)/shard_map/all_to_all | solution.py:89
  (111 shorter events, 62.6 us)
Async XLA Ops:
  6.5 125.9 %all-gather.4.cloned.1.call-start = ((), (), s32[]{:S(2)}) async-start(), calls=%async_computation.1 | async-start | bytes 2621440 | tf_op jit(solution)/shard_map/all_gather | solution.py:54
  9.2 15.1 %collective-permute-start.5 = (bf16[3,48,2048]{2,1,0:T(8,128)(2,1)S(1)}, bf16[3,48,2048]{2,1,0:T(8,128)(2,1)S(1)}, u32[]{:S(2)}, u32[]{:S(2)}) collective-permute-start(bf16[3,48,2048]{2,1,0:T(8,128)(2,1)S(1)} %get-tuple-element.27), channel_id=1, source_target_pairs={{0,1},{1,0},{2,3},{3,2},{4,5},{5,4},{6,7},{7,6},{8,9},{9,8},{10,11... | collective-permute-start | bytes 1769480 | tf_op jit(solution)/shard_map/ppermute | solution.py:34
  10.9 16.3 %collective-permute-start.1 = (bf16[3,48,2048]{2,1,0:T(8,128)(2,1)S(1)}, bf16[3,48,2048]{2,1,0:T(8,128)(2,1)S(1)}, u32[]{:S(2)}, u32[]{:S(2)}) collective-permute-start(bf16[3,48,2048]{2,1,0:T(8,128)(2,1)S(1)} %bitcast.89), channel_id=1, source_target_pairs={{0,6},{2,0},{4,2},{6,4},{1,7},{3,1},{5,3},{7,5},{8,14},{10,8},{12,... | collective-permute-start | bytes 1769480 | tf_op jit(solution)/shard_map/ppermute | solution.py:15
  15.0 16.4 %collective-permute-start.2 = (bf16[3,48,2048]{2,1,0:T(8,128)(2,1)S(1)}, bf16[3,48,2048]{2,1,0:T(8,128)(2,1)S(1)}, u32[]{:S(2)}, u32[]{:S(2)}) collective-permute-start(bf16[3,48,2048]{2,1,0:T(8,128)(2,1)S(1)} %bitcast.90), channel_id=1, source_target_pairs={{0,2},{2,4},{4,6},{6,0},{1,3},{3,5},{5,7},{7,1},{8,10},{10,12},{12... | collective-permute-start | bytes 1769480 | tf_op jit(solution)/shard_map/ppermute | solution.py:14
  24.3 14.6 %collective-permute-start.6 = (bf16[3,48,2048]{2,1,0:T(8,128)(2,1)S(1)}, bf16[3,48,2048]{2,1,0:T(8,128)(2,1)S(1)}, u32[]{:S(2)}, u32[]{:S(2)}) collective-permute-start(bf16[3,48,2048]{2,1,0:T(8,128)(2,1)S(1)} %collective-permute-done.5), channel_id=1, source_target_pairs={{0,24},{8,0},{16,8},{24,16},{1,25},{9,1},{17,9},{25,17},{2,26},{10... | collective-permute-start | bytes 1769480 | tf_op jit(solution)/shard_map/ppermute | solution.py:15
  27.2 15.5 %collective-permute-start.7 = (bf16[3,48,2048]{2,1,0:T(8,128)(2,1)S(1)}, bf16[3,48,2048]{2,1,0:T(8,128)(2,1)S(1)}, u32[]{:S(2)}, u32[]{:S(2)}) collective-permute-start(bf16[3,48,2048]{2,1,0:T(8,128)(2,1)S(1)} %collective-permute-done.5), channel_id=1, source_target_pairs={{0,8},{8,16},{16,24},{24,0},{1,9},{9,17},{17,25},{25,1},{2,10},{10... | collective-permute-start | bytes 1769480 | tf_op jit(solution)/shard_map/ppermute | solution.py:14
  27.3 15.5 %collective-permute-start.4 = (bf16[3,48,1024]{2,1,0:T(8,128)(2,1)S(1)}, bf16[3,48,1024]{2,1,0:T(8,128)(2,1)S(1)}, u32[]{:S(2)}, u32[]{:S(2)}) collective-permute-start(bf16[3,48,1024]{2,1,0:T(8,128)(2,1)S(1)} %slice.95), channel_id=1, source_target_pairs={{0,6},{2,0},{4,2},{6,4},{1,7},{3,1},{5,3},{7,5},{8,14},{10,8},{12,... | collective-permute-start | bytes 884744 | tf_op jit(solution)/shard_map/ppermute | solution.py:20
  31.3 11.5 %collective-permute-start.3 = (bf16[3,48,1024]{2,1,0:T(8,128)(2,1)S(1)}, bf16[3,48,1024]{2,1,0:T(8,128)(2,1)S(1)}, u32[]{:S(2)}, u32[]{:S(2)}) collective-permute-start(bf16[3,48,1024]{2,1,0:T(8,128)(2,1)S(1)} %slice.94), channel_id=1, source_target_pairs={{0,2},{2,4},{4,6},{6,0},{1,3},{3,5},{5,7},{7,1},{8,10},{10,12},{12... | collective-permute-start | bytes 884744 | tf_op jit(solution)/shard_map/ppermute | solution.py:19
  53.4 38.7 %collective-permute-start.11 = (bf16[4,2,48,2048]{3,2,1,0:T(8,128)(2,1)}, bf16[4,2,48,2048]{3,2,1,0:T(8,128)(2,1)}, u32[]{:S(2)}, u32[]{:S(2)}) collective-permute-start(bf16[4,2,48,2048]{3,2,1,0:T(8,128)(2,1)} %get-tuple-element.26), channel_id=1, source_target_pairs={{0,8},{8,16},{16,24},{24,0},{1,9},{9,17},{17,25},{25,1},{2,10},{10... | collective-permute-start | bytes 4718600 | tf_op jit(solution)/shard_map/ppermute | solution.py:14
  53.4 33.7 %collective-permute-start.10 = (bf16[4,2,48,2048]{3,2,1,0:T(8,128)(2,1)}, bf16[4,2,48,2048]{3,2,1,0:T(8,128)(2,1)}, u32[]{:S(2)}, u32[]{:S(2)}) collective-permute-start(bf16[4,2,48,2048]{3,2,1,0:T(8,128)(2,1)} %get-tuple-element.26), channel_id=1, source_target_pairs={{0,24},{8,0},{16,8},{24,16},{1,25},{9,1},{17,9},{25,17},{2,26},{10... | collective-permute-start | bytes 4718600 | tf_op jit(solution)/shard_map/ppermute | solution.py:15
  58.7 34.6 %collective-permute-start.14 = (bf16[4,2,48,2048]{3,2,1,0:T(8,128)(2,1)}, bf16[4,2,48,2048]{3,2,1,0:T(8,128)(2,1)}, u32[]{:S(2)}, u32[]{:S(2)}) collective-permute-start(bf16[4,2,48,2048]{3,2,1,0:T(8,128)(2,1)} %get-tuple-element.24), channel_id=1, source_target_pairs={{0,6},{2,0},{4,2},{6,4},{1,7},{3,1},{5,3},{7,5},{8,14},{10,8},{12,... | collective-permute-start | bytes 4718600 | tf_op jit(solution)/shard_map/ppermute | solution.py:15
  62.8 35.9 %collective-permute-start.15 = (bf16[4,2,48,2048]{3,2,1,0:T(8,128)(2,1)}, bf16[4,2,48,2048]{3,2,1,0:T(8,128)(2,1)}, u32[]{:S(2)}, u32[]{:S(2)}) collective-permute-start(bf16[4,2,48,2048]{3,2,1,0:T(8,128)(2,1)} %get-tuple-element.24), channel_id=1, source_target_pairs={{0,2},{2,4},{4,6},{6,0},{1,3},{3,5},{5,7},{7,1},{8,10},{10,12},{12... | collective-permute-start | bytes 4718600 | tf_op jit(solution)/shard_map/ppermute | solution.py:14
  88.3 16.1 %collective-permute-start.13 = (bf16[4,2,48,1024]{3,2,1,0:T(8,128)(2,1)S(1)}, bf16[4,2,48,1024]{3,2,1,0:T(8,128)(2,1)S(1)}, u32[]{:S(2)}, u32[]{:S(2)}) collective-permute-start(bf16[4,2,48,1024]{3,2,1,0:T(8,128)(2,1)S(1)} %slice.99), channel_id=1, source_target_pairs={{0,24},{8,0},{16,8},{24,16},{1,25},{9,1},{17,9},{25,17},{2,26},{10... | collective-permute-start | bytes 2359304 | tf_op jit(solution)/shard_map/ppermute | solution.py:20
  93.3 15.9 %collective-permute-start.12 = (bf16[4,2,48,1024]{3,2,1,0:T(8,128)(2,1)S(1)}, bf16[4,2,48,1024]{3,2,1,0:T(8,128)(2,1)S(1)}, u32[]{:S(2)}, u32[]{:S(2)}) collective-permute-start(bf16[4,2,48,1024]{3,2,1,0:T(8,128)(2,1)S(1)} %slice.98), channel_id=1, source_target_pairs={{0,8},{8,16},{16,24},{24,0},{1,9},{9,17},{17,25},{25,1},{2,10},{10... | collective-permute-start | bytes 2359304 | tf_op jit(solution)/shard_map/ppermute | solution.py:19
  94.5 16.2 %collective-permute-start.17 = (bf16[4,2,48,1024]{3,2,1,0:T(8,128)(2,1)S(1)}, bf16[4,2,48,1024]{3,2,1,0:T(8,128)(2,1)S(1)}, u32[]{:S(2)}, u32[]{:S(2)}) collective-permute-start(bf16[4,2,48,1024]{3,2,1,0:T(8,128)(2,1)S(1)} %slice.101), channel_id=1, source_target_pairs={{0,6},{2,0},{4,2},{6,4},{1,7},{3,1},{5,3},{7,5},{8,14},{10,8},{12,... | collective-permute-start | bytes 2359304 | tf_op jit(solution)/shard_map/ppermute | solution.py:20
  99.8 15.6 %collective-permute-start.16 = (bf16[4,2,48,1024]{3,2,1,0:T(8,128)(2,1)S(1)}, bf16[4,2,48,1024]{3,2,1,0:T(8,128)(2,1)S(1)}, u32[]{:S(2)}, u32[]{:S(2)}) collective-permute-start(bf16[4,2,48,1024]{3,2,1,0:T(8,128)(2,1)S(1)} %slice.100), channel_id=1, source_target_pairs={{0,2},{2,4},{4,6},{6,0},{1,3},{3,5},{5,7},{7,1},{8,10},{10,12},{12... | collective-permute-start | bytes 2359304 | tf_op jit(solution)/shard_map/ppermute | solution.py:19
  125.9 18.2 %collective-permute-start.23 = (bf16[4,48,2048]{2,1,0:T(8,128)(2,1)S(1)}, bf16[4,48,2048]{2,1,0:T(8,128)(2,1)S(1)}, u32[]{:S(2)}, u32[]{:S(2)}) collective-permute-start(bf16[4,48,2048]{2,1,0:T(8,128)(2,1)S(1)} %slice_bitcast_fusion), channel_id=1, source_target_pairs={{0,2},{2,4},{4,6},{6,0},{1,3},{3,5},{5,7},{7,1},{8,10},{10,12},{12... | collective-permute-start | bytes 2359304 | tf_op jit(solution)/shard_map/ppermute | solution.py:14
  125.9 14.4 %collective-permute-start.22 = (bf16[4,48,2048]{2,1,0:T(8,128)(2,1)S(1)}, bf16[4,48,2048]{2,1,0:T(8,128)(2,1)S(1)}, u32[]{:S(2)}, u32[]{:S(2)}) collective-permute-start(bf16[4,48,2048]{2,1,0:T(8,128)(2,1)S(1)} %slice_bitcast_fusion), channel_id=1, source_target_pairs={{0,6},{2,0},{4,2},{6,4},{1,7},{3,1},{5,3},{7,5},{8,14},{10,8},{12,... | collective-permute-start | bytes 2359304 | tf_op jit(solution)/shard_map/ppermute | solution.py:15
  129.2 19.9 %collective-permute-start.19 = (bf16[4,48,2048]{2,1,0:T(8,128)(2,1)S(1)}, bf16[4,48,2048]{2,1,0:T(8,128)(2,1)}, u32[]{:S(2)}, u32[]{:S(2)}) collective-permute-start(bf16[4,48,2048]{2,1,0:T(8,128)(2,1)S(1)} %slice_bitcast_fusion.1), channel_id=1, source_target_pairs={{0,8},{8,16},{16,24},{24,0},{1,9},{9,17},{17,25},{25,1},{2,10},{10... | collective-permute-start | bytes 2359304 | tf_op jit(solution)/shard_map/ppermute | solution.py:14
  129.2 15.1 %collective-permute-start.18 = (bf16[4,48,2048]{2,1,0:T(8,128)(2,1)S(1)}, bf16[4,48,2048]{2,1,0:T(8,128)(2,1)}, u32[]{:S(2)}, u32[]{:S(2)}) collective-permute-start(bf16[4,48,2048]{2,1,0:T(8,128)(2,1)S(1)} %slice_bitcast_fusion.1), channel_id=1, source_target_pairs={{0,24},{8,0},{16,8},{24,16},{1,25},{9,1},{17,9},{25,17},{2,26},{10... | collective-permute-start | bytes 2359304 | tf_op jit(solution)/shard_map/ppermute | solution.py:15
  132.4 31.9 %collective-permute-start = (bf16[4,128,2048]{2,1,0:T(8,128)(2,1)}, bf16[4,128,2048]{2,1,0:T(8,128)(2,1)S(1)}, u32[]{:S(2)}, u32[]{:S(2)}) collective-permute-start(bf16[4,128,2048]{2,1,0:T(8,128)(2,1)} %bitcast.91), channel_id=1, source_target_pairs={{0,32},{32,0},{1,33},{33,1},{2,34},{34,2},{3,35},{35,3},{4,36},{36... | collective-permute-start | bytes 6291464 | tf_op jit(solution)/shard_map/ppermute | solution.py:55
  140.3 12.4 %collective-permute-start.25 = (bf16[4,48,1024]{2,1,0:T(8,128)(2,1)S(1)}, bf16[4,48,1024]{2,1,0:T(8,128)(2,1)S(1)}, u32[]{:S(2)}, u32[]{:S(2)}) collective-permute-start(bf16[4,48,1024]{2,1,0:T(8,128)(2,1)S(1)} %slice.109), channel_id=1, source_target_pairs={{0,6},{2,0},{4,2},{6,4},{1,7},{3,1},{5,3},{7,5},{8,14},{10,8},{12,... | collective-permute-start | bytes 1179656 | tf_op jit(solution)/shard_map/ppermute | solution.py:20
  144.1 9.1 %collective-permute-start.24 = (bf16[4,48,1024]{2,1,0:T(8,128)(2,1)S(1)}, bf16[4,48,1024]{2,1,0:T(8,128)(2,1)S(1)}, u32[]{:S(2)}, u32[]{:S(2)}) collective-permute-start(bf16[4,48,1024]{2,1,0:T(8,128)(2,1)S(1)} %slice.108), channel_id=1, source_target_pairs={{0,2},{2,4},{4,6},{6,0},{1,3},{3,5},{5,7},{7,1},{8,10},{10,12},{12... | collective-permute-start | bytes 1179656 | tf_op jit(solution)/shard_map/ppermute | solution.py:19
  150.1 9.1 %collective-permute-start.20 = (bf16[4,48,1024]{2,1,0:T(8,128)(2,1)S(1)}, bf16[4,48,1024]{2,1,0:T(8,128)(2,1)S(1)}, u32[]{:S(2)}, u32[]{:S(2)}) collective-permute-start(bf16[4,48,1024]{2,1,0:T(8,128)(2,1)S(1)} %slice.104), channel_id=1, source_target_pairs={{0,8},{8,16},{16,24},{24,0},{1,9},{9,17},{17,25},{25,1},{2,10},{10... | collective-permute-start | bytes 1179656 | tf_op jit(solution)/shard_map/ppermute | solution.py:19
  (19 other events, 171.1 us)
Sparse Core Ops, SparseCore 0:
  62.9 29.9 all-gather.3

commit v3 on v1

--- a/solution.py
+++ b/solution.py
@@ -69,10 +69,16 @@
     weight = jnp.sum(
         jnp.where(expert_ids[:, :, None] == experts, gate_weights[:, :, None], 0.0), axis=1
     )
-    rows_mine, rows_other = spread(tokens, chips)
-    weight_mine, weight_other = spread(weight, chips)
-    rows = jnp.concatenate([rows_mine, rows_other]).reshape(-1, model_width)
-    table = jnp.concatenate([weight_mine, weight_other]).reshape(-1, experts.shape[0])
+    high = weight.astype(jnp.bfloat16)
+    low = (weight - high.astype(jnp.float32)).astype(jnp.bfloat16)
+    packed = jnp.concatenate([high, low], axis=1).reshape(-1, model_width)
+    extra = packed.shape[0]
+    packed = jnp.pad(packed, ((0, 16 - extra), (0, 0)))
+    mine, other = spread(jnp.concatenate([tokens, packed]), chips)
+    both = jnp.concatenate([mine, other])
+    rows = both[:, :token_count].reshape(-1, model_width)
+    halves = both[:, token_count:token_count + extra].reshape(-1, 2, experts.shape[0])
+    table = halves[:, 0].astype(jnp.float32) + halves[:, 1].astype(jnp.float32)
     scale = lax.dynamic_index_in_dim(table, expert, axis=1, keepdims=True)
 
     out = None

time: 247 us -> 242 us (0.980)
  waiting for transfers between devices: 71.2 us -> 59.1 us
  local copies, waits for them, and re-layouts: 26.9 us -> 37 us
  blocking collectives: 39 us -> 30.9 us
  other arithmetic: 20 us -> 23.5 us
    ppermute x6, waiting for transfers between devices: 28.2 us -> 17.9 us  [ring_of_four(): from_plus = lax.ppermute(value, axis, perm=behind)]
    all_to_all x1 -> x0, blocking collectives: 9.63 us -> none  [spread(): mine = lax.all_to_all(sent, CHIPS, split_axis=0, concat_axis=0, tiled=True)]
    ppermute x6, waiting for transfers between devices: 0.02 us -> 8.22 us  [ring_of_four(): from_minus = lax.ppermute(value, axis, perm=ahead)]
    ppermute x6, waiting for transfers between devices: 10.2 us -> 2.39 us  [ring_of_four(): lax.ppermute(from_plus[..., half:], axis, perm=behind)]
    dynamic_slice x0 -> x1, other arithmetic: none -> 4.09 us  [per_device(): scale = lax.dynamic_index_in_dim(table, expert, axis=1, keepdims=True)]
    slice x6, local copies, waits for them, and re-layouts: 3.18 us -> 6.38 us  [ring_of_four(): from_plus[..., half:]]
    all_to_all x1, waiting for transfers between devices: 3.08 us -> 0.01 us  [spread(): mine = lax.all_to_all(sent, CHIPS, split_axis=0, concat_axis=0, tiled=True)]
    ppermute x6, starting transfers between devices: 0.98 us -> 3.66 us  [ring_of_four(): from_minus = lax.ppermute(value, axis, perm=ahead)]
  transfers between devices with their start and end apart: 29 -> 28, of which waited for: 14 -> 9; matrix products, arithmetic and copies ran while one was open for 23% -> 29% of each run, Pallas kernels for 0% -> 0%
where the time goes in v3:
time: 242 us; the launch traced here: 241 us
  waiting for transfers between devices  59.1 us (24%)
  starting transfers between devices  49.4 us (20%)
  matrix products  40.6 us (17%)
  local copies, waits for them, and re-layouts  37 us (15%)
  blocking collectives  30.9 us (13%)
  other arithmetic  23.5 us (10%)
    all_to_all x1, blocking collectives, per_device(): lax.all_to_all(partial, CHIPS, split_axis=0, concat_axis=0, tiled=True)  30.9 us
    dot_general x2, matrix products, per_device(): part = jnp.dot(hidden, weights[2], preferred_element_type=jnp.float32)  30.3 us
    ppermute x6, starting transfers between devices, ring_of_four(): lax.ppermute(from_plus[..., half:], axis, perm=behind)  19.6 us
    ppermute x6, waiting for transfers between devices, ring_of_four(): from_plus = lax.ppermute(value, axis, perm=behind)  17.9 us
    ppermute x6, starting transfers between devices, ring_of_four(): from_plus = lax.ppermute(value, axis, perm=behind)  17.5 us
    another operation x12, other arithmetic, ring_of_four(): return jnp.stack([value, from_plus, far, from_minus])  16.9 us
    ppermute x6, waiting for transfers between devices, ring_of_four(): lax.ppermute(from_minus[..., :half], axis, perm=ahead)  14.2 us
    dot_general x2, matrix products, per_device(): gate_part = jnp.dot(rows, weights[0].T, preferred_element_type=jnp.float32)  10.3 us
  transfers between devices with their start and end apart: 28, of which 9 were waited for; matrix products, arithmetic and copies ran while one was open for 29% of the time, Pallas kernels for 0%

profile of v3, /device:TPU:0, one launch (start us, length us, event | category | flops | bytes accessed | tf_op | source)
XLA Modules:
  0.0 241.0 jit_solution(13197241893643002168)
XLA Ops:
  8.5 9.3 %collective-permute-done.5 = bf16[3,48,2048]{2,1,0:T(8,128)(2,1)S(1)} collective-permute-done((bf16[3,48,2048]{2,1,0:T(8,128)(2,1)S(1)}, bf16[3,48,2048]{2,1,0:T(8,128)(2,1)S(1)}, u32[]{:S(2)}, u32[]{:S(2)}) %collective-permute-start.5) | collective-permute-done | bytes 589856 | tf_op jit(solution)/shard_map/ppermute | solution.py:34
  25.4 7.7 %collective-permute-done.7 = bf16[3,48,2048]{2,1,0:T(8,128)(2,1)S(1)} collective-permute-done((bf16[3,48,2048]{2,1,0:T(8,128)(2,1)S(1)}, bf16[3,48,2048]{2,1,0:T(8,128)(2,1)S(1)}, u32[]{:S(2)}, u32[]{:S(2)}) %collective-permute-start.7) | collective-permute-done | bytes 589856 | tf_op jit(solution)/shard_map/ppermute | solution.py:14
  36.9 4.4 %collective-permute-done.8 = bf16[3,48,1024]{2,1,0:T(8,128)(2,1)S(1)} collective-permute-done((bf16[3,48,1024]{2,1,0:T(8,128)(2,1)S(1)}, bf16[3,48,1024]{2,1,0:T(8,128)(2,1)S(1)}, u32[]{:S(2)}, u32[]{:S(2)}) %collective-permute-start.8) | collective-permute-done | bytes 294944 | tf_op jit(solution)/shard_map/ppermute | solution.py:19
  44.1 3.1 %collective-permute-start.10 = (bf16[4,2,48,2048]{3,2,1,0:T(8,128)(2,1)}, bf16[4,2,48,2048]{3,2,1,0:T(8,128)(2,1)}, u32[]{:S(2)}, u32[]{:S(2)}) collective-permute-start(bf16[4,2,48,2048]{3,2,1,0:T(8,128)(2,1)} %get-tuple-element.28), channel_id=1, source_target_pairs={{0,24},{8,0},{16,8},{24,16},{1,25},{9,1},{17,9},{25,17},{2,26},{10... | collective-permute-start | bytes 4718600 | tf_op jit(solution)/shard_map/ppermute | solution.py:15
  49.4 4.2 %collective-permute-start.14 = (bf16[4,2,48,2048]{3,2,1,0:T(8,128)(2,1)}, bf16[4,2,48,2048]{3,2,1,0:T(8,128)(2,1)}, u32[]{:S(2)}, u32[]{:S(2)}) collective-permute-start(bf16[4,2,48,2048]{3,2,1,0:T(8,128)(2,1)} %get-tuple-element.26), channel_id=1, source_target_pairs={{0,6},{2,0},{4,2},{6,4},{1,7},{3,1},{5,3},{7,5},{8,14},{10,8},{12,... | collective-permute-start | bytes 4718600 | tf_op jit(solution)/shard_map/ppermute | solution.py:15
  55.6 4.5 %all-to-all-start = ((bf16[4,144,2048]{2,1,0:T(8,128)(2,1)}), bf16[4,144,2048]{2,1,0:T(8,128)(2,1)S(1)}, u32[]{:S(2)}, u32[]{:S(2)}) async-start(bf16[4,144,2048]{2,1,0:T(8,128)(2,1)} %broadcast_in_dim.23), calls=%async_computation | async-start | bytes 4718592 | tf_op jit(solution)/shard_map/all_to_all | solution.py:55
  60.1 17.8 %collective-permute-done.10 = bf16[4,2,48,2048]{3,2,1,0:T(8,128)(2,1)} collective-permute-done((bf16[4,2,48,2048]{3,2,1,0:T(8,128)(2,1)}, bf16[4,2,48,2048]{3,2,1,0:T(8,128)(2,1)}, u32[]{:S(2)}, u32[]{:S(2)}) %collective-permute-start.10) | collective-permute-done | bytes 1572896 | tf_op jit(solution)/shard_map/ppermute | solution.py:15
  80.0 3.7 %collective-permute-start.13 = (bf16[4,2,48,1024]{3,2,1,0:T(8,128)(2,1)}, bf16[4,2,48,1024]{3,2,1,0:T(8,128)(2,1)}, u32[]{:S(2)}, u32[]{:S(2)}) collective-permute-start(bf16[4,2,48,1024]{3,2,1,0:T(8,128)(2,1)} %slice.116), channel_id=1, source_target_pairs={{0,24},{8,0},{16,8},{24,16},{1,25},{9,1},{17,9},{25,17},{2,26},{10... | collective-permute-start | bytes 2359304 | tf_op jit(solution)/shard_map/ppermute | solution.py:20
  89.1 4.3 %collective-permute-start.17 = (bf16[4,2,48,1024]{3,2,1,0:T(8,128)(2,1)}, bf16[4,2,48,1024]{3,2,1,0:T(8,128)(2,1)}, u32[]{:S(2)}, u32[]{:S(2)}) collective-permute-start(bf16[4,2,48,1024]{3,2,1,0:T(8,128)(2,1)} %slice.118), channel_id=1, source_target_pairs={{0,6},{2,0},{4,2},{6,4},{1,7},{3,1},{5,3},{7,5},{8,14},{10,8},{12,... | collective-permute-start | bytes 2359304 | tf_op jit(solution)/shard_map/ppermute | solution.py:20
  97.8 4.3 %collective-permute-done.12 = bf16[4,2,48,1024]{3,2,1,0:T(8,128)(2,1)} collective-permute-done((bf16[4,2,48,1024]{3,2,1,0:T(8,128)(2,1)}, bf16[4,2,48,1024]{3,2,1,0:T(8,128)(2,1)}, u32[]{:S(2)}, u32[]{:S(2)}) %collective-permute-start.12) | collective-permute-done | bytes 786464 | tf_op jit(solution)/shard_map/ppermute | solution.py:19
  106.0 5.5 %collective-permute-done.16 = bf16[4,2,48,1024]{3,2,1,0:T(8,128)(2,1)} collective-permute-done((bf16[4,2,48,1024]{3,2,1,0:T(8,128)(2,1)}, bf16[4,2,48,1024]{3,2,1,0:T(8,128)(2,1)}, u32[]{:S(2)}, u32[]{:S(2)}) %collective-permute-start.16) | collective-permute-done | bytes 786464 | tf_op jit(solution)/shard_map/ppermute | solution.py:19
  113.0 3.1 %pad_maximum_fusion = bf16[4,4,2,48,2048]{4,3,2,1,0:T(8,128)(2,1)S(1)} fusion(bf16[1,4,2,48,2048]{4,3,2,1,0:T(8,128)(2,1)} %bitcast.16, bf16[1,4,2,48,2048]{4,3,2,1,0:T(8,128)(2,1)S(1)} %maximum_bitcast_fusion, bf16[1,4,2,48,2048]{4,3,2,1,0:T(8,128)(2,1)} %bitcast.14, bf16[1,4,2,48,2048]{4,3,2,1,0:T(8,128)(2,1)S(1)} %copy-done.2), kind=kLoop, calls=%fused_computation.2 | loop fusion | flops 9437184 | bytes 12582912 | tf_op jit(solution)/shard_map/stack | solution.py:24
  119.3 3.2 %collective-permute-start.18 = (bf16[4,48,2048]{2,1,0:T(8,128)(2,1)S(1)}, bf16[4,48,2048]{2,1,0:T(8,128)(2,1)}, u32[]{:S(2)}, u32[]{:S(2)}) collective-permute-start(bf16[4,48,2048]{2,1,0:T(8,128)(2,1)S(1)} %slice_bitcast_fusion.1), channel_id=1, source_target_pairs={{0,24},{8,0},{16,8},{24,16},{1,25},{9,1},{17,9},{25,17},{2,26},{10... | collective-permute-start | bytes 2359304 | tf_op jit(solution)/shard_map/ppermute | solution.py:15
  122.5 3.2 %collective-permute-start.22 = (bf16[4,48,2048]{2,1,0:T(8,128)(2,1)S(1)}, bf16[4,48,2048]{2,1,0:T(8,128)(2,1)}, u32[]{:S(2)}, u32[]{:S(2)}) collective-permute-start(bf16[4,48,2048]{2,1,0:T(8,128)(2,1)S(1)} %copy-done.5), channel_id=1, source_target_pairs={{0,6},{2,0},{4,2},{6,4},{1,7},{3,1},{5,3},{7,5},{8,14},{10,8},{12,... | collective-permute-start | bytes 2359304 | tf_op jit(solution)/shard_map/ppermute | solution.py:15
  133.0 5.2 %fusion.23 = f32[1024,768]{1,0:T(8,128)} fusion(bf16[1024,2048]{1,0:T(8,128)(2,1)S(1)} %bitcast.69, bf16[768,2048]{1,0:T(8,128)(2,1)S(1)} %bitcast.80), kind=kOutput, calls=%fused_computation.58 | convolution fusion | flops 3221225472 | bytes 10485760 | tf_op jit(solution)/shard_map/dot_general | solution.py:86
  138.1 5.1 %fusion.22 = f32[1024,768]{1,0:T(8,128)} fusion(bf16[1024,2048]{1,0:T(8,128)(2,1)S(1)} %bitcast.70, bf16[768,2048]{1,0:T(8,128)(2,1)S(1)} %bitcast.81), kind=kOutput, calls=%fused_computation.57 | convolution fusion | flops 3221225472 | bytes 10485760 | tf_op jit(solution)/shard_map/dot_general | solution.py:86
  144.6 3.1 %collective-permute-start.25 = (bf16[4,48,1024]{2,1,0:T(8,128)(2,1)S(1)}, bf16[4,48,1024]{2,1,0:T(8,128)(2,1)S(1)}, u32[]{:S(2)}, u32[]{:S(2)}) collective-permute-start(bf16[4,48,1024]{2,1,0:T(8,128)(2,1)S(1)} %slice.126), channel_id=1, source_target_pairs={{0,6},{2,0},{4,2},{6,4},{1,7},{3,1},{5,3},{7,5},{8,14},{10,8},{12,... | collective-permute-start | bytes 1179656 | tf_op jit(solution)/shard_map/ppermute | solution.py:20
  149.2 4.1 %fusion.11 = f32[1024]{0:T(1024)S(1)} fusion(bf16[1024,1,8]{2,1,0:T(2,128)(2,1)S(1)} %get-tuple-element.32, s32[]{:T(128)S(6)} %select_n.18, bf16[1024,1,8]{2,1,0:T(2,128)(2,1)S(1)} %get-tuple-element.31), kind=kLoop, calls=%fused_computation.35 | loop fusion | flops 3072 | bytes 8196 | tf_op jit(solution)/shard_map/jit(dynamic_index_in_dim)/dynamic_slice | solution.py:82
  155.5 3.5 %collective-permute-start.21 = (bf16[4,48,1024]{2,1,0:T(8,128)(2,1)S(1)}, bf16[4,48,1024]{2,1,0:T(8,128)(2,1)}, u32[]{:S(2)}, u32[]{:S(2)}) collective-permute-start(bf16[4,48,1024]{2,1,0:T(8,128)(2,1)S(1)} %slice.122), channel_id=1, source_target_pairs={{0,24},{8,0},{16,8},{24,16},{1,25},{9,1},{17,9},{25,17},{2,26},{10... | collective-permute-start | bytes 1179656 | tf_op jit(solution)/shard_map/ppermute | solution.py:20
  162.0 14.1 %fusion.3 = f32[1024,2048]{1,0:T(8,128)} fusion(bf16[768,2048]{1,0:T(8,128)(2,1)} %bitcast.77, f32[1024,768]{1,0:T(8,128)} %fusion.23, bf16[1024,2048]{1,0:T(8,128)(2,1)} %bitcast.71, bf16[768,2048]{1,0:T(8,128)(2,1)} %bitcast.79), kind=kOutput, calls=%fused_computation.15 | convolution fusion | flops 6447169536 | bytes 22020096 | tf_op jit(solution)/shard_map/dot_general | solution.py:89
  180.2 16.2 %convert_multiply_fusion = f32[1024,2048]{1,0:T(8,128)} fusion(f32[1024,2048]{1,0:T(8,128)} %fusion.3, f32[1024]{0:T(1024)S(1)} %fusion.11, bf16[768,2048]{1,0:T(8,128)(2,1)} %bitcast.76, f32[1024,768]{1,0:T(8,128)} %fusion.22, bf16[1024,2048]{1,0:T(8,128)(2,1)} %bitcast.72, bf16[768,2048]{1,0:T(8,128)(2,1)} %bitcast.78), kind=kOutput, calls=%fused_computation | convolution fusion | flops 6455558144 | bytes 30412800 | tf_op jit(solution)/shard_map/dot_general | solution.py:89
  196.5 4.0 %fusion.14 = (f32[512,2048]{1,0:T(8,128)S(1)}, f32[512,2048]{1,0:T(8,128)S(1)}) fusion(f32[1024,2048]{1,0:T(8,128)} %convert_multiply_fusion), kind=kLoop, calls=%fused_computation.51 | loop fusion | bytes 16777216 | tf_op jit(solution)/shard_map/slice | solution.py:94
  200.6 7.1 %collective-permute-done.26 = f32[4,128,2048]{2,1,0:T(8,128)S(1)} collective-permute-done((f32[4,128,2048]{2,1,0:T(8,128)S(1)}, f32[4,128,2048]{2,1,0:T(8,128)S(1)}, u32[]{:S(2)}, u32[]{:S(2)}) %collective-permute-start.26) | collective-permute-done | bytes 4194336 | tf_op jit(solution)/shard_map/ppermute | solution.py:94
  208.7 30.9 %all_to_all.10 = bf16[4,128,2048]{2,1,0:T(8,128)(2,1)S(1)} all-to-all(bf16[4,128,2048]{2,1,0:T(8,128)(2,1)S(1)} %add_convert_fusion.1), channel_id=1, replica_groups=mesh['yhi'=2,'core'=2,'x'=4,'z'=4,'ylo'=2] {'yhi','ylo'}, dimensions={0} | all-to-all | bytes 4194304 | tf_op jit(solution)/shard_map/all_to_all | solution.py:96
  (112 shorter events, 68.8 us)
Async XLA Ops:
  2.7 15.1 %collective-permute-start.5 = (bf16[3,48,2048]{2,1,0:T(8,128)(2,1)S(1)}, bf16[3,48,2048]{2,1,0:T(8,128)(2,1)S(1)}, u32[]{:S(2)}, u32[]{:S(2)}) collective-permute-start(bf16[3,48,2048]{2,1,0:T(8,128)(2,1)S(1)} %get-tuple-element.29), channel_id=1, source_target_pairs={{0,1},{1,0},{2,3},{3,2},{4,5},{5,4},{6,7},{7,6},{8,9},{9,8},{10,11... | collective-permute-start | bytes 1769480 | tf_op jit(solution)/shard_map/ppermute | solution.py:34
  4.4 17.1 %collective-permute-start.2 = (bf16[3,48,2048]{2,1,0:T(8,128)(2,1)S(1)}, bf16[3,48,2048]{2,1,0:T(8,128)(2,1)S(1)}, u32[]{:S(2)}, u32[]{:S(2)}) collective-permute-start(bf16[3,48,2048]{2,1,0:T(8,128)(2,1)S(1)} %bitcast.82), channel_id=1, source_target_pairs={{0,2},{2,4},{4,6},{6,0},{1,3},{3,5},{5,7},{7,1},{8,10},{10,12},{12... | collective-permute-start | bytes 1769480 | tf_op jit(solution)/shard_map/ppermute | solution.py:14
  6.4 16.8 %collective-permute-start.1 = (bf16[3,48,2048]{2,1,0:T(8,128)(2,1)S(1)}, bf16[3,48,2048]{2,1,0:T(8,128)(2,1)S(1)}, u32[]{:S(2)}, u32[]{:S(2)}) collective-permute-start(bf16[3,48,2048]{2,1,0:T(8,128)(2,1)S(1)} %bitcast.83), channel_id=1, source_target_pairs={{0,6},{2,0},{4,2},{6,4},{1,7},{3,1},{5,3},{7,5},{8,14},{10,8},{12,... | collective-permute-start | bytes 1769480 | tf_op jit(solution)/shard_map/ppermute | solution.py:15
  17.8 15.4 %collective-permute-start.7 = (bf16[3,48,2048]{2,1,0:T(8,128)(2,1)S(1)}, bf16[3,48,2048]{2,1,0:T(8,128)(2,1)S(1)}, u32[]{:S(2)}, u32[]{:S(2)}) collective-permute-start(bf16[3,48,2048]{2,1,0:T(8,128)(2,1)S(1)} %collective-permute-done.5), channel_id=1, source_target_pairs={{0,8},{8,16},{16,24},{24,0},{1,9},{9,17},{17,25},{25,1},{2,10},{10... | collective-permute-start | bytes 1769480 | tf_op jit(solution)/shard_map/ppermute | solution.py:14
  19.4 14.3 %collective-permute-start.6 = (bf16[3,48,2048]{2,1,0:T(8,128)(2,1)S(1)}, bf16[3,48,2048]{2,1,0:T(8,128)(2,1)S(1)}, u32[]{:S(2)}, u32[]{:S(2)}) collective-permute-start(bf16[3,48,2048]{2,1,0:T(8,128)(2,1)S(1)} %collective-permute-done.5), channel_id=1, source_target_pairs={{0,24},{8,0},{16,8},{24,16},{1,25},{9,1},{17,9},{25,17},{2,26},{10... | collective-permute-start | bytes 1769480 | tf_op jit(solution)/shard_map/ppermute | solution.py:15
  21.5 15.0 %collective-permute-start.3 = (bf16[3,48,1024]{2,1,0:T(8,128)(2,1)S(1)}, bf16[3,48,1024]{2,1,0:T(8,128)(2,1)S(1)}, u32[]{:S(2)}, u32[]{:S(2)}) collective-permute-start(bf16[3,48,1024]{2,1,0:T(8,128)(2,1)S(1)} %slice.111), channel_id=1, source_target_pairs={{0,2},{2,4},{4,6},{6,0},{1,3},{3,5},{5,7},{7,1},{8,10},{10,12},{12... | collective-permute-start | bytes 884744 | tf_op jit(solution)/shard_map/ppermute | solution.py:19
  44.1 33.8 %collective-permute-start.10 = (bf16[4,2,48,2048]{3,2,1,0:T(8,128)(2,1)}, bf16[4,2,48,2048]{3,2,1,0:T(8,128)(2,1)}, u32[]{:S(2)}, u32[]{:S(2)}) collective-permute-start(bf16[4,2,48,2048]{3,2,1,0:T(8,128)(2,1)} %get-tuple-element.28), channel_id=1, source_target_pairs={{0,24},{8,0},{16,8},{24,16},{1,25},{9,1},{17,9},{25,17},{2,26},{10... | collective-permute-start | bytes 4718600 | tf_op jit(solution)/shard_map/ppermute | solution.py:15
  47.2 36.5 %collective-permute-start.11 = (bf16[4,2,48,2048]{3,2,1,0:T(8,128)(2,1)}, bf16[4,2,48,2048]{3,2,1,0:T(8,128)(2,1)}, u32[]{:S(2)}, u32[]{:S(2)}) collective-permute-start(bf16[4,2,48,2048]{3,2,1,0:T(8,128)(2,1)} %get-tuple-element.28), channel_id=1, source_target_pairs={{0,8},{8,16},{16,24},{24,0},{1,9},{9,17},{17,25},{25,1},{2,10},{10... | collective-permute-start | bytes 4718600 | tf_op jit(solution)/shard_map/ppermute | solution.py:14
  49.4 37.6 %collective-permute-start.14 = (bf16[4,2,48,2048]{3,2,1,0:T(8,128)(2,1)}, bf16[4,2,48,2048]{3,2,1,0:T(8,128)(2,1)}, u32[]{:S(2)}, u32[]{:S(2)}) collective-permute-start(bf16[4,2,48,2048]{3,2,1,0:T(8,128)(2,1)} %get-tuple-element.26), channel_id=1, source_target_pairs={{0,6},{2,0},{4,2},{6,4},{1,7},{3,1},{5,3},{7,5},{8,14},{10,8},{12,... | collective-permute-start | bytes 4718600 | tf_op jit(solution)/shard_map/ppermute | solution.py:15
  53.6 39.7 %collective-permute-start.15 = (bf16[4,2,48,2048]{3,2,1,0:T(8,128)(2,1)}, bf16[4,2,48,2048]{3,2,1,0:T(8,128)(2,1)}, u32[]{:S(2)}, u32[]{:S(2)}) collective-permute-start(bf16[4,2,48,2048]{3,2,1,0:T(8,128)(2,1)} %get-tuple-element.26), channel_id=1, source_target_pairs={{0,2},{2,4},{4,6},{6,0},{1,3},{3,5},{5,7},{7,1},{8,10},{10,12},{12... | collective-permute-start | bytes 4718600 | tf_op jit(solution)/shard_map/ppermute | solution.py:14
  55.6 41.9 %all-to-all-start = ((bf16[4,144,2048]{2,1,0:T(8,128)(2,1)}), bf16[4,144,2048]{2,1,0:T(8,128)(2,1)S(1)}, u32[]{:S(2)}, u32[]{:S(2)}) async-start(bf16[4,144,2048]{2,1,0:T(8,128)(2,1)} %broadcast_in_dim.23), calls=%async_computation | async-start | bytes 4718592 | tf_op jit(solution)/shard_map/all_to_all | solution.py:55
  80.0 17.8 %collective-permute-start.13 = (bf16[4,2,48,1024]{3,2,1,0:T(8,128)(2,1)}, bf16[4,2,48,1024]{3,2,1,0:T(8,128)(2,1)}, u32[]{:S(2)}, u32[]{:S(2)}) collective-permute-start(bf16[4,2,48,1024]{3,2,1,0:T(8,128)(2,1)} %slice.116), channel_id=1, source_target_pairs={{0,24},{8,0},{16,8},{24,16},{1,25},{9,1},{17,9},{25,17},{2,26},{10... | collective-permute-start | bytes 2359304 | tf_op jit(solution)/shard_map/ppermute | solution.py:20
  85.8 16.3 %collective-permute-start.12 = (bf16[4,2,48,1024]{3,2,1,0:T(8,128)(2,1)}, bf16[4,2,48,1024]{3,2,1,0:T(8,128)(2,1)}, u32[]{:S(2)}, u32[]{:S(2)}) collective-permute-start(bf16[4,2,48,1024]{3,2,1,0:T(8,128)(2,1)} %slice.115), channel_id=1, source_target_pairs={{0,8},{8,16},{16,24},{24,0},{1,9},{9,17},{17,25},{25,1},{2,10},{10... | collective-permute-start | bytes 2359304 | tf_op jit(solution)/shard_map/ppermute | solution.py:19
  89.1 17.0 %collective-permute-start.17 = (bf16[4,2,48,1024]{3,2,1,0:T(8,128)(2,1)}, bf16[4,2,48,1024]{3,2,1,0:T(8,128)(2,1)}, u32[]{:S(2)}, u32[]{:S(2)}) collective-permute-start(bf16[4,2,48,1024]{3,2,1,0:T(8,128)(2,1)} %slice.118), channel_id=1, source_target_pairs={{0,6},{2,0},{4,2},{6,4},{1,7},{3,1},{5,3},{7,5},{8,14},{10,8},{12,... | collective-permute-start | bytes 2359304 | tf_op jit(solution)/shard_map/ppermute | solution.py:20
  95.4 16.1 %collective-permute-start.16 = (bf16[4,2,48,1024]{3,2,1,0:T(8,128)(2,1)}, bf16[4,2,48,1024]{3,2,1,0:T(8,128)(2,1)}, u32[]{:S(2)}, u32[]{:S(2)}) collective-permute-start(bf16[4,2,48,1024]{3,2,1,0:T(8,128)(2,1)} %slice.117), channel_id=1, source_target_pairs={{0,2},{2,4},{4,6},{6,0},{1,3},{3,5},{5,7},{7,1},{8,10},{10,12},{12... | collective-permute-start | bytes 2359304 | tf_op jit(solution)/shard_map/ppermute | solution.py:19
  97.5 33.3 %collective-permute-start = (bf16[4,144,2048]{2,1,0:T(8,128)(2,1)S(1)}, bf16[4,144,2048]{2,1,0:T(8,128)(2,1)}, u32[]{:S(2)}, u32[]{:S(2)}) collective-permute-start(bf16[4,144,2048]{2,1,0:T(8,128)(2,1)S(1)} %all-to-all-done), channel_id=1, source_target_pairs={{0,32},{32,0},{1,33},{33,1},{2,34},{34,2},{3,35},{35,3},{4,36},{36... | collective-permute-start | bytes 7077896 | tf_op jit(solution)/shard_map/ppermute | solution.py:56
  119.2 34.1 %collective-permute-start.19 = (bf16[4,48,2048]{2,1,0:T(8,128)(2,1)S(1)}, bf16[4,48,2048]{2,1,0:T(8,128)(2,1)}, u32[]{:S(2)}, u32[]{:S(2)}) collective-permute-start(bf16[4,48,2048]{2,1,0:T(8,128)(2,1)S(1)} %slice_bitcast_fusion.1), channel_id=1, source_target_pairs={{0,8},{8,16},{16,24},{24,0},{1,9},{9,17},{17,25},{25,1},{2,10},{10... | collective-permute-start | bytes 2359304 | tf_op jit(solution)/shard_map/ppermute | solution.py:14
  119.3 35.2 %collective-permute-start.18 = (bf16[4,48,2048]{2,1,0:T(8,128)(2,1)S(1)}, bf16[4,48,2048]{2,1,0:T(8,128)(2,1)}, u32[]{:S(2)}, u32[]{:S(2)}) collective-permute-start(bf16[4,48,2048]{2,1,0:T(8,128)(2,1)S(1)} %slice_bitcast_fusion.1), channel_id=1, source_target_pairs={{0,24},{8,0},{16,8},{24,16},{1,25},{9,1},{17,9},{25,17},{2,26},{10... | collective-permute-start | bytes 2359304 | tf_op jit(solution)/shard_map/ppermute | solution.py:15
  122.5 20.7 %collective-permute-start.23 = (bf16[4,48,2048]{2,1,0:T(8,128)(2,1)S(1)}, bf16[4,48,2048]{2,1,0:T(8,128)(2,1)S(1)}, u32[]{:S(2)}, u32[]{:S(2)}) collective-permute-start(bf16[4,48,2048]{2,1,0:T(8,128)(2,1)S(1)} %copy-done.5), channel_id=1, source_target_pairs={{0,2},{2,4},{4,6},{6,0},{1,3},{3,5},{5,7},{7,1},{8,10},{10,12},{12... | collective-permute-start | bytes 2359304 | tf_op jit(solution)/shard_map/ppermute | solution.py:14
  122.5 20.8 %collective-permute-start.22 = (bf16[4,48,2048]{2,1,0:T(8,128)(2,1)S(1)}, bf16[4,48,2048]{2,1,0:T(8,128)(2,1)}, u32[]{:S(2)}, u32[]{:S(2)}) collective-permute-start(bf16[4,48,2048]{2,1,0:T(8,128)(2,1)S(1)} %copy-done.5), channel_id=1, source_target_pairs={{0,6},{2,0},{4,2},{6,4},{1,7},{3,1},{5,3},{7,5},{8,14},{10,8},{12,... | collective-permute-start | bytes 2359304 | tf_op jit(solution)/shard_map/ppermute | solution.py:15
  143.3 15.7 %collective-permute-start.24 = (bf16[4,48,1024]{2,1,0:T(8,128)(2,1)S(1)}, bf16[4,48,1024]{2,1,0:T(8,128)(2,1)S(1)}, u32[]{:S(2)}, u32[]{:S(2)}) collective-permute-start(bf16[4,48,1024]{2,1,0:T(8,128)(2,1)S(1)} %slice.125), channel_id=1, source_target_pairs={{0,2},{2,4},{4,6},{6,0},{1,3},{3,5},{5,7},{7,1},{8,10},{10,12},{12... | collective-permute-start | bytes 1179656 | tf_op jit(solution)/shard_map/ppermute | solution.py:19
  144.6 14.4 %collective-permute-start.25 = (bf16[4,48,1024]{2,1,0:T(8,128)(2,1)S(1)}, bf16[4,48,1024]{2,1,0:T(8,128)(2,1)S(1)}, u32[]{:S(2)}, u32[]{:S(2)}) collective-permute-start(bf16[4,48,1024]{2,1,0:T(8,128)(2,1)S(1)} %slice.126), channel_id=1, source_target_pairs={{0,6},{2,0},{4,2},{6,4},{1,7},{3,1},{5,3},{7,5},{8,14},{10,8},{12,... | collective-permute-start | bytes 1179656 | tf_op jit(solution)/shard_map/ppermute | solution.py:20
  154.4 21.7 %collective-permute-start.20 = (bf16[4,48,1024]{2,1,0:T(8,128)(2,1)S(1)}, bf16[4,48,1024]{2,1,0:T(8,128)(2,1)}, u32[]{:S(2)}, u32[]{:S(2)}) collective-permute-start(bf16[4,48,1024]{2,1,0:T(8,128)(2,1)S(1)} %slice.121), channel_id=1, source_target_pairs={{0,8},{8,16},{16,24},{24,0},{1,9},{9,17},{17,25},{25,1},{2,10},{10... | collective-permute-start | bytes 1179656 | tf_op jit(solution)/shard_map/ppermute | solution.py:19
  155.5 20.5 %collective-permute-start.21 = (bf16[4,48,1024]{2,1,0:T(8,128)(2,1)S(1)}, bf16[4,48,1024]{2,1,0:T(8,128)(2,1)}, u32[]{:S(2)}, u32[]{:S(2)}) collective-permute-start(bf16[4,48,1024]{2,1,0:T(8,128)(2,1)S(1)} %slice.122), channel_id=1, source_target_pairs={{0,24},{8,0},{16,8},{24,16},{1,25},{9,1},{17,9},{25,17},{2,26},{10... | collective-permute-start | bytes 1179656 | tf_op jit(solution)/shard_map/ppermute | solution.py:20
  (16 other events, 162.5 us)

commit v4 on v3

--- a/solution.py
+++ b/solution.py
@@ -69,16 +69,16 @@
     weight = jnp.sum(
         jnp.where(expert_ids[:, :, None] == experts, gate_weights[:, :, None], 0.0), axis=1
     )
-    high = weight.astype(jnp.bfloat16)
-    low = (weight - high.astype(jnp.float32)).astype(jnp.bfloat16)
-    packed = jnp.concatenate([high, low], axis=1).reshape(-1, model_width)
+    high = lax.reduce_precision(weight, exponent_bits=8, mantissa_bits=7)
+    low = weight - high
+    packed = jnp.concatenate([high, low], axis=1).astype(jnp.bfloat16).T
     extra = packed.shape[0]
-    packed = jnp.pad(packed, ((0, 16 - extra), (0, 0)))
+    packed = jnp.pad(packed, ((0, 0), (0, model_width - token_count)))
     mine, other = spread(jnp.concatenate([tokens, packed]), chips)
     both = jnp.concatenate([mine, other])
     rows = both[:, :token_count].reshape(-1, model_width)
-    halves = both[:, token_count:token_count + extra].reshape(-1, 2, experts.shape[0])
-    table = halves[:, 0].astype(jnp.float32) + halves[:, 1].astype(jnp.float32)
+    halves = jnp.swapaxes(both[:, token_count:, :token_count], 1, 2).astype(jnp.float32)
+    table = (halves[..., : extra // 2] + halves[..., extra // 2 :]).reshape(-1, extra // 2)
     scale = lax.dynamic_index_in_dim(table, expert, axis=1, keepdims=True)
 
     out = None

time: 242 us -> 236 us (0.975)
  other arithmetic: 23.5 us -> 18.3 us
    dynamic_slice x1 -> x0, other arithmetic: 4.09 us -> none  [per_device(): scale = lax.dynamic_index_in_dim(table, expert, axis=1, keepdims=True)]
  transfers between devices with their start and end apart: 28 -> 28, of which waited for: 9 -> 10; matrix products, arithmetic and copies ran while one was open for 29% -> 27% of each run, Pallas kernels for 0% -> 0%
where the time goes in v4:
time: 236 us; the launch traced here: 235 us
  waiting for transfers between devices  59.9 us (25%)
  starting transfers between devices  49.4 us (21%)
  matrix products  40.5 us (17%)
  local copies, waits for them, and re-layouts  35.2 us (15%)
  blocking collectives  30.9 us (13%)
  other arithmetic  18.3 us (8%)
    all_to_all x1, blocking collectives, per_device(): lax.all_to_all(partial, CHIPS, split_axis=0, concat_axis=0, tiled=True)  30.9 us
    dot_general x2, matrix products, per_device(): part = jnp.dot(hidden, weights[2], preferred_element_type=jnp.float32)  30.2 us
    ppermute x6, starting transfers between devices, ring_of_four(): lax.ppermute(from_plus[..., half:], axis, perm=behind)  19.6 us
    ppermute x6, waiting for transfers between devices, ring_of_four(): from_plus = lax.ppermute(value, axis, perm=behind)  18.1 us
    ppermute x6, starting transfers between devices, ring_of_four(): from_plus = lax.ppermute(value, axis, perm=behind)  17.5 us
    another operation x12, other arithmetic, ring_of_four(): return jnp.stack([value, from_plus, far, from_minus])  15.8 us
    ppermute x6, waiting for transfers between devices, ring_of_four(): lax.ppermute(from_minus[..., :half], axis, perm=ahead)  14.2 us
    dot_general x2, matrix products, per_device(): gate_part = jnp.dot(rows, weights[0].T, preferred_element_type=jnp.float32)  10.3 us
  transfers between devices with their start and end apart: 28, of which 10 were waited for; matrix products, arithmetic and copies ran while one was open for 27% of the time, Pallas kernels for 0%

profile of v4, /device:TPU:0, one launch (start us, length us, event | category | flops | bytes accessed | tf_op | source)
XLA Modules:
  0.0 234.7 jit_solution(8480732185558832902)
XLA Ops:
  8.5 9.3 %collective-permute-done.5 = bf16[3,48,2048]{2,1,0:T(8,128)(2,1)S(1)} collective-permute-done((bf16[3,48,2048]{2,1,0:T(8,128)(2,1)S(1)}, bf16[3,48,2048]{2,1,0:T(8,128)(2,1)S(1)}, u32[]{:S(2)}, u32[]{:S(2)}) %collective-permute-start.5) | collective-permute-done | bytes 589856 | tf_op jit(solution)/shard_map/ppermute | solution.py:34
  25.4 7.7 %collective-permute-done.7 = bf16[3,48,2048]{2,1,0:T(8,128)(2,1)S(1)} collective-permute-done((bf16[3,48,2048]{2,1,0:T(8,128)(2,1)S(1)}, bf16[3,48,2048]{2,1,0:T(8,128)(2,1)S(1)}, u32[]{:S(2)}, u32[]{:S(2)}) %collective-permute-start.7) | collective-permute-done | bytes 589856 | tf_op jit(solution)/shard_map/ppermute | solution.py:14
  36.9 4.4 %collective-permute-done.8 = bf16[3,48,1024]{2,1,0:T(8,128)(2,1)S(1)} collective-permute-done((bf16[3,48,1024]{2,1,0:T(8,128)(2,1)S(1)}, bf16[3,48,1024]{2,1,0:T(8,128)(2,1)S(1)}, u32[]{:S(2)}, u32[]{:S(2)}) %collective-permute-start.8) | collective-permute-done | bytes 294944 | tf_op jit(solution)/shard_map/ppermute | solution.py:19
  44.1 3.1 %collective-permute-start.10 = (bf16[4,2,48,2048]{3,2,1,0:T(8,128)(2,1)}, bf16[4,2,48,2048]{3,2,1,0:T(8,128)(2,1)}, u32[]{:S(2)}, u32[]{:S(2)}) collective-permute-start(bf16[4,2,48,2048]{3,2,1,0:T(8,128)(2,1)} %get-tuple-element.26), channel_id=1, source_target_pairs={{0,24},{8,0},{16,8},{24,16},{1,25},{9,1},{17,9},{25,17},{2,26},{10... | collective-permute-start | bytes 4718600 | tf_op jit(solution)/shard_map/ppermute | solution.py:15
  49.4 4.2 %collective-permute-start.14 = (bf16[4,2,48,2048]{3,2,1,0:T(8,128)(2,1)}, bf16[4,2,48,2048]{3,2,1,0:T(8,128)(2,1)}, u32[]{:S(2)}, u32[]{:S(2)}) collective-permute-start(bf16[4,2,48,2048]{3,2,1,0:T(8,128)(2,1)} %get-tuple-element.24), channel_id=1, source_target_pairs={{0,6},{2,0},{4,2},{6,4},{1,7},{3,1},{5,3},{7,5},{8,14},{10,8},{12,... | collective-permute-start | bytes 4718600 | tf_op jit(solution)/shard_map/ppermute | solution.py:15
  55.4 4.5 %all-to-all-start = ((bf16[4,144,2048]{2,1,0:T(8,128)(2,1)}), bf16[4,144,2048]{2,1,0:T(8,128)(2,1)S(1)}, u32[]{:S(2)}, u32[]{:S(2)}) async-start(bf16[4,144,2048]{2,1,0:T(8,128)(2,1)} %broadcast_in_dim.23), calls=%async_computation | async-start | bytes 4718592 | tf_op jit(solution)/shard_map/all_to_all | solution.py:55
  59.9 18.1 %collective-permute-done.10 = bf16[4,2,48,2048]{3,2,1,0:T(8,128)(2,1)} collective-permute-done((bf16[4,2,48,2048]{3,2,1,0:T(8,128)(2,1)}, bf16[4,2,48,2048]{3,2,1,0:T(8,128)(2,1)}, u32[]{:S(2)}, u32[]{:S(2)}) %collective-permute-start.10) | collective-permute-done | bytes 1572896 | tf_op jit(solution)/shard_map/ppermute | solution.py:15
  80.0 3.7 %collective-permute-start.13 = (bf16[4,2,48,1024]{3,2,1,0:T(8,128)(2,1)}, bf16[4,2,48,1024]{3,2,1,0:T(8,128)(2,1)}, u32[]{:S(2)}, u32[]{:S(2)}) collective-permute-start(bf16[4,2,48,1024]{3,2,1,0:T(8,128)(2,1)} %slice.116), channel_id=1, source_target_pairs={{0,24},{8,0},{16,8},{24,16},{1,25},{9,1},{17,9},{25,17},{2,26},{10... | collective-permute-start | bytes 2359304 | tf_op jit(solution)/shard_map/ppermute | solution.py:20
  89.1 4.3 %collective-permute-start.17 = (bf16[4,2,48,1024]{3,2,1,0:T(8,128)(2,1)}, bf16[4,2,48,1024]{3,2,1,0:T(8,128)(2,1)}, u32[]{:S(2)}, u32[]{:S(2)}) collective-permute-start(bf16[4,2,48,1024]{3,2,1,0:T(8,128)(2,1)} %slice.118), channel_id=1, source_target_pairs={{0,6},{2,0},{4,2},{6,4},{1,7},{3,1},{5,3},{7,5},{8,14},{10,8},{12,... | collective-permute-start | bytes 2359304 | tf_op jit(solution)/shard_map/ppermute | solution.py:20
  97.8 4.3 %collective-permute-done.12 = bf16[4,2,48,1024]{3,2,1,0:T(8,128)(2,1)} collective-permute-done((bf16[4,2,48,1024]{3,2,1,0:T(8,128)(2,1)}, bf16[4,2,48,1024]{3,2,1,0:T(8,128)(2,1)}, u32[]{:S(2)}, u32[]{:S(2)}) %collective-permute-start.12) | collective-permute-done | bytes 786464 | tf_op jit(solution)/shard_map/ppermute | solution.py:19
  106.0 5.5 %collective-permute-done.16 = bf16[4,2,48,1024]{3,2,1,0:T(8,128)(2,1)} collective-permute-done((bf16[4,2,48,1024]{3,2,1,0:T(8,128)(2,1)}, bf16[4,2,48,1024]{3,2,1,0:T(8,128)(2,1)}, u32[]{:S(2)}, u32[]{:S(2)}) %collective-permute-start.16) | collective-permute-done | bytes 786464 | tf_op jit(solution)/shard_map/ppermute | solution.py:19
  113.0 3.1 %pad_maximum_fusion = bf16[4,4,2,48,2048]{4,3,2,1,0:T(8,128)(2,1)S(1)} fusion(bf16[1,4,2,48,2048]{4,3,2,1,0:T(8,128)(2,1)} %bitcast.17, bf16[1,4,2,48,2048]{4,3,2,1,0:T(8,128)(2,1)S(1)} %maximum_bitcast_fusion, bf16[1,4,2,48,2048]{4,3,2,1,0:T(8,128)(2,1)} %bitcast.15, bf16[1,4,2,48,2048]{4,3,2,1,0:T(8,128)(2,1)S(1)} %copy-done.2), kind=kLoop, calls=%fused_computation.2 | loop fusion | flops 9437184 | bytes 12582912 | tf_op jit(solution)/shard_map/stack | solution.py:24
  116.1 3.0 %pad_maximum_fusion.1 = bf16[4,4,2,48,2048]{4,3,2,1,0:T(8,128)(2,1)S(1)} fusion(bf16[1,4,2,48,2048]{4,3,2,1,0:T(8,128)(2,1)} %bitcast.21, bf16[1,4,2,48,2048]{4,3,2,1,0:T(8,128)(2,1)S(1)} %maximum_bitcast_fusion.1, bf16[1,4,2,48,2048]{4,3,2,1,0:T(8,128)(2,1)} %bitcast.19, bf16[1,4,2,48,2048]{4,3,2,1,0:T(8,128)(2,1)S(1)} %copy-done.3), kind=kLoop, calls=%fused_computation.3 | loop fusion | flops 9437184 | bytes 12582912 | tf_op jit(solution)/shard_map/stack | solution.py:24
  119.3 3.2 %collective-permute-start.18 = (bf16[4,48,2048]{2,1,0:T(8,128)(2,1)S(1)}, bf16[4,48,2048]{2,1,0:T(8,128)(2,1)}, u32[]{:S(2)}, u32[]{:S(2)}) collective-permute-start(bf16[4,48,2048]{2,1,0:T(8,128)(2,1)S(1)} %slice_bitcast_fusion.1), channel_id=1, source_target_pairs={{0,24},{8,0},{16,8},{24,16},{1,25},{9,1},{17,9},{25,17},{2,26},{10... | collective-permute-start | bytes 2359304 | tf_op jit(solution)/shard_map/ppermute | solution.py:15
  122.5 3.2 %collective-permute-start.22 = (bf16[4,48,2048]{2,1,0:T(8,128)(2,1)S(1)}, bf16[4,48,2048]{2,1,0:T(8,128)(2,1)}, u32[]{:S(2)}, u32[]{:S(2)}) collective-permute-start(bf16[4,48,2048]{2,1,0:T(8,128)(2,1)S(1)} %copy-done.5), channel_id=1, source_target_pairs={{0,6},{2,0},{4,2},{6,4},{1,7},{3,1},{5,3},{7,5},{8,14},{10,8},{12,... | collective-permute-start | bytes 2359304 | tf_op jit(solution)/shard_map/ppermute | solution.py:15
  132.9 5.2 %fusion.22 = f32[1024,768]{1,0:T(8,128)} fusion(bf16[1024,2048]{1,0:T(8,128)(2,1)S(1)} %bitcast.76, bf16[768,2048]{1,0:T(8,128)(2,1)S(1)} %bitcast.87), kind=kOutput, calls=%fused_computation.58 | convolution fusion | flops 3221225472 | bytes 10485760 | tf_op jit(solution)/shard_map/dot_general | solution.py:86
  138.1 5.1 %fusion.21 = f32[1024,768]{1,0:T(8,128)} fusion(bf16[1024,2048]{1,0:T(8,128)(2,1)S(1)} %bitcast.77, bf16[768,2048]{1,0:T(8,128)(2,1)S(1)} %bitcast.88), kind=kOutput, calls=%fused_computation.57 | convolution fusion | flops 3221225472 | bytes 10485760 | tf_op jit(solution)/shard_map/dot_general | solution.py:86
  145.4 3.3 %collective-permute-start.25 = (bf16[4,48,1024]{2,1,0:T(8,128)(2,1)S(1)}, bf16[4,48,1024]{2,1,0:T(8,128)(2,1)S(1)}, u32[]{:S(2)}, u32[]{:S(2)}) collective-permute-start(bf16[4,48,1024]{2,1,0:T(8,128)(2,1)S(1)} %slice.126), channel_id=1, source_target_pairs={{0,6},{2,0},{4,2},{6,4},{1,7},{3,1},{5,3},{7,5},{8,14},{10,8},{12,... | collective-permute-start | bytes 1179656 | tf_op jit(solution)/shard_map/ppermute | solution.py:20
  150.0 3.4 %collective-permute-start.21 = (bf16[4,48,1024]{2,1,0:T(8,128)(2,1)S(1)}, bf16[4,48,1024]{2,1,0:T(8,128)(2,1)S(1)}, u32[]{:S(2)}, u32[]{:S(2)}) collective-permute-start(bf16[4,48,1024]{2,1,0:T(8,128)(2,1)S(1)} %slice.122), channel_id=1, source_target_pairs={{0,24},{8,0},{16,8},{24,16},{1,25},{9,1},{17,9},{25,17},{2,26},{10... | collective-permute-start | bytes 1179656 | tf_op jit(solution)/shard_map/ppermute | solution.py:20
  157.0 14.0 %fusion.3 = f32[1024,2048]{1,0:T(8,128)} fusion(bf16[768,2048]{1,0:T(8,128)(2,1)} %bitcast.84, f32[1024,768]{1,0:T(8,128)} %fusion.22, bf16[1024,2048]{1,0:T(8,128)(2,1)} %bitcast.78, bf16[768,2048]{1,0:T(8,128)(2,1)} %bitcast.86), kind=kOutput, calls=%fused_computation.15 | convolution fusion | flops 6447169536 | bytes 22020096 | tf_op jit(solution)/shard_map/dot_general | solution.py:89
  174.0 16.2 %convert_multiply_fusion = f32[1024,2048]{1,0:T(8,128)} fusion(f32[1024,2048]{1,0:T(8,128)} %fusion.3, f32[1024]{0:T(1024)S(1)} %bitcast.98, bf16[768,2048]{1,0:T(8,128)(2,1)} %bitcast.83, f32[1024,768]{1,0:T(8,128)} %fusion.21, bf16[1024,2048]{1,0:T(8,128)(2,1)} %bitcast.79, bf16[768,2048]{1,0:T(8,128)(2,1)} %bitcast.85), kind=kOutput, calls=%fused_computation | convolution fusion | flops 6455558144 | bytes 30412800 | tf_op jit(solution)/shard_map/dot_general | solution.py:89
  190.2 4.0 %fusion.14 = (f32[512,2048]{1,0:T(8,128)S(1)}, f32[512,2048]{1,0:T(8,128)S(1)}) fusion(f32[1024,2048]{1,0:T(8,128)} %convert_multiply_fusion), kind=kLoop, calls=%fused_computation.52 | loop fusion | bytes 16777216 | tf_op jit(solution)/shard_map/slice | solution.py:94
  194.3 7.1 %collective-permute-done.26 = f32[4,128,2048]{2,1,0:T(8,128)S(1)} collective-permute-done((f32[4,128,2048]{2,1,0:T(8,128)S(1)}, f32[4,128,2048]{2,1,0:T(8,128)S(1)}, u32[]{:S(2)}, u32[]{:S(2)}) %collective-permute-start.26) | collective-permute-done | bytes 4194336 | tf_op jit(solution)/shard_map/ppermute | solution.py:94
  202.5 30.9 %all_to_all.10 = bf16[4,128,2048]{2,1,0:T(8,128)(2,1)S(1)} all-to-all(bf16[4,128,2048]{2,1,0:T(8,128)(2,1)S(1)} %add_convert_fusion.1), channel_id=1, replica_groups=mesh['yhi'=2,'core'=2,'x'=4,'z'=4,'ylo'=2] {'yhi','ylo'}, dimensions={0} | all-to-all | bytes 4194304 | tf_op jit(solution)/shard_map/all_to_all | solution.py:96
  (107 shorter events, 63.4 us)
Async XLA Ops:
  2.7 15.1 %collective-permute-start.5 = (bf16[3,48,2048]{2,1,0:T(8,128)(2,1)S(1)}, bf16[3,48,2048]{2,1,0:T(8,128)(2,1)S(1)}, u32[]{:S(2)}, u32[]{:S(2)}) collective-permute-start(bf16[3,48,2048]{2,1,0:T(8,128)(2,1)S(1)} %get-tuple-element.27), channel_id=1, source_target_pairs={{0,1},{1,0},{2,3},{3,2},{4,5},{5,4},{6,7},{7,6},{8,9},{9,8},{10,11... | collective-permute-start | bytes 1769480 | tf_op jit(solution)/shard_map/ppermute | solution.py:34
  4.4 17.1 %collective-permute-start.2 = (bf16[3,48,2048]{2,1,0:T(8,128)(2,1)S(1)}, bf16[3,48,2048]{2,1,0:T(8,128)(2,1)S(1)}, u32[]{:S(2)}, u32[]{:S(2)}) collective-permute-start(bf16[3,48,2048]{2,1,0:T(8,128)(2,1)S(1)} %bitcast.89), channel_id=1, source_target_pairs={{0,2},{2,4},{4,6},{6,0},{1,3},{3,5},{5,7},{7,1},{8,10},{10,12},{12... | collective-permute-start | bytes 1769480 | tf_op jit(solution)/shard_map/ppermute | solution.py:14
  6.4 16.8 %collective-permute-start.1 = (bf16[3,48,2048]{2,1,0:T(8,128)(2,1)S(1)}, bf16[3,48,2048]{2,1,0:T(8,128)(2,1)S(1)}, u32[]{:S(2)}, u32[]{:S(2)}) collective-permute-start(bf16[3,48,2048]{2,1,0:T(8,128)(2,1)S(1)} %bitcast.90), channel_id=1, source_target_pairs={{0,6},{2,0},{4,2},{6,4},{1,7},{3,1},{5,3},{7,5},{8,14},{10,8},{12,... | collective-permute-start | bytes 1769480 | tf_op jit(solution)/shard_map/ppermute | solution.py:15
  17.8 15.4 %collective-permute-start.7 = (bf16[3,48,2048]{2,1,0:T(8,128)(2,1)S(1)}, bf16[3,48,2048]{2,1,0:T(8,128)(2,1)S(1)}, u32[]{:S(2)}, u32[]{:S(2)}) collective-permute-start(bf16[3,48,2048]{2,1,0:T(8,128)(2,1)S(1)} %collective-permute-done.5), channel_id=1, source_target_pairs={{0,8},{8,16},{16,24},{24,0},{1,9},{9,17},{17,25},{25,1},{2,10},{10... | collective-permute-start | bytes 1769480 | tf_op jit(solution)/shard_map/ppermute | solution.py:14
  19.4 14.3 %collective-permute-start.6 = (bf16[3,48,2048]{2,1,0:T(8,128)(2,1)S(1)}, bf16[3,48,2048]{2,1,0:T(8,128)(2,1)S(1)}, u32[]{:S(2)}, u32[]{:S(2)}) collective-permute-start(bf16[3,48,2048]{2,1,0:T(8,128)(2,1)S(1)} %collective-permute-done.5), channel_id=1, source_target_pairs={{0,24},{8,0},{16,8},{24,16},{1,25},{9,1},{17,9},{25,17},{2,26},{10... | collective-permute-start | bytes 1769480 | tf_op jit(solution)/shard_map/ppermute | solution.py:15
  21.5 15.0 %collective-permute-start.3 = (bf16[3,48,1024]{2,1,0:T(8,128)(2,1)S(1)}, bf16[3,48,1024]{2,1,0:T(8,128)(2,1)S(1)}, u32[]{:S(2)}, u32[]{:S(2)}) collective-permute-start(bf16[3,48,1024]{2,1,0:T(8,128)(2,1)S(1)} %slice.111), channel_id=1, source_target_pairs={{0,2},{2,4},{4,6},{6,0},{1,3},{3,5},{5,7},{7,1},{8,10},{10,12},{12... | collective-permute-start | bytes 884744 | tf_op jit(solution)/shard_map/ppermute | solution.py:19
  23.2 13.4 %collective-permute-start.4 = (bf16[3,48,1024]{2,1,0:T(8,128)(2,1)S(1)}, bf16[3,48,1024]{2,1,0:T(8,128)(2,1)S(1)}, u32[]{:S(2)}, u32[]{:S(2)}) collective-permute-start(bf16[3,48,1024]{2,1,0:T(8,128)(2,1)S(1)} %slice.112), channel_id=1, source_target_pairs={{0,6},{2,0},{4,2},{6,4},{1,7},{3,1},{5,3},{7,5},{8,14},{10,8},{12,... | collective-permute-start | bytes 884744 | tf_op jit(solution)/shard_map/ppermute | solution.py:20
  44.1 33.8 %collective-permute-start.10 = (bf16[4,2,48,2048]{3,2,1,0:T(8,128)(2,1)}, bf16[4,2,48,2048]{3,2,1,0:T(8,128)(2,1)}, u32[]{:S(2)}, u32[]{:S(2)}) collective-permute-start(bf16[4,2,48,2048]{3,2,1,0:T(8,128)(2,1)} %get-tuple-element.26), channel_id=1, source_target_pairs={{0,24},{8,0},{16,8},{24,16},{1,25},{9,1},{17,9},{25,17},{2,26},{10... | collective-permute-start | bytes 4718600 | tf_op jit(solution)/shard_map/ppermute | solution.py:15
  47.2 36.5 %collective-permute-start.11 = (bf16[4,2,48,2048]{3,2,1,0:T(8,128)(2,1)}, bf16[4,2,48,2048]{3,2,1,0:T(8,128)(2,1)}, u32[]{:S(2)}, u32[]{:S(2)}) collective-permute-start(bf16[4,2,48,2048]{3,2,1,0:T(8,128)(2,1)} %get-tuple-element.26), channel_id=1, source_target_pairs={{0,8},{8,16},{16,24},{24,0},{1,9},{9,17},{17,25},{25,1},{2,10},{10... | collective-permute-start | bytes 4718600 | tf_op jit(solution)/shard_map/ppermute | solution.py:14
  49.4 37.6 %collective-permute-start.14 = (bf16[4,2,48,2048]{3,2,1,0:T(8,128)(2,1)}, bf16[4,2,48,2048]{3,2,1,0:T(8,128)(2,1)}, u32[]{:S(2)}, u32[]{:S(2)}) collective-permute-start(bf16[4,2,48,2048]{3,2,1,0:T(8,128)(2,1)} %get-tuple-element.24), channel_id=1, source_target_pairs={{0,6},{2,0},{4,2},{6,4},{1,7},{3,1},{5,3},{7,5},{8,14},{10,8},{12,... | collective-permute-start | bytes 4718600 | tf_op jit(solution)/shard_map/ppermute | solution.py:15
  53.6 39.7 %collective-permute-start.15 = (bf16[4,2,48,2048]{3,2,1,0:T(8,128)(2,1)}, bf16[4,2,48,2048]{3,2,1,0:T(8,128)(2,1)}, u32[]{:S(2)}, u32[]{:S(2)}) collective-permute-start(bf16[4,2,48,2048]{3,2,1,0:T(8,128)(2,1)} %get-tuple-element.24), channel_id=1, source_target_pairs={{0,2},{2,4},{4,6},{6,0},{1,3},{3,5},{5,7},{7,1},{8,10},{10,12},{12... | collective-permute-start | bytes 4718600 | tf_op jit(solution)/shard_map/ppermute | solution.py:14
  55.4 42.1 %all-to-all-start = ((bf16[4,144,2048]{2,1,0:T(8,128)(2,1)}), bf16[4,144,2048]{2,1,0:T(8,128)(2,1)S(1)}, u32[]{:S(2)}, u32[]{:S(2)}) async-start(bf16[4,144,2048]{2,1,0:T(8,128)(2,1)} %broadcast_in_dim.23), calls=%async_computation | async-start | bytes 4718592 | tf_op jit(solution)/shard_map/all_to_all | solution.py:55
  80.0 17.8 %collective-permute-start.13 = (bf16[4,2,48,1024]{3,2,1,0:T(8,128)(2,1)}, bf16[4,2,48,1024]{3,2,1,0:T(8,128)(2,1)}, u32[]{:S(2)}, u32[]{:S(2)}) collective-permute-start(bf16[4,2,48,1024]{3,2,1,0:T(8,128)(2,1)} %slice.116), channel_id=1, source_target_pairs={{0,24},{8,0},{16,8},{24,16},{1,25},{9,1},{17,9},{25,17},{2,26},{10... | collective-permute-start | bytes 2359304 | tf_op jit(solution)/shard_map/ppermute | solution.py:20
  85.8 16.3 %collective-permute-start.12 = (bf16[4,2,48,1024]{3,2,1,0:T(8,128)(2,1)}, bf16[4,2,48,1024]{3,2,1,0:T(8,128)(2,1)}, u32[]{:S(2)}, u32[]{:S(2)}) collective-permute-start(bf16[4,2,48,1024]{3,2,1,0:T(8,128)(2,1)} %slice.115), channel_id=1, source_target_pairs={{0,8},{8,16},{16,24},{24,0},{1,9},{9,17},{17,25},{25,1},{2,10},{10... | collective-permute-start | bytes 2359304 | tf_op jit(solution)/shard_map/ppermute | solution.py:19
  89.1 17.0 %collective-permute-start.17 = (bf16[4,2,48,1024]{3,2,1,0:T(8,128)(2,1)}, bf16[4,2,48,1024]{3,2,1,0:T(8,128)(2,1)}, u32[]{:S(2)}, u32[]{:S(2)}) collective-permute-start(bf16[4,2,48,1024]{3,2,1,0:T(8,128)(2,1)} %slice.118), channel_id=1, source_target_pairs={{0,6},{2,0},{4,2},{6,4},{1,7},{3,1},{5,3},{7,5},{8,14},{10,8},{12,... | collective-permute-start | bytes 2359304 | tf_op jit(solution)/shard_map/ppermute | solution.py:20
  95.4 16.1 %collective-permute-start.16 = (bf16[4,2,48,1024]{3,2,1,0:T(8,128)(2,1)}, bf16[4,2,48,1024]{3,2,1,0:T(8,128)(2,1)}, u32[]{:S(2)}, u32[]{:S(2)}) collective-permute-start(bf16[4,2,48,1024]{3,2,1,0:T(8,128)(2,1)} %slice.117), channel_id=1, source_target_pairs={{0,2},{2,4},{4,6},{6,0},{1,3},{3,5},{5,7},{7,1},{8,10},{10,12},{12... | collective-permute-start | bytes 2359304 | tf_op jit(solution)/shard_map/ppermute | solution.py:19
  97.5 33.3 %collective-permute-start = (bf16[4,144,2048]{2,1,0:T(8,128)(2,1)S(1)}, bf16[4,144,2048]{2,1,0:T(8,128)(2,1)}, u32[]{:S(2)}, u32[]{:S(2)}) collective-permute-start(bf16[4,144,2048]{2,1,0:T(8,128)(2,1)S(1)} %all-to-all-done), channel_id=1, source_target_pairs={{0,32},{32,0},{1,33},{33,1},{2,34},{34,2},{3,35},{35,3},{4,36},{36... | collective-permute-start | bytes 7077896 | tf_op jit(solution)/shard_map/ppermute | solution.py:56
  119.2 29.5 %collective-permute-start.19 = (bf16[4,48,2048]{2,1,0:T(8,128)(2,1)S(1)}, bf16[4,48,2048]{2,1,0:T(8,128)(2,1)S(1)}, u32[]{:S(2)}, u32[]{:S(2)}) collective-permute-start(bf16[4,48,2048]{2,1,0:T(8,128)(2,1)S(1)} %slice_bitcast_fusion.1), channel_id=1, source_target_pairs={{0,8},{8,16},{16,24},{24,0},{1,9},{9,17},{17,25},{25,1},{2,10},{10... | collective-permute-start | bytes 2359304 | tf_op jit(solution)/shard_map/ppermute | solution.py:14
  119.3 29.6 %collective-permute-start.18 = (bf16[4,48,2048]{2,1,0:T(8,128)(2,1)S(1)}, bf16[4,48,2048]{2,1,0:T(8,128)(2,1)}, u32[]{:S(2)}, u32[]{:S(2)}) collective-permute-start(bf16[4,48,2048]{2,1,0:T(8,128)(2,1)S(1)} %slice_bitcast_fusion.1), channel_id=1, source_target_pairs={{0,24},{8,0},{16,8},{24,16},{1,25},{9,1},{17,9},{25,17},{2,26},{10... | collective-permute-start | bytes 2359304 | tf_op jit(solution)/shard_map/ppermute | solution.py:15
  122.5 20.7 %collective-permute-start.23 = (bf16[4,48,2048]{2,1,0:T(8,128)(2,1)S(1)}, bf16[4,48,2048]{2,1,0:T(8,128)(2,1)}, u32[]{:S(2)}, u32[]{:S(2)}) collective-permute-start(bf16[4,48,2048]{2,1,0:T(8,128)(2,1)S(1)} %copy-done.5), channel_id=1, source_target_pairs={{0,2},{2,4},{4,6},{6,0},{1,3},{3,5},{5,7},{7,1},{8,10},{10,12},{12... | collective-permute-start | bytes 2359304 | tf_op jit(solution)/shard_map/ppermute | solution.py:14
  122.5 21.8 %collective-permute-start.22 = (bf16[4,48,2048]{2,1,0:T(8,128)(2,1)S(1)}, bf16[4,48,2048]{2,1,0:T(8,128)(2,1)}, u32[]{:S(2)}, u32[]{:S(2)}) collective-permute-start(bf16[4,48,2048]{2,1,0:T(8,128)(2,1)S(1)} %copy-done.5), channel_id=1, source_target_pairs={{0,6},{2,0},{4,2},{6,4},{1,7},{3,1},{5,3},{7,5},{8,14},{10,8},{12,... | collective-permute-start | bytes 2359304 | tf_op jit(solution)/shard_map/ppermute | solution.py:15
  144.3 9.1 %collective-permute-start.24 = (bf16[4,48,1024]{2,1,0:T(8,128)(2,1)S(1)}, bf16[4,48,1024]{2,1,0:T(8,128)(2,1)S(1)}, u32[]{:S(2)}, u32[]{:S(2)}) collective-permute-start(bf16[4,48,1024]{2,1,0:T(8,128)(2,1)S(1)} %slice.125), channel_id=1, source_target_pairs={{0,2},{2,4},{4,6},{6,0},{1,3},{3,5},{5,7},{7,1},{8,10},{10,12},{12... | collective-permute-start | bytes 1179656 | tf_op jit(solution)/shard_map/ppermute | solution.py:19
  148.8 22.2 %collective-permute-start.20 = (bf16[4,48,1024]{2,1,0:T(8,128)(2,1)S(1)}, bf16[4,48,1024]{2,1,0:T(8,128)(2,1)S(1)}, u32[]{:S(2)}, u32[]{:S(2)}) collective-permute-start(bf16[4,48,1024]{2,1,0:T(8,128)(2,1)S(1)} %slice.121), channel_id=1, source_target_pairs={{0,8},{8,16},{16,24},{24,0},{1,9},{9,17},{17,25},{25,1},{2,10},{10... | collective-permute-start | bytes 1179656 | tf_op jit(solution)/shard_map/ppermute | solution.py:19
  150.0 21.0 %collective-permute-start.21 = (bf16[4,48,1024]{2,1,0:T(8,128)(2,1)S(1)}, bf16[4,48,1024]{2,1,0:T(8,128)(2,1)S(1)}, u32[]{:S(2)}, u32[]{:S(2)}) collective-permute-start(bf16[4,48,1024]{2,1,0:T(8,128)(2,1)S(1)} %slice.122), channel_id=1, source_target_pairs={{0,24},{8,0},{16,8},{24,16},{1,25},{9,1},{17,9},{25,17},{2,26},{10... | collective-permute-start | bytes 1179656 | tf_op jit(solution)/shard_map/ppermute | solution.py:20
  (15 other events, 154.2 us)

commit v5 on v4

--- a/solution.py
+++ b/solution.py
@@ -86,6 +86,7 @@
         gate_part = jnp.dot(rows, weights[0].T, preferred_element_type=jnp.float32)
         up_part = jnp.dot(rows, weights[1].T, preferred_element_type=jnp.float32)
         hidden = (jax.nn.silu(gate_part) * up_part).astype(jnp.bfloat16)
+        hidden = lax.optimization_barrier(hidden)
         part = jnp.dot(hidden, weights[2], preferred_element_type=jnp.float32)
         out = part if out is None else out + part
     out = out.astype(jnp.bfloat16)

time: 236 us -> 212 us (0.90)
  matrix products: 40.5 us -> 21.4 us
  other arithmetic: 18.3 us -> 15.6 us
    dot_general x2, matrix products: 30.2 us -> 6.88 us  [per_device(): part = jnp.dot(hidden, weights[2], preferred_element_type=jnp.float32)]
    ppermute x6, waiting for transfers between devices: 8.22 us -> 28.7 us  [ring_of_four(): from_minus = lax.ppermute(value, axis, perm=ahead)]
    ppermute x6, waiting for transfers between devices: 18.1 us -> 0.02 us  [ring_of_four(): from_plus = lax.ppermute(value, axis, perm=behind)]
    dot_general x0 -> x2, matrix products: none -> 7.64 us  [per_device(): up_part = jnp.dot(rows, weights[1].T, preferred_element_type=jnp.float32)]
    ppermute x6, starting transfers between devices: 3.65 us -> 7.22 us  [ring_of_four(): from_minus = lax.ppermute(value, axis, perm=ahead)]
    ppermute x6, waiting for transfers between devices: 14.2 us -> 10.8 us  [ring_of_four(): lax.ppermute(from_minus[..., :half], axis, perm=ahead)]
    dot_general x2, matrix products: 10.3 us -> 6.88 us  [per_device(): gate_part = jnp.dot(rows, weights[0].T, preferred_element_type=jnp.float32)]
    slice x1, local copies, waits for them, and re-layouts: 4.05 us -> 1.1 us  [per_device(): partner = lax.ppermute(scaled[1], 'core', perm=SWAP)]
  transfers between devices with their start and end apart: 28 -> 28, of which waited for: 10 -> 11; matrix products, arithmetic and copies ran while one was open for 27% -> 27% of each run, Pallas kernels for 0% -> 0%
where the time goes in v5:
time: 212 us; the launch traced here: 210 us
  waiting for transfers between devices  58.7 us (28%)
  starting transfers between devices  48.6 us (23%)
  local copies, waits for them, and re-layouts  34.6 us (16%)
  blocking collectives  30.9 us (15%)
  matrix products  21.4 us (10%)
  other arithmetic  15.6 us (7%)
    all_to_all x1, blocking collectives, per_device(): lax.all_to_all(partial, CHIPS, split_axis=0, concat_axis=0, tiled=True)  30.9 us
    ppermute x6, waiting for transfers between devices, ring_of_four(): from_minus = lax.ppermute(value, axis, perm=ahead)  28.7 us
    ppermute x6, starting transfers between devices, ring_of_four(): lax.ppermute(from_plus[..., half:], axis, perm=behind)  17.9 us
    ppermute x6, starting transfers between devices, ring_of_four(): from_plus = lax.ppermute(value, axis, perm=behind)  14.6 us
    another operation x12, other arithmetic, ring_of_four(): return jnp.stack([value, from_plus, far, from_minus])  13 us
    ppermute x6, waiting for transfers between devices, ring_of_four(): lax.ppermute(from_minus[..., :half], axis, perm=ahead)  10.8 us
    ppermute x1, waiting for transfers between devices, expert_weights(): got = lax.ppermute(send, 'ylo', perm=SWAP)  9.29 us
    dot_general x2, matrix products, per_device(): up_part = jnp.dot(rows, weights[1].T, preferred_element_type=jnp.float32)  7.64 us
  transfers between devices with their start and end apart: 28, of which 11 were waited for; matrix products, arithmetic and copies ran while one was open for 27% of the time, Pallas kernels for 0%

profile of v5, /device:TPU:0, one launch (start us, length us, event | category | flops | bytes accessed | tf_op | source)
XLA Modules:
  0.0 210.3 jit_solution(14006278352304952312)
XLA Ops:
  8.5 9.3 %collective-permute-done.5 = bf16[3,48,2048]{2,1,0:T(8,128)(2,1)S(1)} collective-permute-done((bf16[3,48,2048]{2,1,0:T(8,128)(2,1)S(1)}, bf16[3,48,2048]{2,1,0:T(8,128)(2,1)S(1)}, u32[]{:S(2)}, u32[]{:S(2)}) %collective-permute-start.5) | collective-permute-done | bytes 589856 | tf_op jit(solution)/shard_map/ppermute | solution.py:34
  25.4 7.7 %collective-permute-done.7 = bf16[3,48,2048]{2,1,0:T(8,128)(2,1)S(1)} collective-permute-done((bf16[3,48,2048]{2,1,0:T(8,128)(2,1)S(1)}, bf16[3,48,2048]{2,1,0:T(8,128)(2,1)S(1)}, u32[]{:S(2)}, u32[]{:S(2)}) %collective-permute-start.7) | collective-permute-done | bytes 589856 | tf_op jit(solution)/shard_map/ppermute | solution.py:14
  33.7 2.8 %collective-permute-start.9 = (bf16[3,48,1024]{2,1,0:T(8,128)(2,1)S(1)}, bf16[3,48,1024]{2,1,0:T(8,128)(2,1)S(1)}, u32[]{:S(2)}, u32[]{:S(2)}) collective-permute-start(bf16[3,48,1024]{2,1,0:T(8,128)(2,1)S(1)} %slice.114), channel_id=1, source_target_pairs={{0,24},{8,0},{16,8},{24,16},{1,25},{9,1},{17,9},{25,17},{2,26},{10... | collective-permute-start | bytes 884744 | tf_op jit(solution)/shard_map/ppermute | solution.py:20
  36.9 4.4 %collective-permute-done.8 = bf16[3,48,1024]{2,1,0:T(8,128)(2,1)S(1)} collective-permute-done((bf16[3,48,1024]{2,1,0:T(8,128)(2,1)S(1)}, bf16[3,48,1024]{2,1,0:T(8,128)(2,1)S(1)}, u32[]{:S(2)}, u32[]{:S(2)}) %collective-permute-start.8) | collective-permute-done | bytes 294944 | tf_op jit(solution)/shard_map/ppermute | solution.py:19
  50.9 2.8 %collective-permute-start.10 = (bf16[4,2,48,2048]{3,2,1,0:T(8,128)(2,1)}, bf16[4,2,48,2048]{3,2,1,0:T(8,128)(2,1)}, u32[]{:S(2)}, u32[]{:S(2)}) collective-permute-start(bf16[4,2,48,2048]{3,2,1,0:T(8,128)(2,1)} %get-tuple-element.26), channel_id=1, source_target_pairs={{0,24},{8,0},{16,8},{24,16},{1,25},{9,1},{17,9},{25,17},{2,26},{10... | collective-permute-start | bytes 4718600 | tf_op jit(solution)/shard_map/ppermute | solution.py:15
  55.5 4.5 %all-to-all-start = ((bf16[4,144,2048]{2,1,0:T(8,128)(2,1)}), bf16[4,144,2048]{2,1,0:T(8,128)(2,1)S(1)}, u32[]{:S(2)}, u32[]{:S(2)}) async-start(bf16[4,144,2048]{2,1,0:T(8,128)(2,1)} %broadcast_in_dim.23), calls=%async_computation | async-start | bytes 4718592 | tf_op jit(solution)/shard_map/all_to_all | solution.py:55
  59.9 20.5 %collective-permute-done.15 = bf16[4,2,48,2048]{3,2,1,0:T(8,128)(2,1)} collective-permute-done((bf16[4,2,48,2048]{3,2,1,0:T(8,128)(2,1)}, bf16[4,2,48,2048]{3,2,1,0:T(8,128)(2,1)}, u32[]{:S(2)}, u32[]{:S(2)}) %collective-permute-start.15) | collective-permute-done | bytes 1572896 | tf_op jit(solution)/shard_map/ppermute | solution.py:14
  84.5 3.2 %collective-permute-start.17 = (bf16[4,2,48,1024]{3,2,1,0:T(8,128)(2,1)}, bf16[4,2,48,1024]{3,2,1,0:T(8,128)(2,1)}, u32[]{:S(2)}, u32[]{:S(2)}) collective-permute-start(bf16[4,2,48,1024]{3,2,1,0:T(8,128)(2,1)} %slice.118), channel_id=1, source_target_pairs={{0,6},{2,0},{4,2},{6,4},{1,7},{3,1},{5,3},{7,5},{8,14},{10,8},{12,... | collective-permute-start | bytes 2359304 | tf_op jit(solution)/shard_map/ppermute | solution.py:20
  93.3 3.0 %collective-permute-start.13 = (bf16[4,2,48,1024]{3,2,1,0:T(8,128)(2,1)}, bf16[4,2,48,1024]{3,2,1,0:T(8,128)(2,1)}, u32[]{:S(2)}, u32[]{:S(2)}) collective-permute-start(bf16[4,2,48,1024]{3,2,1,0:T(8,128)(2,1)} %slice.116), channel_id=1, source_target_pairs={{0,24},{8,0},{16,8},{24,16},{1,25},{9,1},{17,9},{25,17},{2,26},{10... | collective-permute-start | bytes 2359304 | tf_op jit(solution)/shard_map/ppermute | solution.py:20
  102.8 5.2 %collective-permute-done.12 = bf16[4,2,48,1024]{3,2,1,0:T(8,128)(2,1)} collective-permute-done((bf16[4,2,48,1024]{3,2,1,0:T(8,128)(2,1)}, bf16[4,2,48,1024]{3,2,1,0:T(8,128)(2,1)}, u32[]{:S(2)}, u32[]{:S(2)}) %collective-permute-start.12) | collective-permute-done | bytes 786464 | tf_op jit(solution)/shard_map/ppermute | solution.py:19
  110.8 3.1 %pad_maximum_fusion.1 = bf16[4,4,2,48,2048]{4,3,2,1,0:T(8,128)(2,1)S(1)} fusion(bf16[1,4,2,48,2048]{4,3,2,1,0:T(8,128)(2,1)} %bitcast.21, bf16[1,4,2,48,2048]{4,3,2,1,0:T(8,128)(2,1)S(1)} %maximum_bitcast_fusion.1, bf16[1,4,2,48,2048]{4,3,2,1,0:T(8,128)(2,1)} %bitcast.19, bf16[1,4,2,48,2048]{4,3,2,1,0:T(8,128)(2,1)S(1)} %copy-done.2), kind=kLoop, calls=%fused_computation.3 | loop fusion | flops 9437184 | bytes 12582912 | tf_op jit(solution)/shard_map/stack | solution.py:24
  113.9 3.0 %pad_maximum_fusion = bf16[4,4,2,48,2048]{4,3,2,1,0:T(8,128)(2,1)S(1)} fusion(bf16[1,4,2,48,2048]{4,3,2,1,0:T(8,128)(2,1)} %bitcast.17, bf16[1,4,2,48,2048]{4,3,2,1,0:T(8,128)(2,1)S(1)} %maximum_bitcast_fusion, bf16[1,4,2,48,2048]{4,3,2,1,0:T(8,128)(2,1)} %bitcast.15, bf16[1,4,2,48,2048]{4,3,2,1,0:T(8,128)(2,1)S(1)} %copy-done.3), kind=kLoop, calls=%fused_computation.2 | loop fusion | flops 9437184 | bytes 12582912 | tf_op jit(solution)/shard_map/stack | solution.py:24
  118.0 2.8 %collective-permute-start.18 = (bf16[4,48,2048]{2,1,0:T(8,128)(2,1)S(1)}, bf16[4,48,2048]{2,1,0:T(8,128)(2,1)}, u32[]{:S(2)}, u32[]{:S(2)}) collective-permute-start(bf16[4,48,2048]{2,1,0:T(8,128)(2,1)S(1)} %copy-done.4), channel_id=1, source_target_pairs={{0,24},{8,0},{16,8},{24,16},{1,25},{9,1},{17,9},{25,17},{2,26},{10... | collective-permute-start | bytes 2359304 | tf_op jit(solution)/shard_map/ppermute | solution.py:15
  120.8 3.2 %collective-permute-start.22 = (bf16[4,48,2048]{2,1,0:T(8,128)(2,1)S(1)}, bf16[4,48,2048]{2,1,0:T(8,128)(2,1)}, u32[]{:S(2)}, u32[]{:S(2)}) collective-permute-start(bf16[4,48,2048]{2,1,0:T(8,128)(2,1)S(1)} %slice_bitcast_fusion), channel_id=1, source_target_pairs={{0,6},{2,0},{4,2},{6,4},{1,7},{3,1},{5,3},{7,5},{8,14},{10,8},{12,... | collective-permute-start | bytes 2359304 | tf_op jit(solution)/shard_map/ppermute | solution.py:15
  132.8 3.4 %fusion.12 = f32[1024,768]{1,0:T(8,128)S(1)} fusion(bf16[1024,2048]{1,0:T(8,128)(2,1)S(1)} %bitcast.78, bf16[768,2048]{1,0:T(8,128)(2,1)S(1)} %bitcast.89), kind=kOutput, calls=%fused_computation.50 | convolution fusion | flops 3221225472 | bytes 10485760 | tf_op jit(solution)/shard_map/dot_general | solution.py:86
  136.3 3.4 %fusion.13 = f32[1024,768]{1,0:T(8,128)S(1)} fusion(bf16[1024,2048]{1,0:T(8,128)(2,1)S(1)} %bitcast.79, bf16[768,2048]{1,0:T(8,128)(2,1)S(1)} %bitcast.90), kind=kOutput, calls=%fused_computation.51 | convolution fusion | flops 3221225472 | bytes 10485760 | tf_op jit(solution)/shard_map/dot_general | solution.py:86
  139.7 3.7 %multiply_convert_fusion.1 = bf16[1024,768]{1,0:T(8,128)(2,1)S(1)} fusion(f32[1024,768]{1,0:T(8,128)S(1)} %fusion.12, bf16[1024,2048]{1,0:T(8,128)(2,1)S(1)} %bitcast.80, bf16[768,2048]{1,0:T(8,128)(2,1)S(1)} %bitcast.87), kind=kOutput, calls=%fused_computation.8 | convolution fusion | flops 3225944064 | bytes 12058624 | tf_op jit(solution)/shard_map/dot_general | solution.py:87
  143.4 3.9 %multiply_convert_fusion = bf16[1024,768]{1,0:T(8,128)(2,1)S(1)} fusion(f32[1024,768]{1,0:T(8,128)S(1)} %fusion.13, bf16[1024,2048]{1,0:T(8,128)(2,1)S(1)} %bitcast.81, bf16[768,2048]{1,0:T(8,128)(2,1)S(1)} %bitcast.88), kind=kOutput, calls=%fused_computation.7 | convolution fusion | flops 3225944064 | bytes 12058624 | tf_op jit(solution)/shard_map/dot_general | solution.py:87
  149.5 3.3 %collective-permute-start.25 = (bf16[4,48,1024]{2,1,0:T(8,128)(2,1)S(1)}, bf16[4,48,1024]{2,1,0:T(8,128)(2,1)S(1)}, u32[]{:S(2)}, u32[]{:S(2)}) collective-permute-start(bf16[4,48,1024]{2,1,0:T(8,128)(2,1)S(1)} %slice.126), channel_id=1, source_target_pairs={{0,6},{2,0},{4,2},{6,4},{1,7},{3,1},{5,3},{7,5},{8,14},{10,8},{12,... | collective-permute-start | bytes 1179656 | tf_op jit(solution)/shard_map/ppermute | solution.py:20
  155.0 3.3 %collective-permute-start.21 = (bf16[4,48,1024]{2,1,0:T(8,128)(2,1)S(1)}, bf16[4,48,1024]{2,1,0:T(8,128)(2,1)S(1)}, u32[]{:S(2)}, u32[]{:S(2)}) collective-permute-start(bf16[4,48,1024]{2,1,0:T(8,128)(2,1)S(1)} %slice.122), channel_id=1, source_target_pairs={{0,24},{8,0},{16,8},{24,16},{1,25},{9,1},{17,9},{25,17},{2,26},{10... | collective-permute-start | bytes 1179656 | tf_op jit(solution)/shard_map/ppermute | solution.py:20
  160.0 3.4 %fusion.14 = f32[1024,2048]{1,0:T(8,128)S(1)} fusion(bf16[1024,768]{1,0:T(8,128)(2,1)S(1)} %multiply_convert_fusion, bf16[768,2048]{1,0:T(8,128)(2,1)S(1)} %bitcast.86), kind=kOutput, calls=%fused_computation.52 | convolution fusion | flops 3221225472 | bytes 13107200 | tf_op jit(solution)/shard_map/dot_general | solution.py:90
  165.2 3.4 %convert_multiply_fusion = f32[1024,2048]{1,0:T(8,128)S(1)} fusion(f32[1024,2048]{1,0:T(8,128)S(1)} %fusion.14, f32[1024]{0:T(1024)S(1)} %bitcast.99, bf16[1024,768]{1,0:T(8,128)(2,1)S(1)} %multiply_convert_fusion.1, bf16[768,2048]{1,0:T(8,128)(2,1)S(1)} %bitcast.85), kind=kOutput, calls=%fused_computation | convolution fusion | flops 3229614080 | bytes 21499904 | tf_op jit(solution)/shard_map/dot_general | solution.py:90
  169.9 7.1 %collective-permute-done.26 = f32[4,128,2048]{2,1,0:T(8,128)S(1)} collective-permute-done((f32[4,128,2048]{2,1,0:T(8,128)S(1)}, f32[4,128,2048]{2,1,0:T(8,128)S(1)}, u32[]{:S(2)}, u32[]{:S(2)}) %collective-permute-start.26) | collective-permute-done | bytes 4194336 | tf_op jit(solution)/shard_map/ppermute | solution.py:95
  178.0 30.9 %all_to_all.10 = bf16[4,128,2048]{2,1,0:T(8,128)(2,1)S(1)} all-to-all(bf16[4,128,2048]{2,1,0:T(8,128)(2,1)S(1)} %add_convert_fusion.1), channel_id=1, replica_groups=mesh['yhi'=2,'core'=2,'x'=4,'z'=4,'ylo'=2] {'yhi','ylo'}, dimensions={0} | all-to-all | bytes 4194304 | tf_op jit(solution)/shard_map/all_to_all | solution.py:97
  (107 shorter events, 68.2 us)
Async XLA Ops:
  2.7 15.1 %collective-permute-start.5 = (bf16[3,48,2048]{2,1,0:T(8,128)(2,1)S(1)}, bf16[3,48,2048]{2,1,0:T(8,128)(2,1)S(1)}, u32[]{:S(2)}, u32[]{:S(2)}) collective-permute-start(bf16[3,48,2048]{2,1,0:T(8,128)(2,1)S(1)} %get-tuple-element.27), channel_id=1, source_target_pairs={{0,1},{1,0},{2,3},{3,2},{4,5},{5,4},{6,7},{7,6},{8,9},{9,8},{10,11... | collective-permute-start | bytes 1769480 | tf_op jit(solution)/shard_map/ppermute | solution.py:34
  4.4 17.1 %collective-permute-start.2 = (bf16[3,48,2048]{2,1,0:T(8,128)(2,1)S(1)}, bf16[3,48,2048]{2,1,0:T(8,128)(2,1)S(1)}, u32[]{:S(2)}, u32[]{:S(2)}) collective-permute-start(bf16[3,48,2048]{2,1,0:T(8,128)(2,1)S(1)} %bitcast.91), channel_id=1, source_target_pairs={{0,2},{2,4},{4,6},{6,0},{1,3},{3,5},{5,7},{7,1},{8,10},{10,12},{12... | collective-permute-start | bytes 1769480 | tf_op jit(solution)/shard_map/ppermute | solution.py:14
  6.4 16.8 %collective-permute-start.1 = (bf16[3,48,2048]{2,1,0:T(8,128)(2,1)S(1)}, bf16[3,48,2048]{2,1,0:T(8,128)(2,1)S(1)}, u32[]{:S(2)}, u32[]{:S(2)}) collective-permute-start(bf16[3,48,2048]{2,1,0:T(8,128)(2,1)S(1)} %bitcast.92), channel_id=1, source_target_pairs={{0,6},{2,0},{4,2},{6,4},{1,7},{3,1},{5,3},{7,5},{8,14},{10,8},{12,... | collective-permute-start | bytes 1769480 | tf_op jit(solution)/shard_map/ppermute | solution.py:15
  17.8 15.4 %collective-permute-start.7 = (bf16[3,48,2048]{2,1,0:T(8,128)(2,1)S(1)}, bf16[3,48,2048]{2,1,0:T(8,128)(2,1)S(1)}, u32[]{:S(2)}, u32[]{:S(2)}) collective-permute-start(bf16[3,48,2048]{2,1,0:T(8,128)(2,1)S(1)} %collective-permute-done.5), channel_id=1, source_target_pairs={{0,8},{8,16},{16,24},{24,0},{1,9},{9,17},{17,25},{25,1},{2,10},{10... | collective-permute-start | bytes 1769480 | tf_op jit(solution)/shard_map/ppermute | solution.py:14
  19.4 14.3 %collective-permute-start.6 = (bf16[3,48,2048]{2,1,0:T(8,128)(2,1)S(1)}, bf16[3,48,2048]{2,1,0:T(8,128)(2,1)S(1)}, u32[]{:S(2)}, u32[]{:S(2)}) collective-permute-start(bf16[3,48,2048]{2,1,0:T(8,128)(2,1)S(1)} %collective-permute-done.5), channel_id=1, source_target_pairs={{0,24},{8,0},{16,8},{24,16},{1,25},{9,1},{17,9},{25,17},{2,26},{10... | collective-permute-start | bytes 1769480 | tf_op jit(solution)/shard_map/ppermute | solution.py:15
  21.5 15.0 %collective-permute-start.3 = (bf16[3,48,1024]{2,1,0:T(8,128)(2,1)S(1)}, bf16[3,48,1024]{2,1,0:T(8,128)(2,1)S(1)}, u32[]{:S(2)}, u32[]{:S(2)}) collective-permute-start(bf16[3,48,1024]{2,1,0:T(8,128)(2,1)S(1)} %slice.111), channel_id=1, source_target_pairs={{0,2},{2,4},{4,6},{6,0},{1,3},{3,5},{5,7},{7,1},{8,10},{10,12},{12... | collective-permute-start | bytes 884744 | tf_op jit(solution)/shard_map/ppermute | solution.py:19
  23.2 13.4 %collective-permute-start.4 = (bf16[3,48,1024]{2,1,0:T(8,128)(2,1)S(1)}, bf16[3,48,1024]{2,1,0:T(8,128)(2,1)S(1)}, u32[]{:S(2)}, u32[]{:S(2)}) collective-permute-start(bf16[3,48,1024]{2,1,0:T(8,128)(2,1)S(1)} %slice.112), channel_id=1, source_target_pairs={{0,6},{2,0},{4,2},{6,4},{1,7},{3,1},{5,3},{7,5},{8,14},{10,8},{12,... | collective-permute-start | bytes 884744 | tf_op jit(solution)/shard_map/ppermute | solution.py:20
  44.1 36.3 %collective-permute-start.15 = (bf16[4,2,48,2048]{3,2,1,0:T(8,128)(2,1)}, bf16[4,2,48,2048]{3,2,1,0:T(8,128)(2,1)}, u32[]{:S(2)}, u32[]{:S(2)}) collective-permute-start(bf16[4,2,48,2048]{3,2,1,0:T(8,128)(2,1)} %get-tuple-element.24), channel_id=1, source_target_pairs={{0,2},{2,4},{4,6},{6,0},{1,3},{3,5},{5,7},{7,1},{8,10},{10,12},{12... | collective-permute-start | bytes 4718600 | tf_op jit(solution)/shard_map/ppermute | solution.py:14
  46.3 36.2 %collective-permute-start.14 = (bf16[4,2,48,2048]{3,2,1,0:T(8,128)(2,1)}, bf16[4,2,48,2048]{3,2,1,0:T(8,128)(2,1)}, u32[]{:S(2)}, u32[]{:S(2)}) collective-permute-start(bf16[4,2,48,2048]{3,2,1,0:T(8,128)(2,1)} %get-tuple-element.24), channel_id=1, source_target_pairs={{0,6},{2,0},{4,2},{6,4},{1,7},{3,1},{5,3},{7,5},{8,14},{10,8},{12,... | collective-permute-start | bytes 4718600 | tf_op jit(solution)/shard_map/ppermute | solution.py:15
  50.4 38.5 %collective-permute-start.11 = (bf16[4,2,48,2048]{3,2,1,0:T(8,128)(2,1)}, bf16[4,2,48,2048]{3,2,1,0:T(8,128)(2,1)}, u32[]{:S(2)}, u32[]{:S(2)}) collective-permute-start(bf16[4,2,48,2048]{3,2,1,0:T(8,128)(2,1)} %get-tuple-element.26), channel_id=1, source_target_pairs={{0,8},{8,16},{16,24},{24,0},{1,9},{9,17},{17,25},{25,1},{2,10},{10... | collective-permute-start | bytes 4718600 | tf_op jit(solution)/shard_map/ppermute | solution.py:14
  50.9 40.4 %collective-permute-start.10 = (bf16[4,2,48,2048]{3,2,1,0:T(8,128)(2,1)}, bf16[4,2,48,2048]{3,2,1,0:T(8,128)(2,1)}, u32[]{:S(2)}, u32[]{:S(2)}) collective-permute-start(bf16[4,2,48,2048]{3,2,1,0:T(8,128)(2,1)} %get-tuple-element.26), channel_id=1, source_target_pairs={{0,24},{8,0},{16,8},{24,16},{1,25},{9,1},{17,9},{25,17},{2,26},{10... | collective-permute-start | bytes 4718600 | tf_op jit(solution)/shard_map/ppermute | solution.py:15
  55.5 43.0 %all-to-all-start = ((bf16[4,144,2048]{2,1,0:T(8,128)(2,1)}), bf16[4,144,2048]{2,1,0:T(8,128)(2,1)S(1)}, u32[]{:S(2)}, u32[]{:S(2)}) async-start(bf16[4,144,2048]{2,1,0:T(8,128)(2,1)} %broadcast_in_dim.23), calls=%async_computation | async-start | bytes 4718592 | tf_op jit(solution)/shard_map/all_to_all | solution.py:55
  82.5 17.5 %collective-permute-start.16 = (bf16[4,2,48,1024]{3,2,1,0:T(8,128)(2,1)}, bf16[4,2,48,1024]{3,2,1,0:T(8,128)(2,1)}, u32[]{:S(2)}, u32[]{:S(2)}) collective-permute-start(bf16[4,2,48,1024]{3,2,1,0:T(8,128)(2,1)} %slice.117), channel_id=1, source_target_pairs={{0,2},{2,4},{4,6},{6,0},{1,3},{3,5},{5,7},{7,1},{8,10},{10,12},{12... | collective-permute-start | bytes 2359304 | tf_op jit(solution)/shard_map/ppermute | solution.py:19
  84.5 16.7 %collective-permute-start.17 = (bf16[4,2,48,1024]{3,2,1,0:T(8,128)(2,1)}, bf16[4,2,48,1024]{3,2,1,0:T(8,128)(2,1)}, u32[]{:S(2)}, u32[]{:S(2)}) collective-permute-start(bf16[4,2,48,1024]{3,2,1,0:T(8,128)(2,1)} %slice.118), channel_id=1, source_target_pairs={{0,6},{2,0},{4,2},{6,4},{1,7},{3,1},{5,3},{7,5},{8,14},{10,8},{12,... | collective-permute-start | bytes 2359304 | tf_op jit(solution)/shard_map/ppermute | solution.py:20
  91.0 16.9 %collective-permute-start.12 = (bf16[4,2,48,1024]{3,2,1,0:T(8,128)(2,1)}, bf16[4,2,48,1024]{3,2,1,0:T(8,128)(2,1)}, u32[]{:S(2)}, u32[]{:S(2)}) collective-permute-start(bf16[4,2,48,1024]{3,2,1,0:T(8,128)(2,1)} %slice.115), channel_id=1, source_target_pairs={{0,8},{8,16},{16,24},{24,0},{1,9},{9,17},{17,25},{25,1},{2,10},{10... | collective-permute-start | bytes 2359304 | tf_op jit(solution)/shard_map/ppermute | solution.py:19
  93.3 15.9 %collective-permute-start.13 = (bf16[4,2,48,1024]{3,2,1,0:T(8,128)(2,1)}, bf16[4,2,48,1024]{3,2,1,0:T(8,128)(2,1)}, u32[]{:S(2)}, u32[]{:S(2)}) collective-permute-start(bf16[4,2,48,1024]{3,2,1,0:T(8,128)(2,1)} %slice.116), channel_id=1, source_target_pairs={{0,24},{8,0},{16,8},{24,16},{1,25},{9,1},{17,9},{25,17},{2,26},{10... | collective-permute-start | bytes 2359304 | tf_op jit(solution)/shard_map/ppermute | solution.py:20
  98.5 30.6 %collective-permute-start = (bf16[4,144,2048]{2,1,0:T(8,128)(2,1)S(1)}, bf16[4,144,2048]{2,1,0:T(8,128)(2,1)}, u32[]{:S(2)}, u32[]{:S(2)}) collective-permute-start(bf16[4,144,2048]{2,1,0:T(8,128)(2,1)S(1)} %all-to-all-done), channel_id=1, source_target_pairs={{0,32},{32,0},{1,33},{33,1},{2,34},{34,2},{3,35},{35,3},{4,36},{36... | collective-permute-start | bytes 7077896 | tf_op jit(solution)/shard_map/ppermute | solution.py:56
  117.0 35.9 %collective-permute-start.19 = (bf16[4,48,2048]{2,1,0:T(8,128)(2,1)S(1)}, bf16[4,48,2048]{2,1,0:T(8,128)(2,1)}, u32[]{:S(2)}, u32[]{:S(2)}) collective-permute-start(bf16[4,48,2048]{2,1,0:T(8,128)(2,1)S(1)} %copy-done.4), channel_id=1, source_target_pairs={{0,8},{8,16},{16,24},{24,0},{1,9},{9,17},{17,25},{25,1},{2,10},{10... | collective-permute-start | bytes 2359304 | tf_op jit(solution)/shard_map/ppermute | solution.py:14
  118.0 35.9 %collective-permute-start.18 = (bf16[4,48,2048]{2,1,0:T(8,128)(2,1)S(1)}, bf16[4,48,2048]{2,1,0:T(8,128)(2,1)}, u32[]{:S(2)}, u32[]{:S(2)}) collective-permute-start(bf16[4,48,2048]{2,1,0:T(8,128)(2,1)S(1)} %copy-done.4), channel_id=1, source_target_pairs={{0,24},{8,0},{16,8},{24,16},{1,25},{9,1},{17,9},{25,17},{2,26},{10... | collective-permute-start | bytes 2359304 | tf_op jit(solution)/shard_map/ppermute | solution.py:15
  120.8 26.6 %collective-permute-start.23 = (bf16[4,48,2048]{2,1,0:T(8,128)(2,1)S(1)}, bf16[4,48,2048]{2,1,0:T(8,128)(2,1)}, u32[]{:S(2)}, u32[]{:S(2)}) collective-permute-start(bf16[4,48,2048]{2,1,0:T(8,128)(2,1)S(1)} %slice_bitcast_fusion), channel_id=1, source_target_pairs={{0,2},{2,4},{4,6},{6,0},{1,3},{3,5},{5,7},{7,1},{8,10},{10,12},{12... | collective-permute-start | bytes 2359304 | tf_op jit(solution)/shard_map/ppermute | solution.py:14
  120.8 27.7 %collective-permute-start.22 = (bf16[4,48,2048]{2,1,0:T(8,128)(2,1)S(1)}, bf16[4,48,2048]{2,1,0:T(8,128)(2,1)}, u32[]{:S(2)}, u32[]{:S(2)}) collective-permute-start(bf16[4,48,2048]{2,1,0:T(8,128)(2,1)S(1)} %slice_bitcast_fusion), channel_id=1, source_target_pairs={{0,6},{2,0},{4,2},{6,4},{1,7},{3,1},{5,3},{7,5},{8,14},{10,8},{12,... | collective-permute-start | bytes 2359304 | tf_op jit(solution)/shard_map/ppermute | solution.py:15
  148.4 9.9 %collective-permute-start.24 = (bf16[4,48,1024]{2,1,0:T(8,128)(2,1)S(1)}, bf16[4,48,1024]{2,1,0:T(8,128)(2,1)S(1)}, u32[]{:S(2)}, u32[]{:S(2)}) collective-permute-start(bf16[4,48,1024]{2,1,0:T(8,128)(2,1)S(1)} %slice.125), channel_id=1, source_target_pairs={{0,2},{2,4},{4,6},{6,0},{1,3},{3,5},{5,7},{7,1},{8,10},{10,12},{12... | collective-permute-start | bytes 1179656 | tf_op jit(solution)/shard_map/ppermute | solution.py:19
  149.5 8.8 %collective-permute-start.25 = (bf16[4,48,1024]{2,1,0:T(8,128)(2,1)S(1)}, bf16[4,48,1024]{2,1,0:T(8,128)(2,1)S(1)}, u32[]{:S(2)}, u32[]{:S(2)}) collective-permute-start(bf16[4,48,1024]{2,1,0:T(8,128)(2,1)S(1)} %slice.126), channel_id=1, source_target_pairs={{0,6},{2,0},{4,2},{6,4},{1,7},{3,1},{5,3},{7,5},{8,14},{10,8},{12,... | collective-permute-start | bytes 1179656 | tf_op jit(solution)/shard_map/ppermute | solution.py:20
  153.9 9.5 %collective-permute-start.20 = (bf16[4,48,1024]{2,1,0:T(8,128)(2,1)S(1)}, bf16[4,48,1024]{2,1,0:T(8,128)(2,1)S(1)}, u32[]{:S(2)}, u32[]{:S(2)}) collective-permute-start(bf16[4,48,1024]{2,1,0:T(8,128)(2,1)S(1)} %slice.121), channel_id=1, source_target_pairs={{0,8},{8,16},{16,24},{24,0},{1,9},{9,17},{17,25},{25,1},{2,10},{10... | collective-permute-start | bytes 1179656 | tf_op jit(solution)/shard_map/ppermute | solution.py:19
  (14 other events, 130.9 us)

commit v6 on v4

--- a/solution.py
+++ b/solution.py
@@ -81,18 +81,26 @@
     table = (halves[..., : extra // 2] + halves[..., extra // 2 :]).reshape(-1, extra // 2)
     scale = lax.dynamic_index_in_dim(table, expert, axis=1, keepdims=True)
 
-    out = None
+    hiddens = []
     for weights in sets:
         gate_part = jnp.dot(rows, weights[0].T, preferred_element_type=jnp.float32)
         up_part = jnp.dot(rows, weights[1].T, preferred_element_type=jnp.float32)
         hidden = (jax.nn.silu(gate_part) * up_part).astype(jnp.bfloat16)
-        part = jnp.dot(hidden, weights[2], preferred_element_type=jnp.float32)
-        out = part if out is None else out + part
-    out = out.astype(jnp.bfloat16)
-    scaled = (out.astype(jnp.float32) * scale).reshape(2, chips, token_count, model_width)
+        hiddens.append(lax.optimization_barrier(hidden))
 
-    partner = lax.ppermute(scaled[1], "core", perm=SWAP)
-    partial = (scaled[0] + partner).astype(jnp.bfloat16)
+    def down(hiddens, first, last):
+        out = None
+        for hidden, weights in zip(hiddens, sets):
+            part = jnp.dot(hidden[first:last], weights[2], preferred_element_type=jnp.float32)
+            out = part if out is None else out + part
+        weighted = out.astype(jnp.bfloat16).astype(jnp.float32) * scale[first:last]
+        return weighted.reshape(chips, token_count, model_width)
+
+    half = chips * token_count
+    theirs = down(hiddens, half, 2 * half)
+    hiddens, theirs = lax.optimization_barrier((hiddens, theirs))
+    partner = lax.ppermute(theirs, "core", perm=SWAP)
+    partial = (down(hiddens, 0, half) + partner).astype(jnp.bfloat16)
     back = lax.all_to_all(partial, CHIPS, split_axis=0, concat_axis=0, tiled=True)
     mixed = jnp.sum(back.astype(jnp.float32), axis=0)
     return mixed.astype(jnp.bfloat16)

time: 236 us -> 211 us (0.89)
  matrix products: 40.5 us -> 21.9 us
  other arithmetic: 18.3 us -> 15.6 us
  waiting for transfers between devices: 59.9 us -> 57.5 us
    dot_general x2 -> x6, matrix products: 30.2 us -> 15 us  [the longest x2 7.64 us: per_device(): up_part = jnp.dot(rows, weights[1].T, preferred_element_type=jnp.float32)]
    slice x1, local copies, waits for them, and re-layouts: 4.05 us -> 0.08 us  [down(): weighted = out.astype(jnp.bfloat16).astype(jnp.float32) * scale[first:last]]
    ppermute x1, waiting for transfers between devices: 7.15 us -> 3.44 us  [per_device(): partner = lax.ppermute(theirs, 'core', perm=SWAP)]
    dot_general x2, matrix products: 10.3 us -> 6.88 us  [per_device(): gate_part = jnp.dot(rows, weights[0].T, preferred_element_type=jnp.float32)]
    another operation x12, other arithmetic: 15.8 us -> 13 us  [ring_of_four(): return jnp.stack([value, from_plus, far, from_minus])]
  transfers between devices with their start and end apart: 28 -> 28, of which waited for: 10 -> 11; matrix products, arithmetic and copies ran while one was open for 27% -> 28% of each run, Pallas kernels for 0% -> 0%
where the time goes in v6:
time: 211 us; the launch traced here: 209 us
  waiting for transfers between devices  57.5 us (27%)
  starting transfers between devices  49.4 us (23%)
  local copies, waits for them, and re-layouts  33.5 us (16%)
  blocking collectives  30.9 us (15%)
  matrix products  21.9 us (10%)
  other arithmetic  15.6 us (7%)
    all_to_all x1, blocking collectives, per_device(): lax.all_to_all(partial, CHIPS, split_axis=0, concat_axis=0, tiled=True)  30.9 us
    ppermute x6, starting transfers between devices, ring_of_four(): lax.ppermute(from_plus[..., half:], axis, perm=behind)  19.6 us
    ppermute x6, waiting for transfers between devices, ring_of_four(): from_plus = lax.ppermute(value, axis, perm=behind)  18.2 us
    ppermute x6, starting transfers between devices, ring_of_four(): from_plus = lax.ppermute(value, axis, perm=behind)  17.5 us
    ppermute x6, waiting for transfers between devices, ring_of_four(): lax.ppermute(from_minus[..., :half], axis, perm=ahead)  15.4 us
    another operation x12, other arithmetic, ring_of_four(): return jnp.stack([value, from_plus, far, from_minus])  13 us
    ppermute x1, waiting for transfers between devices, expert_weights(): got = lax.ppermute(send, 'ylo', perm=SWAP)  9.29 us
    ppermute x6, waiting for transfers between devices, ring_of_four(): from_minus = lax.ppermute(value, axis, perm=ahead)  8.22 us
  transfers between devices with their start and end apart: 28, of which 11 were waited for; matrix products, arithmetic and copies ran while one was open for 28% of the time, Pallas kernels for 0%

profile of v6, /device:TPU:0, one launch (start us, length us, event | category | flops | bytes accessed | tf_op | source)
XLA Modules:
  0.0 209.3 jit_solution(6614837574580779400)
XLA Ops:
  8.5 9.3 %collective-permute-done.5 = bf16[3,48,2048]{2,1,0:T(8,128)(2,1)S(1)} collective-permute-done((bf16[3,48,2048]{2,1,0:T(8,128)(2,1)S(1)}, bf16[3,48,2048]{2,1,0:T(8,128)(2,1)S(1)}, u32[]{:S(2)}, u32[]{:S(2)}) %collective-permute-start.5) | collective-permute-done | bytes 589856 | tf_op jit(solution)/shard_map/ppermute | solution.py:34
  25.4 7.7 %collective-permute-done.7 = bf16[3,48,2048]{2,1,0:T(8,128)(2,1)S(1)} collective-permute-done((bf16[3,48,2048]{2,1,0:T(8,128)(2,1)S(1)}, bf16[3,48,2048]{2,1,0:T(8,128)(2,1)S(1)}, u32[]{:S(2)}, u32[]{:S(2)}) %collective-permute-start.7) | collective-permute-done | bytes 589856 | tf_op jit(solution)/shard_map/ppermute | solution.py:14
  33.7 2.8 %collective-permute-start.9 = (bf16[3,48,1024]{2,1,0:T(8,128)(2,1)S(1)}, bf16[3,48,1024]{2,1,0:T(8,128)(2,1)S(1)}, u32[]{:S(2)}, u32[]{:S(2)}) collective-permute-start(bf16[3,48,1024]{2,1,0:T(8,128)(2,1)S(1)} %slice.128), channel_id=1, source_target_pairs={{0,24},{8,0},{16,8},{24,16},{1,25},{9,1},{17,9},{25,17},{2,26},{10... | collective-permute-start | bytes 884744 | tf_op jit(solution)/shard_map/ppermute | solution.py:20
  36.9 4.4 %collective-permute-done.8 = bf16[3,48,1024]{2,1,0:T(8,128)(2,1)S(1)} collective-permute-done((bf16[3,48,1024]{2,1,0:T(8,128)(2,1)S(1)}, bf16[3,48,1024]{2,1,0:T(8,128)(2,1)S(1)}, u32[]{:S(2)}, u32[]{:S(2)}) %collective-permute-start.8) | collective-permute-done | bytes 294944 | tf_op jit(solution)/shard_map/ppermute | solution.py:19
  44.0 3.1 %collective-permute-start.10 = (bf16[4,2,48,2048]{3,2,1,0:T(8,128)(2,1)}, bf16[4,2,48,2048]{3,2,1,0:T(8,128)(2,1)}, u32[]{:S(2)}, u32[]{:S(2)}) collective-permute-start(bf16[4,2,48,2048]{3,2,1,0:T(8,128)(2,1)} %get-tuple-element.30), channel_id=1, source_target_pairs={{0,24},{8,0},{16,8},{24,16},{1,25},{9,1},{17,9},{25,17},{2,26},{10... | collective-permute-start | bytes 4718600 | tf_op jit(solution)/shard_map/ppermute | solution.py:15
  49.2 4.2 %collective-permute-start.14 = (bf16[4,2,48,2048]{3,2,1,0:T(8,128)(2,1)}, bf16[4,2,48,2048]{3,2,1,0:T(8,128)(2,1)}, u32[]{:S(2)}, u32[]{:S(2)}) collective-permute-start(bf16[4,2,48,2048]{3,2,1,0:T(8,128)(2,1)} %get-tuple-element.28), channel_id=1, source_target_pairs={{0,6},{2,0},{4,2},{6,4},{1,7},{3,1},{5,3},{7,5},{8,14},{10,8},{12,... | collective-permute-start | bytes 4718600 | tf_op jit(solution)/shard_map/ppermute | solution.py:15
  55.2 4.5 %all-to-all-start = ((bf16[4,144,2048]{2,1,0:T(8,128)(2,1)}), bf16[4,144,2048]{2,1,0:T(8,128)(2,1)S(1)}, u32[]{:S(2)}, u32[]{:S(2)}) async-start(bf16[4,144,2048]{2,1,0:T(8,128)(2,1)} %broadcast_in_dim.23), calls=%async_computation | async-start | bytes 4718592 | tf_op jit(solution)/shard_map/all_to_all | solution.py:55
  59.7 18.2 %collective-permute-done.10 = bf16[4,2,48,2048]{3,2,1,0:T(8,128)(2,1)} collective-permute-done((bf16[4,2,48,2048]{3,2,1,0:T(8,128)(2,1)}, bf16[4,2,48,2048]{3,2,1,0:T(8,128)(2,1)}, u32[]{:S(2)}, u32[]{:S(2)}) %collective-permute-start.10) | collective-permute-done | bytes 1572896 | tf_op jit(solution)/shard_map/ppermute | solution.py:15
  79.9 3.7 %collective-permute-start.13 = (bf16[4,2,48,1024]{3,2,1,0:T(8,128)(2,1)}, bf16[4,2,48,1024]{3,2,1,0:T(8,128)(2,1)}, u32[]{:S(2)}, u32[]{:S(2)}) collective-permute-start(bf16[4,2,48,1024]{3,2,1,0:T(8,128)(2,1)} %slice.130), channel_id=1, source_target_pairs={{0,24},{8,0},{16,8},{24,16},{1,25},{9,1},{17,9},{25,17},{2,26},{10... | collective-permute-start | bytes 2359304 | tf_op jit(solution)/shard_map/ppermute | solution.py:20
  89.0 4.3 %collective-permute-start.17 = (bf16[4,2,48,1024]{3,2,1,0:T(8,128)(2,1)}, bf16[4,2,48,1024]{3,2,1,0:T(8,128)(2,1)}, u32[]{:S(2)}, u32[]{:S(2)}) collective-permute-start(bf16[4,2,48,1024]{3,2,1,0:T(8,128)(2,1)} %slice.132), channel_id=1, source_target_pairs={{0,6},{2,0},{4,2},{6,4},{1,7},{3,1},{5,3},{7,5},{8,14},{10,8},{12,... | collective-permute-start | bytes 2359304 | tf_op jit(solution)/shard_map/ppermute | solution.py:20
  97.8 4.3 %collective-permute-done.12 = bf16[4,2,48,1024]{3,2,1,0:T(8,128)(2,1)} collective-permute-done((bf16[4,2,48,1024]{3,2,1,0:T(8,128)(2,1)}, bf16[4,2,48,1024]{3,2,1,0:T(8,128)(2,1)}, u32[]{:S(2)}, u32[]{:S(2)}) %collective-permute-start.12) | collective-permute-done | bytes 786464 | tf_op jit(solution)/shard_map/ppermute | solution.py:19
  105.9 5.5 %collective-permute-done.16 = bf16[4,2,48,1024]{3,2,1,0:T(8,128)(2,1)} collective-permute-done((bf16[4,2,48,1024]{3,2,1,0:T(8,128)(2,1)}, bf16[4,2,48,1024]{3,2,1,0:T(8,128)(2,1)}, u32[]{:S(2)}, u32[]{:S(2)}) %collective-permute-start.16) | collective-permute-done | bytes 786464 | tf_op jit(solution)/shard_map/ppermute | solution.py:19
  112.9 3.1 %pad_maximum_fusion = bf16[4,4,2,48,2048]{4,3,2,1,0:T(8,128)(2,1)S(1)} fusion(bf16[1,4,2,48,2048]{4,3,2,1,0:T(8,128)(2,1)} %bitcast.17, bf16[1,4,2,48,2048]{4,3,2,1,0:T(8,128)(2,1)S(1)} %maximum_bitcast_fusion, bf16[1,4,2,48,2048]{4,3,2,1,0:T(8,128)(2,1)} %bitcast.15, bf16[1,4,2,48,2048]{4,3,2,1,0:T(8,128)(2,1)S(1)} %copy-done.2), kind=kLoop, calls=%fused_computation | loop fusion | flops 9437184 | bytes 12582912 | tf_op jit(solution)/shard_map/stack | solution.py:24
  116.0 3.0 %pad_maximum_fusion.1 = bf16[4,4,2,48,2048]{4,3,2,1,0:T(8,128)(2,1)S(1)} fusion(bf16[1,4,2,48,2048]{4,3,2,1,0:T(8,128)(2,1)} %bitcast.21, bf16[1,4,2,48,2048]{4,3,2,1,0:T(8,128)(2,1)S(1)} %maximum_bitcast_fusion.1, bf16[1,4,2,48,2048]{4,3,2,1,0:T(8,128)(2,1)} %bitcast.19, bf16[1,4,2,48,2048]{4,3,2,1,0:T(8,128)(2,1)S(1)} %copy-done.3), kind=kLoop, calls=%fused_computation.1 | loop fusion | flops 9437184 | bytes 12582912 | tf_op jit(solution)/shard_map/stack | solution.py:24
  119.2 3.2 %collective-permute-start.18 = (bf16[4,48,2048]{2,1,0:T(8,128)(2,1)S(1)}, bf16[4,48,2048]{2,1,0:T(8,128)(2,1)}, u32[]{:S(2)}, u32[]{:S(2)}) collective-permute-start(bf16[4,48,2048]{2,1,0:T(8,128)(2,1)S(1)} %slice_bitcast_fusion.1), channel_id=1, source_target_pairs={{0,24},{8,0},{16,8},{24,16},{1,25},{9,1},{17,9},{25,17},{2,26},{10... | collective-permute-start | bytes 2359304 | tf_op jit(solution)/shard_map/ppermute | solution.py:15
  122.4 3.2 %collective-permute-start.22 = (bf16[4,48,2048]{2,1,0:T(8,128)(2,1)S(1)}, bf16[4,48,2048]{2,1,0:T(8,128)(2,1)}, u32[]{:S(2)}, u32[]{:S(2)}) collective-permute-start(bf16[4,48,2048]{2,1,0:T(8,128)(2,1)S(1)} %copy-done.4), channel_id=1, source_target_pairs={{0,6},{2,0},{4,2},{6,4},{1,7},{3,1},{5,3},{7,5},{8,14},{10,8},{12,... | collective-permute-start | bytes 2359304 | tf_op jit(solution)/shard_map/ppermute | solution.py:15
  134.5 3.4 %fusion.18 = f32[1024,768]{1,0:T(8,128)S(1)} fusion(bf16[1024,2048]{1,0:T(8,128)(2,1)S(1)} %bitcast.81, bf16[768,2048]{1,0:T(8,128)(2,1)S(1)} %bitcast.92), kind=kOutput, calls=%fused_computation.58 | convolution fusion | flops 3221225472 | bytes 10485760 | tf_op jit(solution)/shard_map/dot_general | solution.py:86
  137.9 3.4 %fusion.17 = f32[1024,768]{1,0:T(8,128)S(1)} fusion(bf16[1024,2048]{1,0:T(8,128)(2,1)S(1)} %bitcast.82, bf16[768,2048]{1,0:T(8,128)(2,1)S(1)} %bitcast.93), kind=kOutput, calls=%fused_computation.57 | convolution fusion | flops 3221225472 | bytes 10485760 | tf_op jit(solution)/shard_map/dot_general | solution.py:86
  141.4 3.7 %multiply_convert_fusion = bf16[1024,768]{1,0:T(8,128)(2,1)S(1)} fusion(f32[1024,768]{1,0:T(8,128)S(1)} %fusion.18, bf16[1024,2048]{1,0:T(8,128)(2,1)S(1)} %bitcast.83, bf16[768,2048]{1,0:T(8,128)(2,1)S(1)} %bitcast.90), kind=kOutput, calls=%fused_computation.9 | convolution fusion | flops 3225944064 | bytes 12058624 | tf_op jit(solution)/shard_map/dot_general | solution.py:87
  145.1 3.9 %multiply_convert_fusion.1 = bf16[1024,768]{1,0:T(8,128)(2,1)S(1)} fusion(f32[1024,768]{1,0:T(8,128)S(1)} %fusion.17, bf16[1024,2048]{1,0:T(8,128)(2,1)S(1)} %bitcast.84, bf16[768,2048]{1,0:T(8,128)(2,1)S(1)} %bitcast.91), kind=kOutput, calls=%fused_computation.10 | convolution fusion | flops 3225944064 | bytes 12058624 | tf_op jit(solution)/shard_map/dot_general | solution.py:87
  151.2 3.3 %collective-permute-start.25 = (bf16[4,48,1024]{2,1,0:T(8,128)(2,1)S(1)}, bf16[4,48,1024]{2,1,0:T(8,128)(2,1)S(1)}, u32[]{:S(2)}, u32[]{:S(2)}) collective-permute-start(bf16[4,48,1024]{2,1,0:T(8,128)(2,1)S(1)} %slice.142), channel_id=1, source_target_pairs={{0,6},{2,0},{4,2},{6,4},{1,7},{3,1},{5,3},{7,5},{8,14},{10,8},{12,... | collective-permute-start | bytes 1179656 | tf_op jit(solution)/shard_map/ppermute | solution.py:20
  156.7 3.3 %collective-permute-start.21 = (bf16[4,48,1024]{2,1,0:T(8,128)(2,1)S(1)}, bf16[4,48,1024]{2,1,0:T(8,128)(2,1)S(1)}, u32[]{:S(2)}, u32[]{:S(2)}) collective-permute-start(bf16[4,48,1024]{2,1,0:T(8,128)(2,1)S(1)} %slice.139), channel_id=1, source_target_pairs={{0,24},{8,0},{16,8},{24,16},{1,25},{9,1},{17,9},{25,17},{2,26},{10... | collective-permute-start | bytes 1179656 | tf_op jit(solution)/shard_map/ppermute | solution.py:20
  172.6 3.4 %collective-permute-done.26 = f32[4,128,2048]{2,1,0:T(8,128)S(1)} collective-permute-done((f32[4,128,2048]{2,1,0:T(8,128)S(1)}, f32[4,128,2048]{2,1,0:T(8,128)S(1)}, u32[]{:S(2)}, u32[]{:S(2)}) %collective-permute-start.26) | collective-permute-done | bytes 4194336 | tf_op jit(solution)/shard_map/ppermute | solution.py:102
  177.1 30.9 %all_to_all.10 = bf16[4,128,2048]{2,1,0:T(8,128)(2,1)S(1)} all-to-all(bf16[4,128,2048]{2,1,0:T(8,128)(2,1)S(1)} %add_convert_fusion), channel_id=1, replica_groups=mesh['yhi'=2,'core'=2,'x'=4,'z'=4,'ylo'=2] {'yhi','ylo'}, dimensions={0} | all-to-all | bytes 4194304 | tf_op jit(solution)/shard_map/all_to_all | solution.py:104
  (108 shorter events, 68.8 us)
Async XLA Ops:
  2.7 15.1 %collective-permute-start.5 = (bf16[3,48,2048]{2,1,0:T(8,128)(2,1)S(1)}, bf16[3,48,2048]{2,1,0:T(8,128)(2,1)S(1)}, u32[]{:S(2)}, u32[]{:S(2)}) collective-permute-start(bf16[3,48,2048]{2,1,0:T(8,128)(2,1)S(1)} %get-tuple-element.31), channel_id=1, source_target_pairs={{0,1},{1,0},{2,3},{3,2},{4,5},{5,4},{6,7},{7,6},{8,9},{9,8},{10,11... | collective-permute-start | bytes 1769480 | tf_op jit(solution)/shard_map/ppermute | solution.py:34
  4.4 17.1 %collective-permute-start.2 = (bf16[3,48,2048]{2,1,0:T(8,128)(2,1)S(1)}, bf16[3,48,2048]{2,1,0:T(8,128)(2,1)S(1)}, u32[]{:S(2)}, u32[]{:S(2)}) collective-permute-start(bf16[3,48,2048]{2,1,0:T(8,128)(2,1)S(1)} %bitcast.94), channel_id=1, source_target_pairs={{0,2},{2,4},{4,6},{6,0},{1,3},{3,5},{5,7},{7,1},{8,10},{10,12},{12... | collective-permute-start | bytes 1769480 | tf_op jit(solution)/shard_map/ppermute | solution.py:14
  6.4 16.8 %collective-permute-start.1 = (bf16[3,48,2048]{2,1,0:T(8,128)(2,1)S(1)}, bf16[3,48,2048]{2,1,0:T(8,128)(2,1)S(1)}, u32[]{:S(2)}, u32[]{:S(2)}) collective-permute-start(bf16[3,48,2048]{2,1,0:T(8,128)(2,1)S(1)} %bitcast.95), channel_id=1, source_target_pairs={{0,6},{2,0},{4,2},{6,4},{1,7},{3,1},{5,3},{7,5},{8,14},{10,8},{12,... | collective-permute-start | bytes 1769480 | tf_op jit(solution)/shard_map/ppermute | solution.py:15
  17.8 15.4 %collective-permute-start.7 = (bf16[3,48,2048]{2,1,0:T(8,128)(2,1)S(1)}, bf16[3,48,2048]{2,1,0:T(8,128)(2,1)S(1)}, u32[]{:S(2)}, u32[]{:S(2)}) collective-permute-start(bf16[3,48,2048]{2,1,0:T(8,128)(2,1)S(1)} %collective-permute-done.5), channel_id=1, source_target_pairs={{0,8},{8,16},{16,24},{24,0},{1,9},{9,17},{17,25},{25,1},{2,10},{10... | collective-permute-start | bytes 1769480 | tf_op jit(solution)/shard_map/ppermute | solution.py:14
  19.4 14.3 %collective-permute-start.6 = (bf16[3,48,2048]{2,1,0:T(8,128)(2,1)S(1)}, bf16[3,48,2048]{2,1,0:T(8,128)(2,1)S(1)}, u32[]{:S(2)}, u32[]{:S(2)}) collective-permute-start(bf16[3,48,2048]{2,1,0:T(8,128)(2,1)S(1)} %collective-permute-done.5), channel_id=1, source_target_pairs={{0,24},{8,0},{16,8},{24,16},{1,25},{9,1},{17,9},{25,17},{2,26},{10... | collective-permute-start | bytes 1769480 | tf_op jit(solution)/shard_map/ppermute | solution.py:15
  21.5 15.0 %collective-permute-start.3 = (bf16[3,48,1024]{2,1,0:T(8,128)(2,1)S(1)}, bf16[3,48,1024]{2,1,0:T(8,128)(2,1)S(1)}, u32[]{:S(2)}, u32[]{:S(2)}) collective-permute-start(bf16[3,48,1024]{2,1,0:T(8,128)(2,1)S(1)} %slice.125), channel_id=1, source_target_pairs={{0,2},{2,4},{4,6},{6,0},{1,3},{3,5},{5,7},{7,1},{8,10},{10,12},{12... | collective-permute-start | bytes 884744 | tf_op jit(solution)/shard_map/ppermute | solution.py:19
  23.2 13.4 %collective-permute-start.4 = (bf16[3,48,1024]{2,1,0:T(8,128)(2,1)S(1)}, bf16[3,48,1024]{2,1,0:T(8,128)(2,1)S(1)}, u32[]{:S(2)}, u32[]{:S(2)}) collective-permute-start(bf16[3,48,1024]{2,1,0:T(8,128)(2,1)S(1)} %slice.126), channel_id=1, source_target_pairs={{0,6},{2,0},{4,2},{6,4},{1,7},{3,1},{5,3},{7,5},{8,14},{10,8},{12,... | collective-permute-start | bytes 884744 | tf_op jit(solution)/shard_map/ppermute | solution.py:20
  44.0 33.8 %collective-permute-start.10 = (bf16[4,2,48,2048]{3,2,1,0:T(8,128)(2,1)}, bf16[4,2,48,2048]{3,2,1,0:T(8,128)(2,1)}, u32[]{:S(2)}, u32[]{:S(2)}) collective-permute-start(bf16[4,2,48,2048]{3,2,1,0:T(8,128)(2,1)} %get-tuple-element.30), channel_id=1, source_target_pairs={{0,24},{8,0},{16,8},{24,16},{1,25},{9,1},{17,9},{25,17},{2,26},{10... | collective-permute-start | bytes 4718600 | tf_op jit(solution)/shard_map/ppermute | solution.py:15
  47.1 36.5 %collective-permute-start.11 = (bf16[4,2,48,2048]{3,2,1,0:T(8,128)(2,1)}, bf16[4,2,48,2048]{3,2,1,0:T(8,128)(2,1)}, u32[]{:S(2)}, u32[]{:S(2)}) collective-permute-start(bf16[4,2,48,2048]{3,2,1,0:T(8,128)(2,1)} %get-tuple-element.30), channel_id=1, source_target_pairs={{0,8},{8,16},{16,24},{24,0},{1,9},{9,17},{17,25},{25,1},{2,10},{10... | collective-permute-start | bytes 4718600 | tf_op jit(solution)/shard_map/ppermute | solution.py:14
  49.2 37.7 %collective-permute-start.14 = (bf16[4,2,48,2048]{3,2,1,0:T(8,128)(2,1)}, bf16[4,2,48,2048]{3,2,1,0:T(8,128)(2,1)}, u32[]{:S(2)}, u32[]{:S(2)}) collective-permute-start(bf16[4,2,48,2048]{3,2,1,0:T(8,128)(2,1)} %get-tuple-element.28), channel_id=1, source_target_pairs={{0,6},{2,0},{4,2},{6,4},{1,7},{3,1},{5,3},{7,5},{8,14},{10,8},{12,... | collective-permute-start | bytes 4718600 | tf_op jit(solution)/shard_map/ppermute | solution.py:15
  53.5 39.8 %collective-permute-start.15 = (bf16[4,2,48,2048]{3,2,1,0:T(8,128)(2,1)}, bf16[4,2,48,2048]{3,2,1,0:T(8,128)(2,1)}, u32[]{:S(2)}, u32[]{:S(2)}) collective-permute-start(bf16[4,2,48,2048]{3,2,1,0:T(8,128)(2,1)} %get-tuple-element.28), channel_id=1, source_target_pairs={{0,2},{2,4},{4,6},{6,0},{1,3},{3,5},{5,7},{7,1},{8,10},{10,12},{12... | collective-permute-start | bytes 4718600 | tf_op jit(solution)/shard_map/ppermute | solution.py:14
  55.2 42.2 %all-to-all-start = ((bf16[4,144,2048]{2,1,0:T(8,128)(2,1)}), bf16[4,144,2048]{2,1,0:T(8,128)(2,1)S(1)}, u32[]{:S(2)}, u32[]{:S(2)}) async-start(bf16[4,144,2048]{2,1,0:T(8,128)(2,1)} %broadcast_in_dim.23), calls=%async_computation | async-start | bytes 4718592 | tf_op jit(solution)/shard_map/all_to_all | solution.py:55
  79.9 17.8 %collective-permute-start.13 = (bf16[4,2,48,1024]{3,2,1,0:T(8,128)(2,1)}, bf16[4,2,48,1024]{3,2,1,0:T(8,128)(2,1)}, u32[]{:S(2)}, u32[]{:S(2)}) collective-permute-start(bf16[4,2,48,1024]{3,2,1,0:T(8,128)(2,1)} %slice.130), channel_id=1, source_target_pairs={{0,24},{8,0},{16,8},{24,16},{1,25},{9,1},{17,9},{25,17},{2,26},{10... | collective-permute-start | bytes 2359304 | tf_op jit(solution)/shard_map/ppermute | solution.py:20
  85.7 16.3 %collective-permute-start.12 = (bf16[4,2,48,1024]{3,2,1,0:T(8,128)(2,1)}, bf16[4,2,48,1024]{3,2,1,0:T(8,128)(2,1)}, u32[]{:S(2)}, u32[]{:S(2)}) collective-permute-start(bf16[4,2,48,1024]{3,2,1,0:T(8,128)(2,1)} %slice.129), channel_id=1, source_target_pairs={{0,8},{8,16},{16,24},{24,0},{1,9},{9,17},{17,25},{25,1},{2,10},{10... | collective-permute-start | bytes 2359304 | tf_op jit(solution)/shard_map/ppermute | solution.py:19
  89.0 17.0 %collective-permute-start.17 = (bf16[4,2,48,1024]{3,2,1,0:T(8,128)(2,1)}, bf16[4,2,48,1024]{3,2,1,0:T(8,128)(2,1)}, u32[]{:S(2)}, u32[]{:S(2)}) collective-permute-start(bf16[4,2,48,1024]{3,2,1,0:T(8,128)(2,1)} %slice.132), channel_id=1, source_target_pairs={{0,6},{2,0},{4,2},{6,4},{1,7},{3,1},{5,3},{7,5},{8,14},{10,8},{12,... | collective-permute-start | bytes 2359304 | tf_op jit(solution)/shard_map/ppermute | solution.py:20
  95.3 16.1 %collective-permute-start.16 = (bf16[4,2,48,1024]{3,2,1,0:T(8,128)(2,1)}, bf16[4,2,48,1024]{3,2,1,0:T(8,128)(2,1)}, u32[]{:S(2)}, u32[]{:S(2)}) collective-permute-start(bf16[4,2,48,1024]{3,2,1,0:T(8,128)(2,1)} %slice.131), channel_id=1, source_target_pairs={{0,2},{2,4},{4,6},{6,0},{1,3},{3,5},{5,7},{7,1},{8,10},{10,12},{12... | collective-permute-start | bytes 2359304 | tf_op jit(solution)/shard_map/ppermute | solution.py:19
  97.5 33.3 %collective-permute-start = (bf16[4,144,2048]{2,1,0:T(8,128)(2,1)S(1)}, bf16[4,144,2048]{2,1,0:T(8,128)(2,1)}, u32[]{:S(2)}, u32[]{:S(2)}) collective-permute-start(bf16[4,144,2048]{2,1,0:T(8,128)(2,1)S(1)} %all-to-all-done), channel_id=1, source_target_pairs={{0,32},{32,0},{1,33},{33,1},{2,34},{34,2},{3,35},{35,3},{4,36},{36... | collective-permute-start | bytes 7077896 | tf_op jit(solution)/shard_map/ppermute | solution.py:56
  119.1 35.5 %collective-permute-start.19 = (bf16[4,48,2048]{2,1,0:T(8,128)(2,1)S(1)}, bf16[4,48,2048]{2,1,0:T(8,128)(2,1)}, u32[]{:S(2)}, u32[]{:S(2)}) collective-permute-start(bf16[4,48,2048]{2,1,0:T(8,128)(2,1)S(1)} %slice_bitcast_fusion.1), channel_id=1, source_target_pairs={{0,8},{8,16},{16,24},{24,0},{1,9},{9,17},{17,25},{25,1},{2,10},{10... | collective-permute-start | bytes 2359304 | tf_op jit(solution)/shard_map/ppermute | solution.py:14
  119.2 36.5 %collective-permute-start.18 = (bf16[4,48,2048]{2,1,0:T(8,128)(2,1)S(1)}, bf16[4,48,2048]{2,1,0:T(8,128)(2,1)}, u32[]{:S(2)}, u32[]{:S(2)}) collective-permute-start(bf16[4,48,2048]{2,1,0:T(8,128)(2,1)S(1)} %slice_bitcast_fusion.1), channel_id=1, source_target_pairs={{0,24},{8,0},{16,8},{24,16},{1,25},{9,1},{17,9},{25,17},{2,26},{10... | collective-permute-start | bytes 2359304 | tf_op jit(solution)/shard_map/ppermute | solution.py:15
  122.4 26.6 %collective-permute-start.23 = (bf16[4,48,2048]{2,1,0:T(8,128)(2,1)S(1)}, bf16[4,48,2048]{2,1,0:T(8,128)(2,1)}, u32[]{:S(2)}, u32[]{:S(2)}) collective-permute-start(bf16[4,48,2048]{2,1,0:T(8,128)(2,1)S(1)} %copy-done.4), channel_id=1, source_target_pairs={{0,2},{2,4},{4,6},{6,0},{1,3},{3,5},{5,7},{7,1},{8,10},{10,12},{12... | collective-permute-start | bytes 2359304 | tf_op jit(solution)/shard_map/ppermute | solution.py:14
  122.4 27.7 %collective-permute-start.22 = (bf16[4,48,2048]{2,1,0:T(8,128)(2,1)S(1)}, bf16[4,48,2048]{2,1,0:T(8,128)(2,1)}, u32[]{:S(2)}, u32[]{:S(2)}) collective-permute-start(bf16[4,48,2048]{2,1,0:T(8,128)(2,1)S(1)} %copy-done.4), channel_id=1, source_target_pairs={{0,6},{2,0},{4,2},{6,4},{1,7},{3,1},{5,3},{7,5},{8,14},{10,8},{12,... | collective-permute-start | bytes 2359304 | tf_op jit(solution)/shard_map/ppermute | solution.py:15
  150.1 10.0 %collective-permute-start.24 = (bf16[4,48,1024]{2,1,0:T(8,128)(2,1)S(1)}, bf16[4,48,1024]{2,1,0:T(8,128)(2,1)S(1)}, u32[]{:S(2)}, u32[]{:S(2)}) collective-permute-start(bf16[4,48,1024]{2,1,0:T(8,128)(2,1)S(1)} %slice.141), channel_id=1, source_target_pairs={{0,2},{2,4},{4,6},{6,0},{1,3},{3,5},{5,7},{7,1},{8,10},{10,12},{12... | collective-permute-start | bytes 1179656 | tf_op jit(solution)/shard_map/ppermute | solution.py:19
  151.2 8.8 %collective-permute-start.25 = (bf16[4,48,1024]{2,1,0:T(8,128)(2,1)S(1)}, bf16[4,48,1024]{2,1,0:T(8,128)(2,1)S(1)}, u32[]{:S(2)}, u32[]{:S(2)}) collective-permute-start(bf16[4,48,1024]{2,1,0:T(8,128)(2,1)S(1)} %slice.142), channel_id=1, source_target_pairs={{0,6},{2,0},{4,2},{6,4},{1,7},{3,1},{5,3},{7,5},{8,14},{10,8},{12,... | collective-permute-start | bytes 1179656 | tf_op jit(solution)/shard_map/ppermute | solution.py:20
  155.6 9.1 %collective-permute-start.20 = (bf16[4,48,1024]{2,1,0:T(8,128)(2,1)S(1)}, bf16[4,48,1024]{2,1,0:T(8,128)(2,1)S(1)}, u32[]{:S(2)}, u32[]{:S(2)}) collective-permute-start(bf16[4,48,1024]{2,1,0:T(8,128)(2,1)S(1)} %slice.138), channel_id=1, source_target_pairs={{0,8},{8,16},{16,24},{24,0},{1,9},{9,17},{17,25},{25,1},{2,10},{10... | collective-permute-start | bytes 1179656 | tf_op jit(solution)/shard_map/ppermute | solution.py:19
  (14 other events, 131.7 us)

commit v7 on v6

--- a/solution.py
+++ b/solution.py
@@ -8,20 +8,29 @@
 SWAP = [(0, 1), (1, 0)]
 
 
-def ring_of_four(value, axis):
-    ahead = [(i, (i + 1) % 4) for i in range(4)]
-    behind = [(i, (i - 1) % 4) for i in range(4)]
-    from_minus = lax.ppermute(value, axis, perm=ahead)
-    from_plus = lax.ppermute(value, axis, perm=behind)
+AHEAD = [(i, (i + 1) % 4) for i in range(4)]
+BEHIND = [(i, (i - 1) % 4) for i in range(4)]
+
+
+def first_hop(value, axis):
+    return lax.ppermute(value, axis, perm=AHEAD), lax.ppermute(value, axis, perm=BEHIND)
+
+
+def far_hop(value, near, axis):
+    from_minus, from_plus = near
     half = value.shape[-1] // 2
     far = jnp.concatenate(
         [
-            lax.ppermute(from_minus[..., :half], axis, perm=ahead),
-            lax.ppermute(from_plus[..., half:], axis, perm=behind),
+            lax.ppermute(from_minus[..., :half], axis, perm=AHEAD),
+            lax.ppermute(from_plus[..., half:], axis, perm=BEHIND),
         ],
         axis=-1,
     )
     return jnp.stack([value, from_plus, far, from_minus])
+
+
+def ring_of_four(value, axis):
+    return far_hop(value, first_hop(value, axis), axis)
 
 
 def expert_weights(w_gate, w_up, w_down, ylo):
@@ -40,14 +49,17 @@
     gate_up_a, gate_up_b, down_a, down_b = lax.optimization_barrier(
         (gate_up_a, gate_up_b, first_a[:, 2], first_b[:, 2])
     )
-    down_a = ring_of_four(down_a, "x")
-    down_b = ring_of_four(down_b, "z")
     width = stacked.shape[-1]
-    sets = []
-    for gate_up, down in ((gate_up_a, down_a), (gate_up_b, down_b)):
-        gate_up = jnp.moveaxis(gate_up, 2, 0).reshape(2, -1, width)
-        sets.append((gate_up[0], gate_up[1], down.reshape(-1, width)))
-    return sets
+    gate_ups = [jnp.moveaxis(g, 2, 0).reshape(2, -1, width) for g in (gate_up_a, gate_up_b)]
+    return gate_ups, (down_a, first_hop(down_a, "x")), (down_b, first_hop(down_b, "z"))
+
+
+def finish_down(pending_a, pending_b):
+    width = pending_a[0].shape[-1]
+    return [
+        far_hop(*pending_a, "x").reshape(-1, width),
+        far_hop(*pending_b, "z").reshape(-1, width),
+    ]
 
 
 def spread(value, chips):
@@ -63,7 +75,7 @@
     expert = (lax.axis_index("yhi") * lax.axis_size("core") + lax.axis_index("core")) * 2 + ylo
     token_count, model_width = tokens.shape
 
-    sets = expert_weights(w_gate, w_up, w_down, ylo)
+    gate_ups, pending_a, pending_b = expert_weights(w_gate, w_up, w_down, ylo)
 
     experts = jnp.arange(lax.axis_size("core") * chips, dtype=jnp.int32)
     weight = jnp.sum(
@@ -81,10 +93,14 @@
     table = (halves[..., : extra // 2] + halves[..., extra // 2 :]).reshape(-1, extra // 2)
     scale = lax.dynamic_index_in_dim(table, expert, axis=1, keepdims=True)
 
+    gate_parts = [
+        jnp.dot(rows, g[0].T, preferred_element_type=jnp.float32) for g in gate_ups
+    ]
+    late_rows, pending_a, pending_b = lax.optimization_barrier((rows, pending_a, pending_b))
+    sets = [(g[0], g[1], d) for g, d in zip(gate_ups, finish_down(pending_a, pending_b))]
     hiddens = []
-    for weights in sets:
-        gate_part = jnp.dot(rows, weights[0].T, preferred_element_type=jnp.float32)
-        up_part = jnp.dot(rows, weights[1].T, preferred_element_type=jnp.float32)
+    for gate_part, weights in zip(gate_parts, sets):
+        up_part = jnp.dot(late_rows, weights[1].T, preferred_element_type=jnp.float32)
         hidden = (jax.nn.silu(gate_part) * up_part).astype(jnp.bfloat16)
         hiddens.append(lax.optimization_barrier(hidden))
 

time: 211 us -> 208 us (0.986)
  transfers between devices with their start and end apart: 28 -> 28, of which waited for: 11 -> 10; matrix products, arithmetic and copies ran while one was open for 28% -> 26% of each run, Pallas kernels for 0% -> 0%
where the time goes in v7:
time: 208 us; the launch traced here: 207 us
  waiting for transfers between devices  58 us (28%)
  starting transfers between devices  48.3 us (23%)
  local copies, waits for them, and re-layouts  32.1 us (15%)
  blocking collectives  30.9 us (15%)
  matrix products  21.6 us (10%)
  other arithmetic  15.6 us (8%)
    all_to_all x1, blocking collectives, per_device(): lax.all_to_all(partial, CHIPS, split_axis=0, concat_axis=0, tiled=True)  30.9 us
    ppermute x6, starting transfers between devices, far_hop(): lax.ppermute(from_plus[..., half:], axis, perm=BEHIND)  19.7 us
    ppermute x6, waiting for transfers between devices, first_hop(): lax.ppermute(value, axis, perm=BEHIND)  18.2 us
    ppermute x6, waiting for transfers between devices, far_hop(): lax.ppermute(from_minus[..., :half], axis, perm=AHEAD)  16.5 us
    ppermute x6, starting transfers between devices, first_hop(): lax.ppermute(value, axis, perm=BEHIND)  14.1 us
    another operation x12, other arithmetic, far_hop(): return jnp.stack([value, from_plus, far, from_minus])  13 us
    ppermute x1, waiting for transfers between devices, expert_weights(): got = lax.ppermute(send, 'ylo', perm=SWAP)  9.29 us
    ppermute x6, waiting for transfers between devices, first_hop(): lax.ppermute(value, axis, perm=AHEAD)  8.22 us
  transfers between devices with their start and end apart: 28, of which 10 were waited for; matrix products, arithmetic and copies ran while one was open for 26% of the time, Pallas kernels for 0%

profile of v7, /device:TPU:0, one launch (start us, length us, event | category | flops | bytes accessed | tf_op | source)
XLA Modules:
  0.0 207.0 jit_solution(10096457651956025928)
XLA Ops:
  8.5 9.3 %collective-permute-done.5 = bf16[3,48,2048]{2,1,0:T(8,128)(2,1)S(1)} collective-permute-done((bf16[3,48,2048]{2,1,0:T(8,128)(2,1)S(1)}, bf16[3,48,2048]{2,1,0:T(8,128)(2,1)S(1)}, u32[]{:S(2)}, u32[]{:S(2)}) %collective-permute-start.5) | collective-permute-done | bytes 589856 | tf_op jit(solution)/shard_map/ppermute | solution.py:43
  25.4 7.7 %collective-permute-done.7 = bf16[3,48,2048]{2,1,0:T(8,128)(2,1)S(1)} collective-permute-done((bf16[3,48,2048]{2,1,0:T(8,128)(2,1)S(1)}, bf16[3,48,2048]{2,1,0:T(8,128)(2,1)S(1)}, u32[]{:S(2)}, u32[]{:S(2)}) %collective-permute-start.7) | collective-permute-done | bytes 589856 | tf_op jit(solution)/shard_map/ppermute | solution.py:16
  33.7 2.8 %collective-permute-start.9 = (bf16[3,48,1024]{2,1,0:T(8,128)(2,1)S(1)}, bf16[3,48,1024]{2,1,0:T(8,128)(2,1)S(1)}, u32[]{:S(2)}, u32[]{:S(2)}) collective-permute-start(bf16[3,48,1024]{2,1,0:T(8,128)(2,1)S(1)} %slice.128), channel_id=1, source_target_pairs={{0,24},{8,0},{16,8},{24,16},{1,25},{9,1},{17,9},{25,17},{2,26},{10... | collective-permute-start | bytes 884744 | tf_op jit(solution)/shard_map/ppermute | solution.py:25
  36.9 4.4 %collective-permute-done.8 = bf16[3,48,1024]{2,1,0:T(8,128)(2,1)S(1)} collective-permute-done((bf16[3,48,1024]{2,1,0:T(8,128)(2,1)S(1)}, bf16[3,48,1024]{2,1,0:T(8,128)(2,1)S(1)}, u32[]{:S(2)}, u32[]{:S(2)}) %collective-permute-start.8) | collective-permute-done | bytes 294944 | tf_op jit(solution)/shard_map/ppermute | solution.py:24
  44.0 3.1 %collective-permute-start.10 = (bf16[4,2,48,2048]{3,2,1,0:T(8,128)(2,1)}, bf16[4,2,48,2048]{3,2,1,0:T(8,128)(2,1)}, u32[]{:S(2)}, u32[]{:S(2)}) collective-permute-start(bf16[4,2,48,2048]{3,2,1,0:T(8,128)(2,1)} %get-tuple-element.44), channel_id=1, source_target_pairs={{0,24},{8,0},{16,8},{24,16},{1,25},{9,1},{17,9},{25,17},{2,26},{10... | collective-permute-start | bytes 4718600 | tf_op jit(solution)/shard_map/ppermute | solution.py:16
  49.3 4.2 %collective-permute-start.14 = (bf16[4,2,48,2048]{3,2,1,0:T(8,128)(2,1)}, bf16[4,2,48,2048]{3,2,1,0:T(8,128)(2,1)}, u32[]{:S(2)}, u32[]{:S(2)}) collective-permute-start(bf16[4,2,48,2048]{3,2,1,0:T(8,128)(2,1)} %get-tuple-element.42), channel_id=1, source_target_pairs={{0,6},{2,0},{4,2},{6,4},{1,7},{3,1},{5,3},{7,5},{8,14},{10,8},{12,... | collective-permute-start | bytes 4718600 | tf_op jit(solution)/shard_map/ppermute | solution.py:16
  55.2 4.5 %all-to-all-start = ((bf16[4,144,2048]{2,1,0:T(8,128)(2,1)}), bf16[4,144,2048]{2,1,0:T(8,128)(2,1)S(1)}, u32[]{:S(2)}, u32[]{:S(2)}) async-start(bf16[4,144,2048]{2,1,0:T(8,128)(2,1)} %broadcast_in_dim.23), calls=%async_computation | async-start | bytes 4718592 | tf_op jit(solution)/shard_map/all_to_all | solution.py:67
  59.7 18.1 %collective-permute-done.10 = bf16[4,2,48,2048]{3,2,1,0:T(8,128)(2,1)} collective-permute-done((bf16[4,2,48,2048]{3,2,1,0:T(8,128)(2,1)}, bf16[4,2,48,2048]{3,2,1,0:T(8,128)(2,1)}, u32[]{:S(2)}, u32[]{:S(2)}) %collective-permute-start.10) | collective-permute-done | bytes 1572896 | tf_op jit(solution)/shard_map/ppermute | solution.py:16
  79.9 3.7 %collective-permute-start.13 = (bf16[4,2,48,1024]{3,2,1,0:T(8,128)(2,1)}, bf16[4,2,48,1024]{3,2,1,0:T(8,128)(2,1)}, u32[]{:S(2)}, u32[]{:S(2)}) collective-permute-start(bf16[4,2,48,1024]{3,2,1,0:T(8,128)(2,1)} %slice.130), channel_id=1, source_target_pairs={{0,24},{8,0},{16,8},{24,16},{1,25},{9,1},{17,9},{25,17},{2,26},{10... | collective-permute-start | bytes 2359304 | tf_op jit(solution)/shard_map/ppermute | solution.py:25
  89.0 4.3 %collective-permute-start.17 = (bf16[4,2,48,1024]{3,2,1,0:T(8,128)(2,1)}, bf16[4,2,48,1024]{3,2,1,0:T(8,128)(2,1)}, u32[]{:S(2)}, u32[]{:S(2)}) collective-permute-start(bf16[4,2,48,1024]{3,2,1,0:T(8,128)(2,1)} %slice.132), channel_id=1, source_target_pairs={{0,6},{2,0},{4,2},{6,4},{1,7},{3,1},{5,3},{7,5},{8,14},{10,8},{12,... | collective-permute-start | bytes 2359304 | tf_op jit(solution)/shard_map/ppermute | solution.py:25
  97.8 4.3 %collective-permute-done.12 = bf16[4,2,48,1024]{3,2,1,0:T(8,128)(2,1)} collective-permute-done((bf16[4,2,48,1024]{3,2,1,0:T(8,128)(2,1)}, bf16[4,2,48,1024]{3,2,1,0:T(8,128)(2,1)}, u32[]{:S(2)}, u32[]{:S(2)}) %collective-permute-start.12) | collective-permute-done | bytes 786464 | tf_op jit(solution)/shard_map/ppermute | solution.py:24
  105.9 5.5 %collective-permute-done.16 = bf16[4,2,48,1024]{3,2,1,0:T(8,128)(2,1)} collective-permute-done((bf16[4,2,48,1024]{3,2,1,0:T(8,128)(2,1)}, bf16[4,2,48,1024]{3,2,1,0:T(8,128)(2,1)}, u32[]{:S(2)}, u32[]{:S(2)}) %collective-permute-start.16) | collective-permute-done | bytes 786464 | tf_op jit(solution)/shard_map/ppermute | solution.py:24
  112.9 3.1 %pad_maximum_fusion = bf16[4,4,2,48,2048]{4,3,2,1,0:T(8,128)(2,1)S(1)} fusion(bf16[1,4,2,48,2048]{4,3,2,1,0:T(8,128)(2,1)} %bitcast.17, bf16[1,4,2,48,2048]{4,3,2,1,0:T(8,128)(2,1)S(1)} %maximum_bitcast_fusion, bf16[1,4,2,48,2048]{4,3,2,1,0:T(8,128)(2,1)} %bitcast.15, bf16[1,4,2,48,2048]{4,3,2,1,0:T(8,128)(2,1)S(1)} %copy-done.2), kind=kLoop, calls=%fused_computation | loop fusion | flops 9437184 | bytes 12582912 | tf_op jit(solution)/shard_map/stack | solution.py:29
  116.0 3.0 %pad_maximum_fusion.1 = bf16[4,4,2,48,2048]{4,3,2,1,0:T(8,128)(2,1)S(1)} fusion(bf16[1,4,2,48,2048]{4,3,2,1,0:T(8,128)(2,1)} %bitcast.21, bf16[1,4,2,48,2048]{4,3,2,1,0:T(8,128)(2,1)S(1)} %maximum_bitcast_fusion.1, bf16[1,4,2,48,2048]{4,3,2,1,0:T(8,128)(2,1)} %bitcast.19, bf16[1,4,2,48,2048]{4,3,2,1,0:T(8,128)(2,1)S(1)} %copy-done.3), kind=kLoop, calls=%fused_computation.1 | loop fusion | flops 9437184 | bytes 12582912 | tf_op jit(solution)/shard_map/stack | solution.py:29
  119.1 3.0 %collective-permute-start.19 = (bf16[4,48,2048]{2,1,0:T(8,128)(2,1)S(1)}, bf16[4,48,2048]{2,1,0:T(8,128)(2,1)}, u32[]{:S(2)}, u32[]{:S(2)}) collective-permute-start(bf16[4,48,2048]{2,1,0:T(8,128)(2,1)S(1)} %slice_bitcast_fusion.1), channel_id=1, source_target_pairs={{0,24},{8,0},{16,8},{24,16},{1,25},{9,1},{17,9},{25,17},{2,26},{10... | collective-permute-start | bytes 2359304 | tf_op jit(solution)/shard_map/ppermute | solution.py:16
  124.2 2.6 %fusion.15 = (bf16[1,4,4,48,2048]{4,3,0,2,1:T(8,128)(2,1)}, bf16[1,4,4,48,2048]{4,3,0,2,1:T(8,128)(2,1)S(1)}) fusion(bf16[2,4,4,48,2048]{4,3,0,2,1:T(8,128)(2,1)S(1)} %bitcast.79), kind=kLoop, calls=%fused_computation.55 | loop fusion | bytes 12582912 | tf_op jit(solution)/shard_map/slice | solution.py:97
  131.6 3.4 %fusion.18 = f32[1024,768]{1,0:T(8,128)S(1)} fusion(bf16[1024,2048]{1,0:T(8,128)(2,1)S(1)} %bitcast.81, bf16[768,2048]{1,0:T(8,128)(2,1)S(1)} %bitcast.93), kind=kOutput, calls=%fused_computation.58 | convolution fusion | flops 3221225472 | bytes 10485760 | tf_op jit(solution)/shard_map/dot_general | solution.py:97
  135.1 3.4 %fusion.17 = f32[1024,768]{1,0:T(8,128)S(1)} fusion(bf16[1024,2048]{1,0:T(8,128)(2,1)S(1)} %bitcast.82, bf16[768,2048]{1,0:T(8,128)(2,1)S(1)} %bitcast.92), kind=kOutput, calls=%fused_computation.57 | convolution fusion | flops 3221225472 | bytes 10485760 | tf_op jit(solution)/shard_map/dot_general | solution.py:97
  140.7 3.5 %collective-permute-start.23 = (bf16[4,48,1024]{2,1,0:T(8,128)(2,1)S(1)}, bf16[4,48,1024]{2,1,0:T(8,128)(2,1)S(1)}, u32[]{:S(2)}, u32[]{:S(2)}) collective-permute-start(bf16[4,48,1024]{2,1,0:T(8,128)(2,1)S(1)} %slice.113), channel_id=1, source_target_pairs={{0,24},{8,0},{16,8},{24,16},{1,25},{9,1},{17,9},{25,17},{2,26},{10... | collective-permute-start | bytes 1179656 | tf_op jit(solution)/shard_map/ppermute | solution.py:25
  144.3 3.7 %multiply_convert_fusion = bf16[1024,768]{1,0:T(8,128)(2,1)S(1)} fusion(f32[1024,768]{1,0:T(8,128)S(1)} %fusion.18, bf16[1024,2048]{1,0:T(8,128)(2,1)S(1)} %bitcast.83, bf16[768,2048]{1,0:T(8,128)(2,1)S(1)} %bitcast.90), kind=kOutput, calls=%fused_computation.9 | convolution fusion | flops 3225944064 | bytes 12058624 | tf_op jit(solution)/shard_map/dot_general | solution.py:103
  148.0 3.7 %multiply_convert_fusion.1 = bf16[1024,768]{1,0:T(8,128)(2,1)S(1)} fusion(f32[1024,768]{1,0:T(8,128)S(1)} %fusion.17, bf16[1024,2048]{1,0:T(8,128)(2,1)S(1)} %bitcast.84, bf16[768,2048]{1,0:T(8,128)(2,1)S(1)} %bitcast.91), kind=kOutput, calls=%fused_computation.10 | convolution fusion | flops 3225944064 | bytes 12058624 | tf_op jit(solution)/shard_map/dot_general | solution.py:103
  153.8 3.2 %collective-permute-start.25 = (bf16[4,48,1024]{2,1,0:T(8,128)(2,1)S(1)}, bf16[4,48,1024]{2,1,0:T(8,128)(2,1)S(1)}, u32[]{:S(2)}, u32[]{:S(2)}) collective-permute-start(bf16[4,48,1024]{2,1,0:T(8,128)(2,1)S(1)} %slice.116), channel_id=1, source_target_pairs={{0,6},{2,0},{4,2},{6,4},{1,7},{3,1},{5,3},{7,5},{8,14},{10,8},{12,... | collective-permute-start | bytes 1179656 | tf_op jit(solution)/shard_map/ppermute | solution.py:25
  170.3 3.5 %collective-permute-done.26 = f32[4,128,2048]{2,1,0:T(8,128)S(1)} collective-permute-done((f32[4,128,2048]{2,1,0:T(8,128)S(1)}, f32[4,128,2048]{2,1,0:T(8,128)S(1)}, u32[]{:S(2)}, u32[]{:S(2)}) %collective-permute-start.26) | collective-permute-done | bytes 4194336 | tf_op jit(solution)/shard_map/ppermute | solution.py:118
  174.8 30.9 %all_to_all.10 = bf16[4,128,2048]{2,1,0:T(8,128)(2,1)S(1)} all-to-all(bf16[4,128,2048]{2,1,0:T(8,128)(2,1)S(1)} %add_convert_fusion), channel_id=1, replica_groups=mesh['yhi'=2,'core'=2,'x'=4,'z'=4,'ylo'=2] {'yhi','ylo'}, dimensions={0} | all-to-all | bytes 4194304 | tf_op jit(solution)/shard_map/all_to_all | solution.py:120
  (106 shorter events, 67.5 us)
Async XLA Ops:
  2.7 15.1 %collective-permute-start.5 = (bf16[3,48,2048]{2,1,0:T(8,128)(2,1)S(1)}, bf16[3,48,2048]{2,1,0:T(8,128)(2,1)S(1)}, u32[]{:S(2)}, u32[]{:S(2)}) collective-permute-start(bf16[3,48,2048]{2,1,0:T(8,128)(2,1)S(1)} %get-tuple-element.45), channel_id=1, source_target_pairs={{0,1},{1,0},{2,3},{3,2},{4,5},{5,4},{6,7},{7,6},{8,9},{9,8},{10,11... | collective-permute-start | bytes 1769480 | tf_op jit(solution)/shard_map/ppermute | solution.py:43
  4.4 17.1 %collective-permute-start.2 = (bf16[3,48,2048]{2,1,0:T(8,128)(2,1)S(1)}, bf16[3,48,2048]{2,1,0:T(8,128)(2,1)S(1)}, u32[]{:S(2)}, u32[]{:S(2)}) collective-permute-start(bf16[3,48,2048]{2,1,0:T(8,128)(2,1)S(1)} %bitcast.94), channel_id=1, source_target_pairs={{0,2},{2,4},{4,6},{6,0},{1,3},{3,5},{5,7},{7,1},{8,10},{10,12},{12... | collective-permute-start | bytes 1769480 | tf_op jit(solution)/shard_map/ppermute | solution.py:16
  6.4 16.8 %collective-permute-start.1 = (bf16[3,48,2048]{2,1,0:T(8,128)(2,1)S(1)}, bf16[3,48,2048]{2,1,0:T(8,128)(2,1)S(1)}, u32[]{:S(2)}, u32[]{:S(2)}) collective-permute-start(bf16[3,48,2048]{2,1,0:T(8,128)(2,1)S(1)} %bitcast.95), channel_id=1, source_target_pairs={{0,6},{2,0},{4,2},{6,4},{1,7},{3,1},{5,3},{7,5},{8,14},{10,8},{12,... | collective-permute-start | bytes 1769480 | tf_op jit(solution)/shard_map/ppermute | solution.py:16
  17.8 15.4 %collective-permute-start.7 = (bf16[3,48,2048]{2,1,0:T(8,128)(2,1)S(1)}, bf16[3,48,2048]{2,1,0:T(8,128)(2,1)S(1)}, u32[]{:S(2)}, u32[]{:S(2)}) collective-permute-start(bf16[3,48,2048]{2,1,0:T(8,128)(2,1)S(1)} %collective-permute-done.5), channel_id=1, source_target_pairs={{0,8},{8,16},{16,24},{24,0},{1,9},{9,17},{17,25},{25,1},{2,10},{10... | collective-permute-start | bytes 1769480 | tf_op jit(solution)/shard_map/ppermute | solution.py:16
  19.4 14.3 %collective-permute-start.6 = (bf16[3,48,2048]{2,1,0:T(8,128)(2,1)S(1)}, bf16[3,48,2048]{2,1,0:T(8,128)(2,1)S(1)}, u32[]{:S(2)}, u32[]{:S(2)}) collective-permute-start(bf16[3,48,2048]{2,1,0:T(8,128)(2,1)S(1)} %collective-permute-done.5), channel_id=1, source_target_pairs={{0,24},{8,0},{16,8},{24,16},{1,25},{9,1},{17,9},{25,17},{2,26},{10... | collective-permute-start | bytes 1769480 | tf_op jit(solution)/shard_map/ppermute | solution.py:16
  21.5 15.0 %collective-permute-start.3 = (bf16[3,48,1024]{2,1,0:T(8,128)(2,1)S(1)}, bf16[3,48,1024]{2,1,0:T(8,128)(2,1)S(1)}, u32[]{:S(2)}, u32[]{:S(2)}) collective-permute-start(bf16[3,48,1024]{2,1,0:T(8,128)(2,1)S(1)} %slice.125), channel_id=1, source_target_pairs={{0,2},{2,4},{4,6},{6,0},{1,3},{3,5},{5,7},{7,1},{8,10},{10,12},{12... | collective-permute-start | bytes 884744 | tf_op jit(solution)/shard_map/ppermute | solution.py:24
  23.2 13.4 %collective-permute-start.4 = (bf16[3,48,1024]{2,1,0:T(8,128)(2,1)S(1)}, bf16[3,48,1024]{2,1,0:T(8,128)(2,1)S(1)}, u32[]{:S(2)}, u32[]{:S(2)}) collective-permute-start(bf16[3,48,1024]{2,1,0:T(8,128)(2,1)S(1)} %slice.126), channel_id=1, source_target_pairs={{0,6},{2,0},{4,2},{6,4},{1,7},{3,1},{5,3},{7,5},{8,14},{10,8},{12,... | collective-permute-start | bytes 884744 | tf_op jit(solution)/shard_map/ppermute | solution.py:25
  44.0 33.8 %collective-permute-start.10 = (bf16[4,2,48,2048]{3,2,1,0:T(8,128)(2,1)}, bf16[4,2,48,2048]{3,2,1,0:T(8,128)(2,1)}, u32[]{:S(2)}, u32[]{:S(2)}) collective-permute-start(bf16[4,2,48,2048]{3,2,1,0:T(8,128)(2,1)} %get-tuple-element.44), channel_id=1, source_target_pairs={{0,24},{8,0},{16,8},{24,16},{1,25},{9,1},{17,9},{25,17},{2,26},{10... | collective-permute-start | bytes 4718600 | tf_op jit(solution)/shard_map/ppermute | solution.py:16
  47.1 36.5 %collective-permute-start.11 = (bf16[4,2,48,2048]{3,2,1,0:T(8,128)(2,1)}, bf16[4,2,48,2048]{3,2,1,0:T(8,128)(2,1)}, u32[]{:S(2)}, u32[]{:S(2)}) collective-permute-start(bf16[4,2,48,2048]{3,2,1,0:T(8,128)(2,1)} %get-tuple-element.44), channel_id=1, source_target_pairs={{0,8},{8,16},{16,24},{24,0},{1,9},{9,17},{17,25},{25,1},{2,10},{10... | collective-permute-start | bytes 4718600 | tf_op jit(solution)/shard_map/ppermute | solution.py:16
  49.3 37.6 %collective-permute-start.14 = (bf16[4,2,48,2048]{3,2,1,0:T(8,128)(2,1)}, bf16[4,2,48,2048]{3,2,1,0:T(8,128)(2,1)}, u32[]{:S(2)}, u32[]{:S(2)}) collective-permute-start(bf16[4,2,48,2048]{3,2,1,0:T(8,128)(2,1)} %get-tuple-element.42), channel_id=1, source_target_pairs={{0,6},{2,0},{4,2},{6,4},{1,7},{3,1},{5,3},{7,5},{8,14},{10,8},{12,... | collective-permute-start | bytes 4718600 | tf_op jit(solution)/shard_map/ppermute | solution.py:16
  53.5 39.8 %collective-permute-start.15 = (bf16[4,2,48,2048]{3,2,1,0:T(8,128)(2,1)}, bf16[4,2,48,2048]{3,2,1,0:T(8,128)(2,1)}, u32[]{:S(2)}, u32[]{:S(2)}) collective-permute-start(bf16[4,2,48,2048]{3,2,1,0:T(8,128)(2,1)} %get-tuple-element.42), channel_id=1, source_target_pairs={{0,2},{2,4},{4,6},{6,0},{1,3},{3,5},{5,7},{7,1},{8,10},{10,12},{12... | collective-permute-start | bytes 4718600 | tf_op jit(solution)/shard_map/ppermute | solution.py:16
  55.2 42.2 %all-to-all-start = ((bf16[4,144,2048]{2,1,0:T(8,128)(2,1)}), bf16[4,144,2048]{2,1,0:T(8,128)(2,1)S(1)}, u32[]{:S(2)}, u32[]{:S(2)}) async-start(bf16[4,144,2048]{2,1,0:T(8,128)(2,1)} %broadcast_in_dim.23), calls=%async_computation | async-start | bytes 4718592 | tf_op jit(solution)/shard_map/all_to_all | solution.py:67
  79.9 17.8 %collective-permute-start.13 = (bf16[4,2,48,1024]{3,2,1,0:T(8,128)(2,1)}, bf16[4,2,48,1024]{3,2,1,0:T(8,128)(2,1)}, u32[]{:S(2)}, u32[]{:S(2)}) collective-permute-start(bf16[4,2,48,1024]{3,2,1,0:T(8,128)(2,1)} %slice.130), channel_id=1, source_target_pairs={{0,24},{8,0},{16,8},{24,16},{1,25},{9,1},{17,9},{25,17},{2,26},{10... | collective-permute-start | bytes 2359304 | tf_op jit(solution)/shard_map/ppermute | solution.py:25
  85.7 16.3 %collective-permute-start.12 = (bf16[4,2,48,1024]{3,2,1,0:T(8,128)(2,1)}, bf16[4,2,48,1024]{3,2,1,0:T(8,128)(2,1)}, u32[]{:S(2)}, u32[]{:S(2)}) collective-permute-start(bf16[4,2,48,1024]{3,2,1,0:T(8,128)(2,1)} %slice.129), channel_id=1, source_target_pairs={{0,8},{8,16},{16,24},{24,0},{1,9},{9,17},{17,25},{25,1},{2,10},{10... | collective-permute-start | bytes 2359304 | tf_op jit(solution)/shard_map/ppermute | solution.py:24
  89.0 17.0 %collective-permute-start.17 = (bf16[4,2,48,1024]{3,2,1,0:T(8,128)(2,1)}, bf16[4,2,48,1024]{3,2,1,0:T(8,128)(2,1)}, u32[]{:S(2)}, u32[]{:S(2)}) collective-permute-start(bf16[4,2,48,1024]{3,2,1,0:T(8,128)(2,1)} %slice.132), channel_id=1, source_target_pairs={{0,6},{2,0},{4,2},{6,4},{1,7},{3,1},{5,3},{7,5},{8,14},{10,8},{12,... | collective-permute-start | bytes 2359304 | tf_op jit(solution)/shard_map/ppermute | solution.py:25
  95.3 16.1 %collective-permute-start.16 = (bf16[4,2,48,1024]{3,2,1,0:T(8,128)(2,1)}, bf16[4,2,48,1024]{3,2,1,0:T(8,128)(2,1)}, u32[]{:S(2)}, u32[]{:S(2)}) collective-permute-start(bf16[4,2,48,1024]{3,2,1,0:T(8,128)(2,1)} %slice.131), channel_id=1, source_target_pairs={{0,2},{2,4},{4,6},{6,0},{1,3},{3,5},{5,7},{7,1},{8,10},{10,12},{12... | collective-permute-start | bytes 2359304 | tf_op jit(solution)/shard_map/ppermute | solution.py:24
  97.5 30.4 %collective-permute-start = (bf16[4,144,2048]{2,1,0:T(8,128)(2,1)S(1)}, bf16[4,144,2048]{2,1,0:T(8,128)(2,1)}, u32[]{:S(2)}, u32[]{:S(2)}) collective-permute-start(bf16[4,144,2048]{2,1,0:T(8,128)(2,1)S(1)} %all-to-all-done), channel_id=1, source_target_pairs={{0,32},{32,0},{1,33},{33,1},{2,34},{34,2},{3,35},{35,3},{4,36},{36... | collective-permute-start | bytes 7077896 | tf_op jit(solution)/shard_map/ppermute | solution.py:68
  119.1 19.5 %collective-permute-start.19 = (bf16[4,48,2048]{2,1,0:T(8,128)(2,1)S(1)}, bf16[4,48,2048]{2,1,0:T(8,128)(2,1)}, u32[]{:S(2)}, u32[]{:S(2)}) collective-permute-start(bf16[4,48,2048]{2,1,0:T(8,128)(2,1)S(1)} %slice_bitcast_fusion.1), channel_id=1, source_target_pairs={{0,24},{8,0},{16,8},{24,16},{1,25},{9,1},{17,9},{25,17},{2,26},{10... | collective-permute-start | bytes 2359304 | tf_op jit(solution)/shard_map/ppermute | solution.py:16
  122.1 16.4 %collective-permute-start.18 = (bf16[4,48,2048]{2,1,0:T(8,128)(2,1)S(1)}, bf16[4,48,2048]{2,1,0:T(8,128)(2,1)}, u32[]{:S(2)}, u32[]{:S(2)}) collective-permute-start(bf16[4,48,2048]{2,1,0:T(8,128)(2,1)S(1)} %slice_bitcast_fusion.1), channel_id=1, source_target_pairs={{0,8},{8,16},{16,24},{24,0},{1,9},{9,17},{17,25},{25,1},{2,10},{10... | collective-permute-start | bytes 2359304 | tf_op jit(solution)/shard_map/ppermute | solution.py:16
  122.1 16.5 %collective-permute-start.21 = (bf16[4,48,2048]{2,1,0:T(8,128)(2,1)S(1)}, bf16[4,48,2048]{2,1,0:T(8,128)(2,1)}, u32[]{:S(2)}, u32[]{:S(2)}) collective-permute-start(bf16[4,48,2048]{2,1,0:T(8,128)(2,1)S(1)} %copy-done.4), channel_id=1, source_target_pairs={{0,6},{2,0},{4,2},{6,4},{1,7},{3,1},{5,3},{7,5},{8,14},{10,8},{12,... | collective-permute-start | bytes 2359304 | tf_op jit(solution)/shard_map/ppermute | solution.py:16
  122.1 16.5 %collective-permute-start.20 = (bf16[4,48,2048]{2,1,0:T(8,128)(2,1)S(1)}, bf16[4,48,2048]{2,1,0:T(8,128)(2,1)}, u32[]{:S(2)}, u32[]{:S(2)}) collective-permute-start(bf16[4,48,2048]{2,1,0:T(8,128)(2,1)S(1)} %copy-done.4), channel_id=1, source_target_pairs={{0,2},{2,4},{4,6},{6,0},{1,3},{3,5},{5,7},{7,1},{8,10},{10,12},{12... | collective-permute-start | bytes 2359304 | tf_op jit(solution)/shard_map/ppermute | solution.py:16
  140.7 16.4 %collective-permute-start.22 = (bf16[4,48,1024]{2,1,0:T(8,128)(2,1)S(1)}, bf16[4,48,1024]{2,1,0:T(8,128)(2,1)S(1)}, u32[]{:S(2)}, u32[]{:S(2)}) collective-permute-start(bf16[4,48,1024]{2,1,0:T(8,128)(2,1)S(1)} %slice.112), channel_id=1, source_target_pairs={{0,8},{8,16},{16,24},{24,0},{1,9},{9,17},{17,25},{25,1},{2,10},{10... | collective-permute-start | bytes 1179656 | tf_op jit(solution)/shard_map/ppermute | solution.py:24
  140.7 16.3 %collective-permute-start.23 = (bf16[4,48,1024]{2,1,0:T(8,128)(2,1)S(1)}, bf16[4,48,1024]{2,1,0:T(8,128)(2,1)S(1)}, u32[]{:S(2)}, u32[]{:S(2)}) collective-permute-start(bf16[4,48,1024]{2,1,0:T(8,128)(2,1)S(1)} %slice.113), channel_id=1, source_target_pairs={{0,24},{8,0},{16,8},{24,16},{1,25},{9,1},{17,9},{25,17},{2,26},{10... | collective-permute-start | bytes 1179656 | tf_op jit(solution)/shard_map/ppermute | solution.py:25
  153.7 9.1 %collective-permute-start.24 = (bf16[4,48,1024]{2,1,0:T(8,128)(2,1)S(1)}, bf16[4,48,1024]{2,1,0:T(8,128)(2,1)S(1)}, u32[]{:S(2)}, u32[]{:S(2)}) collective-permute-start(bf16[4,48,1024]{2,1,0:T(8,128)(2,1)S(1)} %slice.115), channel_id=1, source_target_pairs={{0,2},{2,4},{4,6},{6,0},{1,3},{3,5},{5,7},{7,1},{8,10},{10,12},{12... | collective-permute-start | bytes 1179656 | tf_op jit(solution)/shard_map/ppermute | solution.py:24
  (13 other events, 128.6 us)

commit v8 on v7

--- a/solution.py
+++ b/solution.py
@@ -16,7 +16,7 @@
     return lax.ppermute(value, axis, perm=AHEAD), lax.ppermute(value, axis, perm=BEHIND)
 
 
-def far_hop(value, near, axis):
+def far_pieces(value, near, axis):
     from_minus, from_plus = near
     half = value.shape[-1] // 2
     far = jnp.concatenate(
@@ -26,14 +26,18 @@
         ],
         axis=-1,
     )
-    return jnp.stack([value, from_plus, far, from_minus])
+    return (value, from_plus, far, from_minus)
+
+
+def far_hop(value, near, axis):
+    return jnp.stack(far_pieces(value, near, axis))
 
 
 def ring_of_four(value, axis):
     return far_hop(value, first_hop(value, axis), axis)
 
 
-def expert_weights(w_gate, w_up, w_down, ylo):
+def expert_weights(w_gate, w_up, w_down, ylo, early):
     stacked = jnp.stack([w_gate, w_up, w_down], axis=1)
     rows = stacked.shape[2]
     padded = -(-rows // 16) * 16
@@ -43,15 +47,17 @@
     got = lax.ppermute(send, "ylo", perm=SWAP)
     first_a = ring_of_four(keep, "z")
     first_b = ring_of_four(got, "x")
-    first_a, first_b = lax.optimization_barrier((first_a, first_b))
-    gate_up_a = ring_of_four(first_a[:, :2], "x")
-    gate_up_b = ring_of_four(first_b[:, :2], "z")
+    first_a, first_b, early = lax.optimization_barrier((first_a, first_b, early))
+    lead_a, lead_b = first_a[:, :2], first_b[:, :2]
+    gate_up_a = far_pieces(lead_a, first_hop(lead_a, "x"), "x")
+    gate_up_b = far_pieces(lead_b, first_hop(lead_b, "z"), "z")
     gate_up_a, gate_up_b, down_a, down_b = lax.optimization_barrier(
         (gate_up_a, gate_up_b, first_a[:, 2], first_b[:, 2])
     )
+    gate_up_a, gate_up_b = jnp.stack(gate_up_a), jnp.stack(gate_up_b)
     width = stacked.shape[-1]
     gate_ups = [jnp.moveaxis(g, 2, 0).reshape(2, -1, width) for g in (gate_up_a, gate_up_b)]
-    return gate_ups, (down_a, first_hop(down_a, "x")), (down_b, first_hop(down_b, "z"))
+    return gate_ups, (down_a, first_hop(down_a, "x")), (down_b, first_hop(down_b, "z")), early
 
 
 def finish_down(pending_a, pending_b):
@@ -62,11 +68,9 @@
     ]
 
 
-def spread(value, chips):
+def spread_chips(value, chips):
     sent = jnp.broadcast_to(value[None], (chips,) + value.shape)
-    mine = lax.all_to_all(sent, CHIPS, split_axis=0, concat_axis=0, tiled=True)
-    other = lax.ppermute(mine, "core", perm=SWAP)
-    return mine, other
+    return lax.all_to_all(sent, CHIPS, split_axis=0, concat_axis=0, tiled=True)
 
 
 def per_device(tokens, expert_ids, gate_weights, w_gate, w_up, w_down):
@@ -75,7 +79,6 @@
     expert = (lax.axis_index("yhi") * lax.axis_size("core") + lax.axis_index("core")) * 2 + ylo
     token_count, model_width = tokens.shape
 
-    gate_ups, pending_a, pending_b = expert_weights(w_gate, w_up, w_down, ylo)
 
     experts = jnp.arange(lax.axis_size("core") * chips, dtype=jnp.int32)
     weight = jnp.sum(
@@ -86,7 +89,9 @@
     packed = jnp.concatenate([high, low], axis=1).astype(jnp.bfloat16).T
     extra = packed.shape[0]
     packed = jnp.pad(packed, ((0, 0), (0, model_width - token_count)))
-    mine, other = spread(jnp.concatenate([tokens, packed]), chips)
+    mine = spread_chips(jnp.concatenate([tokens, packed]), chips)
+    gate_ups, pending_a, pending_b, mine = expert_weights(w_gate, w_up, w_down, ylo, mine)
+    other = lax.ppermute(mine, "core", perm=SWAP)
     both = jnp.concatenate([mine, other])
     rows = both[:, :token_count].reshape(-1, model_width)
     halves = jnp.swapaxes(both[:, token_count:, :token_count], 1, 2).astype(jnp.float32)

time: 208 us -> 210 us (level)
  waiting for transfers between devices: 58 us -> 73.8 us
  local copies, waits for them, and re-layouts: 32.1 us -> 23.4 us
  starting transfers between devices: 48.3 us -> 45.3 us
    ppermute x6, waiting for transfers between devices: 8.22 us -> 35.8 us  [first_hop(): lax.ppermute(value, axis, perm=AHEAD)]
    ppermute x6, waiting for transfers between devices: 18.2 us -> 0.02 us  [first_hop(): lax.ppermute(value, axis, perm=BEHIND)]
    another operation x13 -> x9, other arithmetic: 13.1 us -> 5.39 us  [the longest x8 5.39 us: far_hop(): return jnp.stack(far_pieces(value, near, axis))]
    transpose x0 -> x2, other arithmetic: none -> 6.67 us  [expert_weights(): jnp.moveaxis(g, 2, 0).reshape(2, -1, width)]
    another operation x2 -> x0, local copies, waits for them, and re-layouts: 4.38 us -> none  [far_hop(): return jnp.stack([value, from_plus, far, from_minus])]
    all_to_all x1, waiting for transfers between devices: 0.01 us -> 4.26 us  [spread_chips(): return lax.all_to_all(sent, CHIPS, split_axis=0, concat_axis=0, tiled=True)]
    ppermute x13, waiting for transfers between devices: 18.9 us -> 21.9 us  [the longest x6 20.1 us: far_pieces(): lax.ppermute(from_minus[..., :half], axis, perm=AHEAD)]
    ppermute x6, starting transfers between devices: 14.1 us -> 12 us  [first_hop(): lax.ppermute(value, axis, perm=BEHIND)]
  transfers between devices with their start and end apart: 28 -> 28, of which waited for: 10 -> 11; matrix products, arithmetic and copies ran while one was open for 26% -> 20% of each run, Pallas kernels for 0% -> 0%
where the time goes in v8:
time: 210 us; the launch traced here: 209 us
  waiting for transfers between devices  73.8 us (35%)
  starting transfers between devices  45.3 us (22%)
  blocking collectives  29.4 us (14%)
  local copies, waits for them, and re-layouts  23.4 us (11%)
  matrix products  21.6 us (10%)
  other arithmetic  14.8 us (7%)
    ppermute x6, waiting for transfers between devices, first_hop(): lax.ppermute(value, axis, perm=AHEAD)  35.8 us
    all_to_all x1, blocking collectives, per_device(): lax.all_to_all(partial, CHIPS, split_axis=0, concat_axis=0, tiled=True)  29.4 us
    ppermute x6, waiting for transfers between devices, far_pieces(): lax.ppermute(from_minus[..., :half], axis, perm=AHEAD)  20.1 us
    ppermute x6, starting transfers between devices, far_pieces(): lax.ppermute(from_plus[..., half:], axis, perm=BEHIND)  16.3 us
    ppermute x6, starting transfers between devices, first_hop(): lax.ppermute(value, axis, perm=BEHIND)  12 us
    ppermute x1, waiting for transfers between devices, expert_weights(): got = lax.ppermute(send, 'ylo', perm=SWAP)  8.32 us
    dot_general x2, matrix products, per_device(): jnp.dot(late_rows, weights[1].T, preferred_element_type=jnp.float32)  7.43 us
    dot_general x4, matrix products, down(): jnp.dot(hidden[first:last], weights[2], preferred_element_type=jnp.float32)  7.29 us
  transfers between devices with their start and end apart: 28, of which 11 were waited for; matrix products, arithmetic and copies ran while one was open for 20% of the time, Pallas kernels for 0%

profile of v8, /device:TPU:0, one launch (start us, length us, event | category | flops | bytes accessed | tf_op | source)
XLA Modules:
  0.0 208.8 jit_solution(13664865294654976954)
XLA Ops:
  10.5 4.5 %all-to-all-start = ((bf16[4,144,2048]{2,1,0:T(8,128)(2,1)}), bf16[4,144,2048]{2,1,0:T(8,128)(2,1)}, u32[]{:S(2)}, u32[]{:S(2)}) async-start(bf16[4,144,2048]{2,1,0:T(8,128)(2,1)} %broadcast_in_dim.23), calls=%async_computation | async-start | bytes 4718592 | tf_op jit(solution)/shard_map/all_to_all | solution.py:73
  15.0 8.3 %collective-permute-done.4 = bf16[3,48,2048]{2,1,0:T(8,128)(2,1)S(1)} collective-permute-done((bf16[3,48,2048]{2,1,0:T(8,128)(2,1)S(1)}, bf16[3,48,2048]{2,1,0:T(8,128)(2,1)S(1)}, u32[]{:S(2)}, u32[]{:S(2)}) %collective-permute-start.4) | collective-permute-done | bytes 589856 | tf_op jit(solution)/shard_map/ppermute | solution.py:47
  26.7 3.3 %collective-permute-start.3 = (bf16[3,48,1024]{2,1,0:T(8,128)(2,1)S(1)}, bf16[3,48,1024]{2,1,0:T(8,128)(2,1)S(1)}, u32[]{:S(2)}, u32[]{:S(2)}) collective-permute-start(bf16[3,48,1024]{2,1,0:T(8,128)(2,1)S(1)} %slice.125), channel_id=1, source_target_pairs={{0,6},{2,0},{4,2},{6,4},{1,7},{3,1},{5,3},{7,5},{8,14},{10,8},{12,... | collective-permute-start | bytes 884744 | tf_op jit(solution)/shard_map/ppermute | solution.py:25
  30.0 7.1 %collective-permute-done.6 = bf16[3,48,2048]{2,1,0:T(8,128)(2,1)S(1)} collective-permute-done((bf16[3,48,2048]{2,1,0:T(8,128)(2,1)S(1)}, bf16[3,48,2048]{2,1,0:T(8,128)(2,1)S(1)}, u32[]{:S(2)}, u32[]{:S(2)}) %collective-permute-start.6) | collective-permute-done | bytes 589856 | tf_op jit(solution)/shard_map/ppermute | solution.py:16
  38.2 2.3 %collective-permute-start.8 = (bf16[3,48,1024]{2,1,0:T(8,128)(2,1)S(1)}, bf16[3,48,1024]{2,1,0:T(8,128)(2,1)S(1)}, u32[]{:S(2)}, u32[]{:S(2)}) collective-permute-start(bf16[3,48,1024]{2,1,0:T(8,128)(2,1)S(1)} %slice.127), channel_id=1, source_target_pairs={{0,24},{8,0},{16,8},{24,16},{1,25},{9,1},{17,9},{25,17},{2,26},{10... | collective-permute-start | bytes 884744 | tf_op jit(solution)/shard_map/ppermute | solution.py:25
  42.2 2.8 %collective-permute-done.7 = bf16[3,48,1024]{2,1,0:T(8,128)(2,1)S(1)} collective-permute-done((bf16[3,48,1024]{2,1,0:T(8,128)(2,1)S(1)}, bf16[3,48,1024]{2,1,0:T(8,128)(2,1)S(1)}, u32[]{:S(2)}, u32[]{:S(2)}) %collective-permute-start.7) | collective-permute-done | bytes 294944 | tf_op jit(solution)/shard_map/ppermute | solution.py:24
  45.4 4.3 %all-to-all-done = bf16[4,144,2048]{2,1,0:T(8,128)(2,1)} async-done(((bf16[4,144,2048]{2,1,0:T(8,128)(2,1)}), bf16[4,144,2048]{2,1,0:T(8,128)(2,1)}, u32[]{:S(2)}, u32[]{:S(2)}) %all-to-all-start) | async-done | bytes 2359328 | tf_op jit(solution)/shard_map/all_to_all | solution.py:73
  51.0 3.2 %collective-permute-start.14 = (bf16[4,2,48,2048]{3,2,1,0:T(8,128)(2,1)}, bf16[4,2,48,2048]{3,2,1,0:T(8,128)(2,1)}, u32[]{:S(2)}, u32[]{:S(2)}) collective-permute-start(bf16[4,2,48,2048]{3,2,1,0:T(8,128)(2,1)} %slice.102), channel_id=1, source_target_pairs={{0,6},{2,0},{4,2},{6,4},{1,7},{3,1},{5,3},{7,5},{8,14},{10,8},{12,... | collective-permute-start | bytes 4718600 | tf_op jit(solution)/shard_map/ppermute | solution.py:16
  58.7 28.7 %collective-permute-done.15 = bf16[4,2,48,2048]{3,2,1,0:T(8,128)(2,1)} collective-permute-done((bf16[4,2,48,2048]{3,2,1,0:T(8,128)(2,1)}, bf16[4,2,48,2048]{3,2,1,0:T(8,128)(2,1)}, u32[]{:S(2)}, u32[]{:S(2)}) %collective-permute-start.15) | collective-permute-done | bytes 1572896 | tf_op jit(solution)/shard_map/ppermute | solution.py:16
  90.0 3.3 %collective-permute-start.17 = (bf16[4,2,48,1024]{3,2,1,0:T(8,128)(2,1)S(1)}, bf16[4,2,48,1024]{3,2,1,0:T(8,128)(2,1)S(1)}, u32[]{:S(2)}, u32[]{:S(2)}) collective-permute-start(bf16[4,2,48,1024]{3,2,1,0:T(8,128)(2,1)S(1)} %slice.132), channel_id=1, source_target_pairs={{0,6},{2,0},{4,2},{6,4},{1,7},{3,1},{5,3},{7,5},{8,14},{10,8},{12,... | collective-permute-start | bytes 2359304 | tf_op jit(solution)/shard_map/ppermute | solution.py:25
  102.3 4.9 %collective-permute-done.16 = bf16[4,2,48,1024]{3,2,1,0:T(8,128)(2,1)S(1)} collective-permute-done((bf16[4,2,48,1024]{3,2,1,0:T(8,128)(2,1)S(1)}, bf16[4,2,48,1024]{3,2,1,0:T(8,128)(2,1)S(1)}, u32[]{:S(2)}, u32[]{:S(2)}) %collective-permute-start.16) | collective-permute-done | bytes 786464 | tf_op jit(solution)/shard_map/ppermute | solution.py:24
  107.8 9.2 %collective-permute-done.12 = bf16[4,2,48,1024]{3,2,1,0:T(8,128)(2,1)S(1)} collective-permute-done((bf16[4,2,48,1024]{3,2,1,0:T(8,128)(2,1)S(1)}, bf16[4,2,48,1024]{3,2,1,0:T(8,128)(2,1)S(1)}, u32[]{:S(2)}, u32[]{:S(2)}) %collective-permute-start.12) | collective-permute-done | bytes 786464 | tf_op jit(solution)/shard_map/ppermute | solution.py:24
  118.4 3.0 %collective-permute-start.19 = (bf16[4,48,2048]{2,1,0:T(8,128)(2,1)S(1)}, bf16[4,48,2048]{2,1,0:T(8,128)(2,1)}, u32[]{:S(2)}, u32[]{:S(2)}) collective-permute-start(bf16[4,48,2048]{2,1,0:T(8,128)(2,1)S(1)} %slice_bitcast_fusion.1), channel_id=1, source_target_pairs={{0,24},{8,0},{16,8},{24,16},{1,25},{9,1},{17,9},{25,17},{2,26},{10... | collective-permute-start | bytes 2359304 | tf_op jit(solution)/shard_map/ppermute | solution.py:16
  123.5 3.3 %maximum_bitcast_fusion = bf16[2,4,4,48,2048]{4,3,0,2,1:T(8,128)(2,1)S(1)} fusion(bf16[1,4,2,48,2048]{4,3,2,1,0:T(8,128)(2,1)} %bitcast.19, bf16[1,4,2,48,2048]{4,3,2,1,0:T(8,128)(2,1)S(1)} %bitcast.78, bf16[1,4,2,48,2048]{4,3,2,1,0:T(8,128)(2,1)} %bitcast.17, bf16[1,4,2,48,2048]{4,3,2,1,0:T(8,128)(2,1)} %bitcast.16), kind=kLoop, calls=%fused_computation | loop fusion | flops 9437184 | bytes 12582912 | tf_op jit(solution)/shard_map/transpose | solution.py:59
  126.8 3.3 %maximum_bitcast_fusion.1 = bf16[2,4,4,48,2048]{4,3,0,2,1:T(8,128)(2,1)S(1)} fusion(bf16[1,4,2,48,2048]{4,3,2,1,0:T(8,128)(2,1)} %bitcast.26, bf16[1,4,2,48,2048]{4,3,2,1,0:T(8,128)(2,1)S(1)} %bitcast.77, bf16[1,4,2,48,2048]{4,3,2,1,0:T(8,128)(2,1)} %bitcast.24, bf16[1,4,2,48,2048]{4,3,2,1,0:T(8,128)(2,1)} %bitcast.23), kind=kLoop, calls=%fused_computation.1 | loop fusion | flops 9437184 | bytes 12582912 | tf_op jit(solution)/shard_map/transpose | solution.py:59
  134.6 3.4 %fusion.17 = f32[1024,768]{1,0:T(8,128)S(1)} fusion(bf16[1024,2048]{1,0:T(8,128)(2,1)S(1)} %bitcast.79, bf16[768,2048]{1,0:T(8,128)(2,1)S(1)} %bitcast.91), kind=kOutput, calls=%fused_computation.55 | convolution fusion | flops 3221225472 | bytes 10485760 | tf_op jit(solution)/shard_map/dot_general | solution.py:102
  138.1 3.4 %fusion.18 = f32[1024,768]{1,0:T(8,128)S(1)} fusion(bf16[1024,2048]{1,0:T(8,128)(2,1)S(1)} %bitcast.80, bf16[768,2048]{1,0:T(8,128)(2,1)S(1)} %bitcast.90), kind=kOutput, calls=%fused_computation.56 | convolution fusion | flops 3221225472 | bytes 10485760 | tf_op jit(solution)/shard_map/dot_general | solution.py:102
  141.6 3.7 %multiply_convert_fusion.1 = bf16[1024,768]{1,0:T(8,128)(2,1)S(1)} fusion(f32[1024,768]{1,0:T(8,128)S(1)} %fusion.17, bf16[1024,2048]{1,0:T(8,128)(2,1)S(1)} %bitcast.81, bf16[768,2048]{1,0:T(8,128)(2,1)S(1)} %bitcast.89), kind=kOutput, calls=%fused_computation.10 | convolution fusion | flops 3225944064 | bytes 12058624 | tf_op jit(solution)/shard_map/dot_general | solution.py:108
  149.7 3.0 %collective-permute-start.25 = (bf16[4,48,1024]{2,1,0:T(8,128)(2,1)S(1)}, bf16[4,48,1024]{2,1,0:T(8,128)(2,1)S(1)}, u32[]{:S(2)}, u32[]{:S(2)}) collective-permute-start(bf16[4,48,1024]{2,1,0:T(8,128)(2,1)S(1)} %slice.116), channel_id=1, source_target_pairs={{0,6},{2,0},{4,2},{6,4},{1,7},{3,1},{5,3},{7,5},{8,14},{10,8},{12,... | collective-permute-start | bytes 1179656 | tf_op jit(solution)/shard_map/ppermute | solution.py:25
  153.3 2.7 %collective-permute-start.23 = (bf16[4,48,1024]{2,1,0:T(8,128)(2,1)S(1)}, bf16[4,48,1024]{2,1,0:T(8,128)(2,1)S(1)}, u32[]{:S(2)}, u32[]{:S(2)}) collective-permute-start(bf16[4,48,1024]{2,1,0:T(8,128)(2,1)S(1)} %slice.113), channel_id=1, source_target_pairs={{0,24},{8,0},{16,8},{24,16},{1,25},{9,1},{17,9},{25,17},{2,26},{10... | collective-permute-start | bytes 1179656 | tf_op jit(solution)/shard_map/ppermute | solution.py:25
  156.0 3.7 %multiply_convert_fusion = bf16[1024,768]{1,0:T(8,128)(2,1)S(1)} fusion(f32[1024,768]{1,0:T(8,128)S(1)} %fusion.18, bf16[1024,2048]{1,0:T(8,128)(2,1)S(1)} %bitcast.82, bf16[768,2048]{1,0:T(8,128)(2,1)S(1)} %bitcast.88), kind=kOutput, calls=%fused_computation.9 | convolution fusion | flops 3225944064 | bytes 12058624 | tf_op jit(solution)/shard_map/dot_general | solution.py:108
  159.7 3.2 %collective-permute-done.22 = bf16[4,48,1024]{2,1,0:T(8,128)(2,1)S(1)} collective-permute-done((bf16[4,48,1024]{2,1,0:T(8,128)(2,1)S(1)}, bf16[4,48,1024]{2,1,0:T(8,128)(2,1)S(1)}, u32[]{:S(2)}, u32[]{:S(2)}) %collective-permute-start.22) | collective-permute-done | bytes 393248 | tf_op jit(solution)/shard_map/ppermute | solution.py:24
  173.7 3.5 %collective-permute-done.26 = f32[4,128,2048]{2,1,0:T(8,128)S(1)} collective-permute-done((f32[4,128,2048]{2,1,0:T(8,128)S(1)}, f32[4,128,2048]{2,1,0:T(8,128)S(1)}, u32[]{:S(2)}, u32[]{:S(2)}) %collective-permute-start.26) | collective-permute-done | bytes 4194336 | tf_op jit(solution)/shard_map/ppermute | solution.py:123
  178.2 29.4 %all_to_all.10 = bf16[4,128,2048]{2,1,0:T(8,128)(2,1)S(1)} all-to-all(bf16[4,128,2048]{2,1,0:T(8,128)(2,1)S(1)} %add_convert_fusion), channel_id=1, replica_groups=mesh['yhi'=2,'core'=2,'x'=4,'z'=4,'ylo'=2] {'yhi','ylo'}, dimensions={0} | all-to-all | bytes 4194304 | tf_op jit(solution)/shard_map/all_to_all | solution.py:125
  (96 shorter events, 60.8 us)
Async XLA Ops:
  2.8 23.8 %collective-permute-start.1 = (bf16[3,48,2048]{2,1,0:T(8,128)(2,1)S(1)}, bf16[3,48,2048]{2,1,0:T(8,128)(2,1)S(1)}, u32[]{:S(2)}, u32[]{:S(2)}) collective-permute-start(bf16[3,48,2048]{2,1,0:T(8,128)(2,1)S(1)} %bitcast.92), channel_id=1, source_target_pairs={{0,2},{2,4},{4,6},{6,0},{1,3},{3,5},{5,7},{7,1},{8,10},{10,12},{12... | collective-permute-start | bytes 1769480 | tf_op jit(solution)/shard_map/ppermute | solution.py:16
  4.8 21.8 %collective-permute-start = (bf16[3,48,2048]{2,1,0:T(8,128)(2,1)S(1)}, bf16[3,48,2048]{2,1,0:T(8,128)(2,1)S(1)}, u32[]{:S(2)}, u32[]{:S(2)}) collective-permute-start(bf16[3,48,2048]{2,1,0:T(8,128)(2,1)S(1)} %bitcast.93), channel_id=1, source_target_pairs={{0,6},{2,0},{4,2},{6,4},{1,7},{3,1},{5,3},{7,5},{8,14},{10,8},{12,... | collective-permute-start | bytes 1769480 | tf_op jit(solution)/shard_map/ppermute | solution.py:16
  7.0 16.3 %collective-permute-start.4 = (bf16[3,48,2048]{2,1,0:T(8,128)(2,1)S(1)}, bf16[3,48,2048]{2,1,0:T(8,128)(2,1)S(1)}, u32[]{:S(2)}, u32[]{:S(2)}) collective-permute-start(bf16[3,48,2048]{2,1,0:T(8,128)(2,1)S(1)} %get-tuple-element.55), channel_id=1, source_target_pairs={{0,1},{1,0},{2,3},{3,2},{4,5},{5,4},{6,7},{7,6},{8,9},{9,8},{10,11... | collective-permute-start | bytes 1769480 | tf_op jit(solution)/shard_map/ppermute | solution.py:47
  10.5 39.2 %all-to-all-start = ((bf16[4,144,2048]{2,1,0:T(8,128)(2,1)}), bf16[4,144,2048]{2,1,0:T(8,128)(2,1)}, u32[]{:S(2)}, u32[]{:S(2)}) async-start(bf16[4,144,2048]{2,1,0:T(8,128)(2,1)} %broadcast_in_dim.23), calls=%async_computation | async-start | bytes 4718592 | tf_op jit(solution)/shard_map/all_to_all | solution.py:73
  23.3 13.7 %collective-permute-start.6 = (bf16[3,48,2048]{2,1,0:T(8,128)(2,1)S(1)}, bf16[3,48,2048]{2,1,0:T(8,128)(2,1)S(1)}, u32[]{:S(2)}, u32[]{:S(2)}) collective-permute-start(bf16[3,48,2048]{2,1,0:T(8,128)(2,1)S(1)} %collective-permute-done.4), channel_id=1, source_target_pairs={{0,8},{8,16},{16,24},{24,0},{1,9},{9,17},{17,25},{25,1},{2,10},{10... | collective-permute-start | bytes 1769480 | tf_op jit(solution)/shard_map/ppermute | solution.py:16
  24.8 13.4 %collective-permute-start.5 = (bf16[3,48,2048]{2,1,0:T(8,128)(2,1)S(1)}, bf16[3,48,2048]{2,1,0:T(8,128)(2,1)S(1)}, u32[]{:S(2)}, u32[]{:S(2)}) collective-permute-start(bf16[3,48,2048]{2,1,0:T(8,128)(2,1)S(1)} %collective-permute-done.4), channel_id=1, source_target_pairs={{0,24},{8,0},{16,8},{24,16},{1,25},{9,1},{17,9},{25,17},{2,26},{10... | collective-permute-start | bytes 1769480 | tf_op jit(solution)/shard_map/ppermute | solution.py:16
  26.6 13.9 %collective-permute-start.2 = (bf16[3,48,1024]{2,1,0:T(8,128)(2,1)S(1)}, bf16[3,48,1024]{2,1,0:T(8,128)(2,1)S(1)}, u32[]{:S(2)}, u32[]{:S(2)}) collective-permute-start(bf16[3,48,1024]{2,1,0:T(8,128)(2,1)S(1)} %slice.124), channel_id=1, source_target_pairs={{0,2},{2,4},{4,6},{6,0},{1,3},{3,5},{5,7},{7,1},{8,10},{10,12},{12... | collective-permute-start | bytes 884744 | tf_op jit(solution)/shard_map/ppermute | solution.py:24
  26.7 13.8 %collective-permute-start.3 = (bf16[3,48,1024]{2,1,0:T(8,128)(2,1)S(1)}, bf16[3,48,1024]{2,1,0:T(8,128)(2,1)S(1)}, u32[]{:S(2)}, u32[]{:S(2)}) collective-permute-start(bf16[3,48,1024]{2,1,0:T(8,128)(2,1)S(1)} %slice.125), channel_id=1, source_target_pairs={{0,6},{2,0},{4,2},{6,4},{1,7},{3,1},{5,3},{7,5},{8,14},{10,8},{12,... | collective-permute-start | bytes 884744 | tf_op jit(solution)/shard_map/ppermute | solution.py:25
  51.0 36.5 %collective-permute-start.15 = (bf16[4,2,48,2048]{3,2,1,0:T(8,128)(2,1)}, bf16[4,2,48,2048]{3,2,1,0:T(8,128)(2,1)}, u32[]{:S(2)}, u32[]{:S(2)}) collective-permute-start(bf16[4,2,48,2048]{3,2,1,0:T(8,128)(2,1)} %slice.102), channel_id=1, source_target_pairs={{0,2},{2,4},{4,6},{6,0},{1,3},{3,5},{5,7},{7,1},{8,10},{10,12},{12... | collective-permute-start | bytes 4718600 | tf_op jit(solution)/shard_map/ppermute | solution.py:16
  51.0 37.8 %collective-permute-start.14 = (bf16[4,2,48,2048]{3,2,1,0:T(8,128)(2,1)}, bf16[4,2,48,2048]{3,2,1,0:T(8,128)(2,1)}, u32[]{:S(2)}, u32[]{:S(2)}) collective-permute-start(bf16[4,2,48,2048]{3,2,1,0:T(8,128)(2,1)} %slice.102), channel_id=1, source_target_pairs={{0,6},{2,0},{4,2},{6,4},{1,7},{3,1},{5,3},{7,5},{8,14},{10,8},{12,... | collective-permute-start | bytes 4718600 | tf_op jit(solution)/shard_map/ppermute | solution.py:16
  55.5 39.1 %collective-permute-start.11 = (bf16[4,2,48,2048]{3,2,1,0:T(8,128)(2,1)}, bf16[4,2,48,2048]{3,2,1,0:T(8,128)(2,1)}, u32[]{:S(2)}, u32[]{:S(2)}) collective-permute-start(bf16[4,2,48,2048]{3,2,1,0:T(8,128)(2,1)} %slice.99), channel_id=1, source_target_pairs={{0,8},{8,16},{16,24},{24,0},{1,9},{9,17},{17,25},{25,1},{2,10},{10... | collective-permute-start | bytes 4718600 | tf_op jit(solution)/shard_map/ppermute | solution.py:16
  57.0 40.4 %collective-permute-start.10 = (bf16[4,2,48,2048]{3,2,1,0:T(8,128)(2,1)}, bf16[4,2,48,2048]{3,2,1,0:T(8,128)(2,1)}, u32[]{:S(2)}, u32[]{:S(2)}) collective-permute-start(bf16[4,2,48,2048]{3,2,1,0:T(8,128)(2,1)} %slice.99), channel_id=1, source_target_pairs={{0,24},{8,0},{16,8},{24,16},{1,25},{9,1},{17,9},{25,17},{2,26},{10... | collective-permute-start | bytes 4718600 | tf_op jit(solution)/shard_map/ppermute | solution.py:16
  88.7 18.4 %collective-permute-start.16 = (bf16[4,2,48,1024]{3,2,1,0:T(8,128)(2,1)S(1)}, bf16[4,2,48,1024]{3,2,1,0:T(8,128)(2,1)S(1)}, u32[]{:S(2)}, u32[]{:S(2)}) collective-permute-start(bf16[4,2,48,1024]{3,2,1,0:T(8,128)(2,1)S(1)} %slice.131), channel_id=1, source_target_pairs={{0,2},{2,4},{4,6},{6,0},{1,3},{3,5},{5,7},{7,1},{8,10},{10,12},{12... | collective-permute-start | bytes 2359304 | tf_op jit(solution)/shard_map/ppermute | solution.py:24
  90.0 17.7 %collective-permute-start.17 = (bf16[4,2,48,1024]{3,2,1,0:T(8,128)(2,1)S(1)}, bf16[4,2,48,1024]{3,2,1,0:T(8,128)(2,1)S(1)}, u32[]{:S(2)}, u32[]{:S(2)}) collective-permute-start(bf16[4,2,48,1024]{3,2,1,0:T(8,128)(2,1)S(1)} %slice.132), channel_id=1, source_target_pairs={{0,6},{2,0},{4,2},{6,4},{1,7},{3,1},{5,3},{7,5},{8,14},{10,8},{12,... | collective-permute-start | bytes 2359304 | tf_op jit(solution)/shard_map/ppermute | solution.py:25
  94.4 37.9 %collective-permute-start.9 = (bf16[4,144,2048]{2,1,0:T(8,128)(2,1)}, bf16[4,144,2048]{2,1,0:T(8,128)(2,1)}, u32[]{:S(2)}, u32[]{:S(2)}) collective-permute-start(bf16[4,144,2048]{2,1,0:T(8,128)(2,1)} %all-to-all-done), channel_id=1, source_target_pairs={{0,32},{32,0},{1,33},{33,1},{2,34},{34,2},{3,35},{35,3},{4,36},{36... | collective-permute-start | bytes 7077896 | tf_op jit(solution)/shard_map/ppermute | solution.py:94
  95.8 21.2 %collective-permute-start.12 = (bf16[4,2,48,1024]{3,2,1,0:T(8,128)(2,1)S(1)}, bf16[4,2,48,1024]{3,2,1,0:T(8,128)(2,1)S(1)}, u32[]{:S(2)}, u32[]{:S(2)}) collective-permute-start(bf16[4,2,48,1024]{3,2,1,0:T(8,128)(2,1)S(1)} %slice.129), channel_id=1, source_target_pairs={{0,8},{8,16},{16,24},{24,0},{1,9},{9,17},{17,25},{25,1},{2,10},{10... | collective-permute-start | bytes 2359304 | tf_op jit(solution)/shard_map/ppermute | solution.py:24
  98.5 19.7 %collective-permute-start.13 = (bf16[4,2,48,1024]{3,2,1,0:T(8,128)(2,1)S(1)}, bf16[4,2,48,1024]{3,2,1,0:T(8,128)(2,1)S(1)}, u32[]{:S(2)}, u32[]{:S(2)}) collective-permute-start(bf16[4,2,48,1024]{3,2,1,0:T(8,128)(2,1)S(1)} %slice.130), channel_id=1, source_target_pairs={{0,24},{8,0},{16,8},{24,16},{1,25},{9,1},{17,9},{25,17},{2,26},{10... | collective-permute-start | bytes 2359304 | tf_op jit(solution)/shard_map/ppermute | solution.py:25
  118.4 23.2 %collective-permute-start.19 = (bf16[4,48,2048]{2,1,0:T(8,128)(2,1)S(1)}, bf16[4,48,2048]{2,1,0:T(8,128)(2,1)}, u32[]{:S(2)}, u32[]{:S(2)}) collective-permute-start(bf16[4,48,2048]{2,1,0:T(8,128)(2,1)S(1)} %slice_bitcast_fusion.1), channel_id=1, source_target_pairs={{0,24},{8,0},{16,8},{24,16},{1,25},{9,1},{17,9},{25,17},{2,26},{10... | collective-permute-start | bytes 2359304 | tf_op jit(solution)/shard_map/ppermute | solution.py:16
  121.4 20.1 %collective-permute-start.18 = (bf16[4,48,2048]{2,1,0:T(8,128)(2,1)S(1)}, bf16[4,48,2048]{2,1,0:T(8,128)(2,1)}, u32[]{:S(2)}, u32[]{:S(2)}) collective-permute-start(bf16[4,48,2048]{2,1,0:T(8,128)(2,1)S(1)} %slice_bitcast_fusion.1), channel_id=1, source_target_pairs={{0,8},{8,16},{16,24},{24,0},{1,9},{9,17},{17,25},{25,1},{2,10},{10... | collective-permute-start | bytes 2359304 | tf_op jit(solution)/shard_map/ppermute | solution.py:16
  121.4 20.2 %collective-permute-start.21 = (bf16[4,48,2048]{2,1,0:T(8,128)(2,1)S(1)}, bf16[4,48,2048]{2,1,0:T(8,128)(2,1)}, u32[]{:S(2)}, u32[]{:S(2)}) collective-permute-start(bf16[4,48,2048]{2,1,0:T(8,128)(2,1)S(1)} %slice_bitcast_fusion), channel_id=1, source_target_pairs={{0,6},{2,0},{4,2},{6,4},{1,7},{3,1},{5,3},{7,5},{8,14},{10,8},{12,... | collective-permute-start | bytes 2359304 | tf_op jit(solution)/shard_map/ppermute | solution.py:16
  121.4 20.1 %collective-permute-start.20 = (bf16[4,48,2048]{2,1,0:T(8,128)(2,1)S(1)}, bf16[4,48,2048]{2,1,0:T(8,128)(2,1)}, u32[]{:S(2)}, u32[]{:S(2)}) collective-permute-start(bf16[4,48,2048]{2,1,0:T(8,128)(2,1)S(1)} %slice_bitcast_fusion), channel_id=1, source_target_pairs={{0,2},{2,4},{4,6},{6,0},{1,3},{3,5},{5,7},{7,1},{8,10},{10,12},{12... | collective-permute-start | bytes 2359304 | tf_op jit(solution)/shard_map/ppermute | solution.py:16
  149.4 17.0 %collective-permute-start.24 = (bf16[4,48,1024]{2,1,0:T(8,128)(2,1)S(1)}, bf16[4,48,1024]{2,1,0:T(8,128)(2,1)S(1)}, u32[]{:S(2)}, u32[]{:S(2)}) collective-permute-start(bf16[4,48,1024]{2,1,0:T(8,128)(2,1)S(1)} %slice.115), channel_id=1, source_target_pairs={{0,2},{2,4},{4,6},{6,0},{1,3},{3,5},{5,7},{7,1},{8,10},{10,12},{12... | collective-permute-start | bytes 1179656 | tf_op jit(solution)/shard_map/ppermute | solution.py:24
  149.7 16.7 %collective-permute-start.25 = (bf16[4,48,1024]{2,1,0:T(8,128)(2,1)S(1)}, bf16[4,48,1024]{2,1,0:T(8,128)(2,1)S(1)}, u32[]{:S(2)}, u32[]{:S(2)}) collective-permute-start(bf16[4,48,1024]{2,1,0:T(8,128)(2,1)S(1)} %slice.116), channel_id=1, source_target_pairs={{0,6},{2,0},{4,2},{6,4},{1,7},{3,1},{5,3},{7,5},{8,14},{10,8},{12,... | collective-permute-start | bytes 1179656 | tf_op jit(solution)/shard_map/ppermute | solution.py:25
  152.7 10.2 %collective-permute-start.22 = (bf16[4,48,1024]{2,1,0:T(8,128)(2,1)S(1)}, bf16[4,48,1024]{2,1,0:T(8,128)(2,1)S(1)}, u32[]{:S(2)}, u32[]{:S(2)}) collective-permute-start(bf16[4,48,1024]{2,1,0:T(8,128)(2,1)S(1)} %slice.112), channel_id=1, source_target_pairs={{0,8},{8,16},{16,24},{24,0},{1,9},{9,17},{17,25},{25,1},{2,10},{10... | collective-permute-start | bytes 1179656 | tf_op jit(solution)/shard_map/ppermute | solution.py:24
  (8 other events, 58.9 us)

commit v9 on v6

--- a/solution.py
+++ b/solution.py
@@ -8,20 +8,29 @@
 SWAP = [(0, 1), (1, 0)]
 
 
-def ring_of_four(value, axis):
-    ahead = [(i, (i + 1) % 4) for i in range(4)]
-    behind = [(i, (i - 1) % 4) for i in range(4)]
-    from_minus = lax.ppermute(value, axis, perm=ahead)
-    from_plus = lax.ppermute(value, axis, perm=behind)
+AHEAD = [(i, (i + 1) % 4) for i in range(4)]
+BEHIND = [(i, (i - 1) % 4) for i in range(4)]
+
+
+def first_hop(value, axis):
+    return lax.ppermute(value, axis, perm=AHEAD), lax.ppermute(value, axis, perm=BEHIND)
+
+
+def far_hop(value, near, axis):
+    from_minus, from_plus = near
     half = value.shape[-1] // 2
     far = jnp.concatenate(
         [
-            lax.ppermute(from_minus[..., :half], axis, perm=ahead),
-            lax.ppermute(from_plus[..., half:], axis, perm=behind),
+            lax.ppermute(from_minus[..., :half], axis, perm=AHEAD),
+            lax.ppermute(from_plus[..., half:], axis, perm=BEHIND),
         ],
         axis=-1,
     )
     return jnp.stack([value, from_plus, far, from_minus])
+
+
+def ring_of_four(value, axis):
+    return far_hop(value, first_hop(value, axis), axis)
 
 
 def expert_weights(w_gate, w_up, w_down, ylo):
@@ -32,20 +41,22 @@
     keep = lax.dynamic_index_in_dim(stacked, ylo, axis=0, keepdims=False)
     send = lax.dynamic_index_in_dim(stacked, 1 - ylo, axis=0, keepdims=False)
     got = lax.ppermute(send, "ylo", perm=SWAP)
-    first_a = ring_of_four(keep, "z")
-    first_b = ring_of_four(got, "x")
+    down_a = lax.all_gather(keep[2], ("x", "z"), axis=0, tiled=False)
+    down_b = lax.all_gather(got[2], ("x", "z"), axis=0, tiled=False)
+    first_a = ring_of_four(keep[:2], "z")
+    first_b = ring_of_four(got[:2], "x")
     first_a, first_b = lax.optimization_barrier((first_a, first_b))
-    gate_up_a = ring_of_four(first_a[:, :2], "x")
-    gate_up_b = ring_of_four(first_b[:, :2], "z")
-    gate_up_a, gate_up_b, down_a, down_b = lax.optimization_barrier(
-        (gate_up_a, gate_up_b, first_a[:, 2], first_b[:, 2])
-    )
-    down_a = ring_of_four(down_a, "x")
-    down_b = ring_of_four(down_b, "z")
+    gate_up_a = ring_of_four(first_a, "x")
+    gate_up_b = ring_of_four(first_b, "z")
     width = stacked.shape[-1]
+    x, z = lax.axis_index("x"), lax.axis_index("z")
     sets = []
-    for gate_up, down in ((gate_up_a, down_a), (gate_up_b, down_b)):
+    for gate_up, down, z_first in ((gate_up_a, down_a, True), (gate_up_b, down_b, False)):
         gate_up = jnp.moveaxis(gate_up, 2, 0).reshape(2, -1, width)
+        down = down.reshape((4, 4) + down.shape[1:])
+        down = jnp.roll(jnp.roll(down, -x, axis=0), -z, axis=1)
+        if not z_first:
+            down = jnp.swapaxes(down, 0, 1)
         sets.append((gate_up[0], gate_up[1], down.reshape(-1, width)))
     return sets
 

time: 211 us -> 219 us (1.038)
  starting transfers between devices: 49.4 us -> 34.4 us
  between operations: 0.46 us -> 13.8 us
  waiting for transfers between devices: 57.5 us -> 68.3 us
  local copies, waits for them, and re-layouts: 33.5 us -> 23.3 us
  other arithmetic: 15.6 us -> 23.6 us
    ppermute x24 -> x16, waiting for transfers between devices: 44.8 us -> 64.8 us  [the longest x4 44.4 us: first_hop(): lax.ppermute(value, axis, perm=AHEAD)]
    ppermute x24 -> x16, starting transfers between devices: 43.1 us -> 28.2 us  [the longest x4 12 us: far_hop(): lax.ppermute(from_plus[..., half:], axis, perm=BEHIND)]
    ppermute x1, waiting for transfers between devices: 9.29 us -> 0.01 us  [expert_weights(): got = lax.ppermute(send, 'ylo', perm=SWAP)]
    transpose x0 -> x3, other arithmetic: none -> 9.21 us  [the longest x2 6.69 us: expert_weights(): gate_up = jnp.moveaxis(gate_up, 2, 0).reshape(2, -1, width)]
    another operation x13 -> x7, other arithmetic: 13.1 us -> 5.85 us  [the longest x6 5.85 us: far_hop(): return jnp.stack([value, from_plus, far, from_minus])]
    concatenate x0 -> x2, other arithmetic: none -> 6.03 us  [expert_weights(): down = jnp.roll(jnp.roll(down, -x, axis=0), -z, axis=1)]
    another operation x3 -> x1, local copies, waits for them, and re-layouts: 5.67 us -> 0.05 us  [far_hop(): return jnp.stack([value, from_plus, far, from_minus])]
    squeeze x2 -> x0, local copies, waits for them, and re-layouts: 3.31 us -> none  [the longest x1 2.12 us: expert_weights(): first_b[:, 2]]
  transfers between devices with their start and end apart: 28 -> 22, of which waited for: 11 -> 12; matrix products, arithmetic and copies ran while one was open for 28% -> 25% of each run, Pallas kernels for 0% -> 0%
where the time goes in v9:
time: 219 us; the launch traced here: 218 us
  waiting for transfers between devices  68.3 us (31%)
  starting transfers between devices  34.4 us (16%)
  blocking collectives  31.1 us (14%)
  matrix products  23.8 us (11%)
  other arithmetic  23.6 us (11%)
  local copies, waits for them, and re-layouts  23.3 us (11%)
  between operations  13.8 us (6%)
    ppermute x4, waiting for transfers between devices, first_hop(): lax.ppermute(value, axis, perm=AHEAD)  44.4 us
    all_to_all x1, blocking collectives, per_device(): lax.all_to_all(partial, CHIPS, split_axis=0, concat_axis=0, tiled=True)  31.1 us
    ppermute x4, starting transfers between devices, far_hop(): lax.ppermute(from_plus[..., half:], axis, perm=BEHIND)  12 us
    ppermute x4, waiting for transfers between devices, far_hop(): lax.ppermute(from_minus[..., :half], axis, perm=AHEAD)  11.6 us
    ppermute x4, starting transfers between devices, first_hop(): lax.ppermute(value, axis, perm=BEHIND)  10.9 us
    dot_general x2, matrix products, per_device(): up_part = jnp.dot(rows, weights[1].T, preferred_element_type=jnp.float32)  9.49 us
    ppermute x4, waiting for transfers between devices, far_hop(): lax.ppermute(from_plus[..., half:], axis, perm=BEHIND)  8.54 us
    dot_general x4, matrix products, down(): jnp.dot(hidden[first:last], weights[2], preferred_element_type=jnp.float32)  7.41 us
  transfers between devices with their start and end apart: 22, of which 12 were waited for; matrix products, arithmetic and copies ran while one was open for 25% of the time, Pallas kernels for 0%

profile of v9, /device:TPU:0, one launch (start us, length us, event | category | flops | bytes accessed | tf_op | source)
XLA Modules:
  0.0 218.3 jit_solution(16580303201247810863)
XLA Ops:
  16.8 8.7 %collective-permute-done.2 = bf16[2,48,2048]{2,1,0:T(8,128)(2,1)S(1)} collective-permute-done((bf16[2,48,2048]{2,1,0:T(8,128)(2,1)S(1)}, bf16[2,48,2048]{2,1,0:T(8,128)(2,1)S(1)}, u32[]{:S(2)}, u32[]{:S(2)}) %collective-permute-start.2) | collective-permute-done | bytes 393248 | tf_op jit(solution)/shard_map/ppermute | solution.py:16
  25.9 3.8 %collective-permute-start.4 = (bf16[2,48,1024]{2,1,0:T(8,128)(2,1)S(1)}, bf16[2,48,1024]{2,1,0:T(8,128)(2,1)S(1)}, u32[]{:S(2)}, u32[]{:S(2)}) collective-permute-start(bf16[2,48,1024]{2,1,0:T(8,128)(2,1)S(1)} %slice.118), channel_id=1, source_target_pairs={{0,6},{2,0},{4,2},{6,4},{1,7},{3,1},{5,3},{7,5},{8,14},{10,8},{12,... | collective-permute-start | bytes 589832 | tf_op jit(solution)/shard_map/ppermute | solution.py:25
  34.1 7.4 %collective-permute-done.7 = bf16[2,48,2048]{2,1,0:T(8,128)(2,1)S(1)} collective-permute-done((bf16[2,48,2048]{2,1,0:T(8,128)(2,1)S(1)}, bf16[2,48,2048]{2,1,0:T(8,128)(2,1)S(1)}, u32[]{:S(2)}, u32[]{:S(2)}) %collective-permute-start.7) | collective-permute-done | bytes 393248 | tf_op jit(solution)/shard_map/ppermute | solution.py:16
  41.7 3.2 %collective-permute-start.9 = (bf16[2,48,1024]{2,1,0:T(8,128)(2,1)S(1)}, bf16[2,48,1024]{2,1,0:T(8,128)(2,1)S(1)}, u32[]{:S(2)}, u32[]{:S(2)}) collective-permute-start(bf16[2,48,1024]{2,1,0:T(8,128)(2,1)S(1)} %slice.121), channel_id=1, source_target_pairs={{0,24},{8,0},{16,8},{24,16},{1,25},{9,1},{17,9},{25,17},{2,26},{10... | collective-permute-start | bytes 589832 | tf_op jit(solution)/shard_map/ppermute | solution.py:25
  46.3 3.1 %collective-permute-done.8 = bf16[2,48,1024]{2,1,0:T(8,128)(2,1)S(1)} collective-permute-done((bf16[2,48,1024]{2,1,0:T(8,128)(2,1)S(1)}, bf16[2,48,1024]{2,1,0:T(8,128)(2,1)S(1)}, u32[]{:S(2)}, u32[]{:S(2)}) %collective-permute-start.8) | collective-permute-done | bytes 196640 | tf_op jit(solution)/shard_map/ppermute | solution.py:24
  53.6 3.2 %collective-permute-start.14 = (bf16[4,2,48,2048]{3,2,1,0:T(8,128)(2,1)}, bf16[4,2,48,2048]{3,2,1,0:T(8,128)(2,1)}, u32[]{:S(2)}, u32[]{:S(2)}) collective-permute-start(bf16[4,2,48,2048]{3,2,1,0:T(8,128)(2,1)} %pad_maximum_fusion.1), channel_id=1, source_target_pairs={{0,6},{2,0},{4,2},{6,4},{1,7},{3,1},{5,3},{7,5},{8,14},{10,8},{12,... | collective-permute-start | bytes 4718600 | tf_op jit(solution)/shard_map/ppermute | solution.py:16
  56.8 3.7 %collective-permute-start.10 = (bf16[4,2,48,2048]{3,2,1,0:T(8,128)(2,1)}, bf16[4,2,48,2048]{3,2,1,0:T(8,128)(2,1)}, u32[]{:S(2)}, u32[]{:S(2)}) collective-permute-start(bf16[4,2,48,2048]{3,2,1,0:T(8,128)(2,1)} %pad_maximum_fusion), channel_id=1, source_target_pairs={{0,24},{8,0},{16,8},{24,16},{1,25},{9,1},{17,9},{25,17},{2,26},{10... | collective-permute-start | bytes 4718600 | tf_op jit(solution)/shard_map/ppermute | solution.py:16
  62.3 4.1 %all-to-all-start = ((bf16[4,144,2048]{2,1,0:T(8,128)(2,1)}), bf16[4,144,2048]{2,1,0:T(8,128)(2,1)S(1)}, u32[]{:S(2)}, u32[]{:S(2)}) async-start(bf16[4,144,2048]{2,1,0:T(8,128)(2,1)} %broadcast_in_dim.23), calls=%async_computation | async-start | bytes 4718592 | tf_op jit(solution)/shard_map/all_to_all | solution.py:66
  66.4 28.3 %collective-permute-done.15 = bf16[4,2,48,2048]{3,2,1,0:T(8,128)(2,1)} collective-permute-done((bf16[4,2,48,2048]{3,2,1,0:T(8,128)(2,1)}, bf16[4,2,48,2048]{3,2,1,0:T(8,128)(2,1)}, u32[]{:S(2)}, u32[]{:S(2)}) %collective-permute-start.15) | collective-permute-done | bytes 1572896 | tf_op jit(solution)/shard_map/ppermute | solution.py:16
  98.1 3.2 %collective-permute-start.17 = (bf16[4,2,48,1024]{3,2,1,0:T(8,128)(2,1)}, bf16[4,2,48,1024]{3,2,1,0:T(8,128)(2,1)}, u32[]{:S(2)}, u32[]{:S(2)}) collective-permute-start(bf16[4,2,48,1024]{3,2,1,0:T(8,128)(2,1)} %slice.127), channel_id=1, source_target_pairs={{0,6},{2,0},{4,2},{6,4},{1,7},{3,1},{5,3},{7,5},{8,14},{10,8},{12,... | collective-permute-start | bytes 2359304 | tf_op jit(solution)/shard_map/ppermute | solution.py:25
  110.9 3.5 %collective-permute-done.16 = bf16[4,2,48,1024]{3,2,1,0:T(8,128)(2,1)} collective-permute-done((bf16[4,2,48,1024]{3,2,1,0:T(8,128)(2,1)S(1)}, bf16[4,2,48,1024]{3,2,1,0:T(8,128)(2,1)}, u32[]{:S(2)}, u32[]{:S(2)}) %collective-permute-start.16) | collective-permute-done | bytes 786464 | tf_op jit(solution)/shard_map/ppermute | solution.py:24
  117.5 4.0 %collective-permute-done.12 = bf16[4,2,48,1024]{3,2,1,0:T(8,128)(2,1)} collective-permute-done((bf16[4,2,48,1024]{3,2,1,0:T(8,128)(2,1)}, bf16[4,2,48,1024]{3,2,1,0:T(8,128)(2,1)}, u32[]{:S(2)}, u32[]{:S(2)}) %collective-permute-start.12) | collective-permute-done | bytes 786464 | tf_op jit(solution)/shard_map/ppermute | solution.py:24
  121.5 4.3 %collective-permute-done.13 = bf16[4,2,48,1024]{3,2,1,0:T(8,128)(2,1)} collective-permute-done((bf16[4,2,48,1024]{3,2,1,0:T(8,128)(2,1)}, bf16[4,2,48,1024]{3,2,1,0:T(8,128)(2,1)}, u32[]{:S(2)}, u32[]{:S(2)}) %collective-permute-start.13) | collective-permute-done | bytes 786464 | tf_op jit(solution)/shard_map/ppermute | solution.py:25
  127.3 3.4 %maximum_bitcast_fusion.1 = bf16[2,4,4,48,2048]{4,3,0,2,1:T(8,128)(2,1)S(1)} fusion(bf16[1,4,2,48,2048]{4,3,2,1,0:T(8,128)(2,1)} %bitcast.24, bf16[1,4,2,48,2048]{4,3,2,1,0:T(8,128)(2,1)S(1)} %maximum_bitcast_fusion.3, bf16[1,4,2,48,2048]{4,3,2,1,0:T(8,128)(2,1)} %bitcast.22, bf16[1,4,2,48,2048]{4,3,2,1,0:T(8,128)(2,1)} %bitcast.21), kind=kLoop, calls=%fused_computation.1 | loop fusion | flops 9437184 | bytes 12582912 | tf_op jit(solution)/shard_map/transpose | solution.py:55
  131.8 3.3 %maximum_bitcast_fusion = bf16[2,4,4,48,2048]{4,3,0,2,1:T(8,128)(2,1)S(1)} fusion(bf16[1,4,2,48,2048]{4,3,2,1,0:T(8,128)(2,1)} %bitcast.17, bf16[1,4,2,48,2048]{4,3,2,1,0:T(8,128)(2,1)S(1)} %maximum_bitcast_fusion.2, bf16[1,4,2,48,2048]{4,3,2,1,0:T(8,128)(2,1)} %bitcast.15, bf16[1,4,2,48,2048]{4,3,2,1,0:T(8,128)(2,1)} %bitcast.14), kind=kLoop, calls=%fused_computation | loop fusion | flops 9437184 | bytes 12582912 | tf_op jit(solution)/shard_map/transpose | solution.py:55
  135.1 3.3 %fusion.21 = (bf16[1,4,4,48,2048]{4,3,0,2,1:T(8,128)(2,1)}, bf16[1,4,4,48,2048]{4,3,0,2,1:T(8,128)(2,1)}) fusion(bf16[2,4,4,48,2048]{4,3,0,2,1:T(8,128)(2,1)S(1)} %maximum_bitcast_fusion), kind=kLoop, calls=%fused_computation.63 | loop fusion | bytes 12582912 | tf_op jit(solution)/shard_map/slice | solution.py:60
  140.6 3.4 %fusion.23 = f32[1024,768]{1,0:T(8,128)S(1)} fusion(bf16[1024,2048]{1,0:T(8,128)(2,1)S(1)} %bitcast.73, bf16[768,2048]{1,0:T(8,128)(2,1)S(1)} %bitcast.81), kind=kOutput, calls=%fused_computation.65 | convolution fusion | flops 3221225472 | bytes 10485760 | tf_op jit(solution)/shard_map/dot_general | solution.py:97
  144.0 4.8 %multiply_convert_fusion = bf16[1024,768]{1,0:T(8,128)(2,1)} fusion(f32[1024,768]{1,0:T(8,128)S(1)} %fusion.23, bf16[1024,2048]{1,0:T(8,128)(2,1)S(1)} %bitcast.74, bf16[768,2048]{1,0:T(8,128)(2,1)S(1)} %bitcast.80), kind=kOutput, calls=%fused_computation.20 | convolution fusion | flops 3225944064 | bytes 12058624 | tf_op jit(solution)/shard_map/dot_general | solution.py:98
  148.8 3.4 %fusion.22 = f32[1024,768]{1,0:T(8,128)S(1)} fusion(bf16[1024,2048]{1,0:T(8,128)(2,1)S(1)} %bitcast.75, bf16[768,2048]{1,0:T(8,128)(2,1)S(1)} %bitcast.83), kind=kOutput, calls=%fused_computation.64 | convolution fusion | flops 3221225472 | bytes 10485760 | tf_op jit(solution)/shard_map/dot_general | solution.py:97
  152.2 4.7 %multiply_convert_fusion.1 = bf16[1024,768]{1,0:T(8,128)(2,1)} fusion(f32[1024,768]{1,0:T(8,128)S(1)} %fusion.22, bf16[1024,2048]{1,0:T(8,128)(2,1)S(1)} %bitcast.76, bf16[768,2048]{1,0:T(8,128)(2,1)S(1)} %bitcast.82), kind=kOutput, calls=%fused_computation.21 | convolution fusion | flops 3225944064 | bytes 12058624 | tf_op jit(solution)/shard_map/dot_general | solution.py:98
  157.1 3.0 %fusion.4 = bf16[4,4,48,2048]{3,2,1,0:T(8,128)(2,1)S(1)} fusion(s32[]{:T(128)S(6)} %select_n.41, bf16[4,4,48,2048]{3,2,1,0:T(8,128)(2,1)} %bitcast.78), kind=kLoop, calls=%fused_computation.19 | loop fusion | flops 1572864 | bytes 6291460 | tf_op jit(solution)/shard_map/jit(_roll_dynamic)/concatenate | solution.py:57
  160.1 3.0 %fusion.2 = bf16[4,4,48,2048]{3,2,1,0:T(8,128)(2,1)S(1)} fusion(s32[]{:T(128)S(6)} %select_n.41, bf16[4,4,48,2048]{3,2,1,0:T(8,128)(2,1)} %bitcast.79), kind=kLoop, calls=%fused_computation.17 | loop fusion | flops 1572864 | bytes 6291460 | tf_op jit(solution)/shard_map/jit(_roll_dynamic)/concatenate | solution.py:57
  174.6 3.4 %collective-permute-done.18 = f32[4,128,2048]{2,1,0:T(8,128)S(1)} collective-permute-done((f32[4,128,2048]{2,1,0:T(8,128)S(1)}, f32[4,128,2048]{2,1,0:T(8,128)S(1)}, u32[]{:S(2)}, u32[]{:S(2)}) %collective-permute-start.18) | collective-permute-done | bytes 4194336 | tf_op jit(solution)/shard_map/ppermute | solution.py:113
  179.1 31.1 %all_to_all.10 = bf16[4,128,2048]{2,1,0:T(8,128)(2,1)S(1)} all-to-all(bf16[4,128,2048]{2,1,0:T(8,128)(2,1)S(1)} %add_convert_fusion), channel_id=1, replica_groups=mesh['yhi'=2,'core'=2,'x'=4,'z'=4,'ylo'=2] {'yhi','ylo'}, dimensions={0} | all-to-all | bytes 4194304 | tf_op jit(solution)/shard_map/all_to_all | solution.py:115
  (92 shorter events, 57.1 us)
Async XLA Ops:
  6.5 150.5 %all-gather.6.cloned.1.call-start = ((), (), s32[]{:S(2)}) async-start(), calls=%async_computation.3 | async-start | bytes 3342336 | tf_op jit(solution)/shard_map/all_gather | solution.py:44
  10.8 18.9 %collective-permute-start.5 = (bf16[3,48,2048]{2,1,0:T(8,128)(2,1)S(1)}, bf16[3,48,2048]{2,1,0:T(8,128)(2,1)S(1)}, u32[]{:S(2)}, u32[]{:S(2)}) collective-permute-start(bf16[3,48,2048]{2,1,0:T(8,128)(2,1)S(1)} %dynamic-slice_bitcast_fusion), channel_id=1, source_target_pairs={{0,1},{1,0},{2,3},{3,2},{4,5},{5,4},{6,7},{7,6},{8,9},{9,8},{10,11... | collective-permute-start | bytes 1769480 | tf_op jit(solution)/shard_map/ppermute | solution.py:43
  12.6 12.9 %collective-permute-start.2 = (bf16[2,48,2048]{2,1,0:T(8,128)(2,1)S(1)}, bf16[2,48,2048]{2,1,0:T(8,128)(2,1)S(1)}, u32[]{:S(2)}, u32[]{:S(2)}) collective-permute-start(bf16[2,48,2048]{2,1,0:T(8,128)(2,1)S(1)} %fusion.36), channel_id=1, source_target_pairs={{0,2},{2,4},{4,6},{6,0},{1,3},{3,5},{5,7},{7,1},{8,10},{10,12},{12... | collective-permute-start | bytes 1179656 | tf_op jit(solution)/shard_map/ppermute | solution.py:16
  14.6 11.3 %collective-permute-start.1 = (bf16[2,48,2048]{2,1,0:T(8,128)(2,1)S(1)}, bf16[2,48,2048]{2,1,0:T(8,128)(2,1)S(1)}, u32[]{:S(2)}, u32[]{:S(2)}) collective-permute-start(bf16[2,48,2048]{2,1,0:T(8,128)(2,1)S(1)} %fusion.36), channel_id=1, source_target_pairs={{0,6},{2,0},{4,2},{6,4},{1,7},{3,1},{5,3},{7,5},{8,14},{10,8},{12,... | collective-permute-start | bytes 1179656 | tf_op jit(solution)/shard_map/ppermute | solution.py:16
  25.6 8.5 %collective-permute-start.3 = (bf16[2,48,1024]{2,1,0:T(8,128)(2,1)S(1)}, bf16[2,48,1024]{2,1,0:T(8,128)(2,1)S(1)}, u32[]{:S(2)}, u32[]{:S(2)}) collective-permute-start(bf16[2,48,1024]{2,1,0:T(8,128)(2,1)S(1)} %slice.117), channel_id=1, source_target_pairs={{0,2},{2,4},{4,6},{6,0},{1,3},{3,5},{5,7},{7,1},{8,10},{10,12},{12... | collective-permute-start | bytes 589832 | tf_op jit(solution)/shard_map/ppermute | solution.py:24
  25.9 8.2 %collective-permute-start.4 = (bf16[2,48,1024]{2,1,0:T(8,128)(2,1)S(1)}, bf16[2,48,1024]{2,1,0:T(8,128)(2,1)S(1)}, u32[]{:S(2)}, u32[]{:S(2)}) collective-permute-start(bf16[2,48,1024]{2,1,0:T(8,128)(2,1)S(1)} %slice.118), channel_id=1, source_target_pairs={{0,6},{2,0},{4,2},{6,4},{1,7},{3,1},{5,3},{7,5},{8,14},{10,8},{12,... | collective-permute-start | bytes 589832 | tf_op jit(solution)/shard_map/ppermute | solution.py:25
  29.7 12.0 %copy-start.3 = (bf16[3,48,2048]{2,1,0:T(8,128)(2,1)}, bf16[3,48,2048]{2,1,0:T(8,128)(2,1)S(1)}, u32[]{:S(2)}) copy-start(bf16[3,48,2048]{2,1,0:T(8,128)(2,1)S(1)} %collective-permute-done.5) | copy-start | bytes 1769476
  29.8 11.8 %collective-permute-start.7 = (bf16[2,48,2048]{2,1,0:T(8,128)(2,1)S(1)}, bf16[2,48,2048]{2,1,0:T(8,128)(2,1)S(1)}, u32[]{:S(2)}, u32[]{:S(2)}) collective-permute-start(bf16[2,48,2048]{2,1,0:T(8,128)(2,1)S(1)} %get-tuple-element.22), channel_id=1, source_target_pairs={{0,8},{8,16},{16,24},{24,0},{1,9},{9,17},{17,25},{25,1},{2,10},{10... | collective-permute-start | bytes 1179656 | tf_op jit(solution)/shard_map/ppermute | solution.py:16
  31.3 10.4 %collective-permute-start.6 = (bf16[2,48,2048]{2,1,0:T(8,128)(2,1)S(1)}, bf16[2,48,2048]{2,1,0:T(8,128)(2,1)S(1)}, u32[]{:S(2)}, u32[]{:S(2)}) collective-permute-start(bf16[2,48,2048]{2,1,0:T(8,128)(2,1)S(1)} %get-tuple-element.22), channel_id=1, source_target_pairs={{0,24},{8,0},{16,8},{24,16},{1,25},{9,1},{17,9},{25,17},{2,26},{10... | collective-permute-start | bytes 1179656 | tf_op jit(solution)/shard_map/ppermute | solution.py:16
  41.6 7.9 %collective-permute-start.8 = (bf16[2,48,1024]{2,1,0:T(8,128)(2,1)S(1)}, bf16[2,48,1024]{2,1,0:T(8,128)(2,1)S(1)}, u32[]{:S(2)}, u32[]{:S(2)}) collective-permute-start(bf16[2,48,1024]{2,1,0:T(8,128)(2,1)S(1)} %slice.120), channel_id=1, source_target_pairs={{0,8},{8,16},{16,24},{24,0},{1,9},{9,17},{17,25},{25,1},{2,10},{10... | collective-permute-start | bytes 589832 | tf_op jit(solution)/shard_map/ppermute | solution.py:24
  41.7 10.4 %collective-permute-start.9 = (bf16[2,48,1024]{2,1,0:T(8,128)(2,1)S(1)}, bf16[2,48,1024]{2,1,0:T(8,128)(2,1)S(1)}, u32[]{:S(2)}, u32[]{:S(2)}) collective-permute-start(bf16[2,48,1024]{2,1,0:T(8,128)(2,1)S(1)} %slice.121), channel_id=1, source_target_pairs={{0,24},{8,0},{16,8},{24,16},{1,25},{9,1},{17,9},{25,17},{2,26},{10... | collective-permute-start | bytes 589832 | tf_op jit(solution)/shard_map/ppermute | solution.py:25
  45.0 15.6 %copy-start.4 = (bf16[128,2048]{1,0:T(8,128)(2,1)S(1)}, bf16[128,2048]{1,0:T(8,128)(2,1)}, u32[]{:S(2)}) copy-start(bf16[128,2048]{1,0:T(8,128)(2,1)} %param.10) | copy-start | bytes 1572868
  53.6 41.1 %collective-permute-start.15 = (bf16[4,2,48,2048]{3,2,1,0:T(8,128)(2,1)}, bf16[4,2,48,2048]{3,2,1,0:T(8,128)(2,1)}, u32[]{:S(2)}, u32[]{:S(2)}) collective-permute-start(bf16[4,2,48,2048]{3,2,1,0:T(8,128)(2,1)} %pad_maximum_fusion.1), channel_id=1, source_target_pairs={{0,2},{2,4},{4,6},{6,0},{1,3},{3,5},{5,7},{7,1},{8,10},{10,12},{12... | collective-permute-start | bytes 4718600 | tf_op jit(solution)/shard_map/ppermute | solution.py:16
  53.6 42.4 %collective-permute-start.14 = (bf16[4,2,48,2048]{3,2,1,0:T(8,128)(2,1)}, bf16[4,2,48,2048]{3,2,1,0:T(8,128)(2,1)}, u32[]{:S(2)}, u32[]{:S(2)}) collective-permute-start(bf16[4,2,48,2048]{3,2,1,0:T(8,128)(2,1)} %pad_maximum_fusion.1), channel_id=1, source_target_pairs={{0,6},{2,0},{4,2},{6,4},{1,7},{3,1},{5,3},{7,5},{8,14},{10,8},{12,... | collective-permute-start | bytes 4718600 | tf_op jit(solution)/shard_map/ppermute | solution.py:16
  56.8 44.5 %collective-permute-start.11 = (bf16[4,2,48,2048]{3,2,1,0:T(8,128)(2,1)}, bf16[4,2,48,2048]{3,2,1,0:T(8,128)(2,1)}, u32[]{:S(2)}, u32[]{:S(2)}) collective-permute-start(bf16[4,2,48,2048]{3,2,1,0:T(8,128)(2,1)} %pad_maximum_fusion), channel_id=1, source_target_pairs={{0,8},{8,16},{16,24},{24,0},{1,9},{9,17},{17,25},{25,1},{2,10},{10... | collective-permute-start | bytes 4718600 | tf_op jit(solution)/shard_map/ppermute | solution.py:16
  56.8 48.0 %collective-permute-start.10 = (bf16[4,2,48,2048]{3,2,1,0:T(8,128)(2,1)}, bf16[4,2,48,2048]{3,2,1,0:T(8,128)(2,1)}, u32[]{:S(2)}, u32[]{:S(2)}) collective-permute-start(bf16[4,2,48,2048]{3,2,1,0:T(8,128)(2,1)} %pad_maximum_fusion), channel_id=1, source_target_pairs={{0,24},{8,0},{16,8},{24,16},{1,25},{9,1},{17,9},{25,17},{2,26},{10... | collective-permute-start | bytes 4718600 | tf_op jit(solution)/shard_map/ppermute | solution.py:16
  62.3 48.0 %all-to-all-start = ((bf16[4,144,2048]{2,1,0:T(8,128)(2,1)}), bf16[4,144,2048]{2,1,0:T(8,128)(2,1)S(1)}, u32[]{:S(2)}, u32[]{:S(2)}) async-start(bf16[4,144,2048]{2,1,0:T(8,128)(2,1)} %broadcast_in_dim.23), calls=%async_computation | async-start | bytes 4718592 | tf_op jit(solution)/shard_map/all_to_all | solution.py:66
  66.4 93.7 %all-gather.4.cloned.1.call-start = ((), (), s32[]{:S(2)}) async-start(), calls=%async_computation.2 | async-start | bytes 3342336 | tf_op jit(solution)/shard_map/all_gather | solution.py:45
  95.9 18.5 %collective-permute-start.16 = (bf16[4,2,48,1024]{3,2,1,0:T(8,128)(2,1)S(1)}, bf16[4,2,48,1024]{3,2,1,0:T(8,128)(2,1)}, u32[]{:S(2)}, u32[]{:S(2)}) collective-permute-start(bf16[4,2,48,1024]{3,2,1,0:T(8,128)(2,1)S(1)} %slice.126), channel_id=1, source_target_pairs={{0,2},{2,4},{4,6},{6,0},{1,3},{3,5},{5,7},{7,1},{8,10},{10,12},{12... | collective-permute-start | bytes 2359304 | tf_op jit(solution)/shard_map/ppermute | solution.py:24
  98.1 17.9 %collective-permute-start.17 = (bf16[4,2,48,1024]{3,2,1,0:T(8,128)(2,1)}, bf16[4,2,48,1024]{3,2,1,0:T(8,128)(2,1)}, u32[]{:S(2)}, u32[]{:S(2)}) collective-permute-start(bf16[4,2,48,1024]{3,2,1,0:T(8,128)(2,1)} %slice.127), channel_id=1, source_target_pairs={{0,6},{2,0},{4,2},{6,4},{1,7},{3,1},{5,3},{7,5},{8,14},{10,8},{12,... | collective-permute-start | bytes 2359304 | tf_op jit(solution)/shard_map/ppermute | solution.py:25
  103.4 18.1 %collective-permute-start.12 = (bf16[4,2,48,1024]{3,2,1,0:T(8,128)(2,1)}, bf16[4,2,48,1024]{3,2,1,0:T(8,128)(2,1)}, u32[]{:S(2)}, u32[]{:S(2)}) collective-permute-start(bf16[4,2,48,1024]{3,2,1,0:T(8,128)(2,1)} %slice.122), channel_id=1, source_target_pairs={{0,8},{8,16},{16,24},{24,0},{1,9},{9,17},{17,25},{25,1},{2,10},{10... | collective-permute-start | bytes 2359304 | tf_op jit(solution)/shard_map/ppermute | solution.py:24
  106.9 18.9 %collective-permute-start.13 = (bf16[4,2,48,1024]{3,2,1,0:T(8,128)(2,1)}, bf16[4,2,48,1024]{3,2,1,0:T(8,128)(2,1)}, u32[]{:S(2)}, u32[]{:S(2)}) collective-permute-start(bf16[4,2,48,1024]{3,2,1,0:T(8,128)(2,1)} %slice.123), channel_id=1, source_target_pairs={{0,24},{8,0},{16,8},{24,16},{1,25},{9,1},{17,9},{25,17},{2,26},{10... | collective-permute-start | bytes 2359304 | tf_op jit(solution)/shard_map/ppermute | solution.py:25
  110.4 28.0 %collective-permute-start = (bf16[4,144,2048]{2,1,0:T(8,128)(2,1)S(1)}, bf16[4,144,2048]{2,1,0:T(8,128)(2,1)}, u32[]{:S(2)}, u32[]{:S(2)}) collective-permute-start(bf16[4,144,2048]{2,1,0:T(8,128)(2,1)S(1)} %all-to-all-done), channel_id=1, source_target_pairs={{0,32},{32,0},{1,33},{33,1},{2,34},{34,2},{3,35},{35,3},{4,36},{36... | collective-permute-start | bytes 7077896 | tf_op jit(solution)/shard_map/ppermute | solution.py:67
  170.8 7.2 %collective-permute-start.18 = (f32[4,128,2048]{2,1,0:T(8,128)S(1)}, f32[4,128,2048]{2,1,0:T(8,128)S(1)}, u32[]{:S(2)}, u32[]{:S(2)}) collective-permute-start(f32[4,128,2048]{2,1,0:T(8,128)S(1)} %bitcast.77), channel_id=1, source_target_pairs={{0,32},{32,0},{1,33},{33,1},{2,34},{34,2},{3,35},{35,3},{4,36},{36... | collective-permute-start | bytes 12582920 | tf_op jit(solution)/shard_map/ppermute | solution.py:113
  (6 other events, 29.7 us)
Sparse Core Ops, SparseCore 0:
  10.9 57.8 all-gather.5
  110.5 45.5 all-gather.3

commit v10 on v7

--- a/solution.py
+++ b/solution.py
@@ -117,8 +117,12 @@
     hiddens, theirs = lax.optimization_barrier((hiddens, theirs))
     partner = lax.ppermute(theirs, "core", perm=SWAP)
     partial = (down(hiddens, 0, half) + partner).astype(jnp.bfloat16)
-    back = lax.all_to_all(partial, CHIPS, split_axis=0, concat_axis=0, tiled=True)
-    mixed = jnp.sum(back.astype(jnp.float32), axis=0)
+    chip = lax.axis_index("yhi") * lax.axis_size("ylo") + ylo
+    mixed = lax.dynamic_index_in_dim(partial, chip, keepdims=False).astype(jnp.float32)
+    for offset in range(1, chips):
+        piece = lax.dynamic_index_in_dim(partial, (chip + offset) % chips, keepdims=False)
+        ring = [(i, (i + offset) % chips) for i in range(chips)]
+        mixed = mixed + lax.ppermute(piece, CHIPS, perm=ring).astype(jnp.float32)
     return mixed.astype(jnp.bfloat16)
 
 

time: 208 us -> 210 us (level)
  blocking collectives: 30.9 us -> 0 us
  waiting for transfers between devices: 58 us -> 78.8 us
  starting transfers between devices: 48.3 us -> 53.2 us
  matrix products: 21.6 us -> 26 us
  other arithmetic: 15.6 us -> 18.4 us
    all_to_all x1 -> x0, blocking collectives: 30.9 us -> none  [per_device(): lax.all_to_all(partial, CHIPS, split_axis=0, concat_axis=0, tiled=True)]
    ppermute x0 -> x3, waiting for transfers between devices: none -> 22.7 us  [per_device(): mixed = mixed + lax.ppermute(piece, CHIPS, perm=ring).astype(jnp.float32)]
    ppermute x0 -> x3, starting transfers between devices: none -> 5.22 us  [per_device(): mixed = mixed + lax.ppermute(piece, CHIPS, perm=ring).astype(jnp.float32)]
    dot_general x4, matrix products: 7.29 us -> 11.7 us  [down(): jnp.dot(hidden[first:last], weights[2], preferred_element_type=jnp.float32)]
    convert_element_type x0 -> x1, other arithmetic: none -> 2.48 us  [per_device(): return mixed.astype(jnp.bfloat16)]
  transfers between devices with their start and end apart: 28 -> 31, of which waited for: 10 -> 13; matrix products, arithmetic and copies ran while one was open for 26% -> 27% of each run, Pallas kernels for 0% -> 0%
where the time goes in v10:
time: 210 us; the launch traced here: 209 us
  waiting for transfers between devices  78.8 us (38%)
  starting transfers between devices  53.2 us (25%)
  local copies, waits for them, and re-layouts  32.3 us (15%)
  matrix products  26 us (12%)
  other arithmetic  18.4 us (9%)
    ppermute x3, waiting for transfers between devices, per_device(): mixed = mixed + lax.ppermute(piece, CHIPS, perm=ring).astype(jnp.float32)  22.7 us
    ppermute x6, starting transfers between devices, far_hop(): lax.ppermute(from_plus[..., half:], axis, perm=BEHIND)  19.7 us
    ppermute x6, waiting for transfers between devices, first_hop(): lax.ppermute(value, axis, perm=BEHIND)  18.2 us
    ppermute x6, waiting for transfers between devices, far_hop(): lax.ppermute(from_minus[..., :half], axis, perm=AHEAD)  16.4 us
    ppermute x6, starting transfers between devices, first_hop(): lax.ppermute(value, axis, perm=BEHIND)  14.1 us
    another operation x12, other arithmetic, far_hop(): return jnp.stack([value, from_plus, far, from_minus])  12.9 us
    dot_general x4, matrix products, down(): jnp.dot(hidden[first:last], weights[2], preferred_element_type=jnp.float32)  11.7 us
    ppermute x1, waiting for transfers between devices, expert_weights(): got = lax.ppermute(send, 'ylo', perm=SWAP)  9.29 us
  transfers between devices with their start and end apart: 31, of which 13 were waited for; matrix products, arithmetic and copies ran while one was open for 27% of the time, Pallas kernels for 0%

profile of v10, /device:TPU:0, one launch (start us, length us, event | category | flops | bytes accessed | tf_op | source)
XLA Modules:
  0.0 209.2 jit_solution(12391169332524502848)
XLA Ops:
  8.5 9.3 %collective-permute-done.5 = bf16[3,48,2048]{2,1,0:T(8,128)(2,1)S(1)} collective-permute-done((bf16[3,48,2048]{2,1,0:T(8,128)(2,1)S(1)}, bf16[3,48,2048]{2,1,0:T(8,128)(2,1)S(1)}, u32[]{:S(2)}, u32[]{:S(2)}) %collective-permute-start.5) | collective-permute-done | bytes 589856 | tf_op jit(solution)/shard_map/ppermute | solution.py:43
  25.4 7.7 %collective-permute-done.7 = bf16[3,48,2048]{2,1,0:T(8,128)(2,1)S(1)} collective-permute-done((bf16[3,48,2048]{2,1,0:T(8,128)(2,1)S(1)}, bf16[3,48,2048]{2,1,0:T(8,128)(2,1)S(1)}, u32[]{:S(2)}, u32[]{:S(2)}) %collective-permute-start.7) | collective-permute-done | bytes 589856 | tf_op jit(solution)/shard_map/ppermute | solution.py:16
  36.9 4.4 %collective-permute-done.8 = bf16[3,48,1024]{2,1,0:T(8,128)(2,1)S(1)} collective-permute-done((bf16[3,48,1024]{2,1,0:T(8,128)(2,1)S(1)}, bf16[3,48,1024]{2,1,0:T(8,128)(2,1)S(1)}, u32[]{:S(2)}, u32[]{:S(2)}) %collective-permute-start.8) | collective-permute-done | bytes 294944 | tf_op jit(solution)/shard_map/ppermute | solution.py:24
  44.0 3.1 %collective-permute-start.10 = (bf16[4,2,48,2048]{3,2,1,0:T(8,128)(2,1)}, bf16[4,2,48,2048]{3,2,1,0:T(8,128)(2,1)}, u32[]{:S(2)}, u32[]{:S(2)}) collective-permute-start(bf16[4,2,48,2048]{3,2,1,0:T(8,128)(2,1)} %get-tuple-element.44), channel_id=1, source_target_pairs={{0,24},{8,0},{16,8},{24,16},{1,25},{9,1},{17,9},{25,17},{2,26},{10... | collective-permute-start | bytes 4718600 | tf_op jit(solution)/shard_map/ppermute | solution.py:16
  49.2 4.2 %collective-permute-start.14 = (bf16[4,2,48,2048]{3,2,1,0:T(8,128)(2,1)}, bf16[4,2,48,2048]{3,2,1,0:T(8,128)(2,1)}, u32[]{:S(2)}, u32[]{:S(2)}) collective-permute-start(bf16[4,2,48,2048]{3,2,1,0:T(8,128)(2,1)} %get-tuple-element.42), channel_id=1, source_target_pairs={{0,6},{2,0},{4,2},{6,4},{1,7},{3,1},{5,3},{7,5},{8,14},{10,8},{12,... | collective-permute-start | bytes 4718600 | tf_op jit(solution)/shard_map/ppermute | solution.py:16
  55.2 4.5 %all-to-all-start = ((bf16[4,144,2048]{2,1,0:T(8,128)(2,1)}), bf16[4,144,2048]{2,1,0:T(8,128)(2,1)S(1)}, u32[]{:S(2)}, u32[]{:S(2)}) async-start(bf16[4,144,2048]{2,1,0:T(8,128)(2,1)} %broadcast_in_dim.23), calls=%async_computation | async-start | bytes 4718592 | tf_op jit(solution)/shard_map/all_to_all | solution.py:67
  59.7 18.2 %collective-permute-done.10 = bf16[4,2,48,2048]{3,2,1,0:T(8,128)(2,1)} collective-permute-done((bf16[4,2,48,2048]{3,2,1,0:T(8,128)(2,1)}, bf16[4,2,48,2048]{3,2,1,0:T(8,128)(2,1)}, u32[]{:S(2)}, u32[]{:S(2)}) %collective-permute-start.10) | collective-permute-done | bytes 1572896 | tf_op jit(solution)/shard_map/ppermute | solution.py:16
  79.9 3.7 %collective-permute-start.13 = (bf16[4,2,48,1024]{3,2,1,0:T(8,128)(2,1)}, bf16[4,2,48,1024]{3,2,1,0:T(8,128)(2,1)}, u32[]{:S(2)}, u32[]{:S(2)}) collective-permute-start(bf16[4,2,48,1024]{3,2,1,0:T(8,128)(2,1)} %slice.130), channel_id=1, source_target_pairs={{0,24},{8,0},{16,8},{24,16},{1,25},{9,1},{17,9},{25,17},{2,26},{10... | collective-permute-start | bytes 2359304 | tf_op jit(solution)/shard_map/ppermute | solution.py:25
  89.0 4.3 %collective-permute-start.17 = (bf16[4,2,48,1024]{3,2,1,0:T(8,128)(2,1)}, bf16[4,2,48,1024]{3,2,1,0:T(8,128)(2,1)}, u32[]{:S(2)}, u32[]{:S(2)}) collective-permute-start(bf16[4,2,48,1024]{3,2,1,0:T(8,128)(2,1)} %slice.132), channel_id=1, source_target_pairs={{0,6},{2,0},{4,2},{6,4},{1,7},{3,1},{5,3},{7,5},{8,14},{10,8},{12,... | collective-permute-start | bytes 2359304 | tf_op jit(solution)/shard_map/ppermute | solution.py:25
  97.8 4.3 %collective-permute-done.12 = bf16[4,2,48,1024]{3,2,1,0:T(8,128)(2,1)} collective-permute-done((bf16[4,2,48,1024]{3,2,1,0:T(8,128)(2,1)}, bf16[4,2,48,1024]{3,2,1,0:T(8,128)(2,1)}, u32[]{:S(2)}, u32[]{:S(2)}) %collective-permute-start.12) | collective-permute-done | bytes 786464 | tf_op jit(solution)/shard_map/ppermute | solution.py:24
  105.9 5.5 %collective-permute-done.16 = bf16[4,2,48,1024]{3,2,1,0:T(8,128)(2,1)} collective-permute-done((bf16[4,2,48,1024]{3,2,1,0:T(8,128)(2,1)}, bf16[4,2,48,1024]{3,2,1,0:T(8,128)(2,1)}, u32[]{:S(2)}, u32[]{:S(2)}) %collective-permute-start.16) | collective-permute-done | bytes 786464 | tf_op jit(solution)/shard_map/ppermute | solution.py:24
  112.9 3.1 %pad_maximum_fusion = bf16[4,4,2,48,2048]{4,3,2,1,0:T(8,128)(2,1)S(1)} fusion(bf16[1,4,2,48,2048]{4,3,2,1,0:T(8,128)(2,1)} %bitcast.17, bf16[1,4,2,48,2048]{4,3,2,1,0:T(8,128)(2,1)S(1)} %maximum_bitcast_fusion, bf16[1,4,2,48,2048]{4,3,2,1,0:T(8,128)(2,1)} %bitcast.15, bf16[1,4,2,48,2048]{4,3,2,1,0:T(8,128)(2,1)S(1)} %copy-done.2), kind=kLoop, calls=%fused_computation | loop fusion | flops 9437184 | bytes 12582912 | tf_op jit(solution)/shard_map/stack | solution.py:29
  116.1 3.0 %pad_maximum_fusion.1 = bf16[4,4,2,48,2048]{4,3,2,1,0:T(8,128)(2,1)S(1)} fusion(bf16[1,4,2,48,2048]{4,3,2,1,0:T(8,128)(2,1)} %bitcast.21, bf16[1,4,2,48,2048]{4,3,2,1,0:T(8,128)(2,1)S(1)} %maximum_bitcast_fusion.1, bf16[1,4,2,48,2048]{4,3,2,1,0:T(8,128)(2,1)} %bitcast.19, bf16[1,4,2,48,2048]{4,3,2,1,0:T(8,128)(2,1)S(1)} %copy-done.3), kind=kLoop, calls=%fused_computation.1 | loop fusion | flops 9437184 | bytes 12582912 | tf_op jit(solution)/shard_map/stack | solution.py:29
  119.1 3.0 %collective-permute-start.19 = (bf16[4,48,2048]{2,1,0:T(8,128)(2,1)S(1)}, bf16[4,48,2048]{2,1,0:T(8,128)(2,1)}, u32[]{:S(2)}, u32[]{:S(2)}) collective-permute-start(bf16[4,48,2048]{2,1,0:T(8,128)(2,1)S(1)} %slice_bitcast_fusion.1), channel_id=1, source_target_pairs={{0,24},{8,0},{16,8},{24,16},{1,25},{9,1},{17,9},{25,17},{2,26},{10... | collective-permute-start | bytes 2359304 | tf_op jit(solution)/shard_map/ppermute | solution.py:16
  131.6 3.4 %fusion.21 = f32[1024,768]{1,0:T(8,128)S(1)} fusion(bf16[1024,2048]{1,0:T(8,128)(2,1)S(1)} %bitcast.90, bf16[768,2048]{1,0:T(8,128)(2,1)S(1)} %bitcast.101), kind=kOutput, calls=%fused_computation.65 | convolution fusion | flops 3221225472 | bytes 10485760 | tf_op jit(solution)/shard_map/dot_general | solution.py:97
  135.1 3.4 %fusion.20 = f32[1024,768]{1,0:T(8,128)S(1)} fusion(bf16[1024,2048]{1,0:T(8,128)(2,1)S(1)} %bitcast.91, bf16[768,2048]{1,0:T(8,128)(2,1)S(1)} %bitcast.100), kind=kOutput, calls=%fused_computation.64 | convolution fusion | flops 3221225472 | bytes 10485760 | tf_op jit(solution)/shard_map/dot_general | solution.py:97
  140.7 3.5 %collective-permute-start.23 = (bf16[4,48,1024]{2,1,0:T(8,128)(2,1)S(1)}, bf16[4,48,1024]{2,1,0:T(8,128)(2,1)S(1)}, u32[]{:S(2)}, u32[]{:S(2)}) collective-permute-start(bf16[4,48,1024]{2,1,0:T(8,128)(2,1)S(1)} %slice.113), channel_id=1, source_target_pairs={{0,24},{8,0},{16,8},{24,16},{1,25},{9,1},{17,9},{25,17},{2,26},{10... | collective-permute-start | bytes 1179656 | tf_op jit(solution)/shard_map/ppermute | solution.py:25
  144.2 3.7 %multiply_convert_fusion = bf16[1024,768]{1,0:T(8,128)(2,1)S(1)} fusion(f32[1024,768]{1,0:T(8,128)S(1)} %fusion.21, bf16[1024,2048]{1,0:T(8,128)(2,1)S(1)} %bitcast.92, bf16[768,2048]{1,0:T(8,128)(2,1)S(1)} %bitcast.98), kind=kOutput, calls=%fused_computation.9 | convolution fusion | flops 3225944064 | bytes 12058624 | tf_op jit(solution)/shard_map/dot_general | solution.py:103
  147.9 3.7 %multiply_convert_fusion.1 = bf16[1024,768]{1,0:T(8,128)(2,1)S(1)} fusion(f32[1024,768]{1,0:T(8,128)S(1)} %fusion.20, bf16[1024,2048]{1,0:T(8,128)(2,1)S(1)} %bitcast.93, bf16[768,2048]{1,0:T(8,128)(2,1)S(1)} %bitcast.99), kind=kOutput, calls=%fused_computation.10 | convolution fusion | flops 3225944064 | bytes 12058624 | tf_op jit(solution)/shard_map/dot_general | solution.py:103
  153.1 3.2 %collective-permute-start.25 = (bf16[4,48,1024]{2,1,0:T(8,128)(2,1)S(1)}, bf16[4,48,1024]{2,1,0:T(8,128)(2,1)S(1)}, u32[]{:S(2)}, u32[]{:S(2)}) collective-permute-start(bf16[4,48,1024]{2,1,0:T(8,128)(2,1)S(1)} %slice.116), channel_id=1, source_target_pairs={{0,6},{2,0},{4,2},{6,4},{1,7},{3,1},{5,3},{7,5},{8,14},{10,8},{12,... | collective-permute-start | bytes 1179656 | tf_op jit(solution)/shard_map/ppermute | solution.py:25
  163.6 3.9 %convert_multiply_fusion.1 = f32[512,2048]{1,0:T(8,128)} fusion(f32[512,2048]{1,0:T(8,128)S(1)} %fusion.10, bf16[768,2048]{1,0:T(8,128)(2,1)S(1)} %bitcast.85, f32[512]{0:T(512)S(1)} %bitcast.112, bf16[1024,768]{1,0:T(8,128)(2,1)S(1)} %multiply_convert_fusion), kind=kOutput, calls=%fused_computation.5 | convolution fusion | flops 1614807040 | bytes 12322816 | tf_op jit(solution)/shard_map/dot_general | solution.py:110
  167.5 4.0 %fusion.13 = f32[512,2048]{1,0:T(8,128)S(1)} fusion(bf16[768,2048]{1,0:T(8,128)(2,1)} %bitcast.97, bf16[1024,768]{1,0:T(8,128)(2,1)} %copy-done.12), kind=kOutput, calls=%fused_computation.33 | convolution fusion | flops 1610612736 | bytes 8126464 | tf_op jit(solution)/shard_map/dot_general | solution.py:110
  184.0 10.3 %collective-permute-done.27 = bf16[128,2048]{1,0:T(8,128)(2,1)} collective-permute-done((bf16[128,2048]{1,0:T(8,128)(2,1)}, bf16[128,2048]{1,0:T(8,128)(2,1)}, u32[]{:S(2)}, u32[]{:S(2)}) %collective-permute-start.27) | collective-permute-done | bytes 524320 | tf_op jit(solution)/shard_map/ppermute | solution.py:125
  195.3 11.5 %collective-permute-done.28 = bf16[128,2048]{1,0:T(8,128)(2,1)} collective-permute-done((bf16[128,2048]{1,0:T(8,128)(2,1)S(1)}, bf16[128,2048]{1,0:T(8,128)(2,1)}, u32[]{:S(2)}, u32[]{:S(2)}) %collective-permute-start.28) | collective-permute-done | bytes 524320 | tf_op jit(solution)/shard_map/ppermute | solution.py:125
  (120 shorter events, 79.6 us)
Async XLA Ops:
  2.7 15.1 %collective-permute-start.5 = (bf16[3,48,2048]{2,1,0:T(8,128)(2,1)S(1)}, bf16[3,48,2048]{2,1,0:T(8,128)(2,1)S(1)}, u32[]{:S(2)}, u32[]{:S(2)}) collective-permute-start(bf16[3,48,2048]{2,1,0:T(8,128)(2,1)S(1)} %get-tuple-element.48), channel_id=1, source_target_pairs={{0,1},{1,0},{2,3},{3,2},{4,5},{5,4},{6,7},{7,6},{8,9},{9,8},{10,11... | collective-permute-start | bytes 1769480 | tf_op jit(solution)/shard_map/ppermute | solution.py:43
  4.4 17.1 %collective-permute-start.2 = (bf16[3,48,2048]{2,1,0:T(8,128)(2,1)S(1)}, bf16[3,48,2048]{2,1,0:T(8,128)(2,1)S(1)}, u32[]{:S(2)}, u32[]{:S(2)}) collective-permute-start(bf16[3,48,2048]{2,1,0:T(8,128)(2,1)S(1)} %bitcast.102), channel_id=1, source_target_pairs={{0,2},{2,4},{4,6},{6,0},{1,3},{3,5},{5,7},{7,1},{8,10},{10,12},{12... | collective-permute-start | bytes 1769480 | tf_op jit(solution)/shard_map/ppermute | solution.py:16
  6.4 16.8 %collective-permute-start.1 = (bf16[3,48,2048]{2,1,0:T(8,128)(2,1)S(1)}, bf16[3,48,2048]{2,1,0:T(8,128)(2,1)S(1)}, u32[]{:S(2)}, u32[]{:S(2)}) collective-permute-start(bf16[3,48,2048]{2,1,0:T(8,128)(2,1)S(1)} %bitcast.103), channel_id=1, source_target_pairs={{0,6},{2,0},{4,2},{6,4},{1,7},{3,1},{5,3},{7,5},{8,14},{10,8},{12,... | collective-permute-start | bytes 1769480 | tf_op jit(solution)/shard_map/ppermute | solution.py:16
  17.8 15.4 %collective-permute-start.7 = (bf16[3,48,2048]{2,1,0:T(8,128)(2,1)S(1)}, bf16[3,48,2048]{2,1,0:T(8,128)(2,1)S(1)}, u32[]{:S(2)}, u32[]{:S(2)}) collective-permute-start(bf16[3,48,2048]{2,1,0:T(8,128)(2,1)S(1)} %collective-permute-done.5), channel_id=1, source_target_pairs={{0,8},{8,16},{16,24},{24,0},{1,9},{9,17},{17,25},{25,1},{2,10},{10... | collective-permute-start | bytes 1769480 | tf_op jit(solution)/shard_map/ppermute | solution.py:16
  21.5 15.0 %collective-permute-start.3 = (bf16[3,48,1024]{2,1,0:T(8,128)(2,1)S(1)}, bf16[3,48,1024]{2,1,0:T(8,128)(2,1)S(1)}, u32[]{:S(2)}, u32[]{:S(2)}) collective-permute-start(bf16[3,48,1024]{2,1,0:T(8,128)(2,1)S(1)} %slice.125), channel_id=1, source_target_pairs={{0,2},{2,4},{4,6},{6,0},{1,3},{3,5},{5,7},{7,1},{8,10},{10,12},{12... | collective-permute-start | bytes 884744 | tf_op jit(solution)/shard_map/ppermute | solution.py:24
  44.0 33.8 %collective-permute-start.10 = (bf16[4,2,48,2048]{3,2,1,0:T(8,128)(2,1)}, bf16[4,2,48,2048]{3,2,1,0:T(8,128)(2,1)}, u32[]{:S(2)}, u32[]{:S(2)}) collective-permute-start(bf16[4,2,48,2048]{3,2,1,0:T(8,128)(2,1)} %get-tuple-element.44), channel_id=1, source_target_pairs={{0,24},{8,0},{16,8},{24,16},{1,25},{9,1},{17,9},{25,17},{2,26},{10... | collective-permute-start | bytes 4718600 | tf_op jit(solution)/shard_map/ppermute | solution.py:16
  47.1 36.5 %collective-permute-start.11 = (bf16[4,2,48,2048]{3,2,1,0:T(8,128)(2,1)}, bf16[4,2,48,2048]{3,2,1,0:T(8,128)(2,1)}, u32[]{:S(2)}, u32[]{:S(2)}) collective-permute-start(bf16[4,2,48,2048]{3,2,1,0:T(8,128)(2,1)} %get-tuple-element.44), channel_id=1, source_target_pairs={{0,8},{8,16},{16,24},{24,0},{1,9},{9,17},{17,25},{25,1},{2,10},{10... | collective-permute-start | bytes 4718600 | tf_op jit(solution)/shard_map/ppermute | solution.py:16
  49.2 37.7 %collective-permute-start.14 = (bf16[4,2,48,2048]{3,2,1,0:T(8,128)(2,1)}, bf16[4,2,48,2048]{3,2,1,0:T(8,128)(2,1)}, u32[]{:S(2)}, u32[]{:S(2)}) collective-permute-start(bf16[4,2,48,2048]{3,2,1,0:T(8,128)(2,1)} %get-tuple-element.42), channel_id=1, source_target_pairs={{0,6},{2,0},{4,2},{6,4},{1,7},{3,1},{5,3},{7,5},{8,14},{10,8},{12,... | collective-permute-start | bytes 4718600 | tf_op jit(solution)/shard_map/ppermute | solution.py:16
  53.4 39.8 %collective-permute-start.15 = (bf16[4,2,48,2048]{3,2,1,0:T(8,128)(2,1)}, bf16[4,2,48,2048]{3,2,1,0:T(8,128)(2,1)}, u32[]{:S(2)}, u32[]{:S(2)}) collective-permute-start(bf16[4,2,48,2048]{3,2,1,0:T(8,128)(2,1)} %get-tuple-element.42), channel_id=1, source_target_pairs={{0,2},{2,4},{4,6},{6,0},{1,3},{3,5},{5,7},{7,1},{8,10},{10,12},{12... | collective-permute-start | bytes 4718600 | tf_op jit(solution)/shard_map/ppermute | solution.py:16
  55.2 42.2 %all-to-all-start = ((bf16[4,144,2048]{2,1,0:T(8,128)(2,1)}), bf16[4,144,2048]{2,1,0:T(8,128)(2,1)S(1)}, u32[]{:S(2)}, u32[]{:S(2)}) async-start(bf16[4,144,2048]{2,1,0:T(8,128)(2,1)} %broadcast_in_dim.23), calls=%async_computation | async-start | bytes 4718592 | tf_op jit(solution)/shard_map/all_to_all | solution.py:67
  79.9 17.8 %collective-permute-start.13 = (bf16[4,2,48,1024]{3,2,1,0:T(8,128)(2,1)}, bf16[4,2,48,1024]{3,2,1,0:T(8,128)(2,1)}, u32[]{:S(2)}, u32[]{:S(2)}) collective-permute-start(bf16[4,2,48,1024]{3,2,1,0:T(8,128)(2,1)} %slice.130), channel_id=1, source_target_pairs={{0,24},{8,0},{16,8},{24,16},{1,25},{9,1},{17,9},{25,17},{2,26},{10... | collective-permute-start | bytes 2359304 | tf_op jit(solution)/shard_map/ppermute | solution.py:25
  85.7 16.3 %collective-permute-start.12 = (bf16[4,2,48,1024]{3,2,1,0:T(8,128)(2,1)}, bf16[4,2,48,1024]{3,2,1,0:T(8,128)(2,1)}, u32[]{:S(2)}, u32[]{:S(2)}) collective-permute-start(bf16[4,2,48,1024]{3,2,1,0:T(8,128)(2,1)} %slice.129), channel_id=1, source_target_pairs={{0,8},{8,16},{16,24},{24,0},{1,9},{9,17},{17,25},{25,1},{2,10},{10... | collective-permute-start | bytes 2359304 | tf_op jit(solution)/shard_map/ppermute | solution.py:24
  89.0 17.0 %collective-permute-start.17 = (bf16[4,2,48,1024]{3,2,1,0:T(8,128)(2,1)}, bf16[4,2,48,1024]{3,2,1,0:T(8,128)(2,1)}, u32[]{:S(2)}, u32[]{:S(2)}) collective-permute-start(bf16[4,2,48,1024]{3,2,1,0:T(8,128)(2,1)} %slice.132), channel_id=1, source_target_pairs={{0,6},{2,0},{4,2},{6,4},{1,7},{3,1},{5,3},{7,5},{8,14},{10,8},{12,... | collective-permute-start | bytes 2359304 | tf_op jit(solution)/shard_map/ppermute | solution.py:25
  95.3 16.1 %collective-permute-start.16 = (bf16[4,2,48,1024]{3,2,1,0:T(8,128)(2,1)}, bf16[4,2,48,1024]{3,2,1,0:T(8,128)(2,1)}, u32[]{:S(2)}, u32[]{:S(2)}) collective-permute-start(bf16[4,2,48,1024]{3,2,1,0:T(8,128)(2,1)} %slice.131), channel_id=1, source_target_pairs={{0,2},{2,4},{4,6},{6,0},{1,3},{3,5},{5,7},{7,1},{8,10},{10,12},{12... | collective-permute-start | bytes 2359304 | tf_op jit(solution)/shard_map/ppermute | solution.py:24
  97.5 30.4 %collective-permute-start = (bf16[4,144,2048]{2,1,0:T(8,128)(2,1)S(1)}, bf16[4,144,2048]{2,1,0:T(8,128)(2,1)}, u32[]{:S(2)}, u32[]{:S(2)}) collective-permute-start(bf16[4,144,2048]{2,1,0:T(8,128)(2,1)S(1)} %all-to-all-done), channel_id=1, source_target_pairs={{0,32},{32,0},{1,33},{33,1},{2,34},{34,2},{3,35},{35,3},{4,36},{36... | collective-permute-start | bytes 7077896 | tf_op jit(solution)/shard_map/ppermute | solution.py:68
  119.1 19.4 %collective-permute-start.19 = (bf16[4,48,2048]{2,1,0:T(8,128)(2,1)S(1)}, bf16[4,48,2048]{2,1,0:T(8,128)(2,1)}, u32[]{:S(2)}, u32[]{:S(2)}) collective-permute-start(bf16[4,48,2048]{2,1,0:T(8,128)(2,1)S(1)} %slice_bitcast_fusion.1), channel_id=1, source_target_pairs={{0,24},{8,0},{16,8},{24,16},{1,25},{9,1},{17,9},{25,17},{2,26},{10... | collective-permute-start | bytes 2359304 | tf_op jit(solution)/shard_map/ppermute | solution.py:16
  122.1 16.4 %collective-permute-start.18 = (bf16[4,48,2048]{2,1,0:T(8,128)(2,1)S(1)}, bf16[4,48,2048]{2,1,0:T(8,128)(2,1)}, u32[]{:S(2)}, u32[]{:S(2)}) collective-permute-start(bf16[4,48,2048]{2,1,0:T(8,128)(2,1)S(1)} %slice_bitcast_fusion.1), channel_id=1, source_target_pairs={{0,8},{8,16},{16,24},{24,0},{1,9},{9,17},{17,25},{25,1},{2,10},{10... | collective-permute-start | bytes 2359304 | tf_op jit(solution)/shard_map/ppermute | solution.py:16
  122.1 16.4 %collective-permute-start.21 = (bf16[4,48,2048]{2,1,0:T(8,128)(2,1)S(1)}, bf16[4,48,2048]{2,1,0:T(8,128)(2,1)S(1)}, u32[]{:S(2)}, u32[]{:S(2)}) collective-permute-start(bf16[4,48,2048]{2,1,0:T(8,128)(2,1)S(1)} %copy-done.4), channel_id=1, source_target_pairs={{0,6},{2,0},{4,2},{6,4},{1,7},{3,1},{5,3},{7,5},{8,14},{10,8},{12,... | collective-permute-start | bytes 2359304 | tf_op jit(solution)/shard_map/ppermute | solution.py:16
  122.1 16.4 %collective-permute-start.20 = (bf16[4,48,2048]{2,1,0:T(8,128)(2,1)S(1)}, bf16[4,48,2048]{2,1,0:T(8,128)(2,1)}, u32[]{:S(2)}, u32[]{:S(2)}) collective-permute-start(bf16[4,48,2048]{2,1,0:T(8,128)(2,1)S(1)} %copy-done.4), channel_id=1, source_target_pairs={{0,2},{2,4},{4,6},{6,0},{1,3},{3,5},{5,7},{7,1},{8,10},{10,12},{12... | collective-permute-start | bytes 2359304 | tf_op jit(solution)/shard_map/ppermute | solution.py:16
  140.6 15.7 %collective-permute-start.22 = (bf16[4,48,1024]{2,1,0:T(8,128)(2,1)S(1)}, bf16[4,48,1024]{2,1,0:T(8,128)(2,1)S(1)}, u32[]{:S(2)}, u32[]{:S(2)}) collective-permute-start(bf16[4,48,1024]{2,1,0:T(8,128)(2,1)S(1)} %slice.112), channel_id=1, source_target_pairs={{0,8},{8,16},{16,24},{24,0},{1,9},{9,17},{17,25},{25,1},{2,10},{10... | collective-permute-start | bytes 1179656 | tf_op jit(solution)/shard_map/ppermute | solution.py:24
  140.7 15.6 %collective-permute-start.23 = (bf16[4,48,1024]{2,1,0:T(8,128)(2,1)S(1)}, bf16[4,48,1024]{2,1,0:T(8,128)(2,1)S(1)}, u32[]{:S(2)}, u32[]{:S(2)}) collective-permute-start(bf16[4,48,1024]{2,1,0:T(8,128)(2,1)S(1)} %slice.113), channel_id=1, source_target_pairs={{0,24},{8,0},{16,8},{24,16},{1,25},{9,1},{17,9},{25,17},{2,26},{10... | collective-permute-start | bytes 1179656 | tf_op jit(solution)/shard_map/ppermute | solution.py:25
  178.8 15.6 %collective-permute-start.27 = (bf16[128,2048]{1,0:T(8,128)(2,1)}, bf16[128,2048]{1,0:T(8,128)(2,1)}, u32[]{:S(2)}, u32[]{:S(2)}) collective-permute-start(bf16[128,2048]{1,0:T(8,128)(2,1)} %get-tuple-element.45), channel_id=1, source_target_pairs={{0,1},{1,64},{64,65},{65,0},{2,3},{3,66},{66,67},{67,2},{4,5},{5,6... | collective-permute-start | bytes 1572872 | tf_op jit(solution)/shard_map/ppermute | solution.py:125
  180.3 14.9 %collective-permute-start.29 = (bf16[128,2048]{1,0:T(8,128)(2,1)S(1)}, bf16[128,2048]{1,0:T(8,128)(2,1)}, u32[]{:S(2)}, u32[]{:S(2)}) collective-permute-start(bf16[128,2048]{1,0:T(8,128)(2,1)S(1)} %get-tuple-element.46), channel_id=1, source_target_pairs={{0,65},{1,0},{64,1},{65,64},{2,67},{3,2},{66,3},{67,66},{4,69},{5,... | collective-permute-start | bytes 1572872 | tf_op jit(solution)/shard_map/ppermute | solution.py:125
  182.0 24.7 %collective-permute-start.28 = (bf16[128,2048]{1,0:T(8,128)(2,1)S(1)}, bf16[128,2048]{1,0:T(8,128)(2,1)}, u32[]{:S(2)}, u32[]{:S(2)}) collective-permute-start(bf16[128,2048]{1,0:T(8,128)(2,1)S(1)} %get-tuple-element.47), channel_id=1, source_target_pairs={{0,64},{1,65},{64,0},{65,1},{2,66},{3,67},{66,2},{67,3},{4,68},{5,... | collective-permute-start | bytes 1572872 | tf_op jit(solution)/shard_map/ppermute | solution.py:125
  (20 other events, 195.0 us)

commit v11 on v7

--- a/solution.py
+++ b/solution.py
@@ -18,13 +18,16 @@
 
 def far_hop(value, near, axis):
     from_minus, from_plus = near
-    half = value.shape[-1] // 2
+    split = 0 if value.shape[0] % 2 == 0 else value.ndim - 1
+    half = value.shape[split] // 2
     far = jnp.concatenate(
         [
-            lax.ppermute(from_minus[..., :half], axis, perm=AHEAD),
-            lax.ppermute(from_plus[..., half:], axis, perm=BEHIND),
+            lax.ppermute(lax.slice_in_dim(from_minus, 0, half, axis=split), axis, perm=AHEAD),
+            lax.ppermute(
+                lax.slice_in_dim(from_plus, half, 2 * half, axis=split), axis, perm=BEHIND
+            ),
         ],
-        axis=-1,
+        axis=split,
     )
     return jnp.stack([value, from_plus, far, from_minus])
 

time: 208 us -> 208 us (level)
  no operation moved by 1% of the time
where the time goes in v11:
time: 208 us; the launch traced here: 207 us
  waiting for transfers between devices  58 us (28%)
  starting transfers between devices  48.3 us (23%)
  local copies, waits for them, and re-layouts  32.2 us (15%)
  blocking collectives  30.9 us (15%)
  matrix products  21.6 us (10%)
  other arithmetic  15.7 us (8%)
    all_to_all x1, blocking collectives, per_device(): lax.all_to_all(partial, CHIPS, split_axis=0, concat_axis=0, tiled=True)  30.9 us
    ppermute x6, starting transfers between devices, far_hop(): lax.ppermute(lax.slice_in_dim(from_plus, half, 2 * half, axis=split), axi...  19.7 us
    ppermute x6, waiting for transfers between devices, first_hop(): lax.ppermute(value, axis, perm=BEHIND)  18.2 us
    ppermute x6, waiting for transfers between devices, far_hop(): lax.ppermute(lax.slice_in_dim(from_minus, 0, half, axis=split), axis, per...  16.5 us
    ppermute x6, starting transfers between devices, first_hop(): lax.ppermute(value, axis, perm=BEHIND)  14.1 us
    another operation x12, other arithmetic, far_hop(): return jnp.stack([value, from_plus, far, from_minus])  13.1 us
    ppermute x1, waiting for transfers between devices, expert_weights(): got = lax.ppermute(send, 'ylo', perm=SWAP)  9.29 us
    ppermute x6, waiting for transfers between devices, first_hop(): lax.ppermute(value, axis, perm=AHEAD)  8.22 us
  transfers between devices with their start and end apart: 28, of which 10 were waited for; matrix products, arithmetic and copies ran while one was open for 26% of the time, Pallas kernels for 0%

profile of v11, /device:TPU:0, one launch (start us, length us, event | category | flops | bytes accessed | tf_op | source)
XLA Modules:
  0.0 207.2 jit_solution(7291634234578973403)
XLA Ops:
  8.5 9.3 %collective-permute-done.5 = bf16[3,48,2048]{2,1,0:T(8,128)(2,1)S(1)} collective-permute-done((bf16[3,48,2048]{2,1,0:T(8,128)(2,1)S(1)}, bf16[3,48,2048]{2,1,0:T(8,128)(2,1)S(1)}, u32[]{:S(2)}, u32[]{:S(2)}) %collective-permute-start.5) | collective-permute-done | bytes 589856 | tf_op jit(solution)/shard_map/ppermute | solution.py:46
  25.4 7.7 %collective-permute-done.7 = bf16[3,48,2048]{2,1,0:T(8,128)(2,1)S(1)} collective-permute-done((bf16[3,48,2048]{2,1,0:T(8,128)(2,1)S(1)}, bf16[3,48,2048]{2,1,0:T(8,128)(2,1)S(1)}, u32[]{:S(2)}, u32[]{:S(2)}) %collective-permute-start.7) | collective-permute-done | bytes 589856 | tf_op jit(solution)/shard_map/ppermute | solution.py:16
  33.7 2.8 %collective-permute-start.9 = (bf16[3,48,1024]{2,1,0:T(8,128)(2,1)S(1)}, bf16[3,48,1024]{2,1,0:T(8,128)(2,1)S(1)}, u32[]{:S(2)}, u32[]{:S(2)}) collective-permute-start(bf16[3,48,1024]{2,1,0:T(8,128)(2,1)S(1)} %slice.128), channel_id=1, source_target_pairs={{0,24},{8,0},{16,8},{24,16},{1,25},{9,1},{17,9},{25,17},{2,26},{10... | collective-permute-start | bytes 884744 | tf_op jit(solution)/shard_map/ppermute | solution.py:26
  36.9 4.4 %collective-permute-done.8 = bf16[3,48,1024]{2,1,0:T(8,128)(2,1)S(1)} collective-permute-done((bf16[3,48,1024]{2,1,0:T(8,128)(2,1)S(1)}, bf16[3,48,1024]{2,1,0:T(8,128)(2,1)S(1)}, u32[]{:S(2)}, u32[]{:S(2)}) %collective-permute-start.8) | collective-permute-done | bytes 294944 | tf_op jit(solution)/shard_map/ppermute | solution.py:25
  44.0 3.1 %collective-permute-start.10 = (bf16[4,2,48,2048]{3,2,1,0:T(8,128)(2,1)}, bf16[4,2,48,2048]{3,2,1,0:T(8,128)(2,1)}, u32[]{:S(2)}, u32[]{:S(2)}) collective-permute-start(bf16[4,2,48,2048]{3,2,1,0:T(8,128)(2,1)} %get-tuple-element.44), channel_id=1, source_target_pairs={{0,24},{8,0},{16,8},{24,16},{1,25},{9,1},{17,9},{25,17},{2,26},{10... | collective-permute-start | bytes 4718600 | tf_op jit(solution)/shard_map/ppermute | solution.py:16
  49.3 4.2 %collective-permute-start.14 = (bf16[4,2,48,2048]{3,2,1,0:T(8,128)(2,1)}, bf16[4,2,48,2048]{3,2,1,0:T(8,128)(2,1)}, u32[]{:S(2)}, u32[]{:S(2)}) collective-permute-start(bf16[4,2,48,2048]{3,2,1,0:T(8,128)(2,1)} %get-tuple-element.42), channel_id=1, source_target_pairs={{0,6},{2,0},{4,2},{6,4},{1,7},{3,1},{5,3},{7,5},{8,14},{10,8},{12,... | collective-permute-start | bytes 4718600 | tf_op jit(solution)/shard_map/ppermute | solution.py:16
  55.2 4.5 %all-to-all-start = ((bf16[4,144,2048]{2,1,0:T(8,128)(2,1)}), bf16[4,144,2048]{2,1,0:T(8,128)(2,1)S(1)}, u32[]{:S(2)}, u32[]{:S(2)}) async-start(bf16[4,144,2048]{2,1,0:T(8,128)(2,1)} %broadcast_in_dim.23), calls=%async_computation | async-start | bytes 4718592 | tf_op jit(solution)/shard_map/all_to_all | solution.py:70
  59.7 18.1 %collective-permute-done.10 = bf16[4,2,48,2048]{3,2,1,0:T(8,128)(2,1)} collective-permute-done((bf16[4,2,48,2048]{3,2,1,0:T(8,128)(2,1)}, bf16[4,2,48,2048]{3,2,1,0:T(8,128)(2,1)}, u32[]{:S(2)}, u32[]{:S(2)}) %collective-permute-start.10) | collective-permute-done | bytes 1572896 | tf_op jit(solution)/shard_map/ppermute | solution.py:16
  79.9 3.7 %collective-permute-start.13 = (bf16[2,2,48,2048]{3,2,1,0:T(8,128)(2,1)}, bf16[2,2,48,2048]{3,2,1,0:T(8,128)(2,1)}, u32[]{:S(2)}, u32[]{:S(2)}) collective-permute-start(bf16[2,2,48,2048]{3,2,1,0:T(8,128)(2,1)} %slice.130), channel_id=1, source_target_pairs={{0,24},{8,0},{16,8},{24,16},{1,25},{9,1},{17,9},{25,17},{2,26},{10... | collective-permute-start | bytes 2359304 | tf_op jit(solution)/shard_map/ppermute | solution.py:26
  89.1 4.3 %collective-permute-start.17 = (bf16[2,2,48,2048]{3,2,1,0:T(8,128)(2,1)}, bf16[2,2,48,2048]{3,2,1,0:T(8,128)(2,1)}, u32[]{:S(2)}, u32[]{:S(2)}) collective-permute-start(bf16[2,2,48,2048]{3,2,1,0:T(8,128)(2,1)} %slice.132), channel_id=1, source_target_pairs={{0,6},{2,0},{4,2},{6,4},{1,7},{3,1},{5,3},{7,5},{8,14},{10,8},{12,... | collective-permute-start | bytes 2359304 | tf_op jit(solution)/shard_map/ppermute | solution.py:26
  97.9 4.2 %collective-permute-done.12 = bf16[2,2,48,2048]{3,2,1,0:T(8,128)(2,1)} collective-permute-done((bf16[2,2,48,2048]{3,2,1,0:T(8,128)(2,1)}, bf16[2,2,48,2048]{3,2,1,0:T(8,128)(2,1)}, u32[]{:S(2)}, u32[]{:S(2)}) %collective-permute-start.12) | collective-permute-done | bytes 786464 | tf_op jit(solution)/shard_map/ppermute | solution.py:25
  106.0 5.5 %collective-permute-done.16 = bf16[2,2,48,2048]{3,2,1,0:T(8,128)(2,1)} collective-permute-done((bf16[2,2,48,2048]{3,2,1,0:T(8,128)(2,1)}, bf16[2,2,48,2048]{3,2,1,0:T(8,128)(2,1)}, u32[]{:S(2)}, u32[]{:S(2)}) %collective-permute-start.16) | collective-permute-done | bytes 786464 | tf_op jit(solution)/shard_map/ppermute | solution.py:25
  113.1 3.1 %pad_maximum_fusion = bf16[4,4,2,48,2048]{4,3,2,1,0:T(8,128)(2,1)S(1)} fusion(bf16[1,4,2,48,2048]{4,3,2,1,0:T(8,128)(2,1)} %bitcast.17, bf16[1,4,2,48,2048]{4,3,2,1,0:T(8,128)(2,1)S(1)} %maximum_bitcast_fusion, bf16[1,4,2,48,2048]{4,3,2,1,0:T(8,128)(2,1)} %bitcast.15, bf16[1,4,2,48,2048]{4,3,2,1,0:T(8,128)(2,1)S(1)} %copy-done.2), kind=kLoop, calls=%fused_computation | loop fusion | flops 9437184 | bytes 12582912 | tf_op jit(solution)/shard_map/stack | solution.py:32
  116.2 3.0 %pad_maximum_fusion.1 = bf16[4,4,2,48,2048]{4,3,2,1,0:T(8,128)(2,1)S(1)} fusion(bf16[1,4,2,48,2048]{4,3,2,1,0:T(8,128)(2,1)} %bitcast.21, bf16[1,4,2,48,2048]{4,3,2,1,0:T(8,128)(2,1)S(1)} %maximum_bitcast_fusion.1, bf16[1,4,2,48,2048]{4,3,2,1,0:T(8,128)(2,1)} %bitcast.19, bf16[1,4,2,48,2048]{4,3,2,1,0:T(8,128)(2,1)S(1)} %copy-done.3), kind=kLoop, calls=%fused_computation.1 | loop fusion | flops 9437184 | bytes 12582912 | tf_op jit(solution)/shard_map/stack | solution.py:32
  119.2 3.0 %collective-permute-start.19 = (bf16[4,48,2048]{2,1,0:T(8,128)(2,1)S(1)}, bf16[4,48,2048]{2,1,0:T(8,128)(2,1)}, u32[]{:S(2)}, u32[]{:S(2)}) collective-permute-start(bf16[4,48,2048]{2,1,0:T(8,128)(2,1)S(1)} %slice_bitcast_fusion.1), channel_id=1, source_target_pairs={{0,24},{8,0},{16,8},{24,16},{1,25},{9,1},{17,9},{25,17},{2,26},{10... | collective-permute-start | bytes 2359304 | tf_op jit(solution)/shard_map/ppermute | solution.py:16
  124.3 2.6 %fusion.15 = (bf16[1,4,4,48,2048]{4,3,0,2,1:T(8,128)(2,1)}, bf16[1,4,4,48,2048]{4,3,0,2,1:T(8,128)(2,1)S(1)}) fusion(bf16[2,4,4,48,2048]{4,3,0,2,1:T(8,128)(2,1)S(1)} %bitcast.79), kind=kLoop, calls=%fused_computation.55 | loop fusion | bytes 12582912 | tf_op jit(solution)/shard_map/slice | solution.py:100
  131.7 3.4 %fusion.18 = f32[1024,768]{1,0:T(8,128)S(1)} fusion(bf16[1024,2048]{1,0:T(8,128)(2,1)S(1)} %bitcast.81, bf16[768,2048]{1,0:T(8,128)(2,1)S(1)} %bitcast.93), kind=kOutput, calls=%fused_computation.58 | convolution fusion | flops 3221225472 | bytes 10485760 | tf_op jit(solution)/shard_map/dot_general | solution.py:100
  135.2 3.4 %fusion.17 = f32[1024,768]{1,0:T(8,128)S(1)} fusion(bf16[1024,2048]{1,0:T(8,128)(2,1)S(1)} %bitcast.82, bf16[768,2048]{1,0:T(8,128)(2,1)S(1)} %bitcast.92), kind=kOutput, calls=%fused_computation.57 | convolution fusion | flops 3221225472 | bytes 10485760 | tf_op jit(solution)/shard_map/dot_general | solution.py:100
  140.9 3.5 %collective-permute-start.23 = (bf16[2,48,2048]{2,1,0:T(8,128)(2,1)S(1)}, bf16[2,48,2048]{2,1,0:T(8,128)(2,1)S(1)}, u32[]{:S(2)}, u32[]{:S(2)}) collective-permute-start(bf16[2,48,2048]{2,1,0:T(8,128)(2,1)S(1)} %slice.113), channel_id=1, source_target_pairs={{0,24},{8,0},{16,8},{24,16},{1,25},{9,1},{17,9},{25,17},{2,26},{10... | collective-permute-start | bytes 1179656 | tf_op jit(solution)/shard_map/ppermute | solution.py:26
  144.4 3.7 %multiply_convert_fusion = bf16[1024,768]{1,0:T(8,128)(2,1)S(1)} fusion(f32[1024,768]{1,0:T(8,128)S(1)} %fusion.18, bf16[1024,2048]{1,0:T(8,128)(2,1)S(1)} %bitcast.83, bf16[768,2048]{1,0:T(8,128)(2,1)S(1)} %bitcast.90), kind=kOutput, calls=%fused_computation.9 | convolution fusion | flops 3225944064 | bytes 12058624 | tf_op jit(solution)/shard_map/dot_general | solution.py:106
  148.1 3.7 %multiply_convert_fusion.1 = bf16[1024,768]{1,0:T(8,128)(2,1)S(1)} fusion(f32[1024,768]{1,0:T(8,128)S(1)} %fusion.17, bf16[1024,2048]{1,0:T(8,128)(2,1)S(1)} %bitcast.84, bf16[768,2048]{1,0:T(8,128)(2,1)S(1)} %bitcast.91), kind=kOutput, calls=%fused_computation.10 | convolution fusion | flops 3225944064 | bytes 12058624 | tf_op jit(solution)/shard_map/dot_general | solution.py:106
  154.0 3.2 %collective-permute-start.25 = (bf16[2,48,2048]{2,1,0:T(8,128)(2,1)S(1)}, bf16[2,48,2048]{2,1,0:T(8,128)(2,1)S(1)}, u32[]{:S(2)}, u32[]{:S(2)}) collective-permute-start(bf16[2,48,2048]{2,1,0:T(8,128)(2,1)S(1)} %slice.116), channel_id=1, source_target_pairs={{0,6},{2,0},{4,2},{6,4},{1,7},{3,1},{5,3},{7,5},{8,14},{10,8},{12,... | collective-permute-start | bytes 1179656 | tf_op jit(solution)/shard_map/ppermute | solution.py:26
  170.5 3.5 %collective-permute-done.26 = f32[4,128,2048]{2,1,0:T(8,128)S(1)} collective-permute-done((f32[4,128,2048]{2,1,0:T(8,128)S(1)}, f32[4,128,2048]{2,1,0:T(8,128)S(1)}, u32[]{:S(2)}, u32[]{:S(2)}) %collective-permute-start.26) | collective-permute-done | bytes 4194336 | tf_op jit(solution)/shard_map/ppermute | solution.py:121
  175.0 30.9 %all_to_all.10 = bf16[4,128,2048]{2,1,0:T(8,128)(2,1)S(1)} all-to-all(bf16[4,128,2048]{2,1,0:T(8,128)(2,1)S(1)} %add_convert_fusion), channel_id=1, replica_groups=mesh['yhi'=2,'core'=2,'x'=4,'z'=4,'ylo'=2] {'yhi','ylo'}, dimensions={0} | all-to-all | bytes 4194304 | tf_op jit(solution)/shard_map/all_to_all | solution.py:123
  (106 shorter events, 67.7 us)
Async XLA Ops:
  2.7 15.1 %collective-permute-start.5 = (bf16[3,48,2048]{2,1,0:T(8,128)(2,1)S(1)}, bf16[3,48,2048]{2,1,0:T(8,128)(2,1)S(1)}, u32[]{:S(2)}, u32[]{:S(2)}) collective-permute-start(bf16[3,48,2048]{2,1,0:T(8,128)(2,1)S(1)} %get-tuple-element.45), channel_id=1, source_target_pairs={{0,1},{1,0},{2,3},{3,2},{4,5},{5,4},{6,7},{7,6},{8,9},{9,8},{10,11... | collective-permute-start | bytes 1769480 | tf_op jit(solution)/shard_map/ppermute | solution.py:46
  4.4 17.1 %collective-permute-start.2 = (bf16[3,48,2048]{2,1,0:T(8,128)(2,1)S(1)}, bf16[3,48,2048]{2,1,0:T(8,128)(2,1)S(1)}, u32[]{:S(2)}, u32[]{:S(2)}) collective-permute-start(bf16[3,48,2048]{2,1,0:T(8,128)(2,1)S(1)} %bitcast.94), channel_id=1, source_target_pairs={{0,2},{2,4},{4,6},{6,0},{1,3},{3,5},{5,7},{7,1},{8,10},{10,12},{12... | collective-permute-start | bytes 1769480 | tf_op jit(solution)/shard_map/ppermute | solution.py:16
  6.4 16.8 %collective-permute-start.1 = (bf16[3,48,2048]{2,1,0:T(8,128)(2,1)S(1)}, bf16[3,48,2048]{2,1,0:T(8,128)(2,1)S(1)}, u32[]{:S(2)}, u32[]{:S(2)}) collective-permute-start(bf16[3,48,2048]{2,1,0:T(8,128)(2,1)S(1)} %bitcast.95), channel_id=1, source_target_pairs={{0,6},{2,0},{4,2},{6,4},{1,7},{3,1},{5,3},{7,5},{8,14},{10,8},{12,... | collective-permute-start | bytes 1769480 | tf_op jit(solution)/shard_map/ppermute | solution.py:16
  17.8 15.4 %collective-permute-start.7 = (bf16[3,48,2048]{2,1,0:T(8,128)(2,1)S(1)}, bf16[3,48,2048]{2,1,0:T(8,128)(2,1)S(1)}, u32[]{:S(2)}, u32[]{:S(2)}) collective-permute-start(bf16[3,48,2048]{2,1,0:T(8,128)(2,1)S(1)} %collective-permute-done.5), channel_id=1, source_target_pairs={{0,8},{8,16},{16,24},{24,0},{1,9},{9,17},{17,25},{25,1},{2,10},{10... | collective-permute-start | bytes 1769480 | tf_op jit(solution)/shard_map/ppermute | solution.py:16
  19.4 14.3 %collective-permute-start.6 = (bf16[3,48,2048]{2,1,0:T(8,128)(2,1)S(1)}, bf16[3,48,2048]{2,1,0:T(8,128)(2,1)S(1)}, u32[]{:S(2)}, u32[]{:S(2)}) collective-permute-start(bf16[3,48,2048]{2,1,0:T(8,128)(2,1)S(1)} %collective-permute-done.5), channel_id=1, source_target_pairs={{0,24},{8,0},{16,8},{24,16},{1,25},{9,1},{17,9},{25,17},{2,26},{10... | collective-permute-start | bytes 1769480 | tf_op jit(solution)/shard_map/ppermute | solution.py:16
  21.5 15.0 %collective-permute-start.3 = (bf16[3,48,1024]{2,1,0:T(8,128)(2,1)S(1)}, bf16[3,48,1024]{2,1,0:T(8,128)(2,1)S(1)}, u32[]{:S(2)}, u32[]{:S(2)}) collective-permute-start(bf16[3,48,1024]{2,1,0:T(8,128)(2,1)S(1)} %slice.125), channel_id=1, source_target_pairs={{0,2},{2,4},{4,6},{6,0},{1,3},{3,5},{5,7},{7,1},{8,10},{10,12},{12... | collective-permute-start | bytes 884744 | tf_op jit(solution)/shard_map/ppermute | solution.py:25
  23.2 13.4 %collective-permute-start.4 = (bf16[3,48,1024]{2,1,0:T(8,128)(2,1)S(1)}, bf16[3,48,1024]{2,1,0:T(8,128)(2,1)S(1)}, u32[]{:S(2)}, u32[]{:S(2)}) collective-permute-start(bf16[3,48,1024]{2,1,0:T(8,128)(2,1)S(1)} %slice.126), channel_id=1, source_target_pairs={{0,6},{2,0},{4,2},{6,4},{1,7},{3,1},{5,3},{7,5},{8,14},{10,8},{12,... | collective-permute-start | bytes 884744 | tf_op jit(solution)/shard_map/ppermute | solution.py:26
  44.0 33.8 %collective-permute-start.10 = (bf16[4,2,48,2048]{3,2,1,0:T(8,128)(2,1)}, bf16[4,2,48,2048]{3,2,1,0:T(8,128)(2,1)}, u32[]{:S(2)}, u32[]{:S(2)}) collective-permute-start(bf16[4,2,48,2048]{3,2,1,0:T(8,128)(2,1)} %get-tuple-element.44), channel_id=1, source_target_pairs={{0,24},{8,0},{16,8},{24,16},{1,25},{9,1},{17,9},{25,17},{2,26},{10... | collective-permute-start | bytes 4718600 | tf_op jit(solution)/shard_map/ppermute | solution.py:16
  47.1 36.5 %collective-permute-start.11 = (bf16[4,2,48,2048]{3,2,1,0:T(8,128)(2,1)}, bf16[4,2,48,2048]{3,2,1,0:T(8,128)(2,1)}, u32[]{:S(2)}, u32[]{:S(2)}) collective-permute-start(bf16[4,2,48,2048]{3,2,1,0:T(8,128)(2,1)} %get-tuple-element.44), channel_id=1, source_target_pairs={{0,8},{8,16},{16,24},{24,0},{1,9},{9,17},{17,25},{25,1},{2,10},{10... | collective-permute-start | bytes 4718600 | tf_op jit(solution)/shard_map/ppermute | solution.py:16
  49.3 37.7 %collective-permute-start.14 = (bf16[4,2,48,2048]{3,2,1,0:T(8,128)(2,1)}, bf16[4,2,48,2048]{3,2,1,0:T(8,128)(2,1)}, u32[]{:S(2)}, u32[]{:S(2)}) collective-permute-start(bf16[4,2,48,2048]{3,2,1,0:T(8,128)(2,1)} %get-tuple-element.42), channel_id=1, source_target_pairs={{0,6},{2,0},{4,2},{6,4},{1,7},{3,1},{5,3},{7,5},{8,14},{10,8},{12,... | collective-permute-start | bytes 4718600 | tf_op jit(solution)/shard_map/ppermute | solution.py:16
  53.5 39.8 %collective-permute-start.15 = (bf16[4,2,48,2048]{3,2,1,0:T(8,128)(2,1)}, bf16[4,2,48,2048]{3,2,1,0:T(8,128)(2,1)}, u32[]{:S(2)}, u32[]{:S(2)}) collective-permute-start(bf16[4,2,48,2048]{3,2,1,0:T(8,128)(2,1)} %get-tuple-element.42), channel_id=1, source_target_pairs={{0,2},{2,4},{4,6},{6,0},{1,3},{3,5},{5,7},{7,1},{8,10},{10,12},{12... | collective-permute-start | bytes 4718600 | tf_op jit(solution)/shard_map/ppermute | solution.py:16
  55.2 42.3 %all-to-all-start = ((bf16[4,144,2048]{2,1,0:T(8,128)(2,1)}), bf16[4,144,2048]{2,1,0:T(8,128)(2,1)S(1)}, u32[]{:S(2)}, u32[]{:S(2)}) async-start(bf16[4,144,2048]{2,1,0:T(8,128)(2,1)} %broadcast_in_dim.23), calls=%async_computation | async-start | bytes 4718592 | tf_op jit(solution)/shard_map/all_to_all | solution.py:70
  79.9 17.9 %collective-permute-start.13 = (bf16[2,2,48,2048]{3,2,1,0:T(8,128)(2,1)}, bf16[2,2,48,2048]{3,2,1,0:T(8,128)(2,1)}, u32[]{:S(2)}, u32[]{:S(2)}) collective-permute-start(bf16[2,2,48,2048]{3,2,1,0:T(8,128)(2,1)} %slice.130), channel_id=1, source_target_pairs={{0,24},{8,0},{16,8},{24,16},{1,25},{9,1},{17,9},{25,17},{2,26},{10... | collective-permute-start | bytes 2359304 | tf_op jit(solution)/shard_map/ppermute | solution.py:26
  85.7 16.3 %collective-permute-start.12 = (bf16[2,2,48,2048]{3,2,1,0:T(8,128)(2,1)}, bf16[2,2,48,2048]{3,2,1,0:T(8,128)(2,1)}, u32[]{:S(2)}, u32[]{:S(2)}) collective-permute-start(bf16[2,2,48,2048]{3,2,1,0:T(8,128)(2,1)} %slice.129), channel_id=1, source_target_pairs={{0,8},{8,16},{16,24},{24,0},{1,9},{9,17},{17,25},{25,1},{2,10},{10... | collective-permute-start | bytes 2359304 | tf_op jit(solution)/shard_map/ppermute | solution.py:25
  89.1 17.0 %collective-permute-start.17 = (bf16[2,2,48,2048]{3,2,1,0:T(8,128)(2,1)}, bf16[2,2,48,2048]{3,2,1,0:T(8,128)(2,1)}, u32[]{:S(2)}, u32[]{:S(2)}) collective-permute-start(bf16[2,2,48,2048]{3,2,1,0:T(8,128)(2,1)} %slice.132), channel_id=1, source_target_pairs={{0,6},{2,0},{4,2},{6,4},{1,7},{3,1},{5,3},{7,5},{8,14},{10,8},{12,... | collective-permute-start | bytes 2359304 | tf_op jit(solution)/shard_map/ppermute | solution.py:26
  95.4 16.1 %collective-permute-start.16 = (bf16[2,2,48,2048]{3,2,1,0:T(8,128)(2,1)}, bf16[2,2,48,2048]{3,2,1,0:T(8,128)(2,1)}, u32[]{:S(2)}, u32[]{:S(2)}) collective-permute-start(bf16[2,2,48,2048]{3,2,1,0:T(8,128)(2,1)} %slice.131), channel_id=1, source_target_pairs={{0,2},{2,4},{4,6},{6,0},{1,3},{3,5},{5,7},{7,1},{8,10},{10,12},{12... | collective-permute-start | bytes 2359304 | tf_op jit(solution)/shard_map/ppermute | solution.py:25
  97.6 30.4 %collective-permute-start = (bf16[4,144,2048]{2,1,0:T(8,128)(2,1)S(1)}, bf16[4,144,2048]{2,1,0:T(8,128)(2,1)}, u32[]{:S(2)}, u32[]{:S(2)}) collective-permute-start(bf16[4,144,2048]{2,1,0:T(8,128)(2,1)S(1)} %all-to-all-done), channel_id=1, source_target_pairs={{0,32},{32,0},{1,33},{33,1},{2,34},{34,2},{3,35},{35,3},{4,36},{36... | collective-permute-start | bytes 7077896 | tf_op jit(solution)/shard_map/ppermute | solution.py:71
  119.2 19.5 %collective-permute-start.19 = (bf16[4,48,2048]{2,1,0:T(8,128)(2,1)S(1)}, bf16[4,48,2048]{2,1,0:T(8,128)(2,1)}, u32[]{:S(2)}, u32[]{:S(2)}) collective-permute-start(bf16[4,48,2048]{2,1,0:T(8,128)(2,1)S(1)} %slice_bitcast_fusion.1), channel_id=1, source_target_pairs={{0,24},{8,0},{16,8},{24,16},{1,25},{9,1},{17,9},{25,17},{2,26},{10... | collective-permute-start | bytes 2359304 | tf_op jit(solution)/shard_map/ppermute | solution.py:16
  122.3 16.4 %collective-permute-start.18 = (bf16[4,48,2048]{2,1,0:T(8,128)(2,1)S(1)}, bf16[4,48,2048]{2,1,0:T(8,128)(2,1)}, u32[]{:S(2)}, u32[]{:S(2)}) collective-permute-start(bf16[4,48,2048]{2,1,0:T(8,128)(2,1)S(1)} %slice_bitcast_fusion.1), channel_id=1, source_target_pairs={{0,8},{8,16},{16,24},{24,0},{1,9},{9,17},{17,25},{25,1},{2,10},{10... | collective-permute-start | bytes 2359304 | tf_op jit(solution)/shard_map/ppermute | solution.py:16
  122.3 16.5 %collective-permute-start.21 = (bf16[4,48,2048]{2,1,0:T(8,128)(2,1)S(1)}, bf16[4,48,2048]{2,1,0:T(8,128)(2,1)}, u32[]{:S(2)}, u32[]{:S(2)}) collective-permute-start(bf16[4,48,2048]{2,1,0:T(8,128)(2,1)S(1)} %copy-done.4), channel_id=1, source_target_pairs={{0,6},{2,0},{4,2},{6,4},{1,7},{3,1},{5,3},{7,5},{8,14},{10,8},{12,... | collective-permute-start | bytes 2359304 | tf_op jit(solution)/shard_map/ppermute | solution.py:16
  122.3 16.5 %collective-permute-start.20 = (bf16[4,48,2048]{2,1,0:T(8,128)(2,1)S(1)}, bf16[4,48,2048]{2,1,0:T(8,128)(2,1)}, u32[]{:S(2)}, u32[]{:S(2)}) collective-permute-start(bf16[4,48,2048]{2,1,0:T(8,128)(2,1)S(1)} %copy-done.4), channel_id=1, source_target_pairs={{0,2},{2,4},{4,6},{6,0},{1,3},{3,5},{5,7},{7,1},{8,10},{10,12},{12... | collective-permute-start | bytes 2359304 | tf_op jit(solution)/shard_map/ppermute | solution.py:16
  140.8 16.4 %collective-permute-start.22 = (bf16[2,48,2048]{2,1,0:T(8,128)(2,1)S(1)}, bf16[2,48,2048]{2,1,0:T(8,128)(2,1)S(1)}, u32[]{:S(2)}, u32[]{:S(2)}) collective-permute-start(bf16[2,48,2048]{2,1,0:T(8,128)(2,1)S(1)} %slice.112), channel_id=1, source_target_pairs={{0,8},{8,16},{16,24},{24,0},{1,9},{9,17},{17,25},{25,1},{2,10},{10... | collective-permute-start | bytes 1179656 | tf_op jit(solution)/shard_map/ppermute | solution.py:25
  140.9 16.3 %collective-permute-start.23 = (bf16[2,48,2048]{2,1,0:T(8,128)(2,1)S(1)}, bf16[2,48,2048]{2,1,0:T(8,128)(2,1)S(1)}, u32[]{:S(2)}, u32[]{:S(2)}) collective-permute-start(bf16[2,48,2048]{2,1,0:T(8,128)(2,1)S(1)} %slice.113), channel_id=1, source_target_pairs={{0,24},{8,0},{16,8},{24,16},{1,25},{9,1},{17,9},{25,17},{2,26},{10... | collective-permute-start | bytes 1179656 | tf_op jit(solution)/shard_map/ppermute | solution.py:26
  153.9 9.1 %collective-permute-start.24 = (bf16[2,48,2048]{2,1,0:T(8,128)(2,1)S(1)}, bf16[2,48,2048]{2,1,0:T(8,128)(2,1)S(1)}, u32[]{:S(2)}, u32[]{:S(2)}) collective-permute-start(bf16[2,48,2048]{2,1,0:T(8,128)(2,1)S(1)} %slice.115), channel_id=1, source_target_pairs={{0,2},{2,4},{4,6},{6,0},{1,3},{3,5},{5,7},{7,1},{8,10},{10,12},{12... | collective-permute-start | bytes 1179656 | tf_op jit(solution)/shard_map/ppermute | solution.py:25
  (13 other events, 128.7 us)

commit v12 on v7

--- a/solution.py
+++ b/solution.py
@@ -115,8 +115,8 @@
     half = chips * token_count
     theirs = down(hiddens, half, 2 * half)
     hiddens, theirs = lax.optimization_barrier((hiddens, theirs))
-    partner = lax.ppermute(theirs, "core", perm=SWAP)
-    partial = (down(hiddens, 0, half) + partner).astype(jnp.bfloat16)
+    partner = lax.ppermute(theirs.astype(jnp.bfloat16), "core", perm=SWAP)
+    partial = (down(hiddens, 0, half) + partner.astype(jnp.float32)).astype(jnp.bfloat16)
     back = lax.all_to_all(partial, CHIPS, split_axis=0, concat_axis=0, tiled=True)
     mixed = jnp.sum(back.astype(jnp.float32), axis=0)
     return mixed.astype(jnp.bfloat16)

time: 208 us -> 205 us (0.986)
  waiting for transfers between devices: 58 us -> 55 us
    ppermute x1, waiting for transfers between devices: 3.49 us -> 0.44 us  [per_device(): partner = lax.ppermute(theirs.astype(jnp.bfloat16), 'core', perm=SWAP)]
  transfers between devices with their start and end apart: 28 -> 28, of which waited for: 10 -> 10; matrix products, arithmetic and copies ran while one was open for 26% -> 27% of each run, Pallas kernels for 0% -> 0%
where the time goes in v12:
time: 205 us; the launch traced here: 204 us
  waiting for transfers between devices  55 us (27%)
  starting transfers between devices  48.3 us (24%)
  local copies, waits for them, and re-layouts  32.1 us (16%)
  blocking collectives  30.9 us (15%)
  matrix products  21.7 us (11%)
  other arithmetic  15.3 us (7%)
    all_to_all x1, blocking collectives, per_device(): lax.all_to_all(partial, CHIPS, split_axis=0, concat_axis=0, tiled=True)  30.9 us
    ppermute x6, starting transfers between devices, far_hop(): lax.ppermute(from_plus[..., half:], axis, perm=BEHIND)  19.7 us
    ppermute x6, waiting for transfers between devices, first_hop(): lax.ppermute(value, axis, perm=BEHIND)  18.2 us
    ppermute x6, waiting for transfers between devices, far_hop(): lax.ppermute(from_minus[..., :half], axis, perm=AHEAD)  16.5 us
    ppermute x6, starting transfers between devices, first_hop(): lax.ppermute(value, axis, perm=BEHIND)  14.1 us
    another operation x12, other arithmetic, far_hop(): return jnp.stack([value, from_plus, far, from_minus])  13 us
    ppermute x1, waiting for transfers between devices, expert_weights(): got = lax.ppermute(send, 'ylo', perm=SWAP)  9.29 us
    ppermute x6, waiting for transfers between devices, first_hop(): lax.ppermute(value, axis, perm=AHEAD)  8.22 us
  transfers between devices with their start and end apart: 28, of which 10 were waited for; matrix products, arithmetic and copies ran while one was open for 27% of the time, Pallas kernels for 0%

profile of v12, /device:TPU:0, one launch (start us, length us, event | category | flops | bytes accessed | tf_op | source)
XLA Modules:
  0.0 203.8 jit_solution(269018454404014894)
XLA Ops:
  8.5 9.3 %collective-permute-done.5 = bf16[3,48,2048]{2,1,0:T(8,128)(2,1)S(1)} collective-permute-done((bf16[3,48,2048]{2,1,0:T(8,128)(2,1)S(1)}, bf16[3,48,2048]{2,1,0:T(8,128)(2,1)S(1)}, u32[]{:S(2)}, u32[]{:S(2)}) %collective-permute-start.5) | collective-permute-done | bytes 589856 | tf_op jit(solution)/shard_map/ppermute | solution.py:43
  25.4 7.7 %collective-permute-done.7 = bf16[3,48,2048]{2,1,0:T(8,128)(2,1)S(1)} collective-permute-done((bf16[3,48,2048]{2,1,0:T(8,128)(2,1)S(1)}, bf16[3,48,2048]{2,1,0:T(8,128)(2,1)S(1)}, u32[]{:S(2)}, u32[]{:S(2)}) %collective-permute-start.7) | collective-permute-done | bytes 589856 | tf_op jit(solution)/shard_map/ppermute | solution.py:16
  33.7 2.8 %collective-permute-start.9 = (bf16[3,48,1024]{2,1,0:T(8,128)(2,1)S(1)}, bf16[3,48,1024]{2,1,0:T(8,128)(2,1)S(1)}, u32[]{:S(2)}, u32[]{:S(2)}) collective-permute-start(bf16[3,48,1024]{2,1,0:T(8,128)(2,1)S(1)} %slice.128), channel_id=1, source_target_pairs={{0,24},{8,0},{16,8},{24,16},{1,25},{9,1},{17,9},{25,17},{2,26},{10... | collective-permute-start | bytes 884744 | tf_op jit(solution)/shard_map/ppermute | solution.py:25
  36.9 4.4 %collective-permute-done.8 = bf16[3,48,1024]{2,1,0:T(8,128)(2,1)S(1)} collective-permute-done((bf16[3,48,1024]{2,1,0:T(8,128)(2,1)S(1)}, bf16[3,48,1024]{2,1,0:T(8,128)(2,1)S(1)}, u32[]{:S(2)}, u32[]{:S(2)}) %collective-permute-start.8) | collective-permute-done | bytes 294944 | tf_op jit(solution)/shard_map/ppermute | solution.py:24
  44.0 3.1 %collective-permute-start.10 = (bf16[4,2,48,2048]{3,2,1,0:T(8,128)(2,1)}, bf16[4,2,48,2048]{3,2,1,0:T(8,128)(2,1)}, u32[]{:S(2)}, u32[]{:S(2)}) collective-permute-start(bf16[4,2,48,2048]{3,2,1,0:T(8,128)(2,1)} %get-tuple-element.44), channel_id=1, source_target_pairs={{0,24},{8,0},{16,8},{24,16},{1,25},{9,1},{17,9},{25,17},{2,26},{10... | collective-permute-start | bytes 4718600 | tf_op jit(solution)/shard_map/ppermute | solution.py:16
  49.3 4.2 %collective-permute-start.14 = (bf16[4,2,48,2048]{3,2,1,0:T(8,128)(2,1)}, bf16[4,2,48,2048]{3,2,1,0:T(8,128)(2,1)}, u32[]{:S(2)}, u32[]{:S(2)}) collective-permute-start(bf16[4,2,48,2048]{3,2,1,0:T(8,128)(2,1)} %get-tuple-element.42), channel_id=1, source_target_pairs={{0,6},{2,0},{4,2},{6,4},{1,7},{3,1},{5,3},{7,5},{8,14},{10,8},{12,... | collective-permute-start | bytes 4718600 | tf_op jit(solution)/shard_map/ppermute | solution.py:16
  55.2 4.5 %all-to-all-start = ((bf16[4,144,2048]{2,1,0:T(8,128)(2,1)}), bf16[4,144,2048]{2,1,0:T(8,128)(2,1)S(1)}, u32[]{:S(2)}, u32[]{:S(2)}) async-start(bf16[4,144,2048]{2,1,0:T(8,128)(2,1)} %broadcast_in_dim.23), calls=%async_computation | async-start | bytes 4718592 | tf_op jit(solution)/shard_map/all_to_all | solution.py:67
  59.7 18.1 %collective-permute-done.10 = bf16[4,2,48,2048]{3,2,1,0:T(8,128)(2,1)} collective-permute-done((bf16[4,2,48,2048]{3,2,1,0:T(8,128)(2,1)}, bf16[4,2,48,2048]{3,2,1,0:T(8,128)(2,1)}, u32[]{:S(2)}, u32[]{:S(2)}) %collective-permute-start.10) | collective-permute-done | bytes 1572896 | tf_op jit(solution)/shard_map/ppermute | solution.py:16
  79.9 3.7 %collective-permute-start.13 = (bf16[4,2,48,1024]{3,2,1,0:T(8,128)(2,1)}, bf16[4,2,48,1024]{3,2,1,0:T(8,128)(2,1)}, u32[]{:S(2)}, u32[]{:S(2)}) collective-permute-start(bf16[4,2,48,1024]{3,2,1,0:T(8,128)(2,1)} %slice.130), channel_id=1, source_target_pairs={{0,24},{8,0},{16,8},{24,16},{1,25},{9,1},{17,9},{25,17},{2,26},{10... | collective-permute-start | bytes 2359304 | tf_op jit(solution)/shard_map/ppermute | solution.py:25
  89.0 4.3 %collective-permute-start.17 = (bf16[4,2,48,1024]{3,2,1,0:T(8,128)(2,1)}, bf16[4,2,48,1024]{3,2,1,0:T(8,128)(2,1)}, u32[]{:S(2)}, u32[]{:S(2)}) collective-permute-start(bf16[4,2,48,1024]{3,2,1,0:T(8,128)(2,1)} %slice.132), channel_id=1, source_target_pairs={{0,6},{2,0},{4,2},{6,4},{1,7},{3,1},{5,3},{7,5},{8,14},{10,8},{12,... | collective-permute-start | bytes 2359304 | tf_op jit(solution)/shard_map/ppermute | solution.py:25
  97.8 4.3 %collective-permute-done.12 = bf16[4,2,48,1024]{3,2,1,0:T(8,128)(2,1)} collective-permute-done((bf16[4,2,48,1024]{3,2,1,0:T(8,128)(2,1)}, bf16[4,2,48,1024]{3,2,1,0:T(8,128)(2,1)}, u32[]{:S(2)}, u32[]{:S(2)}) %collective-permute-start.12) | collective-permute-done | bytes 786464 | tf_op jit(solution)/shard_map/ppermute | solution.py:24
  103.5 2.4 %collective-permute-done.17 = bf16[4,2,48,1024]{3,2,1,0:T(8,128)(2,1)} collective-permute-done((bf16[4,2,48,1024]{3,2,1,0:T(8,128)(2,1)}, bf16[4,2,48,1024]{3,2,1,0:T(8,128)(2,1)}, u32[]{:S(2)}, u32[]{:S(2)}) %collective-permute-start.17) | collective-permute-done | bytes 786464 | tf_op jit(solution)/shard_map/ppermute | solution.py:25
  105.9 5.5 %collective-permute-done.16 = bf16[4,2,48,1024]{3,2,1,0:T(8,128)(2,1)} collective-permute-done((bf16[4,2,48,1024]{3,2,1,0:T(8,128)(2,1)}, bf16[4,2,48,1024]{3,2,1,0:T(8,128)(2,1)}, u32[]{:S(2)}, u32[]{:S(2)}) %collective-permute-start.16) | collective-permute-done | bytes 786464 | tf_op jit(solution)/shard_map/ppermute | solution.py:24
  112.9 3.1 %pad_maximum_fusion = bf16[4,4,2,48,2048]{4,3,2,1,0:T(8,128)(2,1)S(1)} fusion(bf16[1,4,2,48,2048]{4,3,2,1,0:T(8,128)(2,1)} %bitcast.17, bf16[1,4,2,48,2048]{4,3,2,1,0:T(8,128)(2,1)S(1)} %maximum_bitcast_fusion, bf16[1,4,2,48,2048]{4,3,2,1,0:T(8,128)(2,1)} %bitcast.15, bf16[1,4,2,48,2048]{4,3,2,1,0:T(8,128)(2,1)S(1)} %copy-done.2), kind=kLoop, calls=%fused_computation | loop fusion | flops 9437184 | bytes 12582912 | tf_op jit(solution)/shard_map/stack | solution.py:29
  116.0 3.0 %pad_maximum_fusion.1 = bf16[4,4,2,48,2048]{4,3,2,1,0:T(8,128)(2,1)S(1)} fusion(bf16[1,4,2,48,2048]{4,3,2,1,0:T(8,128)(2,1)} %bitcast.21, bf16[1,4,2,48,2048]{4,3,2,1,0:T(8,128)(2,1)S(1)} %maximum_bitcast_fusion.1, bf16[1,4,2,48,2048]{4,3,2,1,0:T(8,128)(2,1)} %bitcast.19, bf16[1,4,2,48,2048]{4,3,2,1,0:T(8,128)(2,1)S(1)} %copy-done.3), kind=kLoop, calls=%fused_computation.1 | loop fusion | flops 9437184 | bytes 12582912 | tf_op jit(solution)/shard_map/stack | solution.py:29
  119.1 3.0 %collective-permute-start.19 = (bf16[4,48,2048]{2,1,0:T(8,128)(2,1)S(1)}, bf16[4,48,2048]{2,1,0:T(8,128)(2,1)}, u32[]{:S(2)}, u32[]{:S(2)}) collective-permute-start(bf16[4,48,2048]{2,1,0:T(8,128)(2,1)S(1)} %slice_bitcast_fusion.1), channel_id=1, source_target_pairs={{0,24},{8,0},{16,8},{24,16},{1,25},{9,1},{17,9},{25,17},{2,26},{10... | collective-permute-start | bytes 2359304 | tf_op jit(solution)/shard_map/ppermute | solution.py:16
  124.2 2.6 %fusion.15 = (bf16[1,4,4,48,2048]{4,3,0,2,1:T(8,128)(2,1)}, bf16[1,4,4,48,2048]{4,3,0,2,1:T(8,128)(2,1)S(1)}) fusion(bf16[2,4,4,48,2048]{4,3,0,2,1:T(8,128)(2,1)S(1)} %bitcast.77), kind=kLoop, calls=%fused_computation.55 | loop fusion | bytes 12582912 | tf_op jit(solution)/shard_map/slice | solution.py:97
  131.6 3.4 %fusion.18 = f32[1024,768]{1,0:T(8,128)S(1)} fusion(bf16[1024,2048]{1,0:T(8,128)(2,1)S(1)} %bitcast.81, bf16[768,2048]{1,0:T(8,128)(2,1)S(1)} %bitcast.92), kind=kOutput, calls=%fused_computation.58 | convolution fusion | flops 3221225472 | bytes 10485760 | tf_op jit(solution)/shard_map/dot_general | solution.py:97
  135.1 3.4 %fusion.17 = f32[1024,768]{1,0:T(8,128)S(1)} fusion(bf16[1024,2048]{1,0:T(8,128)(2,1)S(1)} %bitcast.82, bf16[768,2048]{1,0:T(8,128)(2,1)S(1)} %bitcast.91), kind=kOutput, calls=%fused_computation.57 | convolution fusion | flops 3221225472 | bytes 10485760 | tf_op jit(solution)/shard_map/dot_general | solution.py:97
  140.7 3.5 %collective-permute-start.23 = (bf16[4,48,1024]{2,1,0:T(8,128)(2,1)S(1)}, bf16[4,48,1024]{2,1,0:T(8,128)(2,1)S(1)}, u32[]{:S(2)}, u32[]{:S(2)}) collective-permute-start(bf16[4,48,1024]{2,1,0:T(8,128)(2,1)S(1)} %slice.113), channel_id=1, source_target_pairs={{0,24},{8,0},{16,8},{24,16},{1,25},{9,1},{17,9},{25,17},{2,26},{10... | collective-permute-start | bytes 1179656 | tf_op jit(solution)/shard_map/ppermute | solution.py:25
  144.3 3.7 %multiply_convert_fusion = bf16[1024,768]{1,0:T(8,128)(2,1)S(1)} fusion(f32[1024,768]{1,0:T(8,128)S(1)} %fusion.18, bf16[1024,2048]{1,0:T(8,128)(2,1)S(1)} %bitcast.83, bf16[768,2048]{1,0:T(8,128)(2,1)S(1)} %bitcast.89), kind=kOutput, calls=%fused_computation.9 | convolution fusion | flops 3225944064 | bytes 12058624 | tf_op jit(solution)/shard_map/dot_general | solution.py:103
  148.0 3.7 %multiply_convert_fusion.1 = bf16[1024,768]{1,0:T(8,128)(2,1)S(1)} fusion(f32[1024,768]{1,0:T(8,128)S(1)} %fusion.17, bf16[1024,2048]{1,0:T(8,128)(2,1)S(1)} %bitcast.84, bf16[768,2048]{1,0:T(8,128)(2,1)S(1)} %bitcast.90), kind=kOutput, calls=%fused_computation.10 | convolution fusion | flops 3225944064 | bytes 12058624 | tf_op jit(solution)/shard_map/dot_general | solution.py:103
  153.8 3.2 %collective-permute-start.25 = (bf16[4,48,1024]{2,1,0:T(8,128)(2,1)S(1)}, bf16[4,48,1024]{2,1,0:T(8,128)(2,1)S(1)}, u32[]{:S(2)}, u32[]{:S(2)}) collective-permute-start(bf16[4,48,1024]{2,1,0:T(8,128)(2,1)S(1)} %slice.116), channel_id=1, source_target_pairs={{0,6},{2,0},{4,2},{6,4},{1,7},{3,1},{5,3},{7,5},{8,14},{10,8},{12,... | collective-permute-start | bytes 1179656 | tf_op jit(solution)/shard_map/ppermute | solution.py:25
  171.6 30.9 %all_to_all.10 = bf16[4,128,2048]{2,1,0:T(8,128)(2,1)S(1)} all-to-all(bf16[4,128,2048]{2,1,0:T(8,128)(2,1)S(1)} %add_convert_fusion), channel_id=1, replica_groups=mesh['yhi'=2,'core'=2,'x'=4,'z'=4,'ylo'=2] {'yhi','ylo'}, dimensions={0} | all-to-all | bytes 4194304 | tf_op jit(solution)/shard_map/all_to_all | solution.py:120
  (106 shorter events, 65.3 us)
Async XLA Ops:
  2.7 15.1 %collective-permute-start.5 = (bf16[3,48,2048]{2,1,0:T(8,128)(2,1)S(1)}, bf16[3,48,2048]{2,1,0:T(8,128)(2,1)S(1)}, u32[]{:S(2)}, u32[]{:S(2)}) collective-permute-start(bf16[3,48,2048]{2,1,0:T(8,128)(2,1)S(1)} %get-tuple-element.45), channel_id=1, source_target_pairs={{0,1},{1,0},{2,3},{3,2},{4,5},{5,4},{6,7},{7,6},{8,9},{9,8},{10,11... | collective-permute-start | bytes 1769480 | tf_op jit(solution)/shard_map/ppermute | solution.py:43
  4.4 17.1 %collective-permute-start.2 = (bf16[3,48,2048]{2,1,0:T(8,128)(2,1)S(1)}, bf16[3,48,2048]{2,1,0:T(8,128)(2,1)S(1)}, u32[]{:S(2)}, u32[]{:S(2)}) collective-permute-start(bf16[3,48,2048]{2,1,0:T(8,128)(2,1)S(1)} %bitcast.93), channel_id=1, source_target_pairs={{0,2},{2,4},{4,6},{6,0},{1,3},{3,5},{5,7},{7,1},{8,10},{10,12},{12... | collective-permute-start | bytes 1769480 | tf_op jit(solution)/shard_map/ppermute | solution.py:16
  6.4 16.8 %collective-permute-start.1 = (bf16[3,48,2048]{2,1,0:T(8,128)(2,1)S(1)}, bf16[3,48,2048]{2,1,0:T(8,128)(2,1)S(1)}, u32[]{:S(2)}, u32[]{:S(2)}) collective-permute-start(bf16[3,48,2048]{2,1,0:T(8,128)(2,1)S(1)} %bitcast.94), channel_id=1, source_target_pairs={{0,6},{2,0},{4,2},{6,4},{1,7},{3,1},{5,3},{7,5},{8,14},{10,8},{12,... | collective-permute-start | bytes 1769480 | tf_op jit(solution)/shard_map/ppermute | solution.py:16
  17.8 15.4 %collective-permute-start.7 = (bf16[3,48,2048]{2,1,0:T(8,128)(2,1)S(1)}, bf16[3,48,2048]{2,1,0:T(8,128)(2,1)S(1)}, u32[]{:S(2)}, u32[]{:S(2)}) collective-permute-start(bf16[3,48,2048]{2,1,0:T(8,128)(2,1)S(1)} %collective-permute-done.5), channel_id=1, source_target_pairs={{0,8},{8,16},{16,24},{24,0},{1,9},{9,17},{17,25},{25,1},{2,10},{10... | collective-permute-start | bytes 1769480 | tf_op jit(solution)/shard_map/ppermute | solution.py:16
  19.4 14.3 %collective-permute-start.6 = (bf16[3,48,2048]{2,1,0:T(8,128)(2,1)S(1)}, bf16[3,48,2048]{2,1,0:T(8,128)(2,1)S(1)}, u32[]{:S(2)}, u32[]{:S(2)}) collective-permute-start(bf16[3,48,2048]{2,1,0:T(8,128)(2,1)S(1)} %collective-permute-done.5), channel_id=1, source_target_pairs={{0,24},{8,0},{16,8},{24,16},{1,25},{9,1},{17,9},{25,17},{2,26},{10... | collective-permute-start | bytes 1769480 | tf_op jit(solution)/shard_map/ppermute | solution.py:16
  21.5 15.0 %collective-permute-start.3 = (bf16[3,48,1024]{2,1,0:T(8,128)(2,1)S(1)}, bf16[3,48,1024]{2,1,0:T(8,128)(2,1)S(1)}, u32[]{:S(2)}, u32[]{:S(2)}) collective-permute-start(bf16[3,48,1024]{2,1,0:T(8,128)(2,1)S(1)} %slice.125), channel_id=1, source_target_pairs={{0,2},{2,4},{4,6},{6,0},{1,3},{3,5},{5,7},{7,1},{8,10},{10,12},{12... | collective-permute-start | bytes 884744 | tf_op jit(solution)/shard_map/ppermute | solution.py:24
  23.2 13.4 %collective-permute-start.4 = (bf16[3,48,1024]{2,1,0:T(8,128)(2,1)S(1)}, bf16[3,48,1024]{2,1,0:T(8,128)(2,1)S(1)}, u32[]{:S(2)}, u32[]{:S(2)}) collective-permute-start(bf16[3,48,1024]{2,1,0:T(8,128)(2,1)S(1)} %slice.126), channel_id=1, source_target_pairs={{0,6},{2,0},{4,2},{6,4},{1,7},{3,1},{5,3},{7,5},{8,14},{10,8},{12,... | collective-permute-start | bytes 884744 | tf_op jit(solution)/shard_map/ppermute | solution.py:25
  44.0 33.8 %collective-permute-start.10 = (bf16[4,2,48,2048]{3,2,1,0:T(8,128)(2,1)}, bf16[4,2,48,2048]{3,2,1,0:T(8,128)(2,1)}, u32[]{:S(2)}, u32[]{:S(2)}) collective-permute-start(bf16[4,2,48,2048]{3,2,1,0:T(8,128)(2,1)} %get-tuple-element.44), channel_id=1, source_target_pairs={{0,24},{8,0},{16,8},{24,16},{1,25},{9,1},{17,9},{25,17},{2,26},{10... | collective-permute-start | bytes 4718600 | tf_op jit(solution)/shard_map/ppermute | solution.py:16
  47.1 36.5 %collective-permute-start.11 = (bf16[4,2,48,2048]{3,2,1,0:T(8,128)(2,1)}, bf16[4,2,48,2048]{3,2,1,0:T(8,128)(2,1)}, u32[]{:S(2)}, u32[]{:S(2)}) collective-permute-start(bf16[4,2,48,2048]{3,2,1,0:T(8,128)(2,1)} %get-tuple-element.44), channel_id=1, source_target_pairs={{0,8},{8,16},{16,24},{24,0},{1,9},{9,17},{17,25},{25,1},{2,10},{10... | collective-permute-start | bytes 4718600 | tf_op jit(solution)/shard_map/ppermute | solution.py:16
  49.3 37.6 %collective-permute-start.14 = (bf16[4,2,48,2048]{3,2,1,0:T(8,128)(2,1)}, bf16[4,2,48,2048]{3,2,1,0:T(8,128)(2,1)}, u32[]{:S(2)}, u32[]{:S(2)}) collective-permute-start(bf16[4,2,48,2048]{3,2,1,0:T(8,128)(2,1)} %get-tuple-element.42), channel_id=1, source_target_pairs={{0,6},{2,0},{4,2},{6,4},{1,7},{3,1},{5,3},{7,5},{8,14},{10,8},{12,... | collective-permute-start | bytes 4718600 | tf_op jit(solution)/shard_map/ppermute | solution.py:16
  53.5 39.8 %collective-permute-start.15 = (bf16[4,2,48,2048]{3,2,1,0:T(8,128)(2,1)}, bf16[4,2,48,2048]{3,2,1,0:T(8,128)(2,1)}, u32[]{:S(2)}, u32[]{:S(2)}) collective-permute-start(bf16[4,2,48,2048]{3,2,1,0:T(8,128)(2,1)} %get-tuple-element.42), channel_id=1, source_target_pairs={{0,2},{2,4},{4,6},{6,0},{1,3},{3,5},{5,7},{7,1},{8,10},{10,12},{12... | collective-permute-start | bytes 4718600 | tf_op jit(solution)/shard_map/ppermute | solution.py:16
  55.2 42.2 %all-to-all-start = ((bf16[4,144,2048]{2,1,0:T(8,128)(2,1)}), bf16[4,144,2048]{2,1,0:T(8,128)(2,1)S(1)}, u32[]{:S(2)}, u32[]{:S(2)}) async-start(bf16[4,144,2048]{2,1,0:T(8,128)(2,1)} %broadcast_in_dim.23), calls=%async_computation | async-start | bytes 4718592 | tf_op jit(solution)/shard_map/all_to_all | solution.py:67
  79.9 17.8 %collective-permute-start.13 = (bf16[4,2,48,1024]{3,2,1,0:T(8,128)(2,1)}, bf16[4,2,48,1024]{3,2,1,0:T(8,128)(2,1)}, u32[]{:S(2)}, u32[]{:S(2)}) collective-permute-start(bf16[4,2,48,1024]{3,2,1,0:T(8,128)(2,1)} %slice.130), channel_id=1, source_target_pairs={{0,24},{8,0},{16,8},{24,16},{1,25},{9,1},{17,9},{25,17},{2,26},{10... | collective-permute-start | bytes 2359304 | tf_op jit(solution)/shard_map/ppermute | solution.py:25
  85.7 16.3 %collective-permute-start.12 = (bf16[4,2,48,1024]{3,2,1,0:T(8,128)(2,1)}, bf16[4,2,48,1024]{3,2,1,0:T(8,128)(2,1)}, u32[]{:S(2)}, u32[]{:S(2)}) collective-permute-start(bf16[4,2,48,1024]{3,2,1,0:T(8,128)(2,1)} %slice.129), channel_id=1, source_target_pairs={{0,8},{8,16},{16,24},{24,0},{1,9},{9,17},{17,25},{25,1},{2,10},{10... | collective-permute-start | bytes 2359304 | tf_op jit(solution)/shard_map/ppermute | solution.py:24
  89.0 17.0 %collective-permute-start.17 = (bf16[4,2,48,1024]{3,2,1,0:T(8,128)(2,1)}, bf16[4,2,48,1024]{3,2,1,0:T(8,128)(2,1)}, u32[]{:S(2)}, u32[]{:S(2)}) collective-permute-start(bf16[4,2,48,1024]{3,2,1,0:T(8,128)(2,1)} %slice.132), channel_id=1, source_target_pairs={{0,6},{2,0},{4,2},{6,4},{1,7},{3,1},{5,3},{7,5},{8,14},{10,8},{12,... | collective-permute-start | bytes 2359304 | tf_op jit(solution)/shard_map/ppermute | solution.py:25
  95.3 16.1 %collective-permute-start.16 = (bf16[4,2,48,1024]{3,2,1,0:T(8,128)(2,1)}, bf16[4,2,48,1024]{3,2,1,0:T(8,128)(2,1)}, u32[]{:S(2)}, u32[]{:S(2)}) collective-permute-start(bf16[4,2,48,1024]{3,2,1,0:T(8,128)(2,1)} %slice.131), channel_id=1, source_target_pairs={{0,2},{2,4},{4,6},{6,0},{1,3},{3,5},{5,7},{7,1},{8,10},{10,12},{12... | collective-permute-start | bytes 2359304 | tf_op jit(solution)/shard_map/ppermute | solution.py:24
  97.5 30.4 %collective-permute-start = (bf16[4,144,2048]{2,1,0:T(8,128)(2,1)S(1)}, bf16[4,144,2048]{2,1,0:T(8,128)(2,1)}, u32[]{:S(2)}, u32[]{:S(2)}) collective-permute-start(bf16[4,144,2048]{2,1,0:T(8,128)(2,1)S(1)} %all-to-all-done), channel_id=1, source_target_pairs={{0,32},{32,0},{1,33},{33,1},{2,34},{34,2},{3,35},{35,3},{4,36},{36... | collective-permute-start | bytes 7077896 | tf_op jit(solution)/shard_map/ppermute | solution.py:68
  119.1 19.5 %collective-permute-start.19 = (bf16[4,48,2048]{2,1,0:T(8,128)(2,1)S(1)}, bf16[4,48,2048]{2,1,0:T(8,128)(2,1)}, u32[]{:S(2)}, u32[]{:S(2)}) collective-permute-start(bf16[4,48,2048]{2,1,0:T(8,128)(2,1)S(1)} %slice_bitcast_fusion.1), channel_id=1, source_target_pairs={{0,24},{8,0},{16,8},{24,16},{1,25},{9,1},{17,9},{25,17},{2,26},{10... | collective-permute-start | bytes 2359304 | tf_op jit(solution)/shard_map/ppermute | solution.py:16
  122.1 16.4 %collective-permute-start.18 = (bf16[4,48,2048]{2,1,0:T(8,128)(2,1)S(1)}, bf16[4,48,2048]{2,1,0:T(8,128)(2,1)}, u32[]{:S(2)}, u32[]{:S(2)}) collective-permute-start(bf16[4,48,2048]{2,1,0:T(8,128)(2,1)S(1)} %slice_bitcast_fusion.1), channel_id=1, source_target_pairs={{0,8},{8,16},{16,24},{24,0},{1,9},{9,17},{17,25},{25,1},{2,10},{10... | collective-permute-start | bytes 2359304 | tf_op jit(solution)/shard_map/ppermute | solution.py:16
  122.1 16.5 %collective-permute-start.21 = (bf16[4,48,2048]{2,1,0:T(8,128)(2,1)S(1)}, bf16[4,48,2048]{2,1,0:T(8,128)(2,1)}, u32[]{:S(2)}, u32[]{:S(2)}) collective-permute-start(bf16[4,48,2048]{2,1,0:T(8,128)(2,1)S(1)} %copy-done.4), channel_id=1, source_target_pairs={{0,6},{2,0},{4,2},{6,4},{1,7},{3,1},{5,3},{7,5},{8,14},{10,8},{12,... | collective-permute-start | bytes 2359304 | tf_op jit(solution)/shard_map/ppermute | solution.py:16
  122.1 16.5 %collective-permute-start.20 = (bf16[4,48,2048]{2,1,0:T(8,128)(2,1)S(1)}, bf16[4,48,2048]{2,1,0:T(8,128)(2,1)}, u32[]{:S(2)}, u32[]{:S(2)}) collective-permute-start(bf16[4,48,2048]{2,1,0:T(8,128)(2,1)S(1)} %copy-done.4), channel_id=1, source_target_pairs={{0,2},{2,4},{4,6},{6,0},{1,3},{3,5},{5,7},{7,1},{8,10},{10,12},{12... | collective-permute-start | bytes 2359304 | tf_op jit(solution)/shard_map/ppermute | solution.py:16
  140.7 16.4 %collective-permute-start.22 = (bf16[4,48,1024]{2,1,0:T(8,128)(2,1)S(1)}, bf16[4,48,1024]{2,1,0:T(8,128)(2,1)S(1)}, u32[]{:S(2)}, u32[]{:S(2)}) collective-permute-start(bf16[4,48,1024]{2,1,0:T(8,128)(2,1)S(1)} %slice.112), channel_id=1, source_target_pairs={{0,8},{8,16},{16,24},{24,0},{1,9},{9,17},{17,25},{25,1},{2,10},{10... | collective-permute-start | bytes 1179656 | tf_op jit(solution)/shard_map/ppermute | solution.py:24
  140.7 16.3 %collective-permute-start.23 = (bf16[4,48,1024]{2,1,0:T(8,128)(2,1)S(1)}, bf16[4,48,1024]{2,1,0:T(8,128)(2,1)S(1)}, u32[]{:S(2)}, u32[]{:S(2)}) collective-permute-start(bf16[4,48,1024]{2,1,0:T(8,128)(2,1)S(1)} %slice.113), channel_id=1, source_target_pairs={{0,24},{8,0},{16,8},{24,16},{1,25},{9,1},{17,9},{25,17},{2,26},{10... | collective-permute-start | bytes 1179656 | tf_op jit(solution)/shard_map/ppermute | solution.py:25
  153.8 9.1 %collective-permute-start.24 = (bf16[4,48,1024]{2,1,0:T(8,128)(2,1)S(1)}, bf16[4,48,1024]{2,1,0:T(8,128)(2,1)S(1)}, u32[]{:S(2)}, u32[]{:S(2)}) collective-permute-start(bf16[4,48,1024]{2,1,0:T(8,128)(2,1)S(1)} %slice.115), channel_id=1, source_target_pairs={{0,2},{2,4},{4,6},{6,0},{1,3},{3,5},{5,7},{7,1},{8,10},{10,12},{12... | collective-permute-start | bytes 1179656 | tf_op jit(solution)/shard_map/ppermute | solution.py:24
  (13 other events, 125.6 us)

commit v13 on v12

--- a/solution.py
+++ b/solution.py
@@ -44,11 +44,13 @@
     first_a = ring_of_four(keep, "z")
     first_b = ring_of_four(got, "x")
     first_a, first_b = lax.optimization_barrier((first_a, first_b))
-    gate_up_a = ring_of_four(first_a[:, :2], "x")
-    gate_up_b = ring_of_four(first_b[:, :2], "z")
-    gate_up_a, gate_up_b, down_a, down_b = lax.optimization_barrier(
-        (gate_up_a, gate_up_b, first_a[:, 2], first_b[:, 2])
+    lead_a, lead_b = first_a[:, :2], first_b[:, :2]
+    near_a, near_b = first_hop(lead_a, "x"), first_hop(lead_b, "z")
+    near_a, near_b, down_a, down_b = lax.optimization_barrier(
+        (near_a, near_b, first_a[:, 2], first_b[:, 2])
     )
+    gate_up_a = far_hop(lead_a, near_a, "x")
+    gate_up_b = far_hop(lead_b, near_b, "z")
     width = stacked.shape[-1]
     gate_ups = [jnp.moveaxis(g, 2, 0).reshape(2, -1, width) for g in (gate_up_a, gate_up_b)]
     return gate_ups, (down_a, first_hop(down_a, "x")), (down_b, first_hop(down_b, "z"))

time: 205 us -> 209 us (1.020)
  waiting for transfers between devices: 55 us -> 63.8 us
  starting transfers between devices: 48.3 us -> 44 us
    ppermute x6, waiting for transfers between devices: 8.22 us -> 27.3 us  [first_hop(): lax.ppermute(value, axis, perm=AHEAD)]
    ppermute x6, waiting for transfers between devices: 18.2 us -> 5.4 us  [first_hop(): lax.ppermute(value, axis, perm=BEHIND)]
    transpose x0 -> x2, other arithmetic: none -> 6.08 us  [expert_weights(): jnp.moveaxis(g, 2, 0).reshape(2, -1, width)]
    another operation x12 -> x10, other arithmetic: 13 us -> 7.14 us  [far_hop(): return jnp.stack([value, from_plus, far, from_minus])]
    ppermute x6, starting transfers between devices: 14.1 us -> 11.4 us  [first_hop(): lax.ppermute(value, axis, perm=BEHIND)]
  transfers between devices with their start and end apart: 28 -> 28, of which waited for: 10 -> 13; matrix products, arithmetic and copies ran while one was open for 27% -> 26% of each run, Pallas kernels for 0% -> 0%
where the time goes in v13:
time: 209 us; the launch traced here: 208 us
  waiting for transfers between devices  63.8 us (31%)
  starting transfers between devices  44 us (21%)
  local copies, waits for them, and re-layouts  32.2 us (15%)
  blocking collectives  30.9 us (15%)
  matrix products  21.6 us (10%)
  other arithmetic  15.5 us (7%)
    all_to_all x1, blocking collectives, per_device(): lax.all_to_all(partial, CHIPS, split_axis=0, concat_axis=0, tiled=True)  30.9 us
    ppermute x6, waiting for transfers between devices, first_hop(): lax.ppermute(value, axis, perm=AHEAD)  27.3 us
    ppermute x6, starting transfers between devices, far_hop(): lax.ppermute(from_plus[..., half:], axis, perm=BEHIND)  18.5 us
    ppermute x6, waiting for transfers between devices, far_hop(): lax.ppermute(from_minus[..., :half], axis, perm=AHEAD)  18.2 us
    ppermute x6, starting transfers between devices, first_hop(): lax.ppermute(value, axis, perm=BEHIND)  11.4 us
    ppermute x1, waiting for transfers between devices, expert_weights(): got = lax.ppermute(send, 'ylo', perm=SWAP)  9.29 us
    dot_general x2, matrix products, per_device(): jnp.dot(late_rows, weights[1].T, preferred_element_type=jnp.float32)  7.4 us
    dot_general x4, matrix products, down(): jnp.dot(hidden[first:last], weights[2], preferred_element_type=jnp.float32)  7.35 us
  transfers between devices with their start and end apart: 28, of which 13 were waited for; matrix products, arithmetic and copies ran while one was open for 26% of the time, Pallas kernels for 0%

profile of v13, /device:TPU:0, one launch (start us, length us, event | category | flops | bytes accessed | tf_op | source)
XLA Modules:
  0.0 208.4 jit_solution(10592440714660574889)
XLA Ops:
  8.5 9.3 %collective-permute-done.5 = bf16[3,48,2048]{2,1,0:T(8,128)(2,1)S(1)} collective-permute-done((bf16[3,48,2048]{2,1,0:T(8,128)(2,1)S(1)}, bf16[3,48,2048]{2,1,0:T(8,128)(2,1)S(1)}, u32[]{:S(2)}, u32[]{:S(2)}) %collective-permute-start.5) | collective-permute-done | bytes 589856 | tf_op jit(solution)/shard_map/ppermute | solution.py:43
  25.4 7.7 %collective-permute-done.7 = bf16[3,48,2048]{2,1,0:T(8,128)(2,1)S(1)} collective-permute-done((bf16[3,48,2048]{2,1,0:T(8,128)(2,1)S(1)}, bf16[3,48,2048]{2,1,0:T(8,128)(2,1)S(1)}, u32[]{:S(2)}, u32[]{:S(2)}) %collective-permute-start.7) | collective-permute-done | bytes 589856 | tf_op jit(solution)/shard_map/ppermute | solution.py:16
  33.7 2.8 %collective-permute-start.9 = (bf16[3,48,1024]{2,1,0:T(8,128)(2,1)S(1)}, bf16[3,48,1024]{2,1,0:T(8,128)(2,1)S(1)}, u32[]{:S(2)}, u32[]{:S(2)}) collective-permute-start(bf16[3,48,1024]{2,1,0:T(8,128)(2,1)S(1)} %slice.128), channel_id=1, source_target_pairs={{0,24},{8,0},{16,8},{24,16},{1,25},{9,1},{17,9},{25,17},{2,26},{10... | collective-permute-start | bytes 884744 | tf_op jit(solution)/shard_map/ppermute | solution.py:25
  36.9 4.4 %collective-permute-done.8 = bf16[3,48,1024]{2,1,0:T(8,128)(2,1)S(1)} collective-permute-done((bf16[3,48,1024]{2,1,0:T(8,128)(2,1)S(1)}, bf16[3,48,1024]{2,1,0:T(8,128)(2,1)S(1)}, u32[]{:S(2)}, u32[]{:S(2)}) %collective-permute-start.8) | collective-permute-done | bytes 294944 | tf_op jit(solution)/shard_map/ppermute | solution.py:24
  44.7 2.6 %collective-permute-start.11 = (bf16[4,2,48,2048]{3,2,1,0:T(8,128)(2,1)}, bf16[4,2,48,2048]{3,2,1,0:T(8,128)(2,1)}, u32[]{:S(2)}, u32[]{:S(2)}) collective-permute-start(bf16[4,2,48,2048]{3,2,1,0:T(8,128)(2,1)} %get-tuple-element.48), channel_id=1, source_target_pairs={{0,24},{8,0},{16,8},{24,16},{1,25},{9,1},{17,9},{25,17},{2,26},{10... | collective-permute-start | bytes 4718600 | tf_op jit(solution)/shard_map/ppermute | solution.py:16
  49.4 4.3 %collective-permute-start.13 = (bf16[4,2,48,2048]{3,2,1,0:T(8,128)(2,1)}, bf16[4,2,48,2048]{3,2,1,0:T(8,128)(2,1)}, u32[]{:S(2)}, u32[]{:S(2)}) collective-permute-start(bf16[4,2,48,2048]{3,2,1,0:T(8,128)(2,1)} %get-tuple-element.46), channel_id=1, source_target_pairs={{0,6},{2,0},{4,2},{6,4},{1,7},{3,1},{5,3},{7,5},{8,14},{10,8},{12,... | collective-permute-start | bytes 4718600 | tf_op jit(solution)/shard_map/ppermute | solution.py:16
  55.5 4.5 %all-to-all-start = ((bf16[4,144,2048]{2,1,0:T(8,128)(2,1)}), bf16[4,144,2048]{2,1,0:T(8,128)(2,1)S(1)}, u32[]{:S(2)}, u32[]{:S(2)}) async-start(bf16[4,144,2048]{2,1,0:T(8,128)(2,1)} %broadcast_in_dim.23), calls=%async_computation | async-start | bytes 4718592 | tf_op jit(solution)/shard_map/all_to_all | solution.py:69
  63.3 15.7 %collective-permute-done.10 = bf16[4,2,48,2048]{3,2,1,0:T(8,128)(2,1)} collective-permute-done((bf16[4,2,48,2048]{3,2,1,0:T(8,128)(2,1)}, bf16[4,2,48,2048]{3,2,1,0:T(8,128)(2,1)}, u32[]{:S(2)}, u32[]{:S(2)}) %collective-permute-start.10) | collective-permute-done | bytes 1572896 | tf_op jit(solution)/shard_map/ppermute | solution.py:16
  79.0 5.4 %collective-permute-done.13 = bf16[4,2,48,2048]{3,2,1,0:T(8,128)(2,1)} collective-permute-done((bf16[4,2,48,2048]{3,2,1,0:T(8,128)(2,1)}, bf16[4,2,48,2048]{3,2,1,0:T(8,128)(2,1)}, u32[]{:S(2)}, u32[]{:S(2)}) %collective-permute-start.13) | collective-permute-done | bytes 1572896 | tf_op jit(solution)/shard_map/ppermute | solution.py:16
  84.4 3.4 %collective-permute-done.12 = bf16[4,2,48,2048]{3,2,1,0:T(8,128)(2,1)} collective-permute-done((bf16[4,2,48,2048]{3,2,1,0:T(8,128)(2,1)}, bf16[4,2,48,2048]{3,2,1,0:T(8,128)(2,1)}, u32[]{:S(2)}, u32[]{:S(2)}) %collective-permute-start.12) | collective-permute-done | bytes 1572896 | tf_op jit(solution)/shard_map/ppermute | solution.py:16
  92.0 3.2 %collective-permute-start.21 = (bf16[4,2,48,1024]{3,2,1,0:T(8,128)(2,1)}, bf16[4,2,48,1024]{3,2,1,0:T(8,128)(2,1)}, u32[]{:S(2)}, u32[]{:S(2)}) collective-permute-start(bf16[4,2,48,1024]{3,2,1,0:T(8,128)(2,1)} %slice.108), channel_id=1, source_target_pairs={{0,6},{2,0},{4,2},{6,4},{1,7},{3,1},{5,3},{7,5},{8,14},{10,8},{12,... | collective-permute-start | bytes 2359304 | tf_op jit(solution)/shard_map/ppermute | solution.py:25
  99.4 3.2 %collective-permute-start.15 = (bf16[4,2,48,1024]{3,2,1,0:T(8,128)(2,1)}, bf16[4,2,48,1024]{3,2,1,0:T(8,128)(2,1)}, u32[]{:S(2)}, u32[]{:S(2)}) collective-permute-start(bf16[4,2,48,1024]{3,2,1,0:T(8,128)(2,1)} %slice.104), channel_id=1, source_target_pairs={{0,24},{8,0},{16,8},{24,16},{1,25},{9,1},{17,9},{25,17},{2,26},{10... | collective-permute-start | bytes 2359304 | tf_op jit(solution)/shard_map/ppermute | solution.py:25
  102.9 3.3 %collective-permute-done.20 = bf16[4,2,48,1024]{3,2,1,0:T(8,128)(2,1)} collective-permute-done((bf16[4,2,48,1024]{3,2,1,0:T(8,128)(2,1)}, bf16[4,2,48,1024]{3,2,1,0:T(8,128)(2,1)}, u32[]{:S(2)}, u32[]{:S(2)}) %collective-permute-start.20) | collective-permute-done | bytes 786464 | tf_op jit(solution)/shard_map/ppermute | solution.py:24
  109.7 8.6 %collective-permute-done.14 = bf16[4,2,48,1024]{3,2,1,0:T(8,128)(2,1)} collective-permute-done((bf16[4,2,48,1024]{3,2,1,0:T(8,128)(2,1)}, bf16[4,2,48,1024]{3,2,1,0:T(8,128)(2,1)}, u32[]{:S(2)}, u32[]{:S(2)}) %collective-permute-start.14) | collective-permute-done | bytes 786464 | tf_op jit(solution)/shard_map/ppermute | solution.py:24
  118.4 2.6 %collective-permute-done.15 = bf16[4,2,48,1024]{3,2,1,0:T(8,128)(2,1)} collective-permute-done((bf16[4,2,48,1024]{3,2,1,0:T(8,128)(2,1)}, bf16[4,2,48,1024]{3,2,1,0:T(8,128)(2,1)}, u32[]{:S(2)}, u32[]{:S(2)}) %collective-permute-start.15) | collective-permute-done | bytes 786464 | tf_op jit(solution)/shard_map/ppermute | solution.py:25
  122.4 3.1 %maximum_bitcast_fusion.1 = bf16[2,4,4,48,2048]{4,3,0,2,1:T(8,128)(2,1)S(1)} fusion(bf16[1,4,2,48,2048]{4,3,2,1,0:T(8,128)(2,1)} %bitcast.26, bf16[1,4,2,48,2048]{4,3,2,1,0:T(8,128)(2,1)S(1)} %maximum_bitcast_fusion.3, bf16[1,4,2,48,2048]{4,3,2,1,0:T(8,128)(2,1)} %bitcast.24, bf16[1,4,2,48,2048]{4,3,2,1,0:T(8,128)(2,1)S(1)} %copy-done.3), kind=kLoop, calls=%fused_computation.1 | loop fusion | flops 9437184 | bytes 12582912 | tf_op jit(solution)/shard_map/transpose | solution.py:55
  125.5 3.0 %maximum_bitcast_fusion = bf16[2,4,4,48,2048]{4,3,0,2,1:T(8,128)(2,1)S(1)} fusion(bf16[1,4,2,48,2048]{4,3,2,1,0:T(8,128)(2,1)} %bitcast.19, bf16[1,4,2,48,2048]{4,3,2,1,0:T(8,128)(2,1)S(1)} %maximum_bitcast_fusion.2, bf16[1,4,2,48,2048]{4,3,2,1,0:T(8,128)(2,1)} %bitcast.17, bf16[1,4,2,48,2048]{4,3,2,1,0:T(8,128)(2,1)S(1)} %copy-done.2), kind=kLoop, calls=%fused_computation | loop fusion | flops 9437184 | bytes 12582912 | tf_op jit(solution)/shard_map/transpose | solution.py:55
  135.9 3.4 %fusion.18 = f32[1024,768]{1,0:T(8,128)S(1)} fusion(bf16[1024,2048]{1,0:T(8,128)(2,1)S(1)} %bitcast.81, bf16[768,2048]{1,0:T(8,128)(2,1)S(1)} %bitcast.90), kind=kOutput, calls=%fused_computation.58 | convolution fusion | flops 3221225472 | bytes 10485760 | tf_op jit(solution)/shard_map/dot_general | solution.py:99
  139.3 3.4 %fusion.17 = f32[1024,768]{1,0:T(8,128)S(1)} fusion(bf16[1024,2048]{1,0:T(8,128)(2,1)S(1)} %bitcast.82, bf16[768,2048]{1,0:T(8,128)(2,1)S(1)} %bitcast.91), kind=kOutput, calls=%fused_computation.57 | convolution fusion | flops 3221225472 | bytes 10485760 | tf_op jit(solution)/shard_map/dot_general | solution.py:99
  145.2 3.7 %collective-permute-start.23 = (bf16[4,48,1024]{2,1,0:T(8,128)(2,1)S(1)}, bf16[4,48,1024]{2,1,0:T(8,128)(2,1)S(1)}, u32[]{:S(2)}, u32[]{:S(2)}) collective-permute-start(bf16[4,48,1024]{2,1,0:T(8,128)(2,1)S(1)} %slice.113), channel_id=1, source_target_pairs={{0,24},{8,0},{16,8},{24,16},{1,25},{9,1},{17,9},{25,17},{2,26},{10... | collective-permute-start | bytes 1179656 | tf_op jit(solution)/shard_map/ppermute | solution.py:25
  148.9 3.7 %multiply_convert_fusion = bf16[1024,768]{1,0:T(8,128)(2,1)S(1)} fusion(f32[1024,768]{1,0:T(8,128)S(1)} %fusion.18, bf16[1024,2048]{1,0:T(8,128)(2,1)S(1)} %bitcast.83, bf16[768,2048]{1,0:T(8,128)(2,1)S(1)} %bitcast.88), kind=kOutput, calls=%fused_computation.9 | convolution fusion | flops 3225944064 | bytes 12058624 | tf_op jit(solution)/shard_map/dot_general | solution.py:105
  152.6 3.7 %multiply_convert_fusion.1 = bf16[1024,768]{1,0:T(8,128)(2,1)S(1)} fusion(f32[1024,768]{1,0:T(8,128)S(1)} %fusion.17, bf16[1024,2048]{1,0:T(8,128)(2,1)S(1)} %bitcast.84, bf16[768,2048]{1,0:T(8,128)(2,1)S(1)} %bitcast.89), kind=kOutput, calls=%fused_computation.10 | convolution fusion | flops 3225944064 | bytes 12058624 | tf_op jit(solution)/shard_map/dot_general | solution.py:105
  158.5 3.3 %collective-permute-start.25 = (bf16[4,48,1024]{2,1,0:T(8,128)(2,1)S(1)}, bf16[4,48,1024]{2,1,0:T(8,128)(2,1)S(1)}, u32[]{:S(2)}, u32[]{:S(2)}) collective-permute-start(bf16[4,48,1024]{2,1,0:T(8,128)(2,1)S(1)} %slice.116), channel_id=1, source_target_pairs={{0,6},{2,0},{4,2},{6,4},{1,7},{3,1},{5,3},{7,5},{8,14},{10,8},{12,... | collective-permute-start | bytes 1179656 | tf_op jit(solution)/shard_map/ppermute | solution.py:25
  176.2 30.9 %all_to_all.10 = bf16[4,128,2048]{2,1,0:T(8,128)(2,1)S(1)} all-to-all(bf16[4,128,2048]{2,1,0:T(8,128)(2,1)S(1)} %add_convert_fusion), channel_id=1, replica_groups=mesh['yhi'=2,'core'=2,'x'=4,'z'=4,'ylo'=2] {'yhi','ylo'}, dimensions={0} | all-to-all | bytes 4194304 | tf_op jit(solution)/shard_map/all_to_all | solution.py:122
  (104 shorter events, 68.8 us)
Async XLA Ops:
  2.7 15.1 %collective-permute-start.5 = (bf16[3,48,2048]{2,1,0:T(8,128)(2,1)S(1)}, bf16[3,48,2048]{2,1,0:T(8,128)(2,1)S(1)}, u32[]{:S(2)}, u32[]{:S(2)}) collective-permute-start(bf16[3,48,2048]{2,1,0:T(8,128)(2,1)S(1)} %get-tuple-element.49), channel_id=1, source_target_pairs={{0,1},{1,0},{2,3},{3,2},{4,5},{5,4},{6,7},{7,6},{8,9},{9,8},{10,11... | collective-permute-start | bytes 1769480 | tf_op jit(solution)/shard_map/ppermute | solution.py:43
  4.4 17.1 %collective-permute-start.2 = (bf16[3,48,2048]{2,1,0:T(8,128)(2,1)S(1)}, bf16[3,48,2048]{2,1,0:T(8,128)(2,1)S(1)}, u32[]{:S(2)}, u32[]{:S(2)}) collective-permute-start(bf16[3,48,2048]{2,1,0:T(8,128)(2,1)S(1)} %bitcast.92), channel_id=1, source_target_pairs={{0,2},{2,4},{4,6},{6,0},{1,3},{3,5},{5,7},{7,1},{8,10},{10,12},{12... | collective-permute-start | bytes 1769480 | tf_op jit(solution)/shard_map/ppermute | solution.py:16
  6.4 16.8 %collective-permute-start.1 = (bf16[3,48,2048]{2,1,0:T(8,128)(2,1)S(1)}, bf16[3,48,2048]{2,1,0:T(8,128)(2,1)S(1)}, u32[]{:S(2)}, u32[]{:S(2)}) collective-permute-start(bf16[3,48,2048]{2,1,0:T(8,128)(2,1)S(1)} %bitcast.93), channel_id=1, source_target_pairs={{0,6},{2,0},{4,2},{6,4},{1,7},{3,1},{5,3},{7,5},{8,14},{10,8},{12,... | collective-permute-start | bytes 1769480 | tf_op jit(solution)/shard_map/ppermute | solution.py:16
  17.8 15.4 %collective-permute-start.7 = (bf16[3,48,2048]{2,1,0:T(8,128)(2,1)S(1)}, bf16[3,48,2048]{2,1,0:T(8,128)(2,1)S(1)}, u32[]{:S(2)}, u32[]{:S(2)}) collective-permute-start(bf16[3,48,2048]{2,1,0:T(8,128)(2,1)S(1)} %collective-permute-done.5), channel_id=1, source_target_pairs={{0,8},{8,16},{16,24},{24,0},{1,9},{9,17},{17,25},{25,1},{2,10},{10... | collective-permute-start | bytes 1769480 | tf_op jit(solution)/shard_map/ppermute | solution.py:16
  19.4 14.3 %collective-permute-start.6 = (bf16[3,48,2048]{2,1,0:T(8,128)(2,1)S(1)}, bf16[3,48,2048]{2,1,0:T(8,128)(2,1)S(1)}, u32[]{:S(2)}, u32[]{:S(2)}) collective-permute-start(bf16[3,48,2048]{2,1,0:T(8,128)(2,1)S(1)} %collective-permute-done.5), channel_id=1, source_target_pairs={{0,24},{8,0},{16,8},{24,16},{1,25},{9,1},{17,9},{25,17},{2,26},{10... | collective-permute-start | bytes 1769480 | tf_op jit(solution)/shard_map/ppermute | solution.py:16
  21.5 15.0 %collective-permute-start.3 = (bf16[3,48,1024]{2,1,0:T(8,128)(2,1)S(1)}, bf16[3,48,1024]{2,1,0:T(8,128)(2,1)S(1)}, u32[]{:S(2)}, u32[]{:S(2)}) collective-permute-start(bf16[3,48,1024]{2,1,0:T(8,128)(2,1)S(1)} %slice.125), channel_id=1, source_target_pairs={{0,2},{2,4},{4,6},{6,0},{1,3},{3,5},{5,7},{7,1},{8,10},{10,12},{12... | collective-permute-start | bytes 884744 | tf_op jit(solution)/shard_map/ppermute | solution.py:24
  23.2 13.4 %collective-permute-start.4 = (bf16[3,48,1024]{2,1,0:T(8,128)(2,1)S(1)}, bf16[3,48,1024]{2,1,0:T(8,128)(2,1)S(1)}, u32[]{:S(2)}, u32[]{:S(2)}) collective-permute-start(bf16[3,48,1024]{2,1,0:T(8,128)(2,1)S(1)} %slice.126), channel_id=1, source_target_pairs={{0,6},{2,0},{4,2},{6,4},{1,7},{3,1},{5,3},{7,5},{8,14},{10,8},{12,... | collective-permute-start | bytes 884744 | tf_op jit(solution)/shard_map/ppermute | solution.py:25
  44.1 34.9 %collective-permute-start.10 = (bf16[4,2,48,2048]{3,2,1,0:T(8,128)(2,1)}, bf16[4,2,48,2048]{3,2,1,0:T(8,128)(2,1)}, u32[]{:S(2)}, u32[]{:S(2)}) collective-permute-start(bf16[4,2,48,2048]{3,2,1,0:T(8,128)(2,1)} %get-tuple-element.48), channel_id=1, source_target_pairs={{0,8},{8,16},{16,24},{24,0},{1,9},{9,17},{17,25},{25,1},{2,10},{10... | collective-permute-start | bytes 4718600 | tf_op jit(solution)/shard_map/ppermute | solution.py:16
  44.7 34.3 %collective-permute-start.11 = (bf16[4,2,48,2048]{3,2,1,0:T(8,128)(2,1)}, bf16[4,2,48,2048]{3,2,1,0:T(8,128)(2,1)}, u32[]{:S(2)}, u32[]{:S(2)}) collective-permute-start(bf16[4,2,48,2048]{3,2,1,0:T(8,128)(2,1)} %get-tuple-element.48), channel_id=1, source_target_pairs={{0,24},{8,0},{16,8},{24,16},{1,25},{9,1},{17,9},{25,17},{2,26},{10... | collective-permute-start | bytes 4718600 | tf_op jit(solution)/shard_map/ppermute | solution.py:16
  49.4 35.0 %collective-permute-start.13 = (bf16[4,2,48,2048]{3,2,1,0:T(8,128)(2,1)}, bf16[4,2,48,2048]{3,2,1,0:T(8,128)(2,1)}, u32[]{:S(2)}, u32[]{:S(2)}) collective-permute-start(bf16[4,2,48,2048]{3,2,1,0:T(8,128)(2,1)} %get-tuple-element.46), channel_id=1, source_target_pairs={{0,6},{2,0},{4,2},{6,4},{1,7},{3,1},{5,3},{7,5},{8,14},{10,8},{12,... | collective-permute-start | bytes 4718600 | tf_op jit(solution)/shard_map/ppermute | solution.py:16
  53.7 34.1 %collective-permute-start.12 = (bf16[4,2,48,2048]{3,2,1,0:T(8,128)(2,1)}, bf16[4,2,48,2048]{3,2,1,0:T(8,128)(2,1)}, u32[]{:S(2)}, u32[]{:S(2)}) collective-permute-start(bf16[4,2,48,2048]{3,2,1,0:T(8,128)(2,1)} %get-tuple-element.46), channel_id=1, source_target_pairs={{0,2},{2,4},{4,6},{6,0},{1,3},{3,5},{5,7},{7,1},{8,10},{10,12},{12... | collective-permute-start | bytes 4718600 | tf_op jit(solution)/shard_map/ppermute | solution.py:16
  55.5 47.1 %all-to-all-start = ((bf16[4,144,2048]{2,1,0:T(8,128)(2,1)}), bf16[4,144,2048]{2,1,0:T(8,128)(2,1)S(1)}, u32[]{:S(2)}, u32[]{:S(2)}) async-start(bf16[4,144,2048]{2,1,0:T(8,128)(2,1)} %broadcast_in_dim.23), calls=%async_computation | async-start | bytes 4718592 | tf_op jit(solution)/shard_map/all_to_all | solution.py:69
  89.9 16.3 %collective-permute-start.20 = (bf16[4,2,48,1024]{3,2,1,0:T(8,128)(2,1)}, bf16[4,2,48,1024]{3,2,1,0:T(8,128)(2,1)}, u32[]{:S(2)}, u32[]{:S(2)}) collective-permute-start(bf16[4,2,48,1024]{3,2,1,0:T(8,128)(2,1)} %slice.107), channel_id=1, source_target_pairs={{0,2},{2,4},{4,6},{6,0},{1,3},{3,5},{5,7},{7,1},{8,10},{10,12},{12... | collective-permute-start | bytes 2359304 | tf_op jit(solution)/shard_map/ppermute | solution.py:24
  92.0 15.6 %collective-permute-start.21 = (bf16[4,2,48,1024]{3,2,1,0:T(8,128)(2,1)}, bf16[4,2,48,1024]{3,2,1,0:T(8,128)(2,1)}, u32[]{:S(2)}, u32[]{:S(2)}) collective-permute-start(bf16[4,2,48,1024]{3,2,1,0:T(8,128)(2,1)} %slice.108), channel_id=1, source_target_pairs={{0,6},{2,0},{4,2},{6,4},{1,7},{3,1},{5,3},{7,5},{8,14},{10,8},{12,... | collective-permute-start | bytes 2359304 | tf_op jit(solution)/shard_map/ppermute | solution.py:25
  97.3 21.1 %collective-permute-start.14 = (bf16[4,2,48,1024]{3,2,1,0:T(8,128)(2,1)}, bf16[4,2,48,1024]{3,2,1,0:T(8,128)(2,1)}, u32[]{:S(2)}, u32[]{:S(2)}) collective-permute-start(bf16[4,2,48,1024]{3,2,1,0:T(8,128)(2,1)} %slice.103), channel_id=1, source_target_pairs={{0,8},{8,16},{16,24},{24,0},{1,9},{9,17},{17,25},{25,1},{2,10},{10... | collective-permute-start | bytes 2359304 | tf_op jit(solution)/shard_map/ppermute | solution.py:24
  99.4 21.5 %collective-permute-start.15 = (bf16[4,2,48,1024]{3,2,1,0:T(8,128)(2,1)}, bf16[4,2,48,1024]{3,2,1,0:T(8,128)(2,1)}, u32[]{:S(2)}, u32[]{:S(2)}) collective-permute-start(bf16[4,2,48,1024]{3,2,1,0:T(8,128)(2,1)} %slice.104), channel_id=1, source_target_pairs={{0,24},{8,0},{16,8},{24,16},{1,25},{9,1},{17,9},{25,17},{2,26},{10... | collective-permute-start | bytes 2359304 | tf_op jit(solution)/shard_map/ppermute | solution.py:25
  102.6 29.5 %collective-permute-start = (bf16[4,144,2048]{2,1,0:T(8,128)(2,1)S(1)}, bf16[4,144,2048]{2,1,0:T(8,128)(2,1)}, u32[]{:S(2)}, u32[]{:S(2)}) collective-permute-start(bf16[4,144,2048]{2,1,0:T(8,128)(2,1)S(1)} %all-to-all-done), channel_id=1, source_target_pairs={{0,32},{32,0},{1,33},{33,1},{2,34},{34,2},{3,35},{35,3},{4,36},{36... | collective-permute-start | bytes 7077896 | tf_op jit(solution)/shard_map/ppermute | solution.py:70
  106.2 36.6 %collective-permute-start.17 = (bf16[4,48,2048]{2,1,0:T(8,128)(2,1)}, bf16[4,48,2048]{2,1,0:T(8,128)(2,1)}, u32[]{:S(2)}, u32[]{:S(2)}) collective-permute-start(bf16[4,48,2048]{2,1,0:T(8,128)(2,1)} %slice_bitcast_fusion.1), channel_id=1, source_target_pairs={{0,24},{8,0},{16,8},{24,16},{1,25},{9,1},{17,9},{25,17},{2,26},{10... | collective-permute-start | bytes 2359304 | tf_op jit(solution)/shard_map/ppermute | solution.py:16
  107.6 35.2 %collective-permute-start.16 = (bf16[4,48,2048]{2,1,0:T(8,128)(2,1)}, bf16[4,48,2048]{2,1,0:T(8,128)(2,1)}, u32[]{:S(2)}, u32[]{:S(2)}) collective-permute-start(bf16[4,48,2048]{2,1,0:T(8,128)(2,1)} %slice_bitcast_fusion.1), channel_id=1, source_target_pairs={{0,8},{8,16},{16,24},{24,0},{1,9},{9,17},{17,25},{25,1},{2,10},{10... | collective-permute-start | bytes 2359304 | tf_op jit(solution)/shard_map/ppermute | solution.py:16
  118.4 24.4 %collective-permute-start.19 = (bf16[4,48,2048]{2,1,0:T(8,128)(2,1)S(1)}, bf16[4,48,2048]{2,1,0:T(8,128)(2,1)}, u32[]{:S(2)}, u32[]{:S(2)}) collective-permute-start(bf16[4,48,2048]{2,1,0:T(8,128)(2,1)S(1)} %slice_bitcast_fusion), channel_id=1, source_target_pairs={{0,6},{2,0},{4,2},{6,4},{1,7},{3,1},{5,3},{7,5},{8,14},{10,8},{12,... | collective-permute-start | bytes 2359304 | tf_op jit(solution)/shard_map/ppermute | solution.py:16
  120.9 21.9 %collective-permute-start.18 = (bf16[4,48,2048]{2,1,0:T(8,128)(2,1)S(1)}, bf16[4,48,2048]{2,1,0:T(8,128)(2,1)}, u32[]{:S(2)}, u32[]{:S(2)}) collective-permute-start(bf16[4,48,2048]{2,1,0:T(8,128)(2,1)S(1)} %slice_bitcast_fusion), channel_id=1, source_target_pairs={{0,2},{2,4},{4,6},{6,0},{1,3},{3,5},{5,7},{7,1},{8,10},{10,12},{12... | collective-permute-start | bytes 2359304 | tf_op jit(solution)/shard_map/ppermute | solution.py:16
  144.9 17.0 %collective-permute-start.22 = (bf16[4,48,1024]{2,1,0:T(8,128)(2,1)S(1)}, bf16[4,48,1024]{2,1,0:T(8,128)(2,1)S(1)}, u32[]{:S(2)}, u32[]{:S(2)}) collective-permute-start(bf16[4,48,1024]{2,1,0:T(8,128)(2,1)S(1)} %slice.112), channel_id=1, source_target_pairs={{0,8},{8,16},{16,24},{24,0},{1,9},{9,17},{17,25},{25,1},{2,10},{10... | collective-permute-start | bytes 1179656 | tf_op jit(solution)/shard_map/ppermute | solution.py:24
  145.2 16.6 %collective-permute-start.23 = (bf16[4,48,1024]{2,1,0:T(8,128)(2,1)S(1)}, bf16[4,48,1024]{2,1,0:T(8,128)(2,1)S(1)}, u32[]{:S(2)}, u32[]{:S(2)}) collective-permute-start(bf16[4,48,1024]{2,1,0:T(8,128)(2,1)S(1)} %slice.113), channel_id=1, source_target_pairs={{0,24},{8,0},{16,8},{24,16},{1,25},{9,1},{17,9},{25,17},{2,26},{10... | collective-permute-start | bytes 1179656 | tf_op jit(solution)/shard_map/ppermute | solution.py:25
  158.4 9.1 %collective-permute-start.24 = (bf16[4,48,1024]{2,1,0:T(8,128)(2,1)S(1)}, bf16[4,48,1024]{2,1,0:T(8,128)(2,1)S(1)}, u32[]{:S(2)}, u32[]{:S(2)}) collective-permute-start(bf16[4,48,1024]{2,1,0:T(8,128)(2,1)S(1)} %slice.115), channel_id=1, source_target_pairs={{0,2},{2,4},{4,6},{6,0},{1,3},{3,5},{5,7},{7,1},{8,10},{10,12},{12... | collective-permute-start | bytes 1179656 | tf_op jit(solution)/shard_map/ppermute | solution.py:24
  (12 other events, 124.3 us)

commit v14 on v11

--- a/solution.py
+++ b/solution.py
@@ -118,8 +118,8 @@
     half = chips * token_count
     theirs = down(hiddens, half, 2 * half)
     hiddens, theirs = lax.optimization_barrier((hiddens, theirs))
-    partner = lax.ppermute(theirs, "core", perm=SWAP)
-    partial = (down(hiddens, 0, half) + partner).astype(jnp.bfloat16)
+    partner = lax.ppermute(theirs.astype(jnp.bfloat16), "core", perm=SWAP)
+    partial = (down(hiddens, 0, half) + partner.astype(jnp.float32)).astype(jnp.bfloat16)
     back = lax.all_to_all(partial, CHIPS, split_axis=0, concat_axis=0, tiled=True)
     mixed = jnp.sum(back.astype(jnp.float32), axis=0)
     return mixed.astype(jnp.bfloat16)

time: 208 us -> 205 us (0.986)
  waiting for transfers between devices: 58 us -> 55 us
    ppermute x1, waiting for transfers between devices: 3.49 us -> 0.44 us  [per_device(): partner = lax.ppermute(theirs.astype(jnp.bfloat16), 'core', perm=SWAP)]
  transfers between devices with their start and end apart: 28 -> 28, of which waited for: 10 -> 10; matrix products, arithmetic and copies ran while one was open for 26% -> 27% of each run, Pallas kernels for 0% -> 0%
where the time goes in v14:
time: 205 us; the launch traced here: 204 us
  waiting for transfers between devices  55 us (27%)
  starting transfers between devices  48.3 us (24%)
  local copies, waits for them, and re-layouts  32.2 us (16%)
  blocking collectives  30.9 us (15%)
  matrix products  21.7 us (11%)
  other arithmetic  15.4 us (8%)
    all_to_all x1, blocking collectives, per_device(): lax.all_to_all(partial, CHIPS, split_axis=0, concat_axis=0, tiled=True)  30.9 us
    ppermute x6, starting transfers between devices, far_hop(): lax.ppermute(lax.slice_in_dim(from_plus, half, 2 * half, axis=split), axi...  19.7 us
    ppermute x6, waiting for transfers between devices, first_hop(): lax.ppermute(value, axis, perm=BEHIND)  18.2 us
    ppermute x6, waiting for transfers between devices, far_hop(): lax.ppermute(lax.slice_in_dim(from_minus, 0, half, axis=split), axis, per...  16.4 us
    ppermute x6, starting transfers between devices, first_hop(): lax.ppermute(value, axis, perm=BEHIND)  14.1 us
    another operation x12, other arithmetic, far_hop(): return jnp.stack([value, from_plus, far, from_minus])  13.1 us
    ppermute x1, waiting for transfers between devices, expert_weights(): got = lax.ppermute(send, 'ylo', perm=SWAP)  9.29 us
    ppermute x6, waiting for transfers between devices, first_hop(): lax.ppermute(value, axis, perm=AHEAD)  8.22 us
  transfers between devices with their start and end apart: 28, of which 10 were waited for; matrix products, arithmetic and copies ran while one was open for 27% of the time, Pallas kernels for 0%

profile of v14, /device:TPU:0, one launch (start us, length us, event | category | flops | bytes accessed | tf_op | source)
XLA Modules:
  0.0 203.9 jit_solution(18044829682549274040)
XLA Ops:
  8.5 9.3 %collective-permute-done.5 = bf16[3,48,2048]{2,1,0:T(8,128)(2,1)S(1)} collective-permute-done((bf16[3,48,2048]{2,1,0:T(8,128)(2,1)S(1)}, bf16[3,48,2048]{2,1,0:T(8,128)(2,1)S(1)}, u32[]{:S(2)}, u32[]{:S(2)}) %collective-permute-start.5) | collective-permute-done | bytes 589856 | tf_op jit(solution)/shard_map/ppermute | solution.py:46
  25.4 7.7 %collective-permute-done.7 = bf16[3,48,2048]{2,1,0:T(8,128)(2,1)S(1)} collective-permute-done((bf16[3,48,2048]{2,1,0:T(8,128)(2,1)S(1)}, bf16[3,48,2048]{2,1,0:T(8,128)(2,1)S(1)}, u32[]{:S(2)}, u32[]{:S(2)}) %collective-permute-start.7) | collective-permute-done | bytes 589856 | tf_op jit(solution)/shard_map/ppermute | solution.py:16
  33.7 2.8 %collective-permute-start.9 = (bf16[3,48,1024]{2,1,0:T(8,128)(2,1)S(1)}, bf16[3,48,1024]{2,1,0:T(8,128)(2,1)S(1)}, u32[]{:S(2)}, u32[]{:S(2)}) collective-permute-start(bf16[3,48,1024]{2,1,0:T(8,128)(2,1)S(1)} %slice.128), channel_id=1, source_target_pairs={{0,24},{8,0},{16,8},{24,16},{1,25},{9,1},{17,9},{25,17},{2,26},{10... | collective-permute-start | bytes 884744 | tf_op jit(solution)/shard_map/ppermute | solution.py:26
  36.9 4.4 %collective-permute-done.8 = bf16[3,48,1024]{2,1,0:T(8,128)(2,1)S(1)} collective-permute-done((bf16[3,48,1024]{2,1,0:T(8,128)(2,1)S(1)}, bf16[3,48,1024]{2,1,0:T(8,128)(2,1)S(1)}, u32[]{:S(2)}, u32[]{:S(2)}) %collective-permute-start.8) | collective-permute-done | bytes 294944 | tf_op jit(solution)/shard_map/ppermute | solution.py:25
  44.0 3.1 %collective-permute-start.10 = (bf16[4,2,48,2048]{3,2,1,0:T(8,128)(2,1)}, bf16[4,2,48,2048]{3,2,1,0:T(8,128)(2,1)}, u32[]{:S(2)}, u32[]{:S(2)}) collective-permute-start(bf16[4,2,48,2048]{3,2,1,0:T(8,128)(2,1)} %get-tuple-element.44), channel_id=1, source_target_pairs={{0,24},{8,0},{16,8},{24,16},{1,25},{9,1},{17,9},{25,17},{2,26},{10... | collective-permute-start | bytes 4718600 | tf_op jit(solution)/shard_map/ppermute | solution.py:16
  49.3 4.2 %collective-permute-start.14 = (bf16[4,2,48,2048]{3,2,1,0:T(8,128)(2,1)}, bf16[4,2,48,2048]{3,2,1,0:T(8,128)(2,1)}, u32[]{:S(2)}, u32[]{:S(2)}) collective-permute-start(bf16[4,2,48,2048]{3,2,1,0:T(8,128)(2,1)} %get-tuple-element.42), channel_id=1, source_target_pairs={{0,6},{2,0},{4,2},{6,4},{1,7},{3,1},{5,3},{7,5},{8,14},{10,8},{12,... | collective-permute-start | bytes 4718600 | tf_op jit(solution)/shard_map/ppermute | solution.py:16
  55.2 4.5 %all-to-all-start = ((bf16[4,144,2048]{2,1,0:T(8,128)(2,1)}), bf16[4,144,2048]{2,1,0:T(8,128)(2,1)S(1)}, u32[]{:S(2)}, u32[]{:S(2)}) async-start(bf16[4,144,2048]{2,1,0:T(8,128)(2,1)} %broadcast_in_dim.23), calls=%async_computation | async-start | bytes 4718592 | tf_op jit(solution)/shard_map/all_to_all | solution.py:70
  59.7 18.1 %collective-permute-done.10 = bf16[4,2,48,2048]{3,2,1,0:T(8,128)(2,1)} collective-permute-done((bf16[4,2,48,2048]{3,2,1,0:T(8,128)(2,1)}, bf16[4,2,48,2048]{3,2,1,0:T(8,128)(2,1)}, u32[]{:S(2)}, u32[]{:S(2)}) %collective-permute-start.10) | collective-permute-done | bytes 1572896 | tf_op jit(solution)/shard_map/ppermute | solution.py:16
  79.9 3.7 %collective-permute-start.13 = (bf16[2,2,48,2048]{3,2,1,0:T(8,128)(2,1)}, bf16[2,2,48,2048]{3,2,1,0:T(8,128)(2,1)}, u32[]{:S(2)}, u32[]{:S(2)}) collective-permute-start(bf16[2,2,48,2048]{3,2,1,0:T(8,128)(2,1)} %slice.130), channel_id=1, source_target_pairs={{0,24},{8,0},{16,8},{24,16},{1,25},{9,1},{17,9},{25,17},{2,26},{10... | collective-permute-start | bytes 2359304 | tf_op jit(solution)/shard_map/ppermute | solution.py:26
  89.1 4.3 %collective-permute-start.17 = (bf16[2,2,48,2048]{3,2,1,0:T(8,128)(2,1)}, bf16[2,2,48,2048]{3,2,1,0:T(8,128)(2,1)}, u32[]{:S(2)}, u32[]{:S(2)}) collective-permute-start(bf16[2,2,48,2048]{3,2,1,0:T(8,128)(2,1)} %slice.132), channel_id=1, source_target_pairs={{0,6},{2,0},{4,2},{6,4},{1,7},{3,1},{5,3},{7,5},{8,14},{10,8},{12,... | collective-permute-start | bytes 2359304 | tf_op jit(solution)/shard_map/ppermute | solution.py:26
  97.9 4.2 %collective-permute-done.12 = bf16[2,2,48,2048]{3,2,1,0:T(8,128)(2,1)} collective-permute-done((bf16[2,2,48,2048]{3,2,1,0:T(8,128)(2,1)}, bf16[2,2,48,2048]{3,2,1,0:T(8,128)(2,1)}, u32[]{:S(2)}, u32[]{:S(2)}) %collective-permute-start.12) | collective-permute-done | bytes 786464 | tf_op jit(solution)/shard_map/ppermute | solution.py:25
  103.6 2.4 %collective-permute-done.17 = bf16[2,2,48,2048]{3,2,1,0:T(8,128)(2,1)} collective-permute-done((bf16[2,2,48,2048]{3,2,1,0:T(8,128)(2,1)}, bf16[2,2,48,2048]{3,2,1,0:T(8,128)(2,1)}, u32[]{:S(2)}, u32[]{:S(2)}) %collective-permute-start.17) | collective-permute-done | bytes 786464 | tf_op jit(solution)/shard_map/ppermute | solution.py:26
  106.0 5.5 %collective-permute-done.16 = bf16[2,2,48,2048]{3,2,1,0:T(8,128)(2,1)} collective-permute-done((bf16[2,2,48,2048]{3,2,1,0:T(8,128)(2,1)}, bf16[2,2,48,2048]{3,2,1,0:T(8,128)(2,1)}, u32[]{:S(2)}, u32[]{:S(2)}) %collective-permute-start.16) | collective-permute-done | bytes 786464 | tf_op jit(solution)/shard_map/ppermute | solution.py:25
  113.1 3.1 %pad_maximum_fusion = bf16[4,4,2,48,2048]{4,3,2,1,0:T(8,128)(2,1)S(1)} fusion(bf16[1,4,2,48,2048]{4,3,2,1,0:T(8,128)(2,1)} %bitcast.17, bf16[1,4,2,48,2048]{4,3,2,1,0:T(8,128)(2,1)S(1)} %maximum_bitcast_fusion, bf16[1,4,2,48,2048]{4,3,2,1,0:T(8,128)(2,1)} %bitcast.15, bf16[1,4,2,48,2048]{4,3,2,1,0:T(8,128)(2,1)S(1)} %copy-done.2), kind=kLoop, calls=%fused_computation | loop fusion | flops 9437184 | bytes 12582912 | tf_op jit(solution)/shard_map/stack | solution.py:32
  116.2 3.0 %pad_maximum_fusion.1 = bf16[4,4,2,48,2048]{4,3,2,1,0:T(8,128)(2,1)S(1)} fusion(bf16[1,4,2,48,2048]{4,3,2,1,0:T(8,128)(2,1)} %bitcast.21, bf16[1,4,2,48,2048]{4,3,2,1,0:T(8,128)(2,1)S(1)} %maximum_bitcast_fusion.1, bf16[1,4,2,48,2048]{4,3,2,1,0:T(8,128)(2,1)} %bitcast.19, bf16[1,4,2,48,2048]{4,3,2,1,0:T(8,128)(2,1)S(1)} %copy-done.3), kind=kLoop, calls=%fused_computation.1 | loop fusion | flops 9437184 | bytes 12582912 | tf_op jit(solution)/shard_map/stack | solution.py:32
  119.2 3.0 %collective-permute-start.19 = (bf16[4,48,2048]{2,1,0:T(8,128)(2,1)S(1)}, bf16[4,48,2048]{2,1,0:T(8,128)(2,1)}, u32[]{:S(2)}, u32[]{:S(2)}) collective-permute-start(bf16[4,48,2048]{2,1,0:T(8,128)(2,1)S(1)} %slice_bitcast_fusion.1), channel_id=1, source_target_pairs={{0,24},{8,0},{16,8},{24,16},{1,25},{9,1},{17,9},{25,17},{2,26},{10... | collective-permute-start | bytes 2359304 | tf_op jit(solution)/shard_map/ppermute | solution.py:16
  124.3 2.6 %fusion.15 = (bf16[1,4,4,48,2048]{4,3,0,2,1:T(8,128)(2,1)}, bf16[1,4,4,48,2048]{4,3,0,2,1:T(8,128)(2,1)S(1)}) fusion(bf16[2,4,4,48,2048]{4,3,0,2,1:T(8,128)(2,1)S(1)} %bitcast.77), kind=kLoop, calls=%fused_computation.55 | loop fusion | bytes 12582912 | tf_op jit(solution)/shard_map/slice | solution.py:100
  131.7 3.4 %fusion.18 = f32[1024,768]{1,0:T(8,128)S(1)} fusion(bf16[1024,2048]{1,0:T(8,128)(2,1)S(1)} %bitcast.81, bf16[768,2048]{1,0:T(8,128)(2,1)S(1)} %bitcast.92), kind=kOutput, calls=%fused_computation.58 | convolution fusion | flops 3221225472 | bytes 10485760 | tf_op jit(solution)/shard_map/dot_general | solution.py:100
  135.2 3.4 %fusion.17 = f32[1024,768]{1,0:T(8,128)S(1)} fusion(bf16[1024,2048]{1,0:T(8,128)(2,1)S(1)} %bitcast.82, bf16[768,2048]{1,0:T(8,128)(2,1)S(1)} %bitcast.91), kind=kOutput, calls=%fused_computation.57 | convolution fusion | flops 3221225472 | bytes 10485760 | tf_op jit(solution)/shard_map/dot_general | solution.py:100
  140.9 3.5 %collective-permute-start.23 = (bf16[2,48,2048]{2,1,0:T(8,128)(2,1)S(1)}, bf16[2,48,2048]{2,1,0:T(8,128)(2,1)S(1)}, u32[]{:S(2)}, u32[]{:S(2)}) collective-permute-start(bf16[2,48,2048]{2,1,0:T(8,128)(2,1)S(1)} %slice.113), channel_id=1, source_target_pairs={{0,24},{8,0},{16,8},{24,16},{1,25},{9,1},{17,9},{25,17},{2,26},{10... | collective-permute-start | bytes 1179656 | tf_op jit(solution)/shard_map/ppermute | solution.py:26
  144.4 3.7 %multiply_convert_fusion = bf16[1024,768]{1,0:T(8,128)(2,1)S(1)} fusion(f32[1024,768]{1,0:T(8,128)S(1)} %fusion.18, bf16[1024,2048]{1,0:T(8,128)(2,1)S(1)} %bitcast.83, bf16[768,2048]{1,0:T(8,128)(2,1)S(1)} %bitcast.89), kind=kOutput, calls=%fused_computation.9 | convolution fusion | flops 3225944064 | bytes 12058624 | tf_op jit(solution)/shard_map/dot_general | solution.py:106
  148.1 3.7 %multiply_convert_fusion.1 = bf16[1024,768]{1,0:T(8,128)(2,1)S(1)} fusion(f32[1024,768]{1,0:T(8,128)S(1)} %fusion.17, bf16[1024,2048]{1,0:T(8,128)(2,1)S(1)} %bitcast.84, bf16[768,2048]{1,0:T(8,128)(2,1)S(1)} %bitcast.90), kind=kOutput, calls=%fused_computation.10 | convolution fusion | flops 3225944064 | bytes 12058624 | tf_op jit(solution)/shard_map/dot_general | solution.py:106
  154.0 3.2 %collective-permute-start.25 = (bf16[2,48,2048]{2,1,0:T(8,128)(2,1)S(1)}, bf16[2,48,2048]{2,1,0:T(8,128)(2,1)S(1)}, u32[]{:S(2)}, u32[]{:S(2)}) collective-permute-start(bf16[2,48,2048]{2,1,0:T(8,128)(2,1)S(1)} %slice.116), channel_id=1, source_target_pairs={{0,6},{2,0},{4,2},{6,4},{1,7},{3,1},{5,3},{7,5},{8,14},{10,8},{12,... | collective-permute-start | bytes 1179656 | tf_op jit(solution)/shard_map/ppermute | solution.py:26
  171.7 30.9 %all_to_all.10 = bf16[4,128,2048]{2,1,0:T(8,128)(2,1)S(1)} all-to-all(bf16[4,128,2048]{2,1,0:T(8,128)(2,1)S(1)} %add_convert_fusion), channel_id=1, replica_groups=mesh['yhi'=2,'core'=2,'x'=4,'z'=4,'ylo'=2] {'yhi','ylo'}, dimensions={0} | all-to-all | bytes 4194304 | tf_op jit(solution)/shard_map/all_to_all | solution.py:123
  (106 shorter events, 65.5 us)
Async XLA Ops:
  2.7 15.1 %collective-permute-start.5 = (bf16[3,48,2048]{2,1,0:T(8,128)(2,1)S(1)}, bf16[3,48,2048]{2,1,0:T(8,128)(2,1)S(1)}, u32[]{:S(2)}, u32[]{:S(2)}) collective-permute-start(bf16[3,48,2048]{2,1,0:T(8,128)(2,1)S(1)} %get-tuple-element.45), channel_id=1, source_target_pairs={{0,1},{1,0},{2,3},{3,2},{4,5},{5,4},{6,7},{7,6},{8,9},{9,8},{10,11... | collective-permute-start | bytes 1769480 | tf_op jit(solution)/shard_map/ppermute | solution.py:46
  4.4 17.1 %collective-permute-start.2 = (bf16[3,48,2048]{2,1,0:T(8,128)(2,1)S(1)}, bf16[3,48,2048]{2,1,0:T(8,128)(2,1)S(1)}, u32[]{:S(2)}, u32[]{:S(2)}) collective-permute-start(bf16[3,48,2048]{2,1,0:T(8,128)(2,1)S(1)} %bitcast.93), channel_id=1, source_target_pairs={{0,2},{2,4},{4,6},{6,0},{1,3},{3,5},{5,7},{7,1},{8,10},{10,12},{12... | collective-permute-start | bytes 1769480 | tf_op jit(solution)/shard_map/ppermute | solution.py:16
  6.4 16.8 %collective-permute-start.1 = (bf16[3,48,2048]{2,1,0:T(8,128)(2,1)S(1)}, bf16[3,48,2048]{2,1,0:T(8,128)(2,1)S(1)}, u32[]{:S(2)}, u32[]{:S(2)}) collective-permute-start(bf16[3,48,2048]{2,1,0:T(8,128)(2,1)S(1)} %bitcast.94), channel_id=1, source_target_pairs={{0,6},{2,0},{4,2},{6,4},{1,7},{3,1},{5,3},{7,5},{8,14},{10,8},{12,... | collective-permute-start | bytes 1769480 | tf_op jit(solution)/shard_map/ppermute | solution.py:16
  17.8 15.4 %collective-permute-start.7 = (bf16[3,48,2048]{2,1,0:T(8,128)(2,1)S(1)}, bf16[3,48,2048]{2,1,0:T(8,128)(2,1)S(1)}, u32[]{:S(2)}, u32[]{:S(2)}) collective-permute-start(bf16[3,48,2048]{2,1,0:T(8,128)(2,1)S(1)} %collective-permute-done.5), channel_id=1, source_target_pairs={{0,8},{8,16},{16,24},{24,0},{1,9},{9,17},{17,25},{25,1},{2,10},{10... | collective-permute-start | bytes 1769480 | tf_op jit(solution)/shard_map/ppermute | solution.py:16
  19.4 14.3 %collective-permute-start.6 = (bf16[3,48,2048]{2,1,0:T(8,128)(2,1)S(1)}, bf16[3,48,2048]{2,1,0:T(8,128)(2,1)S(1)}, u32[]{:S(2)}, u32[]{:S(2)}) collective-permute-start(bf16[3,48,2048]{2,1,0:T(8,128)(2,1)S(1)} %collective-permute-done.5), channel_id=1, source_target_pairs={{0,24},{8,0},{16,8},{24,16},{1,25},{9,1},{17,9},{25,17},{2,26},{10... | collective-permute-start | bytes 1769480 | tf_op jit(solution)/shard_map/ppermute | solution.py:16
  21.5 15.0 %collective-permute-start.3 = (bf16[3,48,1024]{2,1,0:T(8,128)(2,1)S(1)}, bf16[3,48,1024]{2,1,0:T(8,128)(2,1)S(1)}, u32[]{:S(2)}, u32[]{:S(2)}) collective-permute-start(bf16[3,48,1024]{2,1,0:T(8,128)(2,1)S(1)} %slice.125), channel_id=1, source_target_pairs={{0,2},{2,4},{4,6},{6,0},{1,3},{3,5},{5,7},{7,1},{8,10},{10,12},{12... | collective-permute-start | bytes 884744 | tf_op jit(solution)/shard_map/ppermute | solution.py:25
  23.2 13.4 %collective-permute-start.4 = (bf16[3,48,1024]{2,1,0:T(8,128)(2,1)S(1)}, bf16[3,48,1024]{2,1,0:T(8,128)(2,1)S(1)}, u32[]{:S(2)}, u32[]{:S(2)}) collective-permute-start(bf16[3,48,1024]{2,1,0:T(8,128)(2,1)S(1)} %slice.126), channel_id=1, source_target_pairs={{0,6},{2,0},{4,2},{6,4},{1,7},{3,1},{5,3},{7,5},{8,14},{10,8},{12,... | collective-permute-start | bytes 884744 | tf_op jit(solution)/shard_map/ppermute | solution.py:26
  44.0 33.8 %collective-permute-start.10 = (bf16[4,2,48,2048]{3,2,1,0:T(8,128)(2,1)}, bf16[4,2,48,2048]{3,2,1,0:T(8,128)(2,1)}, u32[]{:S(2)}, u32[]{:S(2)}) collective-permute-start(bf16[4,2,48,2048]{3,2,1,0:T(8,128)(2,1)} %get-tuple-element.44), channel_id=1, source_target_pairs={{0,24},{8,0},{16,8},{24,16},{1,25},{9,1},{17,9},{25,17},{2,26},{10... | collective-permute-start | bytes 4718600 | tf_op jit(solution)/shard_map/ppermute | solution.py:16
  47.1 36.5 %collective-permute-start.11 = (bf16[4,2,48,2048]{3,2,1,0:T(8,128)(2,1)}, bf16[4,2,48,2048]{3,2,1,0:T(8,128)(2,1)}, u32[]{:S(2)}, u32[]{:S(2)}) collective-permute-start(bf16[4,2,48,2048]{3,2,1,0:T(8,128)(2,1)} %get-tuple-element.44), channel_id=1, source_target_pairs={{0,8},{8,16},{16,24},{24,0},{1,9},{9,17},{17,25},{25,1},{2,10},{10... | collective-permute-start | bytes 4718600 | tf_op jit(solution)/shard_map/ppermute | solution.py:16
  49.3 37.7 %collective-permute-start.14 = (bf16[4,2,48,2048]{3,2,1,0:T(8,128)(2,1)}, bf16[4,2,48,2048]{3,2,1,0:T(8,128)(2,1)}, u32[]{:S(2)}, u32[]{:S(2)}) collective-permute-start(bf16[4,2,48,2048]{3,2,1,0:T(8,128)(2,1)} %get-tuple-element.42), channel_id=1, source_target_pairs={{0,6},{2,0},{4,2},{6,4},{1,7},{3,1},{5,3},{7,5},{8,14},{10,8},{12,... | collective-permute-start | bytes 4718600 | tf_op jit(solution)/shard_map/ppermute | solution.py:16
  53.5 39.8 %collective-permute-start.15 = (bf16[4,2,48,2048]{3,2,1,0:T(8,128)(2,1)}, bf16[4,2,48,2048]{3,2,1,0:T(8,128)(2,1)}, u32[]{:S(2)}, u32[]{:S(2)}) collective-permute-start(bf16[4,2,48,2048]{3,2,1,0:T(8,128)(2,1)} %get-tuple-element.42), channel_id=1, source_target_pairs={{0,2},{2,4},{4,6},{6,0},{1,3},{3,5},{5,7},{7,1},{8,10},{10,12},{12... | collective-permute-start | bytes 4718600 | tf_op jit(solution)/shard_map/ppermute | solution.py:16
  55.2 42.3 %all-to-all-start = ((bf16[4,144,2048]{2,1,0:T(8,128)(2,1)}), bf16[4,144,2048]{2,1,0:T(8,128)(2,1)S(1)}, u32[]{:S(2)}, u32[]{:S(2)}) async-start(bf16[4,144,2048]{2,1,0:T(8,128)(2,1)} %broadcast_in_dim.23), calls=%async_computation | async-start | bytes 4718592 | tf_op jit(solution)/shard_map/all_to_all | solution.py:70
  79.9 17.9 %collective-permute-start.13 = (bf16[2,2,48,2048]{3,2,1,0:T(8,128)(2,1)}, bf16[2,2,48,2048]{3,2,1,0:T(8,128)(2,1)}, u32[]{:S(2)}, u32[]{:S(2)}) collective-permute-start(bf16[2,2,48,2048]{3,2,1,0:T(8,128)(2,1)} %slice.130), channel_id=1, source_target_pairs={{0,24},{8,0},{16,8},{24,16},{1,25},{9,1},{17,9},{25,17},{2,26},{10... | collective-permute-start | bytes 2359304 | tf_op jit(solution)/shard_map/ppermute | solution.py:26
  85.7 16.3 %collective-permute-start.12 = (bf16[2,2,48,2048]{3,2,1,0:T(8,128)(2,1)}, bf16[2,2,48,2048]{3,2,1,0:T(8,128)(2,1)}, u32[]{:S(2)}, u32[]{:S(2)}) collective-permute-start(bf16[2,2,48,2048]{3,2,1,0:T(8,128)(2,1)} %slice.129), channel_id=1, source_target_pairs={{0,8},{8,16},{16,24},{24,0},{1,9},{9,17},{17,25},{25,1},{2,10},{10... | collective-permute-start | bytes 2359304 | tf_op jit(solution)/shard_map/ppermute | solution.py:25
  89.1 17.0 %collective-permute-start.17 = (bf16[2,2,48,2048]{3,2,1,0:T(8,128)(2,1)}, bf16[2,2,48,2048]{3,2,1,0:T(8,128)(2,1)}, u32[]{:S(2)}, u32[]{:S(2)}) collective-permute-start(bf16[2,2,48,2048]{3,2,1,0:T(8,128)(2,1)} %slice.132), channel_id=1, source_target_pairs={{0,6},{2,0},{4,2},{6,4},{1,7},{3,1},{5,3},{7,5},{8,14},{10,8},{12,... | collective-permute-start | bytes 2359304 | tf_op jit(solution)/shard_map/ppermute | solution.py:26
  95.4 16.1 %collective-permute-start.16 = (bf16[2,2,48,2048]{3,2,1,0:T(8,128)(2,1)}, bf16[2,2,48,2048]{3,2,1,0:T(8,128)(2,1)}, u32[]{:S(2)}, u32[]{:S(2)}) collective-permute-start(bf16[2,2,48,2048]{3,2,1,0:T(8,128)(2,1)} %slice.131), channel_id=1, source_target_pairs={{0,2},{2,4},{4,6},{6,0},{1,3},{3,5},{5,7},{7,1},{8,10},{10,12},{12... | collective-permute-start | bytes 2359304 | tf_op jit(solution)/shard_map/ppermute | solution.py:25
  97.6 30.4 %collective-permute-start = (bf16[4,144,2048]{2,1,0:T(8,128)(2,1)S(1)}, bf16[4,144,2048]{2,1,0:T(8,128)(2,1)}, u32[]{:S(2)}, u32[]{:S(2)}) collective-permute-start(bf16[4,144,2048]{2,1,0:T(8,128)(2,1)S(1)} %all-to-all-done), channel_id=1, source_target_pairs={{0,32},{32,0},{1,33},{33,1},{2,34},{34,2},{3,35},{35,3},{4,36},{36... | collective-permute-start | bytes 7077896 | tf_op jit(solution)/shard_map/ppermute | solution.py:71
  119.2 19.5 %collective-permute-start.19 = (bf16[4,48,2048]{2,1,0:T(8,128)(2,1)S(1)}, bf16[4,48,2048]{2,1,0:T(8,128)(2,1)}, u32[]{:S(2)}, u32[]{:S(2)}) collective-permute-start(bf16[4,48,2048]{2,1,0:T(8,128)(2,1)S(1)} %slice_bitcast_fusion.1), channel_id=1, source_target_pairs={{0,24},{8,0},{16,8},{24,16},{1,25},{9,1},{17,9},{25,17},{2,26},{10... | collective-permute-start | bytes 2359304 | tf_op jit(solution)/shard_map/ppermute | solution.py:16
  122.3 16.4 %collective-permute-start.18 = (bf16[4,48,2048]{2,1,0:T(8,128)(2,1)S(1)}, bf16[4,48,2048]{2,1,0:T(8,128)(2,1)}, u32[]{:S(2)}, u32[]{:S(2)}) collective-permute-start(bf16[4,48,2048]{2,1,0:T(8,128)(2,1)S(1)} %slice_bitcast_fusion.1), channel_id=1, source_target_pairs={{0,8},{8,16},{16,24},{24,0},{1,9},{9,17},{17,25},{25,1},{2,10},{10... | collective-permute-start | bytes 2359304 | tf_op jit(solution)/shard_map/ppermute | solution.py:16
  122.3 16.5 %collective-permute-start.21 = (bf16[4,48,2048]{2,1,0:T(8,128)(2,1)S(1)}, bf16[4,48,2048]{2,1,0:T(8,128)(2,1)}, u32[]{:S(2)}, u32[]{:S(2)}) collective-permute-start(bf16[4,48,2048]{2,1,0:T(8,128)(2,1)S(1)} %copy-done.4), channel_id=1, source_target_pairs={{0,6},{2,0},{4,2},{6,4},{1,7},{3,1},{5,3},{7,5},{8,14},{10,8},{12,... | collective-permute-start | bytes 2359304 | tf_op jit(solution)/shard_map/ppermute | solution.py:16
  122.3 16.5 %collective-permute-start.20 = (bf16[4,48,2048]{2,1,0:T(8,128)(2,1)S(1)}, bf16[4,48,2048]{2,1,0:T(8,128)(2,1)}, u32[]{:S(2)}, u32[]{:S(2)}) collective-permute-start(bf16[4,48,2048]{2,1,0:T(8,128)(2,1)S(1)} %copy-done.4), channel_id=1, source_target_pairs={{0,2},{2,4},{4,6},{6,0},{1,3},{3,5},{5,7},{7,1},{8,10},{10,12},{12... | collective-permute-start | bytes 2359304 | tf_op jit(solution)/shard_map/ppermute | solution.py:16
  140.8 16.4 %collective-permute-start.22 = (bf16[2,48,2048]{2,1,0:T(8,128)(2,1)S(1)}, bf16[2,48,2048]{2,1,0:T(8,128)(2,1)S(1)}, u32[]{:S(2)}, u32[]{:S(2)}) collective-permute-start(bf16[2,48,2048]{2,1,0:T(8,128)(2,1)S(1)} %slice.112), channel_id=1, source_target_pairs={{0,8},{8,16},{16,24},{24,0},{1,9},{9,17},{17,25},{25,1},{2,10},{10... | collective-permute-start | bytes 1179656 | tf_op jit(solution)/shard_map/ppermute | solution.py:25
  140.9 16.3 %collective-permute-start.23 = (bf16[2,48,2048]{2,1,0:T(8,128)(2,1)S(1)}, bf16[2,48,2048]{2,1,0:T(8,128)(2,1)S(1)}, u32[]{:S(2)}, u32[]{:S(2)}) collective-permute-start(bf16[2,48,2048]{2,1,0:T(8,128)(2,1)S(1)} %slice.113), channel_id=1, source_target_pairs={{0,24},{8,0},{16,8},{24,16},{1,25},{9,1},{17,9},{25,17},{2,26},{10... | collective-permute-start | bytes 1179656 | tf_op jit(solution)/shard_map/ppermute | solution.py:26
  153.9 9.1 %collective-permute-start.24 = (bf16[2,48,2048]{2,1,0:T(8,128)(2,1)S(1)}, bf16[2,48,2048]{2,1,0:T(8,128)(2,1)S(1)}, u32[]{:S(2)}, u32[]{:S(2)}) collective-permute-start(bf16[2,48,2048]{2,1,0:T(8,128)(2,1)S(1)} %slice.115), channel_id=1, source_target_pairs={{0,2},{2,4},{4,6},{6,0},{1,3},{3,5},{5,7},{7,1},{8,10},{10,12},{12... | collective-permute-start | bytes 1179656 | tf_op jit(solution)/shard_map/ppermute | solution.py:25
  (13 other events, 125.7 us)

commit v15 on v12

--- a/solution.py
+++ b/solution.py
@@ -63,8 +63,8 @@
 
 
 def spread(value, chips):
-    sent = jnp.broadcast_to(value[None], (chips,) + value.shape)
-    mine = lax.all_to_all(sent, CHIPS, split_axis=0, concat_axis=0, tiled=True)
+    del chips
+    mine = lax.all_gather(value, CHIPS, axis=0, tiled=False)
     other = lax.ppermute(mine, "core", perm=SWAP)
     return mine, other
 

time: 205 us -> 215 us (1.049)
  between operations: 0.47 us -> 13.9 us
  local copies, waits for them, and re-layouts: 32.1 us -> 23 us
  waiting for transfers between devices: 55 us -> 62.5 us
  starting transfers between devices: 48.3 us -> 43.2 us
  other arithmetic: 15.3 us -> 17.7 us
    ppermute x6, waiting for transfers between devices: 18.2 us -> 24.5 us  [first_hop(): lax.ppermute(value, axis, perm=BEHIND)]
    all_to_all x1 -> x0, starting transfers between devices: 4.46 us -> none  [spread(): mine = lax.all_to_all(sent, CHIPS, split_axis=0, concat_axis=0, tiled=True)]
    ppermute x6, waiting for transfers between devices: 16.5 us -> 18.7 us  [far_hop(): lax.ppermute(from_minus[..., :half], axis, perm=AHEAD)]
  transfers between devices with their start and end apart: 28 -> 28, of which waited for: 10 -> 12; matrix products, arithmetic and copies ran while one was open for 27% -> 22% of each run, Pallas kernels for 0% -> 0%
where the time goes in v15:
time: 215 us; the launch traced here: 214 us
  waiting for transfers between devices  62.5 us (29%)
  starting transfers between devices  43.2 us (20%)
  blocking collectives  31.9 us (15%)
  local copies, waits for them, and re-layouts  23 us (11%)
  matrix products  21.6 us (10%)
  other arithmetic  17.7 us (8%)
  between operations  13.9 us (6%)
    all_to_all x1, blocking collectives, per_device(): lax.all_to_all(partial, CHIPS, split_axis=0, concat_axis=0, tiled=True)  31.9 us
    ppermute x6, waiting for transfers between devices, first_hop(): lax.ppermute(value, axis, perm=BEHIND)  24.5 us
    ppermute x6, starting transfers between devices, far_hop(): lax.ppermute(from_plus[..., half:], axis, perm=BEHIND)  19 us
    ppermute x6, waiting for transfers between devices, far_hop(): lax.ppermute(from_minus[..., :half], axis, perm=AHEAD)  18.7 us
    another operation x12, other arithmetic, far_hop(): return jnp.stack([value, from_plus, far, from_minus])  14.2 us
    ppermute x6, starting transfers between devices, first_hop(): lax.ppermute(value, axis, perm=BEHIND)  14 us
    ppermute x1, waiting for transfers between devices, expert_weights(): got = lax.ppermute(send, 'ylo', perm=SWAP)  9.29 us
    dot_general x2, matrix products, per_device(): jnp.dot(late_rows, weights[1].T, preferred_element_type=jnp.float32)  7.44 us
  transfers between devices with their start and end apart: 28, of which 12 were waited for; matrix products, arithmetic and copies ran while one was open for 22% of the time, Pallas kernels for 0%

profile of v15, /device:TPU:0, one launch (start us, length us, event | category | flops | bytes accessed | tf_op | source)
XLA Modules:
  0.0 213.8 jit_solution(2841120918715081441)
XLA Ops:
  15.0 9.3 %collective-permute-done.5 = bf16[3,48,2048]{2,1,0:T(8,128)(2,1)S(1)} collective-permute-done((bf16[3,48,2048]{2,1,0:T(8,128)(2,1)S(1)}, bf16[3,48,2048]{2,1,0:T(8,128)(2,1)S(1)}, u32[]{:S(2)}, u32[]{:S(2)}) %collective-permute-start.5) | collective-permute-done | bytes 589856 | tf_op jit(solution)/shard_map/ppermute | solution.py:43
  31.3 2.1 collective-permute-start.4
  34.3 5.4 %collective-permute-done.7 = bf16[3,48,2048]{2,1,0:T(8,128)(2,1)S(1)} collective-permute-done((bf16[3,48,2048]{2,1,0:T(8,128)(2,1)S(1)}, bf16[3,48,2048]{2,1,0:T(8,128)(2,1)S(1)}, u32[]{:S(2)}, u32[]{:S(2)}) %collective-permute-start.7) | collective-permute-done | bytes 589856 | tf_op jit(solution)/shard_map/ppermute | solution.py:16
  40.3 2.8 %collective-permute-start.9 = (bf16[3,48,1024]{2,1,0:T(8,128)(2,1)S(1)}, bf16[3,48,1024]{2,1,0:T(8,128)(2,1)S(1)}, u32[]{:S(2)}, u32[]{:S(2)}) collective-permute-start(bf16[3,48,1024]{2,1,0:T(8,128)(2,1)S(1)} %slice.129), channel_id=1, source_target_pairs={{0,24},{8,0},{16,8},{24,16},{1,25},{9,1},{17,9},{25,17},{2,26},{10... | collective-permute-start | bytes 884744 | tf_op jit(solution)/shard_map/ppermute | solution.py:25
  48.4 2.3 %slice_bitcast_fusion.3 = (bf16[1,4,2,48,2048]{4,3,2,1,0:T(8,128)(2,1)}, bf16[4,2,48,2048]{3,2,1,0:T(8,128)(2,1)}) fusion(bf16[4,3,48,2048]{3,2,1,0:T(8,128)(2,1)S(1)} %pad_maximum_fusion.4), kind=kLoop, calls=%fused_computation.56 | loop fusion | bytes 4718592 | tf_op jit(solution)/shard_map/stack | solution.py:29
  50.8 3.1 %collective-permute-start.10 = (bf16[4,2,48,2048]{3,2,1,0:T(8,128)(2,1)}, bf16[4,2,48,2048]{3,2,1,0:T(8,128)(2,1)}, u32[]{:S(2)}, u32[]{:S(2)}) collective-permute-start(bf16[4,2,48,2048]{3,2,1,0:T(8,128)(2,1)} %get-tuple-element.44), channel_id=1, source_target_pairs={{0,24},{8,0},{16,8},{24,16},{1,25},{9,1},{17,9},{25,17},{2,26},{10... | collective-permute-start | bytes 4718600 | tf_op jit(solution)/shard_map/ppermute | solution.py:16
  55.9 4.3 %collective-permute-start.14 = (bf16[4,2,48,2048]{3,2,1,0:T(8,128)(2,1)}, bf16[4,2,48,2048]{3,2,1,0:T(8,128)(2,1)}, u32[]{:S(2)}, u32[]{:S(2)}) collective-permute-start(bf16[4,2,48,2048]{3,2,1,0:T(8,128)(2,1)} %get-tuple-element.42), channel_id=1, source_target_pairs={{0,6},{2,0},{4,2},{6,4},{1,7},{3,1},{5,3},{7,5},{8,14},{10,8},{12,... | collective-permute-start | bytes 4718600 | tf_op jit(solution)/shard_map/ppermute | solution.py:16
  60.1 24.5 %collective-permute-done.10 = bf16[4,2,48,2048]{3,2,1,0:T(8,128)(2,1)} collective-permute-done((bf16[4,2,48,2048]{3,2,1,0:T(8,128)(2,1)}, bf16[4,2,48,2048]{3,2,1,0:T(8,128)(2,1)}, u32[]{:S(2)}, u32[]{:S(2)}) %collective-permute-start.10) | collective-permute-done | bytes 1572896 | tf_op jit(solution)/shard_map/ppermute | solution.py:16
  86.7 3.7 %collective-permute-start.13 = (bf16[4,2,48,1024]{3,2,1,0:T(8,128)(2,1)}, bf16[4,2,48,1024]{3,2,1,0:T(8,128)(2,1)}, u32[]{:S(2)}, u32[]{:S(2)}) collective-permute-start(bf16[4,2,48,1024]{3,2,1,0:T(8,128)(2,1)} %slice.131), channel_id=1, source_target_pairs={{0,24},{8,0},{16,8},{24,16},{1,25},{9,1},{17,9},{25,17},{2,26},{10... | collective-permute-start | bytes 2359304 | tf_op jit(solution)/shard_map/ppermute | solution.py:25
  94.6 4.3 %collective-permute-start.17 = (bf16[4,2,48,1024]{3,2,1,0:T(8,128)(2,1)}, bf16[4,2,48,1024]{3,2,1,0:T(8,128)(2,1)}, u32[]{:S(2)}, u32[]{:S(2)}) collective-permute-start(bf16[4,2,48,1024]{3,2,1,0:T(8,128)(2,1)} %slice.133), channel_id=1, source_target_pairs={{0,6},{2,0},{4,2},{6,4},{1,7},{3,1},{5,3},{7,5},{8,14},{10,8},{12,... | collective-permute-start | bytes 2359304 | tf_op jit(solution)/shard_map/ppermute | solution.py:25
  103.4 5.5 %collective-permute-done.12 = bf16[4,2,48,1024]{3,2,1,0:T(8,128)(2,1)} collective-permute-done((bf16[4,2,48,1024]{3,2,1,0:T(8,128)(2,1)}, bf16[4,2,48,1024]{3,2,1,0:T(8,128)(2,1)}, u32[]{:S(2)}, u32[]{:S(2)}) %collective-permute-start.12) | collective-permute-done | bytes 786464 | tf_op jit(solution)/shard_map/ppermute | solution.py:24
  111.6 5.5 %collective-permute-done.16 = bf16[4,2,48,1024]{3,2,1,0:T(8,128)(2,1)} collective-permute-done((bf16[4,2,48,1024]{3,2,1,0:T(8,128)(2,1)}, bf16[4,2,48,1024]{3,2,1,0:T(8,128)(2,1)}, u32[]{:S(2)}, u32[]{:S(2)}) %collective-permute-start.16) | collective-permute-done | bytes 786464 | tf_op jit(solution)/shard_map/ppermute | solution.py:24
  118.6 3.1 %pad_maximum_fusion = bf16[4,4,2,48,2048]{4,3,2,1,0:T(8,128)(2,1)S(1)} fusion(bf16[1,4,2,48,2048]{4,3,2,1,0:T(8,128)(2,1)} %bitcast.18, bf16[1,4,2,48,2048]{4,3,2,1,0:T(8,128)(2,1)S(1)} %maximum_bitcast_fusion, bf16[1,4,2,48,2048]{4,3,2,1,0:T(8,128)(2,1)} %bitcast.16, bf16[1,4,2,48,2048]{4,3,2,1,0:T(8,128)(2,1)S(1)} %copy-done.2), kind=kLoop, calls=%fused_computation | loop fusion | flops 9437184 | bytes 12582912 | tf_op jit(solution)/shard_map/stack | solution.py:29
  121.7 3.0 %pad_maximum_fusion.1 = bf16[4,4,2,48,2048]{4,3,2,1,0:T(8,128)(2,1)S(1)} fusion(bf16[1,4,2,48,2048]{4,3,2,1,0:T(8,128)(2,1)} %bitcast.22, bf16[1,4,2,48,2048]{4,3,2,1,0:T(8,128)(2,1)S(1)} %maximum_bitcast_fusion.1, bf16[1,4,2,48,2048]{4,3,2,1,0:T(8,128)(2,1)} %bitcast.20, bf16[1,4,2,48,2048]{4,3,2,1,0:T(8,128)(2,1)S(1)} %copy-done.3), kind=kLoop, calls=%fused_computation.1 | loop fusion | flops 9437184 | bytes 12582912 | tf_op jit(solution)/shard_map/stack | solution.py:29
  124.7 3.0 %collective-permute-start.19 = (bf16[4,48,2048]{2,1,0:T(8,128)(2,1)S(1)}, bf16[4,48,2048]{2,1,0:T(8,128)(2,1)S(1)}, u32[]{:S(2)}, u32[]{:S(2)}) collective-permute-start(bf16[4,48,2048]{2,1,0:T(8,128)(2,1)S(1)} %slice_bitcast_fusion.1), channel_id=1, source_target_pairs={{0,24},{8,0},{16,8},{24,16},{1,25},{9,1},{17,9},{25,17},{2,26},{10... | collective-permute-start | bytes 2359304 | tf_op jit(solution)/shard_map/ppermute | solution.py:16
  130.9 2.5 %fusion.17 = (bf16[1,4,4,48,2048]{4,3,0,2,1:T(8,128)(2,1)S(1)}, bf16[1,4,4,48,2048]{4,3,0,2,1:T(8,128)(2,1)}) fusion(bf16[2,4,4,48,2048]{4,3,0,2,1:T(8,128)(2,1)S(1)} %bitcast.77), kind=kLoop, calls=%fused_computation.58 | loop fusion | bytes 12582912 | tf_op jit(solution)/shard_map/slice | solution.py:100
  133.8 3.4 %fusion.19 = f32[1024,768]{1,0:T(8,128)S(1)} fusion(bf16[1024,2048]{1,0:T(8,128)(2,1)S(1)} %bitcast.85, bf16[768,2048]{1,0:T(8,128)(2,1)S(1)} %bitcast.95), kind=kOutput, calls=%fused_computation.60 | convolution fusion | flops 3221225472 | bytes 10485760 | tf_op jit(solution)/shard_map/dot_general | solution.py:97
  137.2 3.4 %fusion.18 = f32[1024,768]{1,0:T(8,128)S(1)} fusion(bf16[1024,2048]{1,0:T(8,128)(2,1)S(1)} %bitcast.86, bf16[768,2048]{1,0:T(8,128)(2,1)S(1)} %bitcast.96), kind=kOutput, calls=%fused_computation.59 | convolution fusion | flops 3221225472 | bytes 10485760 | tf_op jit(solution)/shard_map/dot_general | solution.py:97
  142.2 3.7 %multiply_convert_fusion.1 = bf16[1024,768]{1,0:T(8,128)(2,1)S(1)} fusion(f32[1024,768]{1,0:T(8,128)S(1)} %fusion.18, bf16[1024,2048]{1,0:T(8,128)(2,1)S(1)} %bitcast.87, bf16[768,2048]{1,0:T(8,128)(2,1)S(1)} %bitcast.94), kind=kOutput, calls=%fused_computation.13 | convolution fusion | flops 3225944064 | bytes 12058624 | tf_op jit(solution)/shard_map/dot_general | solution.py:103
  145.9 3.7 %multiply_convert_fusion = bf16[1024,768]{1,0:T(8,128)(2,1)S(1)} fusion(f32[1024,768]{1,0:T(8,128)S(1)} %fusion.19, bf16[1024,2048]{1,0:T(8,128)(2,1)S(1)} %bitcast.88, bf16[768,2048]{1,0:T(8,128)(2,1)S(1)} %bitcast.93), kind=kOutput, calls=%fused_computation.12 | convolution fusion | flops 3225944064 | bytes 12058624 | tf_op jit(solution)/shard_map/dot_general | solution.py:103
  151.3 2.8 %collective-permute-start.25 = (bf16[4,48,1024]{2,1,0:T(8,128)(2,1)S(1)}, bf16[4,48,1024]{2,1,0:T(8,128)(2,1)S(1)}, u32[]{:S(2)}, u32[]{:S(2)}) collective-permute-start(bf16[4,48,1024]{2,1,0:T(8,128)(2,1)S(1)} %slice.116), channel_id=1, source_target_pairs={{0,6},{2,0},{4,2},{6,4},{1,7},{3,1},{5,3},{7,5},{8,14},{10,8},{12,... | collective-permute-start | bytes 1179656 | tf_op jit(solution)/shard_map/ppermute | solution.py:25
  154.1 3.2 %collective-permute-start.23 = (bf16[4,48,1024]{2,1,0:T(8,128)(2,1)S(1)}, bf16[4,48,1024]{2,1,0:T(8,128)(2,1)S(1)}, u32[]{:S(2)}, u32[]{:S(2)}) collective-permute-start(bf16[4,48,1024]{2,1,0:T(8,128)(2,1)S(1)} %slice.113), channel_id=1, source_target_pairs={{0,24},{8,0},{16,8},{24,16},{1,25},{9,1},{17,9},{25,17},{2,26},{10... | collective-permute-start | bytes 1179656 | tf_op jit(solution)/shard_map/ppermute | solution.py:25
  157.4 5.6 %collective-permute-done.22 = bf16[4,48,1024]{2,1,0:T(8,128)(2,1)S(1)} collective-permute-done((bf16[4,48,1024]{2,1,0:T(8,128)(2,1)S(1)}, bf16[4,48,1024]{2,1,0:T(8,128)(2,1)S(1)}, u32[]{:S(2)}, u32[]{:S(2)}) %collective-permute-start.22) | collective-permute-done | bytes 393248 | tf_op jit(solution)/shard_map/ppermute | solution.py:24
  173.7 31.9 %all_to_all.5 = bf16[4,128,2048]{2,1,0:T(8,128)(2,1)S(1)} all-to-all(bf16[4,128,2048]{2,1,0:T(8,128)(2,1)S(1)} %add_convert_fusion), channel_id=1, replica_groups=mesh['yhi'=2,'core'=2,'x'=4,'z'=4,'ylo'=2] {'yhi','ylo'}, dimensions={0} | all-to-all | bytes 4194304 | tf_op jit(solution)/shard_map/all_to_all | solution.py:120
  (118 shorter events, 57.7 us)
Async XLA Ops:
  6.5 95.7 %all-gather.3.cloned.1.call-start = ((), (), s32[]{:S(2)}) async-start(), calls=%async_computation.1 | async-start | bytes 2949120 | tf_op jit(solution)/shard_map/all_gather | solution.py:67
  9.2 15.1 %collective-permute-start.5 = (bf16[3,48,2048]{2,1,0:T(8,128)(2,1)S(1)}, bf16[3,48,2048]{2,1,0:T(8,128)(2,1)S(1)}, u32[]{:S(2)}, u32[]{:S(2)}) collective-permute-start(bf16[3,48,2048]{2,1,0:T(8,128)(2,1)S(1)} %get-tuple-element.45), channel_id=1, source_target_pairs={{0,1},{1,0},{2,3},{3,2},{4,5},{5,4},{6,7},{7,6},{8,9},{9,8},{10,11... | collective-permute-start | bytes 1769480 | tf_op jit(solution)/shard_map/ppermute | solution.py:43
  11.0 17.1 %collective-permute-start.2 = (bf16[3,48,2048]{2,1,0:T(8,128)(2,1)S(1)}, bf16[3,48,2048]{2,1,0:T(8,128)(2,1)S(1)}, u32[]{:S(2)}, u32[]{:S(2)}) collective-permute-start(bf16[3,48,2048]{2,1,0:T(8,128)(2,1)S(1)} %bitcast.97), channel_id=1, source_target_pairs={{0,2},{2,4},{4,6},{6,0},{1,3},{3,5},{5,7},{7,1},{8,10},{10,12},{12... | collective-permute-start | bytes 1769480 | tf_op jit(solution)/shard_map/ppermute | solution.py:16
  12.9 17.6 %collective-permute-start.1 = (bf16[3,48,2048]{2,1,0:T(8,128)(2,1)S(1)}, bf16[3,48,2048]{2,1,0:T(8,128)(2,1)S(1)}, u32[]{:S(2)}, u32[]{:S(2)}) collective-permute-start(bf16[3,48,2048]{2,1,0:T(8,128)(2,1)S(1)} %bitcast.98), channel_id=1, source_target_pairs={{0,6},{2,0},{4,2},{6,4},{1,7},{3,1},{5,3},{7,5},{8,14},{10,8},{12,... | collective-permute-start | bytes 1769480 | tf_op jit(solution)/shard_map/ppermute | solution.py:16
  24.3 15.4 %collective-permute-start.7 = (bf16[3,48,2048]{2,1,0:T(8,128)(2,1)S(1)}, bf16[3,48,2048]{2,1,0:T(8,128)(2,1)S(1)}, u32[]{:S(2)}, u32[]{:S(2)}) collective-permute-start(bf16[3,48,2048]{2,1,0:T(8,128)(2,1)S(1)} %collective-permute-done.5), channel_id=1, source_target_pairs={{0,8},{8,16},{16,24},{24,0},{1,9},{9,17},{17,25},{25,1},{2,10},{10... | collective-permute-start | bytes 1769480 | tf_op jit(solution)/shard_map/ppermute | solution.py:16
  26.0 14.3 %collective-permute-start.6 = (bf16[3,48,2048]{2,1,0:T(8,128)(2,1)S(1)}, bf16[3,48,2048]{2,1,0:T(8,128)(2,1)S(1)}, u32[]{:S(2)}, u32[]{:S(2)}) collective-permute-start(bf16[3,48,2048]{2,1,0:T(8,128)(2,1)S(1)} %collective-permute-done.5), channel_id=1, source_target_pairs={{0,24},{8,0},{16,8},{24,16},{1,25},{9,1},{17,9},{25,17},{2,26},{10... | collective-permute-start | bytes 1769480 | tf_op jit(solution)/shard_map/ppermute | solution.py:16
  28.9 14.2 %collective-permute-start.3 = (bf16[3,48,1024]{2,1,0:T(8,128)(2,1)}, bf16[3,48,1024]{2,1,0:T(8,128)(2,1)}, u32[]{:S(2)}, u32[]{:S(2)}) collective-permute-start(bf16[3,48,1024]{2,1,0:T(8,128)(2,1)} %slice.126), channel_id=1, source_target_pairs={{0,2},{2,4},{4,6},{6,0},{1,3},{3,5},{5,7},{7,1},{8,10},{10,12},{12... | collective-permute-start | bytes 884744 | tf_op jit(solution)/shard_map/ppermute | solution.py:24
  31.3 11.8 %collective-permute-start.4 = (bf16[3,48,1024]{2,1,0:T(8,128)(2,1)}, bf16[3,48,1024]{2,1,0:T(8,128)(2,1)}, u32[]{:S(2)}, u32[]{:S(2)}) collective-permute-start(bf16[3,48,1024]{2,1,0:T(8,128)(2,1)} %slice.127), channel_id=1, source_target_pairs={{0,6},{2,0},{4,2},{6,4},{1,7},{3,1},{5,3},{7,5},{8,14},{10,8},{12,... | collective-permute-start | bytes 884744 | tf_op jit(solution)/shard_map/ppermute | solution.py:25
  50.8 33.8 %collective-permute-start.10 = (bf16[4,2,48,2048]{3,2,1,0:T(8,128)(2,1)}, bf16[4,2,48,2048]{3,2,1,0:T(8,128)(2,1)}, u32[]{:S(2)}, u32[]{:S(2)}) collective-permute-start(bf16[4,2,48,2048]{3,2,1,0:T(8,128)(2,1)} %get-tuple-element.44), channel_id=1, source_target_pairs={{0,24},{8,0},{16,8},{24,16},{1,25},{9,1},{17,9},{25,17},{2,26},{10... | collective-permute-start | bytes 4718600 | tf_op jit(solution)/shard_map/ppermute | solution.py:16
  53.8 36.6 %collective-permute-start.11 = (bf16[4,2,48,2048]{3,2,1,0:T(8,128)(2,1)}, bf16[4,2,48,2048]{3,2,1,0:T(8,128)(2,1)}, u32[]{:S(2)}, u32[]{:S(2)}) collective-permute-start(bf16[4,2,48,2048]{3,2,1,0:T(8,128)(2,1)} %get-tuple-element.44), channel_id=1, source_target_pairs={{0,8},{8,16},{16,24},{24,0},{1,9},{9,17},{17,25},{25,1},{2,10},{10... | collective-permute-start | bytes 4718600 | tf_op jit(solution)/shard_map/ppermute | solution.py:16
  55.9 36.6 %collective-permute-start.14 = (bf16[4,2,48,2048]{3,2,1,0:T(8,128)(2,1)}, bf16[4,2,48,2048]{3,2,1,0:T(8,128)(2,1)}, u32[]{:S(2)}, u32[]{:S(2)}) collective-permute-start(bf16[4,2,48,2048]{3,2,1,0:T(8,128)(2,1)} %get-tuple-element.42), channel_id=1, source_target_pairs={{0,6},{2,0},{4,2},{6,4},{1,7},{3,1},{5,3},{7,5},{8,14},{10,8},{12,... | collective-permute-start | bytes 4718600 | tf_op jit(solution)/shard_map/ppermute | solution.py:16
  60.1 38.7 %collective-permute-start.15 = (bf16[4,2,48,2048]{3,2,1,0:T(8,128)(2,1)}, bf16[4,2,48,2048]{3,2,1,0:T(8,128)(2,1)}, u32[]{:S(2)}, u32[]{:S(2)}) collective-permute-start(bf16[4,2,48,2048]{3,2,1,0:T(8,128)(2,1)} %get-tuple-element.42), channel_id=1, source_target_pairs={{0,2},{2,4},{4,6},{6,0},{1,3},{3,5},{5,7},{7,1},{8,10},{10,12},{12... | collective-permute-start | bytes 4718600 | tf_op jit(solution)/shard_map/ppermute | solution.py:16
  86.7 16.7 %collective-permute-start.13 = (bf16[4,2,48,1024]{3,2,1,0:T(8,128)(2,1)}, bf16[4,2,48,1024]{3,2,1,0:T(8,128)(2,1)}, u32[]{:S(2)}, u32[]{:S(2)}) collective-permute-start(bf16[4,2,48,1024]{3,2,1,0:T(8,128)(2,1)} %slice.131), channel_id=1, source_target_pairs={{0,24},{8,0},{16,8},{24,16},{1,25},{9,1},{17,9},{25,17},{2,26},{10... | collective-permute-start | bytes 2359304 | tf_op jit(solution)/shard_map/ppermute | solution.py:25
  92.5 16.4 %collective-permute-start.12 = (bf16[4,2,48,1024]{3,2,1,0:T(8,128)(2,1)}, bf16[4,2,48,1024]{3,2,1,0:T(8,128)(2,1)}, u32[]{:S(2)}, u32[]{:S(2)}) collective-permute-start(bf16[4,2,48,1024]{3,2,1,0:T(8,128)(2,1)} %slice.130), channel_id=1, source_target_pairs={{0,8},{8,16},{16,24},{24,0},{1,9},{9,17},{17,25},{25,1},{2,10},{10... | collective-permute-start | bytes 2359304 | tf_op jit(solution)/shard_map/ppermute | solution.py:24
  94.6 17.0 %collective-permute-start.17 = (bf16[4,2,48,1024]{3,2,1,0:T(8,128)(2,1)}, bf16[4,2,48,1024]{3,2,1,0:T(8,128)(2,1)}, u32[]{:S(2)}, u32[]{:S(2)}) collective-permute-start(bf16[4,2,48,1024]{3,2,1,0:T(8,128)(2,1)} %slice.133), channel_id=1, source_target_pairs={{0,6},{2,0},{4,2},{6,4},{1,7},{3,1},{5,3},{7,5},{8,14},{10,8},{12,... | collective-permute-start | bytes 2359304 | tf_op jit(solution)/shard_map/ppermute | solution.py:25
  100.9 16.1 %collective-permute-start.16 = (bf16[4,2,48,1024]{3,2,1,0:T(8,128)(2,1)}, bf16[4,2,48,1024]{3,2,1,0:T(8,128)(2,1)}, u32[]{:S(2)}, u32[]{:S(2)}) collective-permute-start(bf16[4,2,48,1024]{3,2,1,0:T(8,128)(2,1)} %slice.132), channel_id=1, source_target_pairs={{0,2},{2,4},{4,6},{6,0},{1,3},{3,5},{5,7},{7,1},{8,10},{10,12},{12... | collective-permute-start | bytes 2359304 | tf_op jit(solution)/shard_map/ppermute | solution.py:24
  102.2 31.1 %collective-permute-start = (bf16[4,144,2048]{2,1,0:T(8,128)(2,1)}, bf16[4,144,2048]{2,1,0:T(8,128)(2,1)S(1)}, u32[]{:S(2)}, u32[]{:S(2)}) collective-permute-start(bf16[4,144,2048]{2,1,0:T(8,128)(2,1)} %bitcast.82), channel_id=1, source_target_pairs={{0,32},{32,0},{1,33},{33,1},{2,34},{34,2},{3,35},{35,3},{4,36},{36... | collective-permute-start | bytes 7077896 | tf_op jit(solution)/shard_map/ppermute | solution.py:68
  124.7 16.0 %collective-permute-start.19 = (bf16[4,48,2048]{2,1,0:T(8,128)(2,1)S(1)}, bf16[4,48,2048]{2,1,0:T(8,128)(2,1)S(1)}, u32[]{:S(2)}, u32[]{:S(2)}) collective-permute-start(bf16[4,48,2048]{2,1,0:T(8,128)(2,1)S(1)} %slice_bitcast_fusion.1), channel_id=1, source_target_pairs={{0,24},{8,0},{16,8},{24,16},{1,25},{9,1},{17,9},{25,17},{2,26},{10... | collective-permute-start | bytes 2359304 | tf_op jit(solution)/shard_map/ppermute | solution.py:16
  127.7 14.5 %collective-permute-start.18 = (bf16[4,48,2048]{2,1,0:T(8,128)(2,1)S(1)}, bf16[4,48,2048]{2,1,0:T(8,128)(2,1)}, u32[]{:S(2)}, u32[]{:S(2)}) collective-permute-start(bf16[4,48,2048]{2,1,0:T(8,128)(2,1)S(1)} %slice_bitcast_fusion.1), channel_id=1, source_target_pairs={{0,8},{8,16},{16,24},{24,0},{1,9},{9,17},{17,25},{25,1},{2,10},{10... | collective-permute-start | bytes 2359304 | tf_op jit(solution)/shard_map/ppermute | solution.py:16
  127.7 14.5 %collective-permute-start.21 = (bf16[4,48,2048]{2,1,0:T(8,128)(2,1)S(1)}, bf16[4,48,2048]{2,1,0:T(8,128)(2,1)S(1)}, u32[]{:S(2)}, u32[]{:S(2)}) collective-permute-start(bf16[4,48,2048]{2,1,0:T(8,128)(2,1)S(1)} %slice_bitcast_fusion), channel_id=1, source_target_pairs={{0,6},{2,0},{4,2},{6,4},{1,7},{3,1},{5,3},{7,5},{8,14},{10,8},{12,... | collective-permute-start | bytes 2359304 | tf_op jit(solution)/shard_map/ppermute | solution.py:16
  127.7 14.5 %collective-permute-start.20 = (bf16[4,48,2048]{2,1,0:T(8,128)(2,1)S(1)}, bf16[4,48,2048]{2,1,0:T(8,128)(2,1)S(1)}, u32[]{:S(2)}, u32[]{:S(2)}) collective-permute-start(bf16[4,48,2048]{2,1,0:T(8,128)(2,1)S(1)} %slice_bitcast_fusion), channel_id=1, source_target_pairs={{0,2},{2,4},{4,6},{6,0},{1,3},{3,5},{5,7},{7,1},{8,10},{10,12},{12... | collective-permute-start | bytes 2359304 | tf_op jit(solution)/shard_map/ppermute | solution.py:16
  150.8 15.6 %collective-permute-start.24 = (bf16[4,48,1024]{2,1,0:T(8,128)(2,1)S(1)}, bf16[4,48,1024]{2,1,0:T(8,128)(2,1)S(1)}, u32[]{:S(2)}, u32[]{:S(2)}) collective-permute-start(bf16[4,48,1024]{2,1,0:T(8,128)(2,1)S(1)} %slice.115), channel_id=1, source_target_pairs={{0,2},{2,4},{4,6},{6,0},{1,3},{3,5},{5,7},{7,1},{8,10},{10,12},{12... | collective-permute-start | bytes 1179656 | tf_op jit(solution)/shard_map/ppermute | solution.py:24
  151.3 15.2 %collective-permute-start.25 = (bf16[4,48,1024]{2,1,0:T(8,128)(2,1)S(1)}, bf16[4,48,1024]{2,1,0:T(8,128)(2,1)S(1)}, u32[]{:S(2)}, u32[]{:S(2)}) collective-permute-start(bf16[4,48,1024]{2,1,0:T(8,128)(2,1)S(1)} %slice.116), channel_id=1, source_target_pairs={{0,6},{2,0},{4,2},{6,4},{1,7},{3,1},{5,3},{7,5},{8,14},{10,8},{12,... | collective-permute-start | bytes 1179656 | tf_op jit(solution)/shard_map/ppermute | solution.py:25
  154.1 9.0 %collective-permute-start.22 = (bf16[4,48,1024]{2,1,0:T(8,128)(2,1)S(1)}, bf16[4,48,1024]{2,1,0:T(8,128)(2,1)S(1)}, u32[]{:S(2)}, u32[]{:S(2)}) collective-permute-start(bf16[4,48,1024]{2,1,0:T(8,128)(2,1)S(1)} %slice.112), channel_id=1, source_target_pairs={{0,8},{8,16},{16,24},{24,0},{1,9},{9,17},{17,25},{25,1},{2,10},{10... | collective-permute-start | bytes 1179656 | tf_op jit(solution)/shard_map/ppermute | solution.py:24
  (20 other events, 209.2 us)
Sparse Core Ops, SparseCore 0:
  34.5 32.1 all-gather.2

commit v16 on v12

--- a/solution.py
+++ b/solution.py
@@ -16,7 +16,7 @@
     return lax.ppermute(value, axis, perm=AHEAD), lax.ppermute(value, axis, perm=BEHIND)
 
 
-def far_hop(value, near, axis):
+def far_pieces(value, near, axis):
     from_minus, from_plus = near
     half = value.shape[-1] // 2
     far = jnp.concatenate(
@@ -26,7 +26,11 @@
         ],
         axis=-1,
     )
-    return jnp.stack([value, from_plus, far, from_minus])
+    return (value, from_plus, far, from_minus)
+
+
+def far_hop(value, near, axis):
+    return jnp.stack(far_pieces(value, near, axis))
 
 
 def ring_of_four(value, axis):
@@ -44,11 +48,13 @@
     first_a = ring_of_four(keep, "z")
     first_b = ring_of_four(got, "x")
     first_a, first_b = lax.optimization_barrier((first_a, first_b))
-    gate_up_a = ring_of_four(first_a[:, :2], "x")
-    gate_up_b = ring_of_four(first_b[:, :2], "z")
+    lead_a, lead_b = first_a[:, :2], first_b[:, :2]
+    gate_up_a = far_pieces(lead_a, first_hop(lead_a, "x"), "x")
+    gate_up_b = far_pieces(lead_b, first_hop(lead_b, "z"), "z")
     gate_up_a, gate_up_b, down_a, down_b = lax.optimization_barrier(
         (gate_up_a, gate_up_b, first_a[:, 2], first_b[:, 2])
     )
+    gate_up_a, gate_up_b = jnp.stack(gate_up_a), jnp.stack(gate_up_b)
     width = stacked.shape[-1]
     gate_ups = [jnp.moveaxis(g, 2, 0).reshape(2, -1, width) for g in (gate_up_a, gate_up_b)]
     return gate_ups, (down_a, first_hop(down_a, "x")), (down_b, first_hop(down_b, "z"))

time: 205 us -> 199 us (0.971)
  local copies, waits for them, and re-layouts: 32.1 us -> 27.9 us
    ppermute x6, waiting for transfers between devices: 8.22 us -> 29.3 us  [first_hop(): lax.ppermute(value, axis, perm=AHEAD)]
    ppermute x6, waiting for transfers between devices: 18.2 us -> 0.02 us  [first_hop(): lax.ppermute(value, axis, perm=BEHIND)]
    another operation x13 -> x9, other arithmetic: 13.1 us -> 3.95 us  [the longest x8 3.94 us: far_hop(): return jnp.stack(far_pieces(value, near, axis))]
    transpose x0 -> x2, other arithmetic: none -> 6.67 us  [expert_weights(): jnp.moveaxis(g, 2, 0).reshape(2, -1, width)]
    another operation x2 -> x0, local copies, waits for them, and re-layouts: 4.38 us -> none  [far_hop(): return jnp.stack([value, from_plus, far, from_minus])]
    ppermute x12, waiting for transfers between devices: 18.9 us -> 15.1 us  [the longest x6 12.4 us: far_pieces(): lax.ppermute(from_minus[..., :half], axis, perm=AHEAD)]
    concatenate x0 -> x2, other arithmetic: none -> 2.96 us  [far_pieces(): jnp.concatenate([lax.ppermute(from_minus[..., :half], axis, perm=AHEAD),...]
    slice x12 -> x14, local copies, waits for them, and re-layouts: 12.5 us -> 15.2 us  [the longest x6 6.27 us: far_pieces(): from_minus[..., :half]]
  transfers between devices with their start and end apart: 28 -> 28, of which waited for: 10 -> 11; matrix products, arithmetic and copies ran while one was open for 27% -> 24% of each run, Pallas kernels for 0% -> 0%
where the time goes in v16:
time: 199 us; the launch traced here: 198 us
  waiting for transfers between devices  54.2 us (27%)
  starting transfers between devices  47.1 us (24%)
  blocking collectives  30.9 us (16%)
  local copies, waits for them, and re-layouts  27.9 us (14%)
  matrix products  21.6 us (11%)
  other arithmetic  15.8 us (8%)
    all_to_all x1, blocking collectives, per_device(): lax.all_to_all(partial, CHIPS, split_axis=0, concat_axis=0, tiled=True)  30.9 us
    ppermute x6, waiting for transfers between devices, first_hop(): lax.ppermute(value, axis, perm=AHEAD)  29.3 us
    ppermute x6, starting transfers between devices, far_pieces(): lax.ppermute(from_plus[..., half:], axis, perm=BEHIND)  17.2 us
    ppermute x6, starting transfers between devices, first_hop(): lax.ppermute(value, axis, perm=BEHIND)  12.7 us
    ppermute x6, waiting for transfers between devices, far_pieces(): lax.ppermute(from_minus[..., :half], axis, perm=AHEAD)  12.4 us
    ppermute x1, waiting for transfers between devices, expert_weights(): got = lax.ppermute(send, 'ylo', perm=SWAP)  9.29 us
    ppermute x6, starting transfers between devices, first_hop(): lax.ppermute(value, axis, perm=AHEAD)  7.89 us
    dot_general x2, matrix products, per_device(): jnp.dot(late_rows, weights[1].T, preferred_element_type=jnp.float32)  7.39 us
  transfers between devices with their start and end apart: 28, of which 11 were waited for; matrix products, arithmetic and copies ran while one was open for 24% of the time, Pallas kernels for 0%

profile of v16, /device:TPU:0, one launch (start us, length us, event | category | flops | bytes accessed | tf_op | source)
XLA Modules:
  0.0 198.0 jit_solution(16931303667000877307)
XLA Ops:
  6.3 2.1 %collective-permute-start.1 = (bf16[3,48,2048]{2,1,0:T(8,128)(2,1)S(1)}, bf16[3,48,2048]{2,1,0:T(8,128)(2,1)S(1)}, u32[]{:S(2)}, u32[]{:S(2)}) collective-permute-start(bf16[3,48,2048]{2,1,0:T(8,128)(2,1)S(1)} %bitcast.92), channel_id=1, source_target_pairs={{0,6},{2,0},{4,2},{6,4},{1,7},{3,1},{5,3},{7,5},{8,14},{10,8},{12,... | collective-permute-start | bytes 1769480 | tf_op jit(solution)/shard_map/ppermute | solution.py:16
  8.5 9.3 %collective-permute-done.5 = bf16[3,48,2048]{2,1,0:T(8,128)(2,1)S(1)} collective-permute-done((bf16[3,48,2048]{2,1,0:T(8,128)(2,1)S(1)}, bf16[3,48,2048]{2,1,0:T(8,128)(2,1)S(1)}, u32[]{:S(2)}, u32[]{:S(2)}) %collective-permute-start.5) | collective-permute-done | bytes 589856 | tf_op jit(solution)/shard_map/ppermute | solution.py:47
  23.2 2.2 %collective-permute-start.4 = (bf16[3,48,1024]{2,1,0:T(8,128)(2,1)S(1)}, bf16[3,48,1024]{2,1,0:T(8,128)(2,1)S(1)}, u32[]{:S(2)}, u32[]{:S(2)}) collective-permute-start(bf16[3,48,1024]{2,1,0:T(8,128)(2,1)S(1)} %slice.126), channel_id=1, source_target_pairs={{0,6},{2,0},{4,2},{6,4},{1,7},{3,1},{5,3},{7,5},{8,14},{10,8},{12,... | collective-permute-start | bytes 884744 | tf_op jit(solution)/shard_map/ppermute | solution.py:25
  25.4 7.7 %collective-permute-done.7 = bf16[3,48,2048]{2,1,0:T(8,128)(2,1)S(1)} collective-permute-done((bf16[3,48,2048]{2,1,0:T(8,128)(2,1)S(1)}, bf16[3,48,2048]{2,1,0:T(8,128)(2,1)S(1)}, u32[]{:S(2)}, u32[]{:S(2)}) %collective-permute-start.7) | collective-permute-done | bytes 589856 | tf_op jit(solution)/shard_map/ppermute | solution.py:16
  33.7 2.8 %collective-permute-start.9 = (bf16[3,48,1024]{2,1,0:T(8,128)(2,1)S(1)}, bf16[3,48,1024]{2,1,0:T(8,128)(2,1)S(1)}, u32[]{:S(2)}, u32[]{:S(2)}) collective-permute-start(bf16[3,48,1024]{2,1,0:T(8,128)(2,1)S(1)} %slice.128), channel_id=1, source_target_pairs={{0,24},{8,0},{16,8},{24,16},{1,25},{9,1},{17,9},{25,17},{2,26},{10... | collective-permute-start | bytes 884744 | tf_op jit(solution)/shard_map/ppermute | solution.py:25
  36.9 4.4 %collective-permute-done.8 = bf16[3,48,1024]{2,1,0:T(8,128)(2,1)S(1)} collective-permute-done((bf16[3,48,1024]{2,1,0:T(8,128)(2,1)S(1)}, bf16[3,48,1024]{2,1,0:T(8,128)(2,1)S(1)}, u32[]{:S(2)}, u32[]{:S(2)}) %collective-permute-start.8) | collective-permute-done | bytes 294944 | tf_op jit(solution)/shard_map/ppermute | solution.py:24
  43.1 2.1 %collective-permute-start.15 = (bf16[4,2,48,2048]{3,2,1,0:T(8,128)(2,1)}, bf16[4,2,48,2048]{3,2,1,0:T(8,128)(2,1)}, u32[]{:S(2)}, u32[]{:S(2)}) collective-permute-start(bf16[4,2,48,2048]{3,2,1,0:T(8,128)(2,1)} %slice.102), channel_id=1, source_target_pairs={{0,2},{2,4},{4,6},{6,0},{1,3},{3,5},{5,7},{7,1},{8,10},{10,12},{12... | collective-permute-start | bytes 4718600 | tf_op jit(solution)/shard_map/ppermute | solution.py:16
  45.2 2.1 %collective-permute-start.14 = (bf16[4,2,48,2048]{3,2,1,0:T(8,128)(2,1)}, bf16[4,2,48,2048]{3,2,1,0:T(8,128)(2,1)}, u32[]{:S(2)}, u32[]{:S(2)}) collective-permute-start(bf16[4,2,48,2048]{3,2,1,0:T(8,128)(2,1)} %slice.102), channel_id=1, source_target_pairs={{0,6},{2,0},{4,2},{6,4},{1,7},{3,1},{5,3},{7,5},{8,14},{10,8},{12,... | collective-permute-start | bytes 4718600 | tf_op jit(solution)/shard_map/ppermute | solution.py:16
  49.1 2.8 %collective-permute-start.10 = (bf16[4,2,48,2048]{3,2,1,0:T(8,128)(2,1)}, bf16[4,2,48,2048]{3,2,1,0:T(8,128)(2,1)}, u32[]{:S(2)}, u32[]{:S(2)}) collective-permute-start(bf16[4,2,48,2048]{3,2,1,0:T(8,128)(2,1)} %slice.99), channel_id=1, source_target_pairs={{0,24},{8,0},{16,8},{24,16},{1,25},{9,1},{17,9},{25,17},{2,26},{10... | collective-permute-start | bytes 4718600 | tf_op jit(solution)/shard_map/ppermute | solution.py:16
  53.8 4.5 %all-to-all-start = ((bf16[4,144,2048]{2,1,0:T(8,128)(2,1)}), bf16[4,144,2048]{2,1,0:T(8,128)(2,1)}, u32[]{:S(2)}, u32[]{:S(2)}) async-start(bf16[4,144,2048]{2,1,0:T(8,128)(2,1)} %broadcast_in_dim.23), calls=%async_computation | async-start | bytes 4718592 | tf_op jit(solution)/shard_map/all_to_all | solution.py:73
  58.3 21.0 %collective-permute-done.15 = bf16[4,2,48,2048]{3,2,1,0:T(8,128)(2,1)} collective-permute-done((bf16[4,2,48,2048]{3,2,1,0:T(8,128)(2,1)}, bf16[4,2,48,2048]{3,2,1,0:T(8,128)(2,1)}, u32[]{:S(2)}, u32[]{:S(2)}) %collective-permute-start.15) | collective-permute-done | bytes 1572896 | tf_op jit(solution)/shard_map/ppermute | solution.py:16
  83.5 3.2 %collective-permute-start.17 = (bf16[4,2,48,1024]{3,2,1,0:T(8,128)(2,1)}, bf16[4,2,48,1024]{3,2,1,0:T(8,128)(2,1)}, u32[]{:S(2)}, u32[]{:S(2)}) collective-permute-start(bf16[4,2,48,1024]{3,2,1,0:T(8,128)(2,1)} %slice.132), channel_id=1, source_target_pairs={{0,6},{2,0},{4,2},{6,4},{1,7},{3,1},{5,3},{7,5},{8,14},{10,8},{12,... | collective-permute-start | bytes 2359304 | tf_op jit(solution)/shard_map/ppermute | solution.py:25
  92.4 3.0 %collective-permute-start.13 = (bf16[4,2,48,1024]{3,2,1,0:T(8,128)(2,1)}, bf16[4,2,48,1024]{3,2,1,0:T(8,128)(2,1)}, u32[]{:S(2)}, u32[]{:S(2)}) collective-permute-start(bf16[4,2,48,1024]{3,2,1,0:T(8,128)(2,1)} %slice.130), channel_id=1, source_target_pairs={{0,24},{8,0},{16,8},{24,16},{1,25},{9,1},{17,9},{25,17},{2,26},{10... | collective-permute-start | bytes 2359304 | tf_op jit(solution)/shard_map/ppermute | solution.py:25
  101.7 5.2 %collective-permute-done.12 = bf16[4,2,48,1024]{3,2,1,0:T(8,128)(2,1)} collective-permute-done((bf16[4,2,48,1024]{3,2,1,0:T(8,128)(2,1)}, bf16[4,2,48,1024]{3,2,1,0:T(8,128)(2,1)}, u32[]{:S(2)}, u32[]{:S(2)}) %collective-permute-start.12) | collective-permute-done | bytes 786464 | tf_op jit(solution)/shard_map/ppermute | solution.py:24
  109.8 3.8 %collective-permute-start.19 = (bf16[4,48,2048]{2,1,0:T(8,128)(2,1)S(1)}, bf16[4,48,2048]{2,1,0:T(8,128)(2,1)}, u32[]{:S(2)}, u32[]{:S(2)}) collective-permute-start(bf16[4,48,2048]{2,1,0:T(8,128)(2,1)S(1)} %slice_bitcast_fusion.1), channel_id=1, source_target_pairs={{0,24},{8,0},{16,8},{24,16},{1,25},{9,1},{17,9},{25,17},{2,26},{10... | collective-permute-start | bytes 2359304 | tf_op jit(solution)/shard_map/ppermute | solution.py:16
  115.6 3.3 %maximum_bitcast_fusion = bf16[2,4,4,48,2048]{4,3,0,2,1:T(8,128)(2,1)S(1)} fusion(bf16[1,4,2,48,2048]{4,3,2,1,0:T(8,128)(2,1)} %bitcast.19, bf16[1,4,2,48,2048]{4,3,2,1,0:T(8,128)(2,1)S(1)} %bitcast.78, bf16[1,4,2,48,2048]{4,3,2,1,0:T(8,128)(2,1)} %bitcast.17, bf16[1,4,2,48,2048]{4,3,2,1,0:T(8,128)(2,1)} %bitcast.16), kind=kLoop, calls=%fused_computation | loop fusion | flops 9437184 | bytes 12582912 | tf_op jit(solution)/shard_map/transpose | solution.py:59
  118.9 3.3 %maximum_bitcast_fusion.1 = bf16[2,4,4,48,2048]{4,3,0,2,1:T(8,128)(2,1)S(1)} fusion(bf16[1,4,2,48,2048]{4,3,2,1,0:T(8,128)(2,1)} %bitcast.26, bf16[1,4,2,48,2048]{4,3,2,1,0:T(8,128)(2,1)S(1)} %bitcast.77, bf16[1,4,2,48,2048]{4,3,2,1,0:T(8,128)(2,1)} %bitcast.24, bf16[1,4,2,48,2048]{4,3,2,1,0:T(8,128)(2,1)} %bitcast.23), kind=kLoop, calls=%fused_computation.1 | loop fusion | flops 9437184 | bytes 12582912 | tf_op jit(solution)/shard_map/transpose | solution.py:59
  126.7 3.4 %fusion.17 = f32[1024,768]{1,0:T(8,128)S(1)} fusion(bf16[1024,2048]{1,0:T(8,128)(2,1)S(1)} %bitcast.79, bf16[768,2048]{1,0:T(8,128)(2,1)S(1)} %bitcast.90), kind=kOutput, calls=%fused_computation.55 | convolution fusion | flops 3221225472 | bytes 10485760 | tf_op jit(solution)/shard_map/dot_general | solution.py:103
  130.2 3.4 %fusion.18 = f32[1024,768]{1,0:T(8,128)S(1)} fusion(bf16[1024,2048]{1,0:T(8,128)(2,1)S(1)} %bitcast.80, bf16[768,2048]{1,0:T(8,128)(2,1)S(1)} %bitcast.89), kind=kOutput, calls=%fused_computation.56 | convolution fusion | flops 3221225472 | bytes 10485760 | tf_op jit(solution)/shard_map/dot_general | solution.py:103
  133.7 3.7 %multiply_convert_fusion.1 = bf16[1024,768]{1,0:T(8,128)(2,1)S(1)} fusion(f32[1024,768]{1,0:T(8,128)S(1)} %fusion.17, bf16[1024,2048]{1,0:T(8,128)(2,1)S(1)} %bitcast.81, bf16[768,2048]{1,0:T(8,128)(2,1)S(1)} %bitcast.88), kind=kOutput, calls=%fused_computation.10 | convolution fusion | flops 3225944064 | bytes 12058624 | tf_op jit(solution)/shard_map/dot_general | solution.py:109
  141.6 3.2 %collective-permute-start.25 = (bf16[4,48,1024]{2,1,0:T(8,128)(2,1)S(1)}, bf16[4,48,1024]{2,1,0:T(8,128)(2,1)S(1)}, u32[]{:S(2)}, u32[]{:S(2)}) collective-permute-start(bf16[4,48,1024]{2,1,0:T(8,128)(2,1)S(1)} %slice.116), channel_id=1, source_target_pairs={{0,6},{2,0},{4,2},{6,4},{1,7},{3,1},{5,3},{7,5},{8,14},{10,8},{12,... | collective-permute-start | bytes 1179656 | tf_op jit(solution)/shard_map/ppermute | solution.py:25
  145.4 2.7 %collective-permute-start.23 = (bf16[4,48,1024]{2,1,0:T(8,128)(2,1)S(1)}, bf16[4,48,1024]{2,1,0:T(8,128)(2,1)S(1)}, u32[]{:S(2)}, u32[]{:S(2)}) collective-permute-start(bf16[4,48,1024]{2,1,0:T(8,128)(2,1)S(1)} %slice.113), channel_id=1, source_target_pairs={{0,24},{8,0},{16,8},{24,16},{1,25},{9,1},{17,9},{25,17},{2,26},{10... | collective-permute-start | bytes 1179656 | tf_op jit(solution)/shard_map/ppermute | solution.py:25
  148.1 3.7 %multiply_convert_fusion = bf16[1024,768]{1,0:T(8,128)(2,1)S(1)} fusion(f32[1024,768]{1,0:T(8,128)S(1)} %fusion.18, bf16[1024,2048]{1,0:T(8,128)(2,1)S(1)} %bitcast.82, bf16[768,2048]{1,0:T(8,128)(2,1)S(1)} %bitcast.87), kind=kOutput, calls=%fused_computation.9 | convolution fusion | flops 3225944064 | bytes 12058624 | tf_op jit(solution)/shard_map/dot_general | solution.py:109
  165.8 30.9 %all_to_all.10 = bf16[4,128,2048]{2,1,0:T(8,128)(2,1)S(1)} all-to-all(bf16[4,128,2048]{2,1,0:T(8,128)(2,1)S(1)} %add_convert_fusion), channel_id=1, replica_groups=mesh['yhi'=2,'core'=2,'x'=4,'z'=4,'ylo'=2] {'yhi','ylo'}, dimensions={0} | all-to-all | bytes 4194304 | tf_op jit(solution)/shard_map/all_to_all | solution.py:126
  (98 shorter events, 63.3 us)
Async XLA Ops:
  2.7 15.1 %collective-permute-start.5 = (bf16[3,48,2048]{2,1,0:T(8,128)(2,1)S(1)}, bf16[3,48,2048]{2,1,0:T(8,128)(2,1)S(1)}, u32[]{:S(2)}, u32[]{:S(2)}) collective-permute-start(bf16[3,48,2048]{2,1,0:T(8,128)(2,1)S(1)} %get-tuple-element.53), channel_id=1, source_target_pairs={{0,1},{1,0},{2,3},{3,2},{4,5},{5,4},{6,7},{7,6},{8,9},{9,8},{10,11... | collective-permute-start | bytes 1769480 | tf_op jit(solution)/shard_map/ppermute | solution.py:47
  4.4 17.1 %collective-permute-start.2 = (bf16[3,48,2048]{2,1,0:T(8,128)(2,1)S(1)}, bf16[3,48,2048]{2,1,0:T(8,128)(2,1)S(1)}, u32[]{:S(2)}, u32[]{:S(2)}) collective-permute-start(bf16[3,48,2048]{2,1,0:T(8,128)(2,1)S(1)} %bitcast.91), channel_id=1, source_target_pairs={{0,2},{2,4},{4,6},{6,0},{1,3},{3,5},{5,7},{7,1},{8,10},{10,12},{12... | collective-permute-start | bytes 1769480 | tf_op jit(solution)/shard_map/ppermute | solution.py:16
  6.3 16.8 %collective-permute-start.1 = (bf16[3,48,2048]{2,1,0:T(8,128)(2,1)S(1)}, bf16[3,48,2048]{2,1,0:T(8,128)(2,1)S(1)}, u32[]{:S(2)}, u32[]{:S(2)}) collective-permute-start(bf16[3,48,2048]{2,1,0:T(8,128)(2,1)S(1)} %bitcast.92), channel_id=1, source_target_pairs={{0,6},{2,0},{4,2},{6,4},{1,7},{3,1},{5,3},{7,5},{8,14},{10,8},{12,... | collective-permute-start | bytes 1769480 | tf_op jit(solution)/shard_map/ppermute | solution.py:16
  17.7 15.4 %collective-permute-start.7 = (bf16[3,48,2048]{2,1,0:T(8,128)(2,1)S(1)}, bf16[3,48,2048]{2,1,0:T(8,128)(2,1)S(1)}, u32[]{:S(2)}, u32[]{:S(2)}) collective-permute-start(bf16[3,48,2048]{2,1,0:T(8,128)(2,1)S(1)} %collective-permute-done.5), channel_id=1, source_target_pairs={{0,8},{8,16},{16,24},{24,0},{1,9},{9,17},{17,25},{25,1},{2,10},{10... | collective-permute-start | bytes 1769480 | tf_op jit(solution)/shard_map/ppermute | solution.py:16
  19.4 14.3 %collective-permute-start.6 = (bf16[3,48,2048]{2,1,0:T(8,128)(2,1)S(1)}, bf16[3,48,2048]{2,1,0:T(8,128)(2,1)S(1)}, u32[]{:S(2)}, u32[]{:S(2)}) collective-permute-start(bf16[3,48,2048]{2,1,0:T(8,128)(2,1)S(1)} %collective-permute-done.5), channel_id=1, source_target_pairs={{0,24},{8,0},{16,8},{24,16},{1,25},{9,1},{17,9},{25,17},{2,26},{10... | collective-permute-start | bytes 1769480 | tf_op jit(solution)/shard_map/ppermute | solution.py:16
  21.5 15.0 %collective-permute-start.3 = (bf16[3,48,1024]{2,1,0:T(8,128)(2,1)S(1)}, bf16[3,48,1024]{2,1,0:T(8,128)(2,1)S(1)}, u32[]{:S(2)}, u32[]{:S(2)}) collective-permute-start(bf16[3,48,1024]{2,1,0:T(8,128)(2,1)S(1)} %slice.125), channel_id=1, source_target_pairs={{0,2},{2,4},{4,6},{6,0},{1,3},{3,5},{5,7},{7,1},{8,10},{10,12},{12... | collective-permute-start | bytes 884744 | tf_op jit(solution)/shard_map/ppermute | solution.py:24
  23.2 13.4 %collective-permute-start.4 = (bf16[3,48,1024]{2,1,0:T(8,128)(2,1)S(1)}, bf16[3,48,1024]{2,1,0:T(8,128)(2,1)S(1)}, u32[]{:S(2)}, u32[]{:S(2)}) collective-permute-start(bf16[3,48,1024]{2,1,0:T(8,128)(2,1)S(1)} %slice.126), channel_id=1, source_target_pairs={{0,6},{2,0},{4,2},{6,4},{1,7},{3,1},{5,3},{7,5},{8,14},{10,8},{12,... | collective-permute-start | bytes 884744 | tf_op jit(solution)/shard_map/ppermute | solution.py:25
  43.1 36.3 %collective-permute-start.15 = (bf16[4,2,48,2048]{3,2,1,0:T(8,128)(2,1)}, bf16[4,2,48,2048]{3,2,1,0:T(8,128)(2,1)}, u32[]{:S(2)}, u32[]{:S(2)}) collective-permute-start(bf16[4,2,48,2048]{3,2,1,0:T(8,128)(2,1)} %slice.102), channel_id=1, source_target_pairs={{0,2},{2,4},{4,6},{6,0},{1,3},{3,5},{5,7},{7,1},{8,10},{10,12},{12... | collective-permute-start | bytes 4718600 | tf_op jit(solution)/shard_map/ppermute | solution.py:16
  45.2 36.2 %collective-permute-start.14 = (bf16[4,2,48,2048]{3,2,1,0:T(8,128)(2,1)}, bf16[4,2,48,2048]{3,2,1,0:T(8,128)(2,1)}, u32[]{:S(2)}, u32[]{:S(2)}) collective-permute-start(bf16[4,2,48,2048]{3,2,1,0:T(8,128)(2,1)} %slice.102), channel_id=1, source_target_pairs={{0,6},{2,0},{4,2},{6,4},{1,7},{3,1},{5,3},{7,5},{8,14},{10,8},{12,... | collective-permute-start | bytes 4718600 | tf_op jit(solution)/shard_map/ppermute | solution.py:16
  48.7 39.2 %collective-permute-start.11 = (bf16[4,2,48,2048]{3,2,1,0:T(8,128)(2,1)}, bf16[4,2,48,2048]{3,2,1,0:T(8,128)(2,1)}, u32[]{:S(2)}, u32[]{:S(2)}) collective-permute-start(bf16[4,2,48,2048]{3,2,1,0:T(8,128)(2,1)} %slice.99), channel_id=1, source_target_pairs={{0,8},{8,16},{16,24},{24,0},{1,9},{9,17},{17,25},{25,1},{2,10},{10... | collective-permute-start | bytes 4718600 | tf_op jit(solution)/shard_map/ppermute | solution.py:16
  49.1 41.1 %collective-permute-start.10 = (bf16[4,2,48,2048]{3,2,1,0:T(8,128)(2,1)}, bf16[4,2,48,2048]{3,2,1,0:T(8,128)(2,1)}, u32[]{:S(2)}, u32[]{:S(2)}) collective-permute-start(bf16[4,2,48,2048]{3,2,1,0:T(8,128)(2,1)} %slice.99), channel_id=1, source_target_pairs={{0,24},{8,0},{16,8},{24,16},{1,25},{9,1},{17,9},{25,17},{2,26},{10... | collective-permute-start | bytes 4718600 | tf_op jit(solution)/shard_map/ppermute | solution.py:16
  53.8 42.5 %all-to-all-start = ((bf16[4,144,2048]{2,1,0:T(8,128)(2,1)}), bf16[4,144,2048]{2,1,0:T(8,128)(2,1)}, u32[]{:S(2)}, u32[]{:S(2)}) async-start(bf16[4,144,2048]{2,1,0:T(8,128)(2,1)} %broadcast_in_dim.23), calls=%async_computation | async-start | bytes 4718592 | tf_op jit(solution)/shard_map/all_to_all | solution.py:73
  81.4 17.5 %collective-permute-start.16 = (bf16[4,2,48,1024]{3,2,1,0:T(8,128)(2,1)}, bf16[4,2,48,1024]{3,2,1,0:T(8,128)(2,1)}, u32[]{:S(2)}, u32[]{:S(2)}) collective-permute-start(bf16[4,2,48,1024]{3,2,1,0:T(8,128)(2,1)} %slice.131), channel_id=1, source_target_pairs={{0,2},{2,4},{4,6},{6,0},{1,3},{3,5},{5,7},{7,1},{8,10},{10,12},{12... | collective-permute-start | bytes 2359304 | tf_op jit(solution)/shard_map/ppermute | solution.py:24
  83.5 16.7 %collective-permute-start.17 = (bf16[4,2,48,1024]{3,2,1,0:T(8,128)(2,1)}, bf16[4,2,48,1024]{3,2,1,0:T(8,128)(2,1)}, u32[]{:S(2)}, u32[]{:S(2)}) collective-permute-start(bf16[4,2,48,1024]{3,2,1,0:T(8,128)(2,1)} %slice.132), channel_id=1, source_target_pairs={{0,6},{2,0},{4,2},{6,4},{1,7},{3,1},{5,3},{7,5},{8,14},{10,8},{12,... | collective-permute-start | bytes 2359304 | tf_op jit(solution)/shard_map/ppermute | solution.py:25
  90.0 16.9 %collective-permute-start.12 = (bf16[4,2,48,1024]{3,2,1,0:T(8,128)(2,1)}, bf16[4,2,48,1024]{3,2,1,0:T(8,128)(2,1)}, u32[]{:S(2)}, u32[]{:S(2)}) collective-permute-start(bf16[4,2,48,1024]{3,2,1,0:T(8,128)(2,1)} %slice.129), channel_id=1, source_target_pairs={{0,8},{8,16},{16,24},{24,0},{1,9},{9,17},{17,25},{25,1},{2,10},{10... | collective-permute-start | bytes 2359304 | tf_op jit(solution)/shard_map/ppermute | solution.py:24
  92.4 15.9 %collective-permute-start.13 = (bf16[4,2,48,1024]{3,2,1,0:T(8,128)(2,1)}, bf16[4,2,48,1024]{3,2,1,0:T(8,128)(2,1)}, u32[]{:S(2)}, u32[]{:S(2)}) collective-permute-start(bf16[4,2,48,1024]{3,2,1,0:T(8,128)(2,1)} %slice.130), channel_id=1, source_target_pairs={{0,24},{8,0},{16,8},{24,16},{1,25},{9,1},{17,9},{25,17},{2,26},{10... | collective-permute-start | bytes 2359304 | tf_op jit(solution)/shard_map/ppermute | solution.py:25
  96.3 28.2 %collective-permute-start = (bf16[4,144,2048]{2,1,0:T(8,128)(2,1)}, bf16[4,144,2048]{2,1,0:T(8,128)(2,1)}, u32[]{:S(2)}, u32[]{:S(2)}) collective-permute-start(bf16[4,144,2048]{2,1,0:T(8,128)(2,1)} %all-to-all-done), channel_id=1, source_target_pairs={{0,32},{32,0},{1,33},{33,1},{2,34},{34,2},{3,35},{35,3},{4,36},{36... | collective-permute-start | bytes 7077896 | tf_op jit(solution)/shard_map/ppermute | solution.py:74
  109.8 23.9 %collective-permute-start.19 = (bf16[4,48,2048]{2,1,0:T(8,128)(2,1)S(1)}, bf16[4,48,2048]{2,1,0:T(8,128)(2,1)}, u32[]{:S(2)}, u32[]{:S(2)}) collective-permute-start(bf16[4,48,2048]{2,1,0:T(8,128)(2,1)S(1)} %slice_bitcast_fusion.1), channel_id=1, source_target_pairs={{0,24},{8,0},{16,8},{24,16},{1,25},{9,1},{17,9},{25,17},{2,26},{10... | collective-permute-start | bytes 2359304 | tf_op jit(solution)/shard_map/ppermute | solution.py:16
  113.6 20.1 %collective-permute-start.18 = (bf16[4,48,2048]{2,1,0:T(8,128)(2,1)S(1)}, bf16[4,48,2048]{2,1,0:T(8,128)(2,1)}, u32[]{:S(2)}, u32[]{:S(2)}) collective-permute-start(bf16[4,48,2048]{2,1,0:T(8,128)(2,1)S(1)} %slice_bitcast_fusion.1), channel_id=1, source_target_pairs={{0,8},{8,16},{16,24},{24,0},{1,9},{9,17},{17,25},{25,1},{2,10},{10... | collective-permute-start | bytes 2359304 | tf_op jit(solution)/shard_map/ppermute | solution.py:16
  113.6 20.1 %collective-permute-start.21 = (bf16[4,48,2048]{2,1,0:T(8,128)(2,1)S(1)}, bf16[4,48,2048]{2,1,0:T(8,128)(2,1)}, u32[]{:S(2)}, u32[]{:S(2)}) collective-permute-start(bf16[4,48,2048]{2,1,0:T(8,128)(2,1)S(1)} %copy-done.1), channel_id=1, source_target_pairs={{0,6},{2,0},{4,2},{6,4},{1,7},{3,1},{5,3},{7,5},{8,14},{10,8},{12,... | collective-permute-start | bytes 2359304 | tf_op jit(solution)/shard_map/ppermute | solution.py:16
  113.8 19.9 %collective-permute-start.20 = (bf16[4,48,2048]{2,1,0:T(8,128)(2,1)S(1)}, bf16[4,48,2048]{2,1,0:T(8,128)(2,1)}, u32[]{:S(2)}, u32[]{:S(2)}) collective-permute-start(bf16[4,48,2048]{2,1,0:T(8,128)(2,1)S(1)} %copy-done.1), channel_id=1, source_target_pairs={{0,2},{2,4},{4,6},{6,0},{1,3},{3,5},{5,7},{7,1},{8,10},{10,12},{12... | collective-permute-start | bytes 2359304 | tf_op jit(solution)/shard_map/ppermute | solution.py:16
  141.5 15.7 %collective-permute-start.24 = (bf16[4,48,1024]{2,1,0:T(8,128)(2,1)S(1)}, bf16[4,48,1024]{2,1,0:T(8,128)(2,1)S(1)}, u32[]{:S(2)}, u32[]{:S(2)}) collective-permute-start(bf16[4,48,1024]{2,1,0:T(8,128)(2,1)S(1)} %slice.115), channel_id=1, source_target_pairs={{0,2},{2,4},{4,6},{6,0},{1,3},{3,5},{5,7},{7,1},{8,10},{10,12},{12... | collective-permute-start | bytes 1179656 | tf_op jit(solution)/shard_map/ppermute | solution.py:24
  141.6 15.7 %collective-permute-start.25 = (bf16[4,48,1024]{2,1,0:T(8,128)(2,1)S(1)}, bf16[4,48,1024]{2,1,0:T(8,128)(2,1)S(1)}, u32[]{:S(2)}, u32[]{:S(2)}) collective-permute-start(bf16[4,48,1024]{2,1,0:T(8,128)(2,1)S(1)} %slice.116), channel_id=1, source_target_pairs={{0,6},{2,0},{4,2},{6,4},{1,7},{3,1},{5,3},{7,5},{8,14},{10,8},{12,... | collective-permute-start | bytes 1179656 | tf_op jit(solution)/shard_map/ppermute | solution.py:25
  144.8 9.0 %collective-permute-start.22 = (bf16[4,48,1024]{2,1,0:T(8,128)(2,1)S(1)}, bf16[4,48,1024]{2,1,0:T(8,128)(2,1)S(1)}, u32[]{:S(2)}, u32[]{:S(2)}) collective-permute-start(bf16[4,48,1024]{2,1,0:T(8,128)(2,1)S(1)} %slice.112), channel_id=1, source_target_pairs={{0,8},{8,16},{16,24},{24,0},{1,9},{9,17},{17,25},{25,1},{2,10},{10... | collective-permute-start | bytes 1179656 | tf_op jit(solution)/shard_map/ppermute | solution.py:24
  (9 other events, 76.5 us)
